TPU v7x, 512 devices: a whole 4x4x16 slice. The times are simulated.
512 devices in a mesh: row: 32 (over x_lo, z), col: 16 (over x_hi, y, core).
Axes of the slice: x: 4 (x_hi: 2, x_lo: 2; x = x_hi * 2 + x_lo), y: 4, z: 16, core: 2. Of those that a mesh axis runs over, the one named last changes fastest.
Arguments:
- anc_inv: float32 [12288, 12288], P('row', 'col'), may hold values from -0.0546875 to 0.0546875
- factors_first: float32 [3, 256, 12288], P(None, 'row', 'col'), may hold values from -6 to 6
- factors_second: float32 [2, 256, 12288], P(None, 'row', 'col'), may hold values from -6 to 6
- lists_first: int32 [3, 36], replicated, may hold values from 0 to 47, as said below
- lists_second: int32 [2, 36], replicated, may hold values from 0 to 47, as said below
- parents: int32 [2], replicated, may hold values from 0 to 2, as said below
- parent_link: float32 [2, 256, 256], replicated, may hold values from -0.375 to 0.375
Outputs:
- first_cols: float32 [3, 256, 12288], P(None, 'col', 'row')
- second_cols: float32 [2, 256, 12288], P(None, 'col', 'row')
Inputs may be any that keep to these rules, and one draw needn't show every extreme that they name: `lists_first`: each row holds 36 different tile indices. `lists_second`: each row holds 36 different tile indices. `parents`: the 2 entries are different first-generation indices.
All inputs are finite; a program needn't handle non-finite values.
Results may differ from a plain program's by a relative error of at most 0.000084.
Values sent between devices are 32-bit elements; how exact they have to be, the bound alone decides.
No kernel may reach another device: no remote copies, remote signals or barrier semaphores. Data moves between devices by JAX's collectives and lax.ppermute only.
A program may use at most 64 MiB of HBM per device.

v0:
```python
import jax
import jax.numpy as jnp
from jax import lax
from jax.sharding import PartitionSpec as P

highest = lax.Precision.HIGHEST


def tile_flags(block_lists, anchor, extent, tile_height):
    tile_ids = (anchor + jnp.arange(extent, dtype=jnp.int32)) // tile_height
    matches = block_lists[:, :, None] == tile_ids[None, None, :]
    return jnp.any(matches, axis=1).astype(jnp.float32)


def local(anc_inv, factors_first, factors_second, lists_first, lists_second, parents, parent_link):
    local_rows, local_cols = anc_inv.shape
    members = factors_first.shape[0]
    panel_width = parent_link.shape[1]
    share_cols = panel_width // lax.axis_size("col")
    col_index = lax.axis_index("col")
    row_anchor = lax.axis_index("row") * local_rows
    col_anchor = col_index * local_cols
    out_first = tile_flags(lists_first, row_anchor, local_rows, panel_width)
    out_second = tile_flags(lists_second, row_anchor, local_rows, panel_width)
    panel_first = (
        factors_first * tile_flags(lists_first, col_anchor, local_cols, panel_width)[:, None, :]
    )
    panel_second = (
        factors_second * tile_flags(lists_second, col_anchor, local_cols, panel_width)[:, None, :]
    )

    def apply_single(segment):
        return lax.dot_general(
            segment,
            anc_inv,
            (((1,), (1,)), ((), ())),
            precision=highest,
            preferred_element_type=jnp.float32,
        )

    def generation(panels, coupling):
        reduced = []
        for member in range(panels.shape[0]):
            partial_value = apply_single(lax.all_gather(panels[member], "row", axis=0, tiled=True))
            if coupling is not None:
                partial_value = partial_value + coupling[member]
            reduced.append(lax.psum_scatter(partial_value, "col", scatter_dimension=0, tiled=True))
        return jnp.stack(reduced)

    first_cols = -out_first[:, None, :] * generation(panel_first, None)
    selector = (parents[:, None] == jnp.arange(members, dtype=jnp.int32)[None, :]).astype(
        jnp.float32
    )
    chosen = jnp.einsum("cp,pki->cki", selector, first_cols, precision=highest)
    link_rows = lax.dynamic_slice_in_dim(parent_link, col_index * share_cols, share_cols, 1)
    coupling = jnp.einsum("cqk,cqi->cki", link_rows, chosen, precision=highest)
    second_sums = generation(panel_second, coupling)
    second_cols = -out_second[:, None, :] * second_sums
    return (first_cols, second_cols)


def solution(mesh):
    in_specs = (P("row", "col"), P(None, "row", "col"), P(None, "row", "col"), P(), P(), P(), P())
    out_specs = (P(None, "col", "row"), P(None, "col", "row"))
    return jax.shard_map(local, mesh=mesh, in_specs=in_specs, out_specs=out_specs, check_vma=False)
```

profile of v0, /device:TPU:1, one launch (start us, length us, event | category | flops | bytes accessed | tf_op | source)
XLA Modules:
  0.0 541.2 jit_solution(736146553814404786)
XLA Ops:
  7.2 0.0 copy-start
  7.2 0.0 reduce-scatter.6.cloned.1.call-start
  7.2 0.9 compare_reduce_fusion
  8.2 0.9 broadcast_multiply_fusion
  9.1 59.9 %all-gather = f32[1,256,768]{2,1,0:T(8,128)S(1)} all-gather(f32[1,8,768]{2,1,0:T(8,128)S(1)} %get-tuple-element.2), channel_id=2, replica_groups=mesh['row'=32,'col'=16] {'row'}, dimensions={1}, use_global_device_ids=true | all-gather | bytes 811008 | tf_op jit(solution)/shard_map/all_gather | solution.py:44
  69.0 0.0 copy-done
  69.0 2.2 fusion.6
  71.2 0.0 reduce-scatter.6.cloned.1.call-update
  71.2 0.0 reduce-scatter.8.cloned.1.call-start
  71.3 48.7 %all-gather.1 = f32[1,256,768]{2,1,0:T(8,128)S(1)} all-gather(f32[1,8,768]{2,1,0:T(8,128)S(1)} %get-tuple-element.4), channel_id=3, replica_groups=mesh['row'=32,'col'=16] {'row'}, dimensions={1}, use_global_device_ids=true | all-gather | bytes 811008 | tf_op jit(solution)/shard_map/all_gather | solution.py:44
  119.9 2.2 fusion.4
  122.1 0.0 reduce-scatter.8.cloned.1.call-update
  122.2 0.0 reduce-scatter.10.cloned.1.call-start
  122.2 50.8 %all-gather.2 = f32[1,256,768]{2,1,0:T(8,128)S(1)} all-gather(f32[1,8,768]{2,1,0:T(8,128)S(1)} %get-tuple-element.3), channel_id=4, replica_groups=mesh['row'=32,'col'=16] {'row'}, dimensions={1}, use_global_device_ids=true | all-gather | bytes 811008 | tf_op jit(solution)/shard_map/all_gather | solution.py:44
  173.0 0.0 copy-start.3
  173.0 0.0 copy-start.4
  173.0 0.0 copy-start.2
  173.0 2.2 fusion.2
  175.2 0.0 copy-start.5
  175.2 0.0 reduce-scatter.10.cloned.1.call-update
  175.2 0.0 reduce-scatter.12.cloned.1.call-start
  175.3 0.0 copy-done.3
  175.3 0.1 compare_reduce_fusion.2
  175.4 0.0 copy-done.4
  175.4 0.1 compare_reduce_fusion.1
  175.5 0.0 copy-done.2
  175.6 50.3 %all-gather.3 = f32[1,256,768]{2,1,0:T(8,128)S(1)} all-gather(f32[1,8,768]{2,1,0:T(8,128)S(1)} %get-tuple-element.5), channel_id=5, replica_groups=mesh['row'=32,'col'=16] {'row'}, dimensions={1}, use_global_device_ids=true | all-gather | bytes 811008 | tf_op jit(solution)/shard_map/all_gather | solution.py:44
  225.8 0.0 reduce-scatter.6.cloned.1.call-done
  225.9 30.3 %reduce-scatter.8.cloned.1.call-done = f32[16,384]{1,0:T(8,128)} async-done(((f32[256,384]{1,0:T(8,128)}), f32[16,384]{1,0:T(8,128)}) %reduce-scatter.8.cloned.1.call-update) | async-done | bytes 24592 | tf_op jit(solution)/shard_map/reduce_scatter | solution.py:47
  256.1 92.2 %reduce-scatter.10.cloned.1.call-done = f32[16,384]{1,0:T(8,128)} async-done(((f32[256,384]{1,0:T(8,128)}), f32[16,384]{1,0:T(8,128)}) %reduce-scatter.10.cloned.1.call-update) | async-done | bytes 24592 | tf_op jit(solution)/shard_map/reduce_scatter | solution.py:47
  348.3 0.8 maximum_multiply_fusion
  349.1 0.0 copy-done.5
  349.1 0.0 copy-start.1
  349.1 0.3 fusion.8
  349.4 1.6 fusion.10
  351.0 2.2 convolution_add_fusion.1
  353.2 0.0 copy-done.1
  353.2 0.0 reduce-scatter.12.cloned.1.call-update
  353.2 0.0 reduce-scatter.14.cloned.1.call-start
  353.3 53.7 %all-gather.4 = f32[1,256,768]{2,1,0:T(8,128)S(1)} all-gather(f32[1,8,768]{2,1,0:T(8,128)S(1)} %get-tuple-element.6), channel_id=6, replica_groups=mesh['row'=32,'col'=16] {'row'}, dimensions={1}, use_global_device_ids=true | all-gather | bytes 811008 | tf_op jit(solution)/shard_map/all_gather | solution.py:44
  406.9 2.2 convolution_add_fusion
  409.1 0.0 reduce-scatter.14.cloned.1.call-update
  409.2 0.1 compare_reduce_fusion.3
  409.3 31.9 %reduce-scatter.12.cloned.1.call-done = f32[16,384]{1,0:T(8,128)} async-done(((f32[256,384]{1,0:T(8,128)}), f32[16,384]{1,0:T(8,128)}) %reduce-scatter.12.cloned.1.call-update) | async-done | bytes 24592 | tf_op jit(solution)/shard_map/reduce_scatter | solution.py:47
  441.2 92.1 %reduce-scatter.14.cloned.1.call-done = f32[16,384]{1,0:T(8,128)} async-done(((f32[256,384]{1,0:T(8,128)}), f32[16,384]{1,0:T(8,128)}) %reduce-scatter.14.cloned.1.call-update) | async-done | bytes 24592 | tf_op jit(solution)/shard_map/reduce_scatter | solution.py:47
  533.3 1.4 maximum_multiply_fusion.1
  (9 shorter events, 0.1 us)
Async XLA Ops:
  7.2 61.9 %copy-start = (f32[384,768]{1,0:T(8,128)S(1)}, f32[384,768]{1,0:T(8,128)}, u32[]{:S(2)}) copy-start(f32[384,768]{1,0:T(8,128)} %param.7) | copy-start | bytes 3538948
  7.2 218.7 %reduce-scatter.6.cloned.1.call-start = ((), (), s32[]{:S(2)}) async-start(), calls=%async_computation.5 | async-start | bytes 417792 | tf_op jit(solution)/shard_map/reduce_scatter | solution.py:47
  71.2 184.9 %reduce-scatter.8.cloned.1.call-start = ((), (), s32[]{:S(2)}) async-start(), calls=%async_computation.6 | async-start | bytes 417792 | tf_op jit(solution)/shard_map/reduce_scatter | solution.py:47
  122.2 226.1 %reduce-scatter.10.cloned.1.call-start = ((), (), s32[]{:S(2)}) async-start(), calls=%async_computation.7 | async-start | bytes 417792 | tf_op jit(solution)/shard_map/reduce_scatter | solution.py:47
  173.0 2.3 copy-start.3
  173.0 2.4 copy-start.4
  173.0 2.6 copy-start.2
  175.2 173.9 %copy-start.5 = (s32[2]{0:T(128)S(1)}, s32[2]{0:T(128)}, u32[]{:S(2)}) copy-start(s32[2]{0:T(128)} %param.12) | copy-start | bytes 28
  175.2 266.0 %reduce-scatter.12.cloned.1.call-start = ((), (), s32[]{:S(2)}) async-start(), calls=%async_computation.8 | async-start | bytes 417792 | tf_op jit(solution)/shard_map/reduce_scatter | solution.py:47
  349.1 4.1 copy-start.1
  353.2 180.1 %reduce-scatter.14.cloned.1.call-start = ((), (), s32[]{:S(2)}) async-start(), calls=%async_computation.9 | async-start | bytes 417792 | tf_op jit(solution)/shard_map/reduce_scatter | solution.py:47
Sparse Core Ops, SparseCore 0:
  71.3 91.5 reduce-scatter.5
  168.3 87.7 reduce-scatter.7
  260.8 87.5 reduce-scatter.9
  353.5 87.6 reduce-scatter.11
  445.6 87.6 reduce-scatter.13
where the time goes:
time: 542 us; the launch traced here: 541 us
  blocking collectives  263 us (49%)
  waiting for transfers between devices  247 us (46%)
  between operations  13.9 us (3%)
  matrix products  12.8 us (2%)
    all_gather x5, blocking collectives, generation(): lax.all_gather(panels[member], 'row', axis=0, tiled=True)  263 us
    reduce_scatter x5, waiting for transfers between devices, generation(): lax.psum_scatter(partial_value, 'col', scatter_dimension=0, tiled=True)  246 us
    dot_general x5, matrix products, apply_single(): lax.dot_general(segment, anc_inv, (((1,), (1,)), ((), ())), precision=hig...  11 us
  transfers between devices with their start and end apart: 5, of which 4 were waited for; matrix products, arithmetic and copies ran while one was open for 1% of the time, Pallas kernels for 0%

commit v1 on v0

v1 whole, which is shorter than its diff:
```python
import jax
import jax.numpy as jnp
from jax import lax
from jax.sharding import PartitionSpec as P

highest = lax.Precision.HIGHEST


def tile_flags(block_lists, anchor, extent, tile_height):
    tile_ids = (anchor + jnp.arange(extent, dtype=jnp.int32)) // tile_height
    matches = block_lists[:, :, None] == tile_ids[None, None, :]
    return jnp.any(matches, axis=1).astype(jnp.float32)


def local(anc_inv, factors_first, factors_second, lists_first, lists_second, parents, parent_link):
    local_rows, local_cols = anc_inv.shape
    n_first = factors_first.shape[0]
    n_second = factors_second.shape[0]
    members = n_first + n_second
    share_rows = factors_first.shape[1]
    panel_width = parent_link.shape[1]
    row_anchor = lax.axis_index("row") * local_rows
    col_anchor = lax.axis_index("col") * local_cols
    out_first = tile_flags(lists_first, row_anchor, local_rows, panel_width)
    out_second = tile_flags(lists_second, row_anchor, local_rows, panel_width)
    panels = jnp.concatenate(
        [
            factors_first * tile_flags(lists_first, col_anchor, local_cols, panel_width)[:, None, :],
            factors_second * tile_flags(lists_second, col_anchor, local_cols, panel_width)[:, None, :],
        ],
        axis=0,
    )
    stacked = jnp.transpose(panels, (1, 0, 2)).reshape(share_rows, members * local_cols)
    gathered = lax.all_gather(stacked, "row", axis=0, tiled=True)
    gathered = gathered.reshape(panel_width, members, local_cols)
    partial_value = jnp.einsum(
        "kmj,ij->mki", gathered, anc_inv, precision=highest, preferred_element_type=jnp.float32
    )
    first_partial = partial_value[:n_first]
    second_partial = partial_value[n_first:]
    chosen = jnp.take(first_partial, parents, axis=0)
    chosen_mask = jnp.take(out_first, parents, axis=0)
    coupling = jnp.einsum("cqk,cqi->cki", parent_link, chosen, precision=highest)
    second_partial = second_partial - chosen_mask[:, None, :] * coupling
    combined = jnp.concatenate([first_partial, second_partial], axis=0)
    reduced = lax.psum_scatter(combined, "col", scatter_dimension=1, tiled=True)
    first_cols = -out_first[:, None, :] * reduced[:n_first]
    second_cols = -out_second[:, None, :] * reduced[n_first:]
    return (first_cols, second_cols)


def solution(mesh):
    in_specs = (P("row", "col"), P(None, "row", "col"), P(None, "row", "col"), P(), P(), P(), P())
    out_specs = (P(None, "col", "row"), P(None, "col", "row"))
    return jax.shard_map(local, mesh=mesh, in_specs=in_specs, out_specs=out_specs, check_vma=False)
```

time: 542 us -> 277 us (0.51)
  blocking collectives: 263 us -> 0 us
  waiting for transfers between devices: 247 us -> 224 us
  local copies, waits for them, and re-layouts: 0.04 us -> 8.62 us
  other arithmetic: 4.32 us -> 10.7 us
    all_gather x5 -> x0, blocking collectives: 263 us -> none  [generation(): lax.all_gather(panels[member], 'row', axis=0, tiled=True)]
    reduce_scatter x5 -> x1, waiting for transfers between devices: 246 us -> 103 us  [local(): reduced = lax.psum_scatter(combined, 'col', scatter_dimension=1, tiled=True)]
    all_gather x0 -> x1, waiting for transfers between devices: none -> 121 us  [local(): gathered = lax.all_gather(stacked, 'row', axis=0, tiled=True)]
    all_gather x0 -> x1, local copies, waits for them, and re-layouts: none -> 5.45 us  [local(): gathered = lax.all_gather(stacked, 'row', axis=0, tiled=True)]
    dot_general x7 -> x2, matrix products: 12.8 us -> 17.2 us  [the longest x1 14.7 us: local(): jnp.einsum('kmj,ij->mki', gathered, anc_inv, precision=highest, preferred...]
  transfers between devices with their start and end apart: 5 -> 2, of which waited for: 4 -> 2; matrix products, arithmetic and copies ran while one was open for 1% -> 1% of each run, Pallas kernels for 0% -> 0%
where the time goes in v1:
time: 277 us; the launch traced here: 275 us
  waiting for transfers between devices  224 us (81%)
  matrix products  17.2 us (6%)
  between operations  14.2 us (5%)
  other arithmetic  10.7 us (4%)
  local copies, waits for them, and re-layouts  8.62 us (3%)
    all_gather x1, waiting for transfers between devices, local(): gathered = lax.all_gather(stacked, 'row', axis=0, tiled=True)  121 us
    reduce_scatter x1, waiting for transfers between devices, local(): reduced = lax.psum_scatter(combined, 'col', scatter_dimension=1, tiled=True)  103 us
    dot_general x1, matrix products, local(): jnp.einsum('kmj,ij->mki', gathered, anc_inv, precision=highest, preferred...  14.7 us
  transfers between devices with their start and end apart: 2, of which 2 were waited for; matrix products, arithmetic and copies ran while one was open for 1% of the time, Pallas kernels for 0%

profile of v1, /device:TPU:1, one launch (start us, length us, event | category | flops | bytes accessed | tf_op | source)
XLA Modules:
  0.0 275.3 jit_solution(1879956316999210277)
XLA Ops:
  7.2 0.0 copy-start
  7.2 0.0 all-gather.2.cloned.1.call-start
  7.2 0.9 compare_reduce_fusion
  8.2 0.8 compare_reduce_fusion.1
  9.0 0.9 broadcast_multiply_fusion
  9.9 0.8 broadcast_multiply_fusion.1
  10.7 0.6 pad_maximum_fusion.1
  11.3 0.0 all-gather.2.cloned.1.call-update
  11.3 0.0 reduce-scatter.2.cloned.1.call-start
  11.4 0.8 compare_reduce_fusion.2
  12.2 0.7 compare_select_fusion
  12.9 0.6 gather_fusion
  13.4 0.7 compare_and_fusion
  14.1 0.1 broadcast_select_fusion
  14.2 121.3 %all-gather.2.cloned.1.call-done = f32[256,3840]{1,0:T(8,128)} async-done(((f32[8,3840]{1,0:T(8,128)}), f32[256,3840]{1,0:T(8,128)}) %all-gather.2.cloned.1.call-update) | async-done | bytes 3932176 | tf_op jit(solution)/shard_map/all_gather | solution.py:34
  135.5 5.4 %copy.19 = f32[256,3840]{0,1:T(8,128)} copy(f32[256,3840]{1,0:T(8,128)} %all-gather.2.cloned.1.call-done) | data formatting | bytes 7864320 | tf_op jit(solution)/shard_map/all_gather | solution.py:34
  141.0 0.0 copy-done
  141.0 14.7 %convolution_bitcast_fusion = f32[5,256,384]{2,1,0:T(8,128)S(1)} fusion(f32[256,5,768]{0,2,1:T(8,128)} %bitcast.15, f32[384,768]{1,0:T(8,128)S(1)} %copy-done), kind=kOutput, calls=%fused_computation.3 | convolution fusion | flops 4529848320 | bytes 7077888 | tf_op jit(solution)/shard_map/kmj,ij->mki/dot_general | solution.py:36
  155.7 0.0 copy-start.1
  155.7 1.3 copy-done.1
  157.0 0.1 slice.20
  157.0 0.6 gather_fusion.1
  157.6 2.5 fusion.1
  160.2 1.4 pad_maximum_fusion
  161.6 0.0 copy-start.2
  161.6 0.0 reduce-scatter.2.cloned.1.call-update
  161.6 0.7 copy-done.2
  162.3 0.1 compare_reduce_fusion.3
  162.4 103.1 %reduce-scatter.2.cloned.1.call-done = f32[5,16,384]{2,1,0:T(8,128)} async-done(((f32[5,256,384]{2,1,0:T(8,128)}), f32[5,16,384]{2,1,0:T(8,128)}) %reduce-scatter.2.cloned.1.call-update) | async-done | bytes 122896 | tf_op jit(solution)/shard_map/reduce_scatter | solution.py:46
  265.5 1.5 slice_multiply_fusion
  267.0 1.4 slice_multiply_fusion.1
  (8 shorter events, 0.1 us)
Async XLA Ops:
  7.2 133.8 %copy-start = (f32[384,768]{1,0:T(8,128)S(1)}, f32[384,768]{1,0:T(8,128)}, u32[]{:S(2)}) copy-start(f32[384,768]{1,0:T(8,128)} %param.7) | copy-start | bytes 3538948
  7.2 128.3 %all-gather.2.cloned.1.call-start = ((), (), s32[]{:S(2)}) async-start(), calls=%async_computation.1 | async-start | bytes 4055040 | tf_op jit(solution)/shard_map/all_gather | solution.py:34
  11.3 254.2 %reduce-scatter.2.cloned.1.call-start = ((), (), s32[]{:S(2)}) async-start(), calls=%async_computation.2 | async-start | bytes 2088960 | tf_op jit(solution)/shard_map/reduce_scatter | solution.py:46
  155.7 1.3 copy-start.1
  161.6 0.7 copy-start.2
Sparse Core Ops, SparseCore 0:
  11.5 124.0 all-gather.1
  161.7 103.7 reduce-scatter.1

commit v2 on v1

v2 whole, which is shorter than its diff:
```python
import jax
import jax.numpy as jnp
from jax import lax
from jax.sharding import PartitionSpec as P

highest = lax.Precision.HIGHEST

X_LO = 2
X_HI = 2
CORES = 2


def tile_flags(block_lists, anchor, extent, tile_height):
    tile_ids = (anchor + jnp.arange(extent, dtype=jnp.int32)) // tile_height
    matches = block_lists[:, :, None] == tile_ids[None, None, :]
    return jnp.any(matches, axis=1).astype(jnp.float32)


def shift_pairs(size, inner, stride, shift):
    pairs = []
    for p in range(size):
        q = (p // stride) % inner
        target = p + (((q + shift) % inner) - q) * stride
        pairs.append((p, target))
    return pairs


def gather_rows(block, n_row):
    nz = n_row // X_LO
    r = lax.axis_index("row")
    x_lo = r // nz
    z = r % nz
    partner = lax.ppermute(block, "row", [(p, (p + nz) % n_row) for p in range(n_row)])
    pair = jnp.where(x_lo == 0, jnp.stack([block, partner]), jnp.stack([partner, block]))
    up = shift_pairs(n_row, nz, 1, 1)
    down = shift_pairs(n_row, nz, 1, -1)
    pieces = [None] * nz
    pieces[0] = pair
    fwd = pair
    bwd = pair
    for t in range(1, nz // 2):
        fwd = lax.ppermute(fwd, "row", up)
        bwd = lax.ppermute(bwd, "row", down)
        pieces[nz - t] = fwd
        pieces[t] = bwd
    half = pair.shape[-1] // 2
    last_fwd = lax.ppermute(fwd[..., :half], "row", up)
    last_bwd = lax.ppermute(bwd[..., half:], "row", down)
    pieces[nz // 2] = jnp.concatenate([last_fwd, last_bwd], axis=-1)
    return jnp.stack(pieces), z


def reduce_cols(value, n_col):
    ny = n_col // (X_HI * CORES)
    c = lax.axis_index("col")
    core = c % CORES
    y = (c // CORES) % ny
    x_hi = c // (CORES * ny)
    send = jnp.take(value, 1 - core, axis=2)
    keep = jnp.take(value, core, axis=2)
    value = keep + lax.ppermute(send, "col", [(p, p ^ 1) for p in range(n_col)])
    rows = value.shape[2]
    upper = value[:, :, : rows // 2]
    lower = value[:, :, rows // 2 :]
    up = shift_pairs(n_col, ny, CORES, 1)
    down = shift_pairs(n_col, ny, CORES, -1)
    acc_up = jnp.take(upper, (y - 1) % ny, axis=1)
    acc_down = jnp.take(lower, (y + 1) % ny, axis=1)
    for s in range(1, ny):
        acc_up = lax.ppermute(acc_up, "col", up) + jnp.take(upper, (y - s - 1) % ny, axis=1)
        acc_down = lax.ppermute(acc_down, "col", down) + jnp.take(lower, (y + s + 1) % ny, axis=1)
    value = jnp.concatenate([acc_up, acc_down], axis=1)
    send = jnp.take(value, 1 - x_hi, axis=0)
    keep = jnp.take(value, x_hi, axis=0)
    half = n_col // X_HI
    return keep + lax.ppermute(send, "col", [(p, (p + half) % n_col) for p in range(n_col)])


def local(anc_inv, factors_first, factors_second, lists_first, lists_second, parents, parent_link):
    n_row = lax.axis_size("row")
    n_col = lax.axis_size("col")
    local_rows, local_cols = anc_inv.shape
    n_first = factors_first.shape[0]
    n_second = factors_second.shape[0]
    members = n_first + n_second
    share_rows = factors_first.shape[1]
    panel_width = parent_link.shape[1]
    nz = n_row // X_LO
    row_anchor = lax.axis_index("row") * local_rows
    col_anchor = lax.axis_index("col") * local_cols
    out_first = tile_flags(lists_first, row_anchor, local_rows, panel_width)
    out_second = tile_flags(lists_second, row_anchor, local_rows, panel_width)
    panels = jnp.concatenate(
        [
            factors_first * tile_flags(lists_first, col_anchor, local_cols, panel_width)[:, None, :],
            factors_second * tile_flags(lists_second, col_anchor, local_cols, panel_width)[:, None, :],
        ],
        axis=0,
    )
    stacked = jnp.transpose(panels, (1, 0, 2)).reshape(share_rows, members * local_cols)
    pieces, z = gather_rows(stacked, n_row)
    pieces = pieces.reshape(nz, X_LO, share_rows, members, local_cols)
    partial_value = jnp.einsum(
        "tlkmj,ij->ltkmi", pieces, anc_inv, precision=highest, preferred_element_type=jnp.float32
    )
    partial_value = jnp.roll(partial_value, z, axis=1)
    partial_value = partial_value.reshape(panel_width, members, local_rows)
    first_partial = partial_value[:, :n_first]
    chosen = jnp.take(first_partial, parents, axis=1)
    chosen_mask = jnp.take(out_first, parents, axis=0)
    coupling = jnp.einsum("cqk,qci->kci", parent_link, chosen, precision=highest)
    second_partial = partial_value[:, n_first:] - chosen_mask[None, :, :] * coupling
    combined = jnp.concatenate([first_partial, second_partial], axis=1)
    ny = n_col // (X_HI * CORES)
    combined = combined.reshape(X_HI, ny, CORES, panel_width // n_col, members, local_rows)
    reduced = reduce_cols(combined, n_col)
    reduced = jnp.transpose(reduced, (1, 0, 2))
    first_cols = -out_first[:, None, :] * reduced[:n_first]
    second_cols = -out_second[:, None, :] * reduced[n_first:]
    return (first_cols, second_cols)


def solution(mesh):
    in_specs = (P("row", "col"), P(None, "row", "col"), P(None, "row", "col"), P(), P(), P(), P())
    out_specs = (P(None, "col", "row"), P(None, "col", "row"))
    return jax.shard_map(local, mesh=mesh, in_specs=in_specs, out_specs=out_specs, check_vma=False)
```

time: 277 us -> 156 us (0.56)
  the two profiles are of different devices: /device:TPU:1 before, /device:TPU:24 now
where the time goes in v2:
time: 156 us; the launch traced here: 155 us
  starting transfers between devices  94.3 us (60%)
  waiting for transfers between devices  35.6 us (23%)
  matrix products  9 us (6%)
  other arithmetic  8.93 us (6%)
  local copies, waits for them, and re-layouts  5.11 us (3%)
  between operations  1.6 us (1%)
    ppermute x7, starting transfers between devices, gather_rows(): bwd = lax.ppermute(bwd, 'row', down)  44.9 us
    ppermute x7, starting transfers between devices, gather_rows(): fwd = lax.ppermute(fwd, 'row', up)  13.4 us
    ppermute x7, waiting for transfers between devices, gather_rows(): bwd = lax.ppermute(bwd, 'row', down)  11.9 us
    ppermute x3, starting transfers between devices, reduce_cols(): lax.ppermute(acc_up, 'col', up) + jnp.take(upper, (y - s - 1) % ny, axis=1)  10.2 us
    ppermute x3, starting transfers between devices, reduce_cols(): lax.ppermute(acc_down, 'col', down)  8.07 us
    dot_general x1, matrix products, local(): jnp.einsum('tlkmj,ij->ltkmi', pieces, anc_inv, precision=highest, preferr...  6.48 us
    ppermute x3, waiting for transfers between devices, reduce_cols(): lax.ppermute(acc_down, 'col', down)  5.67 us
    ppermute x1, starting transfers between devices, gather_rows(): last_bwd = lax.ppermute(bwd[..., half:], 'row', down)  5.6 us
  transfers between devices with their start and end apart: 25, of which 16 were waited for; matrix products, arithmetic and copies ran while one was open for 3% of the time, Pallas kernels for 0%

profile of v2, /device:TPU:24, one launch (start us, length us, event | category | flops | bytes accessed | tf_op | source)
XLA Modules:
  0.0 154.5 jit_solution(17000608973784094008)
XLA Ops:
  0.7 0.9 compare_reduce_fusion.1
  1.6 0.8 compare_reduce_fusion
  2.4 0.8 broadcast_multiply_fusion.1
  3.2 0.9 broadcast_multiply_fusion
  4.1 3.4 %collective-permute-start = (f32[8,3840]{1,0:T(8,128)S(1)}, f32[8,3840]{1,0:T(8,128)S(1)}, u32[]{:S(2)}, u32[]{:S(2)}) collective-permute-start(f32[8,3840]{1,0:T(8,128)S(1)} %bitcast.83), channel_id=1, source_target_pairs={{0,256},{16,272},{32,288},{48,304},{64,320},{80,336},{96,352},{112... | collective-permute-start | bytes 368648 | tf_op jit(solution)/shard_map/ppermute | solution.py:33
  7.5 3.5 %collective-permute-done = f32[8,3840]{1,0:T(8,128)S(1)} collective-permute-done((f32[8,3840]{1,0:T(8,128)S(1)}, f32[8,3840]{1,0:T(8,128)S(1)}, u32[]{:S(2)}, u32[]{:S(2)}) %collective-permute-start) | collective-permute-done | bytes 122912 | tf_op jit(solution)/shard_map/ppermute | solution.py:33
  11.1 11.4 %collective-permute-start.1 = (f32[2,8,3840]{2,1,0:T(8,128)S(1)}, f32[2,8,3840]{2,1,0:T(8,128)S(1)}, u32[]{:S(2)}, u32[]{:S(2)}) collective-permute-start(f32[2,8,3840]{2,1,0:T(8,128)S(1)} %maximum_select_fusion.1), channel_id=1, source_target_pairs={{0,240},{16,0},{32,16},{48,32},{64,48},{80,64},{96,80},{112,96},{1... | collective-permute-start | bytes 737288 | tf_op jit(solution)/shard_map/ppermute | solution.py:43
  22.5 1.9 %collective-permute-start.8 = (f32[2,8,3840]{2,1,0:T(8,128)S(1)}, f32[2,8,3840]{2,1,0:T(8,128)S(1)}, u32[]{:S(2)}, u32[]{:S(2)}) collective-permute-start(f32[2,8,3840]{2,1,0:T(8,128)S(1)} %maximum_select_fusion.1), channel_id=1, source_target_pairs={{0,16},{16,32},{32,48},{48,64},{64,80},{80,96},{96,112},{112,128},... | collective-permute-start | bytes 737288 | tf_op jit(solution)/shard_map/ppermute | solution.py:42
  24.4 2.4 %collective-permute-done.1 = f32[2,8,3840]{2,1,0:T(8,128)S(1)} collective-permute-done((f32[2,8,3840]{2,1,0:T(8,128)S(1)}, f32[2,8,3840]{2,1,0:T(8,128)S(1)}, u32[]{:S(2)}, u32[]{:S(2)}) %collective-permute-start.1) | collective-permute-done | bytes 245792 | tf_op jit(solution)/shard_map/ppermute | solution.py:43
  26.8 5.6 %collective-permute-start.2 = (f32[2,8,3840]{2,1,0:T(8,128)S(1)}, f32[2,8,3840]{2,1,0:T(8,128)S(1)}, u32[]{:S(2)}, u32[]{:S(2)}) collective-permute-start(f32[2,8,3840]{2,1,0:T(8,128)S(1)} %collective-permute-done.1), channel_id=1, source_target_pairs={{0,240},{16,0},{32,16},{48,32},{64,48},{80,64},{96,80},{112,96},{1... | collective-permute-start | bytes 737288 | tf_op jit(solution)/shard_map/ppermute | solution.py:43
  32.4 1.9 %collective-permute-start.9 = (f32[2,8,3840]{2,1,0:T(8,128)S(1)}, f32[2,8,3840]{2,1,0:T(8,128)S(1)}, u32[]{:S(2)}, u32[]{:S(2)}) collective-permute-start(f32[2,8,3840]{2,1,0:T(8,128)S(1)} %collective-permute-done.8), channel_id=1, source_target_pairs={{0,16},{16,32},{32,48},{48,64},{64,80},{80,96},{96,112},{112,128},... | collective-permute-start | bytes 737288 | tf_op jit(solution)/shard_map/ppermute | solution.py:42
  34.4 1.8 %collective-permute-done.2 = f32[2,8,3840]{2,1,0:T(8,128)S(1)} collective-permute-done((f32[2,8,3840]{2,1,0:T(8,128)S(1)}, f32[2,8,3840]{2,1,0:T(8,128)S(1)}, u32[]{:S(2)}, u32[]{:S(2)}) %collective-permute-start.2) | collective-permute-done | bytes 245792 | tf_op jit(solution)/shard_map/ppermute | solution.py:43
  36.1 5.6 %collective-permute-start.3 = (f32[2,8,3840]{2,1,0:T(8,128)S(1)}, f32[2,8,3840]{2,1,0:T(8,128)S(1)}, u32[]{:S(2)}, u32[]{:S(2)}) collective-permute-start(f32[2,8,3840]{2,1,0:T(8,128)S(1)} %collective-permute-done.2), channel_id=1, source_target_pairs={{0,240},{16,0},{32,16},{48,32},{64,48},{80,64},{96,80},{112,96},{1... | collective-permute-start | bytes 737288 | tf_op jit(solution)/shard_map/ppermute | solution.py:43
  41.7 1.9 %collective-permute-start.10 = (f32[2,8,3840]{2,1,0:T(8,128)S(1)}, f32[2,8,3840]{2,1,0:T(8,128)S(1)}, u32[]{:S(2)}, u32[]{:S(2)}) collective-permute-start(f32[2,8,3840]{2,1,0:T(8,128)S(1)} %collective-permute-done.9), channel_id=1, source_target_pairs={{0,16},{16,32},{32,48},{48,64},{64,80},{80,96},{96,112},{112,128},... | collective-permute-start | bytes 737288 | tf_op jit(solution)/shard_map/ppermute | solution.py:42
  43.7 0.7 compare_select_fusion
  44.3 1.1 collective-permute-done.3
  45.4 5.6 %collective-permute-start.4 = (f32[2,8,3840]{2,1,0:T(8,128)S(1)}, f32[2,8,3840]{2,1,0:T(8,128)}, u32[]{:S(2)}, u32[]{:S(2)}) collective-permute-start(f32[2,8,3840]{2,1,0:T(8,128)S(1)} %collective-permute-done.3), channel_id=1, source_target_pairs={{0,240},{16,0},{32,16},{48,32},{64,48},{80,64},{96,80},{112,96},{1... | collective-permute-start | bytes 737288 | tf_op jit(solution)/shard_map/ppermute | solution.py:43
  51.0 1.9 %collective-permute-start.11 = (f32[2,8,3840]{2,1,0:T(8,128)S(1)}, f32[2,8,3840]{2,1,0:T(8,128)S(1)}, u32[]{:S(2)}, u32[]{:S(2)}) collective-permute-start(f32[2,8,3840]{2,1,0:T(8,128)S(1)} %collective-permute-done.10), channel_id=1, source_target_pairs={{0,16},{16,32},{32,48},{48,64},{64,80},{80,96},{96,112},{112,128},... | collective-permute-start | bytes 737288 | tf_op jit(solution)/shard_map/ppermute | solution.py:42
  52.9 0.8 compare_reduce_fusion.2
  53.7 0.7 compare_and_fusion
  54.4 0.3 collective-permute-done.4
  54.7 5.7 %collective-permute-start.5 = (f32[2,8,3840]{2,1,0:T(8,128)}, f32[2,8,3840]{2,1,0:T(8,128)}, u32[]{:S(2)}, u32[]{:S(2)}) collective-permute-start(f32[2,8,3840]{2,1,0:T(8,128)} %collective-permute-done.4), channel_id=1, source_target_pairs={{0,240},{16,0},{32,16},{48,32},{64,48},{80,64},{96,80},{112,96},{1... | collective-permute-start | bytes 737288 | tf_op jit(solution)/shard_map/ppermute | solution.py:43
  60.4 1.9 %collective-permute-start.12 = (f32[2,8,3840]{2,1,0:T(8,128)S(1)}, f32[2,8,3840]{2,1,0:T(8,128)S(1)}, u32[]{:S(2)}, u32[]{:S(2)}) collective-permute-start(f32[2,8,3840]{2,1,0:T(8,128)S(1)} %collective-permute-done.11), channel_id=1, source_target_pairs={{0,16},{16,32},{32,48},{48,64},{64,80},{80,96},{96,112},{112,128},... | collective-permute-start | bytes 737288 | tf_op jit(solution)/shard_map/ppermute | solution.py:42
  62.4 0.6 gather_fusion
  63.1 1.8 %collective-permute-done.5 = f32[2,8,3840]{2,1,0:T(8,128)} collective-permute-done((f32[2,8,3840]{2,1,0:T(8,128)}, f32[2,8,3840]{2,1,0:T(8,128)}, u32[]{:S(2)}, u32[]{:S(2)}) %collective-permute-start.5) | collective-permute-done | bytes 245792 | tf_op jit(solution)/shard_map/ppermute | solution.py:43
  64.9 5.6 %collective-permute-start.6 = (f32[2,8,3840]{2,1,0:T(8,128)}, f32[2,8,3840]{2,1,0:T(8,128)S(1)}, u32[]{:S(2)}, u32[]{:S(2)}) collective-permute-start(f32[2,8,3840]{2,1,0:T(8,128)} %collective-permute-done.5), channel_id=1, source_target_pairs={{0,240},{16,0},{32,16},{48,32},{64,48},{80,64},{96,80},{112,96},{1... | collective-permute-start | bytes 737288 | tf_op jit(solution)/shard_map/ppermute | solution.py:43
  70.5 1.9 %collective-permute-start.13 = (f32[2,8,3840]{2,1,0:T(8,128)S(1)}, f32[2,8,3840]{2,1,0:T(8,128)S(1)}, u32[]{:S(2)}, u32[]{:S(2)}) collective-permute-start(f32[2,8,3840]{2,1,0:T(8,128)S(1)} %collective-permute-done.12), channel_id=1, source_target_pairs={{0,16},{16,32},{32,48},{48,64},{64,80},{80,96},{96,112},{112,128},... | collective-permute-start | bytes 737288 | tf_op jit(solution)/shard_map/ppermute | solution.py:42
  72.5 4.0 %collective-permute-done.6 = f32[2,8,3840]{2,1,0:T(8,128)S(1)} collective-permute-done((f32[2,8,3840]{2,1,0:T(8,128)}, f32[2,8,3840]{2,1,0:T(8,128)S(1)}, u32[]{:S(2)}, u32[]{:S(2)}) %collective-permute-start.6) | collective-permute-done | bytes 245792 | tf_op jit(solution)/shard_map/ppermute | solution.py:43
  76.5 5.5 %collective-permute-start.7 = (f32[2,8,3840]{2,1,0:T(8,128)S(1)}, f32[2,8,3840]{2,1,0:T(8,128)S(1)}, u32[]{:S(2)}, u32[]{:S(2)}) collective-permute-start(f32[2,8,3840]{2,1,0:T(8,128)S(1)} %collective-permute-done.6), channel_id=1, source_target_pairs={{0,240},{16,0},{32,16},{48,32},{64,48},{80,64},{96,80},{112,96},{1... | collective-permute-start | bytes 737288 | tf_op jit(solution)/shard_map/ppermute | solution.py:43
  82.0 1.9 %collective-permute-start.14 = (f32[2,8,3840]{2,1,0:T(8,128)S(1)}, f32[2,8,3840]{2,1,0:T(8,128)S(1)}, u32[]{:S(2)}, u32[]{:S(2)}) collective-permute-start(f32[2,8,3840]{2,1,0:T(8,128)S(1)} %collective-permute-done.13), channel_id=1, source_target_pairs={{0,16},{16,32},{32,48},{48,64},{64,80},{80,96},{96,112},{112,128},... | collective-permute-start | bytes 737288 | tf_op jit(solution)/shard_map/ppermute | solution.py:42
  84.0 1.0 constant_dynamic-update-slice_fusion.11
  84.9 1.0 constant_dynamic-update-slice_fusion.10
  85.9 0.6 collective-permute-done.7
  86.5 5.6 %collective-permute-start.16 = (f32[2,8,1920]{2,1,0:T(8,128)S(1)}, f32[2,8,1920]{2,1,0:T(8,128)S(1)}, u32[]{:S(2)}, u32[]{:S(2)}) collective-permute-start(f32[2,8,1920]{2,1,0:T(8,128)S(1)} %slice.76), channel_id=1, source_target_pairs={{0,240},{16,0},{32,16},{48,32},{64,48},{80,64},{96,80},{112,96},{1... | collective-permute-start | bytes 368648 | tf_op jit(solution)/shard_map/ppermute | solution.py:48
  92.2 1.9 %collective-permute-start.15 = (f32[2,8,1920]{2,1,0:T(8,128)S(1)}, f32[2,8,1920]{2,1,0:T(8,128)S(1)}, u32[]{:S(2)}, u32[]{:S(2)}) collective-permute-start(f32[2,8,1920]{2,1,0:T(8,128)S(1)} %slice.75), channel_id=1, source_target_pairs={{0,16},{16,32},{32,48},{48,64},{64,80},{80,96},{96,112},{112,128},... | collective-permute-start | bytes 368648 | tf_op jit(solution)/shard_map/ppermute | solution.py:47
  94.1 0.4 collective-permute-done.16
  94.6 5.6 %collective-permute-done.15 = f32[2,8,1920]{2,1,0:T(8,128)S(1)} collective-permute-done((f32[2,8,1920]{2,1,0:T(8,128)S(1)}, f32[2,8,1920]{2,1,0:T(8,128)S(1)}, u32[]{:S(2)}, u32[]{:S(2)}) %collective-permute-start.15) | collective-permute-done | bytes 122912 | tf_op jit(solution)/shard_map/ppermute | solution.py:47
  100.4 6.5 %convolution_bitcast_fusion = f32[2,16,8,5,384]{4,2,3,0,1:T(8,128)S(1)} fusion(f32[16,2,8,5,768]{4,2,3,1,0:T(8,128)S(1)} %constant_dynamic-update-slice_fusion, f32[384,768]{1,0:T(8,128)S(1)} %copy-done), kind=kOutput, calls=%fused_computation.6 | convolution fusion | flops 4529848320 | bytes 7077888 | tf_op jit(solution)/shard_map/tlkmj,ij->ltkmi/dot_general | solution.py:103
  106.9 0.4 fusion
  107.3 0.2 copy.16
  107.4 1.3 copy-done.1
  108.8 0.6 gather_fusion.1
  109.4 2.5 %fusion.2 = f32[256,2,384]{2,0,1:T(8,128)S(1)} fusion(f32[2,256,256]{2,1,0:T(8,128)} %param.19, f32[256,5,384]{2,0,1:T(8,128)} %bitcast.76, f32[2,256,384]{2,1,0:T(8,128)S(1)} %gather_fusion.1, f32[2,384]{1,0:T(2,128)S(1)} %broadcast_select_fusion, pred[2]{0:T(512)(128)(4,1)S(1)} %compare_and_fusion), kind=kOutput, calls=%fused_computation.9 | convolution fusion | flops 604569600 | bytes 2886658 | tf_op jit(solution)/shard_map/cqk,qci->kci/dot_general | solution.py:111
  111.9 0.1 pad_maximum_fusion
  112.1 0.2 constant_dynamic-slice_fusion.1
  112.3 1.0 fusion.4
  113.3 1.9 %collective-permute-start.17 = (f32[2,4,16,5,384]{4,2,3,0,1:T(8,128)}, f32[2,4,16,5,384]{4,2,3,0,1:T(8,128)S(1)}, u32[]{:S(2)}, u32[]{:S(2)}) collective-permute-start(f32[2,4,16,5,384]{4,2,3,0,1:T(8,128)} %fusion.4), channel_id=1, source_target_pairs={{0,1},{1,0},{2,3},{3,2},{4,5},{5,4},{6,7},{7,6},{8,9},{9,8},{10,11... | collective-permute-start | bytes 2949128 | tf_op jit(solution)/shard_map/ppermute | solution.py:61
  115.3 2.7 %collective-permute-done.17 = f32[2,4,16,5,384]{4,2,3,0,1:T(8,128)S(1)} collective-permute-done((f32[2,4,16,5,384]{4,2,3,0,1:T(8,128)}, f32[2,4,16,5,384]{4,2,3,0,1:T(8,128)S(1)}, u32[]{:S(2)}, u32[]{:S(2)}) %collective-permute-start.17) | collective-permute-done | bytes 983072 | tf_op jit(solution)/shard_map/ppermute | solution.py:61
  118.0 0.1 fusion.6
  118.2 2.1 %collective-permute-start.18 = (f32[2,8,5,384]{3,1,2,0:T(8,128)S(1)}, f32[2,8,5,384]{3,1,2,0:T(8,128)S(1)}, u32[]{:S(2)}, u32[]{:S(2)}) collective-permute-start(f32[2,8,5,384]{3,1,2,0:T(8,128)S(1)} %select_bitcast_fusion.1), channel_id=1, source_target_pairs={{0,2},{1,3},{2,4},{3,5},{4,6},{5,7},{6,0},{7,1},{8,10},{9,11},{10,... | collective-permute-start | bytes 368648 | tf_op jit(solution)/shard_map/ppermute | solution.py:70
  120.3 0.1 compare_reduce_fusion.3
  120.7 3.7 %collective-permute-start.21 = (f32[2,8,5,384]{3,1,2,0:T(8,128)S(1)}, f32[2,8,5,384]{3,1,2,0:T(8,128)S(1)}, u32[]{:S(2)}, u32[]{:S(2)}) collective-permute-start(f32[2,8,5,384]{3,1,2,0:T(8,128)S(1)} %select_bitcast_fusion), channel_id=1, source_target_pairs={{0,6},{1,7},{2,0},{3,1},{4,2},{5,3},{6,4},{7,5},{8,14},{9,15},{10,... | collective-permute-start | bytes 368648 | tf_op jit(solution)/shard_map/ppermute | solution.py:71
  124.4 1.1 collective-permute-done.18
  125.5 3.4 %collective-permute-start.19 = (f32[2,8,5,384]{3,1,2,0:T(8,128)S(1)}, f32[2,8,5,384]{3,1,2,0:T(8,128)S(1)}, u32[]{:S(2)}, u32[]{:S(2)}) collective-permute-start(f32[2,8,5,384]{3,1,2,0:T(8,128)S(1)} %bitcast_add_fusion.5), channel_id=1, source_target_pairs={{0,2},{1,3},{2,4},{3,5},{4,6},{5,7},{6,0},{7,1},{8,10},{9,11},{10,... | collective-permute-start | bytes 368648 | tf_op jit(solution)/shard_map/ppermute | solution.py:70
  128.9 2.4 %collective-permute-start.22 = (f32[2,8,5,384]{3,1,2,0:T(8,128)S(1)}, f32[2,8,5,384]{3,1,2,0:T(8,128)S(1)}, u32[]{:S(2)}, u32[]{:S(2)}) collective-permute-start(f32[2,8,5,384]{3,1,2,0:T(8,128)S(1)} %bitcast_add_fusion.2), channel_id=1, source_target_pairs={{0,6},{1,7},{2,0},{3,1},{4,2},{5,3},{6,4},{7,5},{8,14},{9,15},{10,... | collective-permute-start | bytes 368648 | tf_op jit(solution)/shard_map/ppermute | solution.py:71
  131.4 0.9 collective-permute-done.19
  132.3 4.6 %collective-permute-start.20 = (f32[2,8,5,384]{3,1,2,0:T(8,128)S(1)}, f32[2,8,5,384]{3,1,2,0:T(8,128)S(1)}, u32[]{:S(2)}, u32[]{:S(2)}) collective-permute-start(f32[2,8,5,384]{3,1,2,0:T(8,128)S(1)} %bitcast_add_fusion.4), channel_id=1, source_target_pairs={{0,2},{1,3},{2,4},{3,5},{4,6},{5,7},{6,0},{7,1},{8,10},{9,11},{10,... | collective-permute-start | bytes 368648 | tf_op jit(solution)/shard_map/ppermute | solution.py:70
  136.9 1.9 %collective-permute-start.23 = (f32[2,8,5,384]{3,1,2,0:T(8,128)S(1)}, f32[2,8,5,384]{3,1,2,0:T(8,128)S(1)}, u32[]{:S(2)}, u32[]{:S(2)}) collective-permute-start(f32[2,8,5,384]{3,1,2,0:T(8,128)S(1)} %bitcast_add_fusion.1), channel_id=1, source_target_pairs={{0,6},{1,7},{2,0},{3,1},{4,2},{5,3},{6,4},{7,5},{8,14},{9,15},{10,... | collective-permute-start | bytes 368648 | tf_op jit(solution)/shard_map/ppermute | solution.py:71
  138.9 0.4 collective-permute-done.20
  139.3 5.6 %collective-permute-done.23 = f32[2,8,5,384]{3,1,2,0:T(8,128)S(1)} collective-permute-done((f32[2,8,5,384]{3,1,2,0:T(8,128)S(1)}, f32[2,8,5,384]{3,1,2,0:T(8,128)S(1)}, u32[]{:S(2)}, u32[]{:S(2)}) %collective-permute-start.23) | collective-permute-done | bytes 122912 | tf_op jit(solution)/shard_map/ppermute | solution.py:71
  145.0 4.9 %collective-permute-start.24 = (f32[16,5,384]{2,0,1:T(8,128)S(1)}, f32[16,5,384]{2,0,1:T(8,128)S(1)}, u32[]{:S(2)}, u32[]{:S(2)}) collective-permute-start(f32[16,5,384]{2,0,1:T(8,128)S(1)} %fusion.14), channel_id=1, source_target_pairs={{0,8},{1,9},{2,10},{3,11},{4,12},{5,13},{6,14},{7,15},{8,0},{9,1},... | collective-permute-start | bytes 368648 | tf_op jit(solution)/shard_map/ppermute | solution.py:76
  149.9 3.3 %collective-permute-done.24 = f32[16,5,384]{2,0,1:T(8,128)S(1)} collective-permute-done((f32[16,5,384]{2,0,1:T(8,128)S(1)}, f32[16,5,384]{2,0,1:T(8,128)S(1)}, u32[]{:S(2)}, u32[]{:S(2)}) %collective-permute-start.24) | collective-permute-done | bytes 122912 | tf_op jit(solution)/shard_map/ppermute | solution.py:76
  153.3 0.6 slice_multiply_fusion
  153.9 0.6 slice_multiply_fusion.1
  (54 shorter events, 0.9 us)
Async XLA Ops:
  0.6 99.8 %copy-start = (f32[384,768]{1,0:T(8,128)S(1)}, f32[384,768]{1,0:T(8,128)}, u32[]{:S(2)}) copy-start(f32[384,768]{1,0:T(8,128)} %param.13) | copy-start | bytes 3538948
  4.1 7.0 %collective-permute-start = (f32[8,3840]{1,0:T(8,128)S(1)}, f32[8,3840]{1,0:T(8,128)S(1)}, u32[]{:S(2)}, u32[]{:S(2)}) collective-permute-start(f32[8,3840]{1,0:T(8,128)S(1)} %bitcast.83), channel_id=1, source_target_pairs={{0,256},{16,272},{32,288},{48,304},{64,320},{80,336},{96,352},{112... | collective-permute-start | bytes 368648 | tf_op jit(solution)/shard_map/ppermute | solution.py:33
  11.1 15.7 %collective-permute-start.1 = (f32[2,8,3840]{2,1,0:T(8,128)S(1)}, f32[2,8,3840]{2,1,0:T(8,128)S(1)}, u32[]{:S(2)}, u32[]{:S(2)}) collective-permute-start(f32[2,8,3840]{2,1,0:T(8,128)S(1)} %maximum_select_fusion.1), channel_id=1, source_target_pairs={{0,240},{16,0},{32,16},{48,32},{64,48},{80,64},{96,80},{112,96},{1... | collective-permute-start | bytes 737288 | tf_op jit(solution)/shard_map/ppermute | solution.py:43
  22.5 9.9 %collective-permute-start.8 = (f32[2,8,3840]{2,1,0:T(8,128)S(1)}, f32[2,8,3840]{2,1,0:T(8,128)S(1)}, u32[]{:S(2)}, u32[]{:S(2)}) collective-permute-start(f32[2,8,3840]{2,1,0:T(8,128)S(1)} %maximum_select_fusion.1), channel_id=1, source_target_pairs={{0,16},{16,32},{32,48},{48,64},{64,80},{80,96},{96,112},{112,128},... | collective-permute-start | bytes 737288 | tf_op jit(solution)/shard_map/ppermute | solution.py:42
  26.8 9.3 %collective-permute-start.2 = (f32[2,8,3840]{2,1,0:T(8,128)S(1)}, f32[2,8,3840]{2,1,0:T(8,128)S(1)}, u32[]{:S(2)}, u32[]{:S(2)}) collective-permute-start(f32[2,8,3840]{2,1,0:T(8,128)S(1)} %collective-permute-done.1), channel_id=1, source_target_pairs={{0,240},{16,0},{32,16},{48,32},{64,48},{80,64},{96,80},{112,96},{1... | collective-permute-start | bytes 737288 | tf_op jit(solution)/shard_map/ppermute | solution.py:43
  32.4 9.3 %collective-permute-start.9 = (f32[2,8,3840]{2,1,0:T(8,128)S(1)}, f32[2,8,3840]{2,1,0:T(8,128)S(1)}, u32[]{:S(2)}, u32[]{:S(2)}) collective-permute-start(f32[2,8,3840]{2,1,0:T(8,128)S(1)} %collective-permute-done.8), channel_id=1, source_target_pairs={{0,16},{16,32},{32,48},{48,64},{64,80},{80,96},{96,112},{112,128},... | collective-permute-start | bytes 737288 | tf_op jit(solution)/shard_map/ppermute | solution.py:42
  36.1 9.3 %collective-permute-start.3 = (f32[2,8,3840]{2,1,0:T(8,128)S(1)}, f32[2,8,3840]{2,1,0:T(8,128)S(1)}, u32[]{:S(2)}, u32[]{:S(2)}) collective-permute-start(f32[2,8,3840]{2,1,0:T(8,128)S(1)} %collective-permute-done.2), channel_id=1, source_target_pairs={{0,240},{16,0},{32,16},{48,32},{64,48},{80,64},{96,80},{112,96},{1... | collective-permute-start | bytes 737288 | tf_op jit(solution)/shard_map/ppermute | solution.py:43
  41.7 9.3 %collective-permute-start.10 = (f32[2,8,3840]{2,1,0:T(8,128)S(1)}, f32[2,8,3840]{2,1,0:T(8,128)S(1)}, u32[]{:S(2)}, u32[]{:S(2)}) collective-permute-start(f32[2,8,3840]{2,1,0:T(8,128)S(1)} %collective-permute-done.9), channel_id=1, source_target_pairs={{0,16},{16,32},{32,48},{48,64},{64,80},{80,96},{96,112},{112,128},... | collective-permute-start | bytes 737288 | tf_op jit(solution)/shard_map/ppermute | solution.py:42
  45.4 9.3 %collective-permute-start.4 = (f32[2,8,3840]{2,1,0:T(8,128)S(1)}, f32[2,8,3840]{2,1,0:T(8,128)}, u32[]{:S(2)}, u32[]{:S(2)}) collective-permute-start(f32[2,8,3840]{2,1,0:T(8,128)S(1)} %collective-permute-done.3), channel_id=1, source_target_pairs={{0,240},{16,0},{32,16},{48,32},{64,48},{80,64},{96,80},{112,96},{1... | collective-permute-start | bytes 737288 | tf_op jit(solution)/shard_map/ppermute | solution.py:43
  51.0 9.4 %collective-permute-start.11 = (f32[2,8,3840]{2,1,0:T(8,128)S(1)}, f32[2,8,3840]{2,1,0:T(8,128)S(1)}, u32[]{:S(2)}, u32[]{:S(2)}) collective-permute-start(f32[2,8,3840]{2,1,0:T(8,128)S(1)} %collective-permute-done.10), channel_id=1, source_target_pairs={{0,16},{16,32},{32,48},{48,64},{64,80},{80,96},{96,112},{112,128},... | collective-permute-start | bytes 737288 | tf_op jit(solution)/shard_map/ppermute | solution.py:42
  54.7 10.2 %collective-permute-start.5 = (f32[2,8,3840]{2,1,0:T(8,128)}, f32[2,8,3840]{2,1,0:T(8,128)}, u32[]{:S(2)}, u32[]{:S(2)}) collective-permute-start(f32[2,8,3840]{2,1,0:T(8,128)} %collective-permute-done.4), channel_id=1, source_target_pairs={{0,240},{16,0},{32,16},{48,32},{64,48},{80,64},{96,80},{112,96},{1... | collective-permute-start | bytes 737288 | tf_op jit(solution)/shard_map/ppermute | solution.py:43
  60.4 10.1 %collective-permute-start.12 = (f32[2,8,3840]{2,1,0:T(8,128)S(1)}, f32[2,8,3840]{2,1,0:T(8,128)S(1)}, u32[]{:S(2)}, u32[]{:S(2)}) collective-permute-start(f32[2,8,3840]{2,1,0:T(8,128)S(1)} %collective-permute-done.11), channel_id=1, source_target_pairs={{0,16},{16,32},{32,48},{48,64},{64,80},{80,96},{96,112},{112,128},... | collective-permute-start | bytes 737288 | tf_op jit(solution)/shard_map/ppermute | solution.py:42
  64.9 11.6 %collective-permute-start.6 = (f32[2,8,3840]{2,1,0:T(8,128)}, f32[2,8,3840]{2,1,0:T(8,128)S(1)}, u32[]{:S(2)}, u32[]{:S(2)}) collective-permute-start(f32[2,8,3840]{2,1,0:T(8,128)} %collective-permute-done.5), channel_id=1, source_target_pairs={{0,240},{16,0},{32,16},{48,32},{64,48},{80,64},{96,80},{112,96},{1... | collective-permute-start | bytes 737288 | tf_op jit(solution)/shard_map/ppermute | solution.py:43
  70.5 11.5 %collective-permute-start.13 = (f32[2,8,3840]{2,1,0:T(8,128)S(1)}, f32[2,8,3840]{2,1,0:T(8,128)S(1)}, u32[]{:S(2)}, u32[]{:S(2)}) collective-permute-start(f32[2,8,3840]{2,1,0:T(8,128)S(1)} %collective-permute-done.12), channel_id=1, source_target_pairs={{0,16},{16,32},{32,48},{48,64},{64,80},{80,96},{96,112},{112,128},... | collective-permute-start | bytes 737288 | tf_op jit(solution)/shard_map/ppermute | solution.py:42
  76.5 10.0 %collective-permute-start.7 = (f32[2,8,3840]{2,1,0:T(8,128)S(1)}, f32[2,8,3840]{2,1,0:T(8,128)S(1)}, u32[]{:S(2)}, u32[]{:S(2)}) collective-permute-start(f32[2,8,3840]{2,1,0:T(8,128)S(1)} %collective-permute-done.6), channel_id=1, source_target_pairs={{0,240},{16,0},{32,16},{48,32},{64,48},{80,64},{96,80},{112,96},{1... | collective-permute-start | bytes 737288 | tf_op jit(solution)/shard_map/ppermute | solution.py:43
  82.0 10.1 %collective-permute-start.14 = (f32[2,8,3840]{2,1,0:T(8,128)S(1)}, f32[2,8,3840]{2,1,0:T(8,128)S(1)}, u32[]{:S(2)}, u32[]{:S(2)}) collective-permute-start(f32[2,8,3840]{2,1,0:T(8,128)S(1)} %collective-permute-done.13), channel_id=1, source_target_pairs={{0,16},{16,32},{32,48},{48,64},{64,80},{80,96},{96,112},{112,128},... | collective-permute-start | bytes 737288 | tf_op jit(solution)/shard_map/ppermute | solution.py:42
  86.5 8.0 %collective-permute-start.16 = (f32[2,8,1920]{2,1,0:T(8,128)S(1)}, f32[2,8,1920]{2,1,0:T(8,128)S(1)}, u32[]{:S(2)}, u32[]{:S(2)}) collective-permute-start(f32[2,8,1920]{2,1,0:T(8,128)S(1)} %slice.76), channel_id=1, source_target_pairs={{0,240},{16,0},{32,16},{48,32},{64,48},{80,64},{96,80},{112,96},{1... | collective-permute-start | bytes 368648 | tf_op jit(solution)/shard_map/ppermute | solution.py:48
  92.2 8.0 %collective-permute-start.15 = (f32[2,8,1920]{2,1,0:T(8,128)S(1)}, f32[2,8,1920]{2,1,0:T(8,128)S(1)}, u32[]{:S(2)}, u32[]{:S(2)}) collective-permute-start(f32[2,8,1920]{2,1,0:T(8,128)S(1)} %slice.75), channel_id=1, source_target_pairs={{0,16},{16,32},{32,48},{48,64},{64,80},{80,96},{96,112},{112,128},... | collective-permute-start | bytes 368648 | tf_op jit(solution)/shard_map/ppermute | solution.py:47
  107.4 1.3 copy-start.1
  112.2 8.1 %copy-start.2 = (s32[2,36]{1,0:T(2,128)S(1)}, s32[2,36]{1,0:T(2,128)}, u32[]{:S(2)}) copy-start(s32[2,36]{1,0:T(2,128)} %param.17) | copy-start | bytes 868
  113.3 4.7 %collective-permute-start.17 = (f32[2,4,16,5,384]{4,2,3,0,1:T(8,128)}, f32[2,4,16,5,384]{4,2,3,0,1:T(8,128)S(1)}, u32[]{:S(2)}, u32[]{:S(2)}) collective-permute-start(f32[2,4,16,5,384]{4,2,3,0,1:T(8,128)} %fusion.4), channel_id=1, source_target_pairs={{0,1},{1,0},{2,3},{3,2},{4,5},{5,4},{6,7},{7,6},{8,9},{9,8},{10,11... | collective-permute-start | bytes 2949128 | tf_op jit(solution)/shard_map/ppermute | solution.py:61
  118.2 7.3 %collective-permute-start.18 = (f32[2,8,5,384]{3,1,2,0:T(8,128)S(1)}, f32[2,8,5,384]{3,1,2,0:T(8,128)S(1)}, u32[]{:S(2)}, u32[]{:S(2)}) collective-permute-start(f32[2,8,5,384]{3,1,2,0:T(8,128)S(1)} %select_bitcast_fusion.1), channel_id=1, source_target_pairs={{0,2},{1,3},{2,4},{3,5},{4,6},{5,7},{6,0},{7,1},{8,10},{9,11},{10,... | collective-permute-start | bytes 368648 | tf_op jit(solution)/shard_map/ppermute | solution.py:70
  120.7 8.3 %collective-permute-start.21 = (f32[2,8,5,384]{3,1,2,0:T(8,128)S(1)}, f32[2,8,5,384]{3,1,2,0:T(8,128)S(1)}, u32[]{:S(2)}, u32[]{:S(2)}) collective-permute-start(f32[2,8,5,384]{3,1,2,0:T(8,128)S(1)} %select_bitcast_fusion), channel_id=1, source_target_pairs={{0,6},{1,7},{2,0},{3,1},{4,2},{5,3},{6,4},{7,5},{8,14},{9,15},{10,... | collective-permute-start | bytes 368648 | tf_op jit(solution)/shard_map/ppermute | solution.py:71
  125.5 6.8 %collective-permute-start.19 = (f32[2,8,5,384]{3,1,2,0:T(8,128)S(1)}, f32[2,8,5,384]{3,1,2,0:T(8,128)S(1)}, u32[]{:S(2)}, u32[]{:S(2)}) collective-permute-start(f32[2,8,5,384]{3,1,2,0:T(8,128)S(1)} %bitcast_add_fusion.5), channel_id=1, source_target_pairs={{0,2},{1,3},{2,4},{3,5},{4,6},{5,7},{6,0},{7,1},{8,10},{9,11},{10,... | collective-permute-start | bytes 368648 | tf_op jit(solution)/shard_map/ppermute | solution.py:70
  128.9 8.0 %collective-permute-start.22 = (f32[2,8,5,384]{3,1,2,0:T(8,128)S(1)}, f32[2,8,5,384]{3,1,2,0:T(8,128)S(1)}, u32[]{:S(2)}, u32[]{:S(2)}) collective-permute-start(f32[2,8,5,384]{3,1,2,0:T(8,128)S(1)} %bitcast_add_fusion.2), channel_id=1, source_target_pairs={{0,6},{1,7},{2,0},{3,1},{4,2},{5,3},{6,4},{7,5},{8,14},{9,15},{10,... | collective-permute-start | bytes 368648 | tf_op jit(solution)/shard_map/ppermute | solution.py:71
  132.3 7.1 %collective-permute-start.20 = (f32[2,8,5,384]{3,1,2,0:T(8,128)S(1)}, f32[2,8,5,384]{3,1,2,0:T(8,128)S(1)}, u32[]{:S(2)}, u32[]{:S(2)}) collective-permute-start(f32[2,8,5,384]{3,1,2,0:T(8,128)S(1)} %bitcast_add_fusion.4), channel_id=1, source_target_pairs={{0,2},{1,3},{2,4},{3,5},{4,6},{5,7},{6,0},{7,1},{8,10},{9,11},{10,... | collective-permute-start | bytes 368648 | tf_op jit(solution)/shard_map/ppermute | solution.py:70
  136.9 8.0 %collective-permute-start.23 = (f32[2,8,5,384]{3,1,2,0:T(8,128)S(1)}, f32[2,8,5,384]{3,1,2,0:T(8,128)S(1)}, u32[]{:S(2)}, u32[]{:S(2)}) collective-permute-start(f32[2,8,5,384]{3,1,2,0:T(8,128)S(1)} %bitcast_add_fusion.1), channel_id=1, source_target_pairs={{0,6},{1,7},{2,0},{3,1},{4,2},{5,3},{6,4},{7,5},{8,14},{9,15},{10,... | collective-permute-start | bytes 368648 | tf_op jit(solution)/shard_map/ppermute | solution.py:71
  145.0 8.3 %collective-permute-start.24 = (f32[16,5,384]{2,0,1:T(8,128)S(1)}, f32[16,5,384]{2,0,1:T(8,128)S(1)}, u32[]{:S(2)}, u32[]{:S(2)}) collective-permute-start(f32[16,5,384]{2,0,1:T(8,128)S(1)} %fusion.14), channel_id=1, source_target_pairs={{0,8},{1,9},{2,10},{3,11},{4,12},{5,13},{6,14},{7,15},{8,0},{9,1},... | collective-permute-start | bytes 368648 | tf_op jit(solution)/shard_map/ppermute | solution.py:76

commit v3 on v2

--- a/solution.py
+++ b/solution.py
@@ -90,16 +90,17 @@
     col_anchor = lax.axis_index("col") * local_cols
     out_first = tile_flags(lists_first, row_anchor, local_rows, panel_width)
     out_second = tile_flags(lists_second, row_anchor, local_rows, panel_width)
-    panels = jnp.concatenate(
+    panels = jnp.concatenate([factors_first, factors_second], axis=0)
+    stacked = jnp.transpose(panels, (1, 0, 2)).reshape(share_rows, members * local_cols)
+    pieces, z = gather_rows(stacked, n_row)
+    col_mask = jnp.concatenate(
         [
-            factors_first * tile_flags(lists_first, col_anchor, local_cols, panel_width)[:, None, :],
-            factors_second * tile_flags(lists_second, col_anchor, local_cols, panel_width)[:, None, :],
+            tile_flags(lists_first, col_anchor, local_cols, panel_width),
+            tile_flags(lists_second, col_anchor, local_cols, panel_width),
         ],
         axis=0,
     )
-    stacked = jnp.transpose(panels, (1, 0, 2)).reshape(share_rows, members * local_cols)
-    pieces, z = gather_rows(stacked, n_row)
-    pieces = pieces.reshape(nz, X_LO, share_rows, members, local_cols)
+    pieces = pieces.reshape(nz, X_LO, share_rows, members, local_cols) * col_mask
     partial_value = jnp.einsum(
         "tlkmj,ij->ltkmi", pieces, anc_inv, precision=highest, preferred_element_type=jnp.float32
     )
@@ -111,9 +112,8 @@
     coupling = jnp.einsum("cqk,qci->kci", parent_link, chosen, precision=highest)
     second_partial = partial_value[:, n_first:] - chosen_mask[None, :, :] * coupling
     combined = jnp.concatenate([first_partial, second_partial], axis=1)
-    ny = n_col // (X_HI * CORES)
-    combined = combined.reshape(X_HI, ny, CORES, panel_width // n_col, members, local_rows)
-    reduced = reduce_cols(combined, n_col)
+    combined = combined.reshape(n_col, panel_width // n_col, members, local_rows)
+    reduced = jnp.sum(lax.all_to_all(combined, "col", 0, 0, tiled=True), axis=0)
     reduced = jnp.transpose(reduced, (1, 0, 2))
     first_cols = -out_first[:, None, :] * reduced[:n_first]
     second_cols = -out_second[:, None, :] * reduced[n_first:]

time: 156 us -> 150 us (0.962)
  the two profiles are of different devices: /device:TPU:24 before, /device:TPU:1 now
where the time goes in v3:
time: 150 us; the launch traced here: 149 us
  starting transfers between devices  83.3 us (56%)
  waiting for transfers between devices  41.3 us (28%)
  matrix products  8.85 us (6%)
  local copies, waits for them, and re-layouts  8.13 us (5%)
  other arithmetic  5.89 us (4%)
    ppermute x7, starting transfers between devices, gather_rows(): bwd = lax.ppermute(bwd, 'row', down)  41.5 us
    all_to_all x1, waiting for transfers between devices, local(): reduced = jnp.sum(lax.all_to_all(combined, 'col', 0, 0, tiled=True), axis=0)  26.9 us
    all_to_all x1, starting transfers between devices, local(): reduced = jnp.sum(lax.all_to_all(combined, 'col', 0, 0, tiled=True), axis=0)  17.5 us
    ppermute x7, starting transfers between devices, gather_rows(): fwd = lax.ppermute(fwd, 'row', up)  13.4 us
    dot_general x1, matrix products, local(): jnp.einsum('tlkmj,ij->ltkmi', pieces, anc_inv, precision=highest, preferr...  6.32 us
    ppermute x7, waiting for transfers between devices, gather_rows(): bwd = lax.ppermute(bwd, 'row', down)  6.07 us
    ppermute x1, waiting for transfers between devices, gather_rows(): last_fwd = lax.ppermute(fwd[..., :half], 'row', up)  5.17 us
    ppermute x1, starting transfers between devices, gather_rows(): last_bwd = lax.ppermute(bwd[..., half:], 'row', down)  5.02 us
  transfers between devices with their start and end apart: 18, of which 11 were waited for; matrix products, arithmetic and copies ran while one was open for 4% of the time, Pallas kernels for 0%

profile of v3, /device:TPU:1, one launch (start us, length us, event | category | flops | bytes accessed | tf_op | source)
XLA Modules:
  0.0 148.6 jit_solution(7912964412111559553)
XLA Ops:
  0.6 0.0 copy-start
  0.6 1.0 constant_dynamic-update-slice_fusion.1
  1.6 0.8 constant_dynamic-update-slice_fusion
  2.4 3.9 %collective-permute-start = (f32[8,3840]{1,0:T(8,128)S(1)}, f32[8,3840]{1,0:T(8,128)S(1)}, u32[]{:S(2)}, u32[]{:S(2)}) collective-permute-start(f32[8,3840]{1,0:T(8,128)S(1)} %bitcast.46), channel_id=1, source_target_pairs={{0,256},{16,272},{32,288},{48,304},{64,320},{80,336},{96,352},{112... | collective-permute-start | bytes 368648 | tf_op jit(solution)/shard_map/ppermute | solution.py:33
  6.4 2.2 %collective-permute-done = f32[8,3840]{1,0:T(8,128)S(1)} collective-permute-done((f32[8,3840]{1,0:T(8,128)S(1)}, f32[8,3840]{1,0:T(8,128)S(1)}, u32[]{:S(2)}, u32[]{:S(2)}) %collective-permute-start) | collective-permute-done | bytes 122912 | tf_op jit(solution)/shard_map/ppermute | solution.py:33
  8.7 11.8 %collective-permute-start.1 = (f32[2,8,3840]{2,1,0:T(8,128)S(1)}, f32[2,8,3840]{2,1,0:T(8,128)S(1)}, u32[]{:S(2)}, u32[]{:S(2)}) collective-permute-start(f32[2,8,3840]{2,1,0:T(8,128)S(1)} %maximum_select_fusion.1), channel_id=1, source_target_pairs={{0,240},{16,0},{32,16},{48,32},{64,48},{80,64},{96,80},{112,96},{1... | collective-permute-start | bytes 737288 | tf_op jit(solution)/shard_map/ppermute | solution.py:43
  20.5 1.9 %collective-permute-start.8 = (f32[2,8,3840]{2,1,0:T(8,128)S(1)}, f32[2,8,3840]{2,1,0:T(8,128)S(1)}, u32[]{:S(2)}, u32[]{:S(2)}) collective-permute-start(f32[2,8,3840]{2,1,0:T(8,128)S(1)} %maximum_select_fusion.1), channel_id=1, source_target_pairs={{0,16},{16,32},{32,48},{48,64},{64,80},{80,96},{96,112},{112,128},... | collective-permute-start | bytes 737288 | tf_op jit(solution)/shard_map/ppermute | solution.py:42
  22.4 1.7 %collective-permute-done.1 = f32[2,8,3840]{2,1,0:T(8,128)S(1)} collective-permute-done((f32[2,8,3840]{2,1,0:T(8,128)S(1)}, f32[2,8,3840]{2,1,0:T(8,128)S(1)}, u32[]{:S(2)}, u32[]{:S(2)}) %collective-permute-start.1) | collective-permute-done | bytes 245792 | tf_op jit(solution)/shard_map/ppermute | solution.py:43
  24.2 5.3 %collective-permute-start.2 = (f32[2,8,3840]{2,1,0:T(8,128)S(1)}, f32[2,8,3840]{2,1,0:T(8,128)S(1)}, u32[]{:S(2)}, u32[]{:S(2)}) collective-permute-start(f32[2,8,3840]{2,1,0:T(8,128)S(1)} %collective-permute-done.1), channel_id=1, source_target_pairs={{0,240},{16,0},{32,16},{48,32},{64,48},{80,64},{96,80},{112,96},{1... | collective-permute-start | bytes 737288 | tf_op jit(solution)/shard_map/ppermute | solution.py:43
  29.5 0.0 collective-permute-done.8
  29.5 1.9 %collective-permute-start.9 = (f32[2,8,3840]{2,1,0:T(8,128)S(1)}, f32[2,8,3840]{2,1,0:T(8,128)S(1)}, u32[]{:S(2)}, u32[]{:S(2)}) collective-permute-start(f32[2,8,3840]{2,1,0:T(8,128)S(1)} %collective-permute-done.8), channel_id=1, source_target_pairs={{0,16},{16,32},{32,48},{48,64},{64,80},{80,96},{96,112},{112,128},... | collective-permute-start | bytes 737288 | tf_op jit(solution)/shard_map/ppermute | solution.py:42
  31.4 0.8 compare_reduce_fusion.1
  32.2 0.8 compare_reduce_fusion
  33.0 0.0 collective-permute-done.2
  33.1 4.6 %collective-permute-start.3 = (f32[2,8,3840]{2,1,0:T(8,128)S(1)}, f32[2,8,3840]{2,1,0:T(8,128)S(1)}, u32[]{:S(2)}, u32[]{:S(2)}) collective-permute-start(f32[2,8,3840]{2,1,0:T(8,128)S(1)} %collective-permute-done.2), channel_id=1, source_target_pairs={{0,240},{16,0},{32,16},{48,32},{64,48},{80,64},{96,80},{112,96},{1... | collective-permute-start | bytes 737288 | tf_op jit(solution)/shard_map/ppermute | solution.py:43
  37.6 0.0 collective-permute-done.9
  37.6 1.9 %collective-permute-start.10 = (f32[2,8,3840]{2,1,0:T(8,128)S(1)}, f32[2,8,3840]{2,1,0:T(8,128)S(1)}, u32[]{:S(2)}, u32[]{:S(2)}) collective-permute-start(f32[2,8,3840]{2,1,0:T(8,128)S(1)} %collective-permute-done.9), channel_id=1, source_target_pairs={{0,16},{16,32},{32,48},{48,64},{64,80},{80,96},{96,112},{112,128},... | collective-permute-start | bytes 737288 | tf_op jit(solution)/shard_map/ppermute | solution.py:42
  39.6 0.8 compare_reduce_fusion.2
  40.4 0.7 compare_select_fusion
  41.0 0.0 collective-permute-done.3
  41.0 4.7 %collective-permute-start.4 = (f32[2,8,3840]{2,1,0:T(8,128)S(1)}, f32[2,8,3840]{2,1,0:T(8,128)}, u32[]{:S(2)}, u32[]{:S(2)}) collective-permute-start(f32[2,8,3840]{2,1,0:T(8,128)S(1)} %collective-permute-done.3), channel_id=1, source_target_pairs={{0,240},{16,0},{32,16},{48,32},{64,48},{80,64},{96,80},{112,96},{1... | collective-permute-start | bytes 737288 | tf_op jit(solution)/shard_map/ppermute | solution.py:43
  45.8 0.0 collective-permute-done.10
  45.8 1.9 %collective-permute-start.11 = (f32[2,8,3840]{2,1,0:T(8,128)S(1)}, f32[2,8,3840]{2,1,0:T(8,128)S(1)}, u32[]{:S(2)}, u32[]{:S(2)}) collective-permute-start(f32[2,8,3840]{2,1,0:T(8,128)S(1)} %collective-permute-done.10), channel_id=1, source_target_pairs={{0,16},{16,32},{32,48},{48,64},{64,80},{80,96},{96,112},{112,128},... | collective-permute-start | bytes 737288 | tf_op jit(solution)/shard_map/ppermute | solution.py:42
  47.7 0.7 compare_and_fusion
  48.4 0.5 collective-permute-done.4
  48.9 5.1 %collective-permute-start.5 = (f32[2,8,3840]{2,1,0:T(8,128)}, f32[2,8,3840]{2,1,0:T(8,128)}, u32[]{:S(2)}, u32[]{:S(2)}) collective-permute-start(f32[2,8,3840]{2,1,0:T(8,128)} %collective-permute-done.4), channel_id=1, source_target_pairs={{0,240},{16,0},{32,16},{48,32},{64,48},{80,64},{96,80},{112,96},{1... | collective-permute-start | bytes 737288 | tf_op jit(solution)/shard_map/ppermute | solution.py:43
  54.0 0.0 collective-permute-done.11
  54.0 1.9 %collective-permute-start.12 = (f32[2,8,3840]{2,1,0:T(8,128)S(1)}, f32[2,8,3840]{2,1,0:T(8,128)S(1)}, u32[]{:S(2)}, u32[]{:S(2)}) collective-permute-start(f32[2,8,3840]{2,1,0:T(8,128)S(1)} %collective-permute-done.11), channel_id=1, source_target_pairs={{0,16},{16,32},{32,48},{48,64},{64,80},{80,96},{96,112},{112,128},... | collective-permute-start | bytes 737288 | tf_op jit(solution)/shard_map/ppermute | solution.py:42
  56.0 0.6 gather_fusion
  56.6 0.1 broadcast_select_fusion
  56.7 0.8 collective-permute-done.5
  57.5 5.0 %collective-permute-start.6 = (f32[2,8,3840]{2,1,0:T(8,128)}, f32[2,8,3840]{2,1,0:T(8,128)S(1)}, u32[]{:S(2)}, u32[]{:S(2)}) collective-permute-start(f32[2,8,3840]{2,1,0:T(8,128)} %collective-permute-done.5), channel_id=1, source_target_pairs={{0,240},{16,0},{32,16},{48,32},{64,48},{80,64},{96,80},{112,96},{1... | collective-permute-start | bytes 737288 | tf_op jit(solution)/shard_map/ppermute | solution.py:43
  62.5 0.0 collective-permute-done.12
  62.5 1.9 %collective-permute-start.13 = (f32[2,8,3840]{2,1,0:T(8,128)S(1)}, f32[2,8,3840]{2,1,0:T(8,128)S(1)}, u32[]{:S(2)}, u32[]{:S(2)}) collective-permute-start(f32[2,8,3840]{2,1,0:T(8,128)S(1)} %collective-permute-done.12), channel_id=1, source_target_pairs={{0,16},{16,32},{32,48},{48,64},{64,80},{80,96},{96,112},{112,128},... | collective-permute-start | bytes 737288 | tf_op jit(solution)/shard_map/ppermute | solution.py:42
  64.5 2.0 %collective-permute-done.6 = f32[2,8,3840]{2,1,0:T(8,128)S(1)} collective-permute-done((f32[2,8,3840]{2,1,0:T(8,128)}, f32[2,8,3840]{2,1,0:T(8,128)S(1)}, u32[]{:S(2)}, u32[]{:S(2)}) %collective-permute-start.6) | collective-permute-done | bytes 245792 | tf_op jit(solution)/shard_map/ppermute | solution.py:43
  66.5 4.9 %collective-permute-start.7 = (f32[2,8,3840]{2,1,0:T(8,128)S(1)}, f32[2,8,3840]{2,1,0:T(8,128)S(1)}, u32[]{:S(2)}, u32[]{:S(2)}) collective-permute-start(f32[2,8,3840]{2,1,0:T(8,128)S(1)} %collective-permute-done.6), channel_id=1, source_target_pairs={{0,240},{16,0},{32,16},{48,32},{64,48},{80,64},{96,80},{112,96},{1... | collective-permute-start | bytes 737288 | tf_op jit(solution)/shard_map/ppermute | solution.py:43
  71.4 0.1 collective-permute-done.13
  71.5 1.9 %collective-permute-start.14 = (f32[2,8,3840]{2,1,0:T(8,128)S(1)}, f32[2,8,3840]{2,1,0:T(8,128)S(1)}, u32[]{:S(2)}, u32[]{:S(2)}) collective-permute-start(f32[2,8,3840]{2,1,0:T(8,128)S(1)} %collective-permute-done.13), channel_id=1, source_target_pairs={{0,16},{16,32},{32,48},{48,64},{64,80},{80,96},{96,112},{112,128},... | collective-permute-start | bytes 737288 | tf_op jit(solution)/shard_map/ppermute | solution.py:42
  73.4 1.0 constant_dynamic-update-slice_fusion.13
  74.4 1.0 constant_dynamic-update-slice_fusion.12
  75.3 1.1 collective-permute-done.7
  76.4 5.0 %collective-permute-start.16 = (f32[2,8,1920]{2,1,0:T(8,128)S(1)}, f32[2,8,1920]{2,1,0:T(8,128)S(1)}, u32[]{:S(2)}, u32[]{:S(2)}) collective-permute-start(f32[2,8,1920]{2,1,0:T(8,128)S(1)} %slice.29), channel_id=1, source_target_pairs={{0,240},{16,0},{32,16},{48,32},{64,48},{80,64},{96,80},{112,96},{1... | collective-permute-start | bytes 368648 | tf_op jit(solution)/shard_map/ppermute | solution.py:48
  81.5 0.1 collective-permute-done.14
  81.6 1.9 %collective-permute-start.15 = (f32[2,8,1920]{2,1,0:T(8,128)S(1)}, f32[2,8,1920]{2,1,0:T(8,128)S(1)}, u32[]{:S(2)}, u32[]{:S(2)}) collective-permute-start(f32[2,8,1920]{2,1,0:T(8,128)S(1)} %slice.28), channel_id=1, source_target_pairs={{0,16},{16,32},{32,48},{48,64},{64,80},{80,96},{96,112},{112,128},... | collective-permute-start | bytes 368648 | tf_op jit(solution)/shard_map/ppermute | solution.py:47
  83.5 0.7 collective-permute-done.16
  84.2 5.2 %collective-permute-done.15 = f32[2,8,1920]{2,1,0:T(8,128)S(1)} collective-permute-done((f32[2,8,1920]{2,1,0:T(8,128)S(1)}, f32[2,8,1920]{2,1,0:T(8,128)S(1)}, u32[]{:S(2)}, u32[]{:S(2)}) %collective-permute-start.15) | collective-permute-done | bytes 122912 | tf_op jit(solution)/shard_map/ppermute | solution.py:47
  89.6 0.0 copy-done
  89.6 6.3 %fusion.4 = f32[2,16,8,5,384]{4,2,3,0,1:T(8,128)S(1)} fusion(f32[16,2,8,5,768]{4,2,3,1,0:T(8,128)S(1)} %constant_dynamic-update-slice_fusion.2, f32[5,768]{1,0:T(8,128)S(1)} %add_convert_fusion, f32[384,768]{1,0:T(8,128)S(1)} %copy-done), kind=kOutput, calls=%fused_computation.9 | convolution fusion | flops 4530831360 | bytes 7093248 | tf_op jit(solution)/shard_map/tlkmj,ij->ltkmi/dot_general | solution.py:104
  95.9 0.4 fusion.2
  96.3 0.2 copy.15
  96.5 0.0 copy-start.1
  96.5 1.3 copy-done.1
  97.8 0.1 slice.30
  97.9 0.6 gather_fusion.1
  98.5 2.5 %fusion.8 = f32[256,2,384]{2,0,1:T(8,128)S(1)} fusion(f32[2,256,256]{2,1,0:T(8,128)} %param.13, f32[256,5,384]{2,0,1:T(8,128)} %bitcast.43, f32[2,256,384]{2,1,0:T(8,128)S(1)} %gather_fusion.1, f32[2,384]{1,0:T(2,128)S(1)} %broadcast_select_fusion, pred[2]{0:T(512)(128)(4,1)S(1)} %compare_and_fusion), kind=kOutput, calls=%fused_computation.12 | convolution fusion | flops 604569600 | bytes 2886658 | tf_op jit(solution)/shard_map/cqk,qci->kci/dot_general | solution.py:112
  101.0 0.1 pad_maximum_fusion
  101.2 0.0 copy-start.2
  101.2 1.4 copy.17
  102.6 17.5 %all-to-all-start = ((f32[16,16,5,384]{3,1,2,0:T(8,128)}), f32[16,16,5,384]{3,1,2,0:T(8,128)S(1)}, u32[]{:S(2)}, u32[]{:S(2)}) async-start(f32[16,16,5,384]{3,1,2,0:T(8,128)} %copy.17), calls=%async_computation | async-start | bytes 3932160 | tf_op jit(solution)/shard_map/all_to_all | solution.py:116
  120.1 0.1 compare_reduce_fusion.3
  120.3 26.9 %all-to-all-done = f32[16,16,5,384]{3,1,2,0:T(8,128)S(1)} async-done(((f32[16,16,5,384]{3,1,2,0:T(8,128)}), f32[16,16,5,384]{3,1,2,0:T(8,128)S(1)}, u32[]{:S(2)}, u32[]{:S(2)}) %all-to-all-start) | async-done | bytes 1966112 | tf_op jit(solution)/shard_map/all_to_all | solution.py:116
  147.2 0.1 reduce_sum.9
  147.3 0.6 slice_multiply_fusion
  147.9 0.6 slice_multiply_fusion.1
  (26 shorter events, 0.4 us)
Async XLA Ops:
  0.6 89.0 %copy-start = (f32[384,768]{1,0:T(8,128)S(1)}, f32[384,768]{1,0:T(8,128)}, u32[]{:S(2)}) copy-start(f32[384,768]{1,0:T(8,128)} %param.7) | copy-start | bytes 3538948
  2.4 6.2 %collective-permute-start = (f32[8,3840]{1,0:T(8,128)S(1)}, f32[8,3840]{1,0:T(8,128)S(1)}, u32[]{:S(2)}, u32[]{:S(2)}) collective-permute-start(f32[8,3840]{1,0:T(8,128)S(1)} %bitcast.46), channel_id=1, source_target_pairs={{0,256},{16,272},{32,288},{48,304},{64,320},{80,336},{96,352},{112... | collective-permute-start | bytes 368648 | tf_op jit(solution)/shard_map/ppermute | solution.py:33
  8.7 15.5 %collective-permute-start.1 = (f32[2,8,3840]{2,1,0:T(8,128)S(1)}, f32[2,8,3840]{2,1,0:T(8,128)S(1)}, u32[]{:S(2)}, u32[]{:S(2)}) collective-permute-start(f32[2,8,3840]{2,1,0:T(8,128)S(1)} %maximum_select_fusion.1), channel_id=1, source_target_pairs={{0,240},{16,0},{32,16},{48,32},{64,48},{80,64},{96,80},{112,96},{1... | collective-permute-start | bytes 737288 | tf_op jit(solution)/shard_map/ppermute | solution.py:43
  20.5 9.0 %collective-permute-start.8 = (f32[2,8,3840]{2,1,0:T(8,128)S(1)}, f32[2,8,3840]{2,1,0:T(8,128)S(1)}, u32[]{:S(2)}, u32[]{:S(2)}) collective-permute-start(f32[2,8,3840]{2,1,0:T(8,128)S(1)} %maximum_select_fusion.1), channel_id=1, source_target_pairs={{0,16},{16,32},{32,48},{48,64},{64,80},{80,96},{96,112},{112,128},... | collective-permute-start | bytes 737288 | tf_op jit(solution)/shard_map/ppermute | solution.py:42
  24.2 8.9 %collective-permute-start.2 = (f32[2,8,3840]{2,1,0:T(8,128)S(1)}, f32[2,8,3840]{2,1,0:T(8,128)S(1)}, u32[]{:S(2)}, u32[]{:S(2)}) collective-permute-start(f32[2,8,3840]{2,1,0:T(8,128)S(1)} %collective-permute-done.1), channel_id=1, source_target_pairs={{0,240},{16,0},{32,16},{48,32},{64,48},{80,64},{96,80},{112,96},{1... | collective-permute-start | bytes 737288 | tf_op jit(solution)/shard_map/ppermute | solution.py:43
  29.5 8.2 %collective-permute-start.9 = (f32[2,8,3840]{2,1,0:T(8,128)S(1)}, f32[2,8,3840]{2,1,0:T(8,128)S(1)}, u32[]{:S(2)}, u32[]{:S(2)}) collective-permute-start(f32[2,8,3840]{2,1,0:T(8,128)S(1)} %collective-permute-done.8), channel_id=1, source_target_pairs={{0,16},{16,32},{32,48},{48,64},{64,80},{80,96},{96,112},{112,128},... | collective-permute-start | bytes 737288 | tf_op jit(solution)/shard_map/ppermute | solution.py:42
  33.1 8.0 %collective-permute-start.3 = (f32[2,8,3840]{2,1,0:T(8,128)S(1)}, f32[2,8,3840]{2,1,0:T(8,128)S(1)}, u32[]{:S(2)}, u32[]{:S(2)}) collective-permute-start(f32[2,8,3840]{2,1,0:T(8,128)S(1)} %collective-permute-done.2), channel_id=1, source_target_pairs={{0,240},{16,0},{32,16},{48,32},{64,48},{80,64},{96,80},{112,96},{1... | collective-permute-start | bytes 737288 | tf_op jit(solution)/shard_map/ppermute | solution.py:43
  37.6 8.2 %collective-permute-start.10 = (f32[2,8,3840]{2,1,0:T(8,128)S(1)}, f32[2,8,3840]{2,1,0:T(8,128)S(1)}, u32[]{:S(2)}, u32[]{:S(2)}) collective-permute-start(f32[2,8,3840]{2,1,0:T(8,128)S(1)} %collective-permute-done.9), channel_id=1, source_target_pairs={{0,16},{16,32},{32,48},{48,64},{64,80},{80,96},{96,112},{112,128},... | collective-permute-start | bytes 737288 | tf_op jit(solution)/shard_map/ppermute | solution.py:42
  41.0 7.9 %collective-permute-start.4 = (f32[2,8,3840]{2,1,0:T(8,128)S(1)}, f32[2,8,3840]{2,1,0:T(8,128)}, u32[]{:S(2)}, u32[]{:S(2)}) collective-permute-start(f32[2,8,3840]{2,1,0:T(8,128)S(1)} %collective-permute-done.3), channel_id=1, source_target_pairs={{0,240},{16,0},{32,16},{48,32},{64,48},{80,64},{96,80},{112,96},{1... | collective-permute-start | bytes 737288 | tf_op jit(solution)/shard_map/ppermute | solution.py:43
  45.8 8.2 %collective-permute-start.11 = (f32[2,8,3840]{2,1,0:T(8,128)S(1)}, f32[2,8,3840]{2,1,0:T(8,128)S(1)}, u32[]{:S(2)}, u32[]{:S(2)}) collective-permute-start(f32[2,8,3840]{2,1,0:T(8,128)S(1)} %collective-permute-done.10), channel_id=1, source_target_pairs={{0,16},{16,32},{32,48},{48,64},{64,80},{80,96},{96,112},{112,128},... | collective-permute-start | bytes 737288 | tf_op jit(solution)/shard_map/ppermute | solution.py:42
  48.9 8.6 %collective-permute-start.5 = (f32[2,8,3840]{2,1,0:T(8,128)}, f32[2,8,3840]{2,1,0:T(8,128)}, u32[]{:S(2)}, u32[]{:S(2)}) collective-permute-start(f32[2,8,3840]{2,1,0:T(8,128)} %collective-permute-done.4), channel_id=1, source_target_pairs={{0,240},{16,0},{32,16},{48,32},{64,48},{80,64},{96,80},{112,96},{1... | collective-permute-start | bytes 737288 | tf_op jit(solution)/shard_map/ppermute | solution.py:43
  54.0 8.4 %collective-permute-start.12 = (f32[2,8,3840]{2,1,0:T(8,128)S(1)}, f32[2,8,3840]{2,1,0:T(8,128)S(1)}, u32[]{:S(2)}, u32[]{:S(2)}) collective-permute-start(f32[2,8,3840]{2,1,0:T(8,128)S(1)} %collective-permute-done.11), channel_id=1, source_target_pairs={{0,16},{16,32},{32,48},{48,64},{64,80},{80,96},{96,112},{112,128},... | collective-permute-start | bytes 737288 | tf_op jit(solution)/shard_map/ppermute | solution.py:42
  57.5 9.0 %collective-permute-start.6 = (f32[2,8,3840]{2,1,0:T(8,128)}, f32[2,8,3840]{2,1,0:T(8,128)S(1)}, u32[]{:S(2)}, u32[]{:S(2)}) collective-permute-start(f32[2,8,3840]{2,1,0:T(8,128)} %collective-permute-done.5), channel_id=1, source_target_pairs={{0,240},{16,0},{32,16},{48,32},{64,48},{80,64},{96,80},{112,96},{1... | collective-permute-start | bytes 737288 | tf_op jit(solution)/shard_map/ppermute | solution.py:43
  62.5 9.0 %collective-permute-start.13 = (f32[2,8,3840]{2,1,0:T(8,128)S(1)}, f32[2,8,3840]{2,1,0:T(8,128)S(1)}, u32[]{:S(2)}, u32[]{:S(2)}) collective-permute-start(f32[2,8,3840]{2,1,0:T(8,128)S(1)} %collective-permute-done.12), channel_id=1, source_target_pairs={{0,16},{16,32},{32,48},{48,64},{64,80},{80,96},{96,112},{112,128},... | collective-permute-start | bytes 737288 | tf_op jit(solution)/shard_map/ppermute | solution.py:42
  66.5 10.0 %collective-permute-start.7 = (f32[2,8,3840]{2,1,0:T(8,128)S(1)}, f32[2,8,3840]{2,1,0:T(8,128)S(1)}, u32[]{:S(2)}, u32[]{:S(2)}) collective-permute-start(f32[2,8,3840]{2,1,0:T(8,128)S(1)} %collective-permute-done.6), channel_id=1, source_target_pairs={{0,240},{16,0},{32,16},{48,32},{64,48},{80,64},{96,80},{112,96},{1... | collective-permute-start | bytes 737288 | tf_op jit(solution)/shard_map/ppermute | solution.py:43
  71.5 10.1 %collective-permute-start.14 = (f32[2,8,3840]{2,1,0:T(8,128)S(1)}, f32[2,8,3840]{2,1,0:T(8,128)S(1)}, u32[]{:S(2)}, u32[]{:S(2)}) collective-permute-start(f32[2,8,3840]{2,1,0:T(8,128)S(1)} %collective-permute-done.13), channel_id=1, source_target_pairs={{0,16},{16,32},{32,48},{48,64},{64,80},{80,96},{96,112},{112,128},... | collective-permute-start | bytes 737288 | tf_op jit(solution)/shard_map/ppermute | solution.py:42
  76.4 7.8 %collective-permute-start.16 = (f32[2,8,1920]{2,1,0:T(8,128)S(1)}, f32[2,8,1920]{2,1,0:T(8,128)S(1)}, u32[]{:S(2)}, u32[]{:S(2)}) collective-permute-start(f32[2,8,1920]{2,1,0:T(8,128)S(1)} %slice.29), channel_id=1, source_target_pairs={{0,240},{16,0},{32,16},{48,32},{64,48},{80,64},{96,80},{112,96},{1... | collective-permute-start | bytes 368648 | tf_op jit(solution)/shard_map/ppermute | solution.py:48
  81.6 7.8 %collective-permute-start.15 = (f32[2,8,1920]{2,1,0:T(8,128)S(1)}, f32[2,8,1920]{2,1,0:T(8,128)S(1)}, u32[]{:S(2)}, u32[]{:S(2)}) collective-permute-start(f32[2,8,1920]{2,1,0:T(8,128)S(1)} %slice.28), channel_id=1, source_target_pairs={{0,16},{16,32},{32,48},{48,64},{64,80},{80,96},{96,112},{112,128},... | collective-permute-start | bytes 368648 | tf_op jit(solution)/shard_map/ppermute | solution.py:47
  96.5 1.3 copy-start.1
  101.2 19.0 %copy-start.2 = (s32[2,36]{1,0:T(2,128)S(1)}, s32[2,36]{1,0:T(2,128)}, u32[]{:S(2)}) copy-start(s32[2,36]{1,0:T(2,128)} %param.11) | copy-start | bytes 868
  102.6 44.6 %all-to-all-start = ((f32[16,16,5,384]{3,1,2,0:T(8,128)}), f32[16,16,5,384]{3,1,2,0:T(8,128)S(1)}, u32[]{:S(2)}, u32[]{:S(2)}) async-start(f32[16,16,5,384]{3,1,2,0:T(8,128)} %copy.17), calls=%async_computation | async-start | bytes 3932160 | tf_op jit(solution)/shard_map/all_to_all | solution.py:116

commit v4 on v3

--- a/solution.py
+++ b/solution.py
@@ -59,21 +59,18 @@
     send = jnp.take(value, 1 - core, axis=2)
     keep = jnp.take(value, core, axis=2)
     value = keep + lax.ppermute(send, "col", [(p, p ^ 1) for p in range(n_col)])
-    rows = value.shape[2]
-    upper = value[:, :, : rows // 2]
-    lower = value[:, :, rows // 2 :]
-    up = shift_pairs(n_col, ny, CORES, 1)
-    down = shift_pairs(n_col, ny, CORES, -1)
-    acc_up = jnp.take(upper, (y - 1) % ny, axis=1)
-    acc_down = jnp.take(lower, (y + 1) % ny, axis=1)
-    for s in range(1, ny):
-        acc_up = lax.ppermute(acc_up, "col", up) + jnp.take(upper, (y - s - 1) % ny, axis=1)
-        acc_down = lax.ppermute(acc_down, "col", down) + jnp.take(lower, (y + s + 1) % ny, axis=1)
-    value = jnp.concatenate([acc_up, acc_down], axis=1)
-    send = jnp.take(value, 1 - x_hi, axis=0)
-    keep = jnp.take(value, x_hi, axis=0)
-    half = n_col // X_HI
-    return keep + lax.ppermute(send, "col", [(p, (p + half) % n_col) for p in range(n_col)])
+    total = value[x_hi, y]
+    for dx in range(X_HI):
+        for dy in range(ny):
+            if dx == 0 and dy == 0:
+                continue
+            pairs = []
+            for p in range(n_col):
+                px, py, pc = p // (CORES * ny), (p // CORES) % ny, p % CORES
+                pairs.append((p, ((px + dx) % X_HI * ny + (py + dy) % ny) * CORES + pc))
+            block = value[(x_hi + dx) % X_HI, (y + dy) % ny]
+            total = total + lax.ppermute(block, "col", pairs)
+    return total
 
 
 def local(anc_inv, factors_first, factors_second, lists_first, lists_second, parents, parent_link):
@@ -112,8 +109,9 @@
     coupling = jnp.einsum("cqk,qci->kci", parent_link, chosen, precision=highest)
     second_partial = partial_value[:, n_first:] - chosen_mask[None, :, :] * coupling
     combined = jnp.concatenate([first_partial, second_partial], axis=1)
-    combined = combined.reshape(n_col, panel_width // n_col, members, local_rows)
-    reduced = jnp.sum(lax.all_to_all(combined, "col", 0, 0, tiled=True), axis=0)
+    ny = n_col // (X_HI * CORES)
+    combined = combined.reshape(X_HI, ny, CORES, panel_width // n_col, members, local_rows)
+    reduced = reduce_cols(combined, n_col)
     reduced = jnp.transpose(reduced, (1, 0, 2))
     first_cols = -out_first[:, None, :] * reduced[:n_first]
     second_cols = -out_second[:, None, :] * reduced[n_first:]

time: 150 us -> 154 us (1.027)
  starting transfers between devices: 83.3 us -> 104 us
  waiting for transfers between devices: 41.3 us -> 22.1 us
    ppermute x0 -> x8, starting transfers between devices: none -> 38.1 us  [the longest x7 25.6 us: reduce_cols(): total = total + lax.ppermute(block, 'col', pairs)]
    all_to_all x1 -> x0, waiting for transfers between devices: 26.9 us -> none  [local(): reduced = jnp.sum(lax.all_to_all(combined, 'col', 0, 0, tiled=True), axis=0)]
    all_to_all x1 -> x0, starting transfers between devices: 17.5 us -> none  [local(): reduced = jnp.sum(lax.all_to_all(combined, 'col', 0, 0, tiled=True), axis=0)]
    ppermute x0 -> x8, waiting for transfers between devices: none -> 7.79 us  [the longest x7 5.79 us: reduce_cols(): total = total + lax.ppermute(block, 'col', pairs)]
    unnamed x21 -> x23, local copies, waits for them, and re-layouts: 4.46 us -> 5.72 us
  transfers between devices with their start and end apart: 18 -> 25, of which waited for: 11 -> 13; matrix products, arithmetic and copies ran while one was open for 4% -> 4% of each run, Pallas kernels for 0% -> 0%
where the time goes in v4:
time: 154 us; the launch traced here: 152 us
  starting transfers between devices  104 us (68%)
  waiting for transfers between devices  22.1 us (14%)
  matrix products  9.03 us (6%)
  local copies, waits for them, and re-layouts  8.02 us (5%)
  other arithmetic  7.27 us (5%)
    ppermute x7, starting transfers between devices, gather_rows(): bwd = lax.ppermute(bwd, 'row', down)  41.5 us
    ppermute x7, starting transfers between devices, reduce_cols(): total = total + lax.ppermute(block, 'col', pairs)  25.6 us
    ppermute x7, starting transfers between devices, gather_rows(): fwd = lax.ppermute(fwd, 'row', up)  13.4 us
    ppermute x1, starting transfers between devices, reduce_cols(): value = keep + lax.ppermute(send, 'col', [(p, p ^ 1) for p in range(n_col)])  12.5 us
    dot_general x1, matrix products, local(): jnp.einsum('tlkmj,ij->ltkmi', pieces, anc_inv, precision=highest, preferr...  6.5 us
    ppermute x7, waiting for transfers between devices, gather_rows(): bwd = lax.ppermute(bwd, 'row', down)  6.04 us
    ppermute x7, waiting for transfers between devices, reduce_cols(): total = total + lax.ppermute(block, 'col', pairs)  5.79 us
    unnamed x23, local copies, waits for them, and re-layouts  5.72 us
  transfers between devices with their start and end apart: 25, of which 13 were waited for; matrix products, arithmetic and copies ran while one was open for 4% of the time, Pallas kernels for 0%

profile of v4, /device:TPU:1, one launch (start us, length us, event | category | flops | bytes accessed | tf_op | source)
XLA Modules:
  0.0 151.8 jit_solution(11981476846859751324)
XLA Ops:
  0.6 1.0 constant_dynamic-update-slice_fusion.1
  1.6 0.8 constant_dynamic-update-slice_fusion
  2.4 3.9 %collective-permute-start = (f32[8,3840]{1,0:T(8,128)S(1)}, f32[8,3840]{1,0:T(8,128)S(1)}, u32[]{:S(2)}, u32[]{:S(2)}) collective-permute-start(f32[8,3840]{1,0:T(8,128)S(1)} %bitcast.90), channel_id=1, source_target_pairs={{0,256},{16,272},{32,288},{48,304},{64,320},{80,336},{96,352},{112... | collective-permute-start | bytes 368648 | tf_op jit(solution)/shard_map/ppermute | solution.py:33
  6.4 2.2 %collective-permute-done = f32[8,3840]{1,0:T(8,128)S(1)} collective-permute-done((f32[8,3840]{1,0:T(8,128)S(1)}, f32[8,3840]{1,0:T(8,128)S(1)}, u32[]{:S(2)}, u32[]{:S(2)}) %collective-permute-start) | collective-permute-done | bytes 122912 | tf_op jit(solution)/shard_map/ppermute | solution.py:33
  8.7 11.8 %collective-permute-start.1 = (f32[2,8,3840]{2,1,0:T(8,128)S(1)}, f32[2,8,3840]{2,1,0:T(8,128)S(1)}, u32[]{:S(2)}, u32[]{:S(2)}) collective-permute-start(f32[2,8,3840]{2,1,0:T(8,128)S(1)} %maximum_select_fusion.1), channel_id=1, source_target_pairs={{0,240},{16,0},{32,16},{48,32},{64,48},{80,64},{96,80},{112,96},{1... | collective-permute-start | bytes 737288 | tf_op jit(solution)/shard_map/ppermute | solution.py:43
  20.5 1.9 %collective-permute-start.8 = (f32[2,8,3840]{2,1,0:T(8,128)S(1)}, f32[2,8,3840]{2,1,0:T(8,128)S(1)}, u32[]{:S(2)}, u32[]{:S(2)}) collective-permute-start(f32[2,8,3840]{2,1,0:T(8,128)S(1)} %maximum_select_fusion.1), channel_id=1, source_target_pairs={{0,16},{16,32},{32,48},{48,64},{64,80},{80,96},{96,112},{112,128},... | collective-permute-start | bytes 737288 | tf_op jit(solution)/shard_map/ppermute | solution.py:42
  22.4 1.7 %collective-permute-done.1 = f32[2,8,3840]{2,1,0:T(8,128)S(1)} collective-permute-done((f32[2,8,3840]{2,1,0:T(8,128)S(1)}, f32[2,8,3840]{2,1,0:T(8,128)S(1)}, u32[]{:S(2)}, u32[]{:S(2)}) %collective-permute-start.1) | collective-permute-done | bytes 245792 | tf_op jit(solution)/shard_map/ppermute | solution.py:43
  24.2 5.3 %collective-permute-start.2 = (f32[2,8,3840]{2,1,0:T(8,128)S(1)}, f32[2,8,3840]{2,1,0:T(8,128)S(1)}, u32[]{:S(2)}, u32[]{:S(2)}) collective-permute-start(f32[2,8,3840]{2,1,0:T(8,128)S(1)} %collective-permute-done.1), channel_id=1, source_target_pairs={{0,240},{16,0},{32,16},{48,32},{64,48},{80,64},{96,80},{112,96},{1... | collective-permute-start | bytes 737288 | tf_op jit(solution)/shard_map/ppermute | solution.py:43
  29.5 1.9 %collective-permute-start.9 = (f32[2,8,3840]{2,1,0:T(8,128)S(1)}, f32[2,8,3840]{2,1,0:T(8,128)S(1)}, u32[]{:S(2)}, u32[]{:S(2)}) collective-permute-start(f32[2,8,3840]{2,1,0:T(8,128)S(1)} %collective-permute-done.8), channel_id=1, source_target_pairs={{0,16},{16,32},{32,48},{48,64},{64,80},{80,96},{96,112},{112,128},... | collective-permute-start | bytes 737288 | tf_op jit(solution)/shard_map/ppermute | solution.py:42
  31.4 0.8 compare_reduce_fusion.1
  32.2 0.8 compare_reduce_fusion
  33.1 4.6 %collective-permute-start.3 = (f32[2,8,3840]{2,1,0:T(8,128)S(1)}, f32[2,8,3840]{2,1,0:T(8,128)S(1)}, u32[]{:S(2)}, u32[]{:S(2)}) collective-permute-start(f32[2,8,3840]{2,1,0:T(8,128)S(1)} %collective-permute-done.2), channel_id=1, source_target_pairs={{0,240},{16,0},{32,16},{48,32},{64,48},{80,64},{96,80},{112,96},{1... | collective-permute-start | bytes 737288 | tf_op jit(solution)/shard_map/ppermute | solution.py:43
  37.6 1.9 %collective-permute-start.10 = (f32[2,8,3840]{2,1,0:T(8,128)S(1)}, f32[2,8,3840]{2,1,0:T(8,128)S(1)}, u32[]{:S(2)}, u32[]{:S(2)}) collective-permute-start(f32[2,8,3840]{2,1,0:T(8,128)S(1)} %collective-permute-done.9), channel_id=1, source_target_pairs={{0,16},{16,32},{32,48},{48,64},{64,80},{80,96},{96,112},{112,128},... | collective-permute-start | bytes 737288 | tf_op jit(solution)/shard_map/ppermute | solution.py:42
  39.6 0.8 compare_reduce_fusion.2
  40.4 0.7 compare_select_fusion
  41.0 4.7 %collective-permute-start.4 = (f32[2,8,3840]{2,1,0:T(8,128)S(1)}, f32[2,8,3840]{2,1,0:T(8,128)}, u32[]{:S(2)}, u32[]{:S(2)}) collective-permute-start(f32[2,8,3840]{2,1,0:T(8,128)S(1)} %collective-permute-done.3), channel_id=1, source_target_pairs={{0,240},{16,0},{32,16},{48,32},{64,48},{80,64},{96,80},{112,96},{1... | collective-permute-start | bytes 737288 | tf_op jit(solution)/shard_map/ppermute | solution.py:43
  45.8 1.9 %collective-permute-start.11 = (f32[2,8,3840]{2,1,0:T(8,128)S(1)}, f32[2,8,3840]{2,1,0:T(8,128)S(1)}, u32[]{:S(2)}, u32[]{:S(2)}) collective-permute-start(f32[2,8,3840]{2,1,0:T(8,128)S(1)} %collective-permute-done.10), channel_id=1, source_target_pairs={{0,16},{16,32},{32,48},{48,64},{64,80},{80,96},{96,112},{112,128},... | collective-permute-start | bytes 737288 | tf_op jit(solution)/shard_map/ppermute | solution.py:42
  47.7 0.7 compare_and_fusion
  48.4 0.5 collective-permute-done.4
  48.9 5.1 %collective-permute-start.5 = (f32[2,8,3840]{2,1,0:T(8,128)}, f32[2,8,3840]{2,1,0:T(8,128)}, u32[]{:S(2)}, u32[]{:S(2)}) collective-permute-start(f32[2,8,3840]{2,1,0:T(8,128)} %collective-permute-done.4), channel_id=1, source_target_pairs={{0,240},{16,0},{32,16},{48,32},{64,48},{80,64},{96,80},{112,96},{1... | collective-permute-start | bytes 737288 | tf_op jit(solution)/shard_map/ppermute | solution.py:43
  54.0 1.9 %collective-permute-start.12 = (f32[2,8,3840]{2,1,0:T(8,128)S(1)}, f32[2,8,3840]{2,1,0:T(8,128)S(1)}, u32[]{:S(2)}, u32[]{:S(2)}) collective-permute-start(f32[2,8,3840]{2,1,0:T(8,128)S(1)} %collective-permute-done.11), channel_id=1, source_target_pairs={{0,16},{16,32},{32,48},{48,64},{64,80},{80,96},{96,112},{112,128},... | collective-permute-start | bytes 737288 | tf_op jit(solution)/shard_map/ppermute | solution.py:42
  56.1 0.6 gather_fusion
  56.6 0.1 broadcast_select_fusion
  56.7 0.8 collective-permute-done.5
  57.5 5.0 %collective-permute-start.6 = (f32[2,8,3840]{2,1,0:T(8,128)}, f32[2,8,3840]{2,1,0:T(8,128)S(1)}, u32[]{:S(2)}, u32[]{:S(2)}) collective-permute-start(f32[2,8,3840]{2,1,0:T(8,128)} %collective-permute-done.5), channel_id=1, source_target_pairs={{0,240},{16,0},{32,16},{48,32},{64,48},{80,64},{96,80},{112,96},{1... | collective-permute-start | bytes 737288 | tf_op jit(solution)/shard_map/ppermute | solution.py:43
  62.5 1.9 %collective-permute-start.13 = (f32[2,8,3840]{2,1,0:T(8,128)S(1)}, f32[2,8,3840]{2,1,0:T(8,128)S(1)}, u32[]{:S(2)}, u32[]{:S(2)}) collective-permute-start(f32[2,8,3840]{2,1,0:T(8,128)S(1)} %collective-permute-done.12), channel_id=1, source_target_pairs={{0,16},{16,32},{32,48},{48,64},{64,80},{80,96},{96,112},{112,128},... | collective-permute-start | bytes 737288 | tf_op jit(solution)/shard_map/ppermute | solution.py:42
  64.5 2.0 %collective-permute-done.6 = f32[2,8,3840]{2,1,0:T(8,128)S(1)} collective-permute-done((f32[2,8,3840]{2,1,0:T(8,128)}, f32[2,8,3840]{2,1,0:T(8,128)S(1)}, u32[]{:S(2)}, u32[]{:S(2)}) %collective-permute-start.6) | collective-permute-done | bytes 245792 | tf_op jit(solution)/shard_map/ppermute | solution.py:43
  66.5 4.9 %collective-permute-start.7 = (f32[2,8,3840]{2,1,0:T(8,128)S(1)}, f32[2,8,3840]{2,1,0:T(8,128)S(1)}, u32[]{:S(2)}, u32[]{:S(2)}) collective-permute-start(f32[2,8,3840]{2,1,0:T(8,128)S(1)} %collective-permute-done.6), channel_id=1, source_target_pairs={{0,240},{16,0},{32,16},{48,32},{64,48},{80,64},{96,80},{112,96},{1... | collective-permute-start | bytes 737288 | tf_op jit(solution)/shard_map/ppermute | solution.py:43
  71.4 0.1 collective-permute-done.13
  71.5 1.9 %collective-permute-start.14 = (f32[2,8,3840]{2,1,0:T(8,128)S(1)}, f32[2,8,3840]{2,1,0:T(8,128)S(1)}, u32[]{:S(2)}, u32[]{:S(2)}) collective-permute-start(f32[2,8,3840]{2,1,0:T(8,128)S(1)} %collective-permute-done.13), channel_id=1, source_target_pairs={{0,16},{16,32},{32,48},{48,64},{64,80},{80,96},{96,112},{112,128},... | collective-permute-start | bytes 737288 | tf_op jit(solution)/shard_map/ppermute | solution.py:42
  73.4 1.0 constant_dynamic-update-slice_fusion.13
  74.4 1.0 constant_dynamic-update-slice_fusion.12
  75.3 1.1 collective-permute-done.7
  76.4 5.0 %collective-permute-start.16 = (f32[2,8,1920]{2,1,0:T(8,128)S(1)}, f32[2,8,1920]{2,1,0:T(8,128)S(1)}, u32[]{:S(2)}, u32[]{:S(2)}) collective-permute-start(f32[2,8,1920]{2,1,0:T(8,128)S(1)} %slice.44), channel_id=1, source_target_pairs={{0,240},{16,0},{32,16},{48,32},{64,48},{80,64},{96,80},{112,96},{1... | collective-permute-start | bytes 368648 | tf_op jit(solution)/shard_map/ppermute | solution.py:48
  81.6 1.9 %collective-permute-start.15 = (f32[2,8,1920]{2,1,0:T(8,128)S(1)}, f32[2,8,1920]{2,1,0:T(8,128)S(1)}, u32[]{:S(2)}, u32[]{:S(2)}) collective-permute-start(f32[2,8,1920]{2,1,0:T(8,128)S(1)} %slice.43), channel_id=1, source_target_pairs={{0,16},{16,32},{32,48},{48,64},{64,80},{80,96},{96,112},{112,128},... | collective-permute-start | bytes 368648 | tf_op jit(solution)/shard_map/ppermute | solution.py:47
  83.5 0.7 collective-permute-done.16
  84.2 5.2 %collective-permute-done.15 = f32[2,8,1920]{2,1,0:T(8,128)S(1)} collective-permute-done((f32[2,8,1920]{2,1,0:T(8,128)S(1)}, f32[2,8,1920]{2,1,0:T(8,128)S(1)}, u32[]{:S(2)}, u32[]{:S(2)}) %collective-permute-start.15) | collective-permute-done | bytes 122912 | tf_op jit(solution)/shard_map/ppermute | solution.py:47
  89.6 6.5 %fusion.4 = f32[2,16,8,5,384]{4,2,3,0,1:T(8,128)S(1)} fusion(f32[16,2,8,5,768]{4,2,3,1,0:T(8,128)S(1)} %constant_dynamic-update-slice_fusion.2, f32[5,768]{1,0:T(8,128)S(1)} %add_convert_fusion, f32[384,768]{1,0:T(8,128)S(1)} %copy-done), kind=kOutput, calls=%fused_computation.9 | convolution fusion | flops 4530831360 | bytes 7093248 | tf_op jit(solution)/shard_map/tlkmj,ij->ltkmi/dot_general | solution.py:101
  96.1 0.4 fusion.2
  96.5 0.2 copy.14
  96.7 1.3 copy-done.2
  98.0 0.1 slice.45
  98.0 0.6 gather_fusion.1
  98.7 2.5 %fusion.8 = f32[256,2,384]{2,0,1:T(8,128)S(1)} fusion(f32[2,256,256]{2,1,0:T(8,128)} %param.15, f32[256,5,384]{2,0,1:T(8,128)} %bitcast.88, f32[2,256,384]{2,1,0:T(8,128)S(1)} %gather_fusion.1, f32[2,384]{1,0:T(2,128)S(1)} %broadcast_select_fusion, pred[2]{0:T(512)(128)(4,1)S(1)} %compare_and_fusion), kind=kOutput, calls=%fused_computation.12 | convolution fusion | flops 604569600 | bytes 2886658 | tf_op jit(solution)/shard_map/cqk,qci->kci/dot_general | solution.py:109
  101.2 0.1 pad_maximum_fusion
  101.3 1.3 copy-done.1
  102.6 0.1 select_bitcast_fusion
  102.7 12.5 %collective-permute-start.17 = (f32[2,4,16,5,384]{4,2,1,0,3:T(8,128)S(1)}, f32[2,4,16,5,384]{4,2,1,0,3:T(8,128)S(1)}, u32[]{:S(2)}, u32[]{:S(2)}) collective-permute-start(f32[2,4,16,5,384]{4,2,1,0,3:T(8,128)S(1)} %select_bitcast_fusion), channel_id=1, source_target_pairs={{0,1},{1,0},{2,3},{3,2},{4,5},{5,4},{6,7},{7,6},{8,9},{9,8},{10,11... | collective-permute-start | bytes 2949128 | tf_op jit(solution)/shard_map/ppermute | solution.py:61
  115.4 2.0 %collective-permute-done.17 = f32[2,4,16,5,384]{4,2,1,0,3:T(8,128)S(1)} collective-permute-done((f32[2,4,16,5,384]{4,2,1,0,3:T(8,128)S(1)}, f32[2,4,16,5,384]{4,2,1,0,3:T(8,128)S(1)}, u32[]{:S(2)}, u32[]{:S(2)}) %collective-permute-start.17) | collective-permute-done | bytes 983072 | tf_op jit(solution)/shard_map/ppermute | solution.py:61
  117.4 1.3 fusion.11
  118.7 0.1 dynamic-slice_bitcast_fusion.6
  118.8 7.1 %collective-permute-start.24 = (f32[16,5,384]{2,0,1:T(8,128)S(1)}, f32[16,5,384]{2,0,1:T(8,128)S(1)}, u32[]{:S(2)}, u32[]{:S(2)}) collective-permute-start(f32[16,5,384]{2,0,1:T(8,128)S(1)} %get-tuple-element.15), channel_id=1, source_target_pairs={{0,14},{1,15},{2,8},{3,9},{4,10},{5,11},{6,12},{7,13},{8,6},{9,7},... | collective-permute-start | bytes 368648 | tf_op jit(solution)/shard_map/ppermute | solution.py:72
  125.9 2.2 %collective-permute-start.23 = (f32[16,5,384]{2,0,1:T(8,128)S(1)}, f32[16,5,384]{2,0,1:T(8,128)S(1)}, u32[]{:S(2)}, u32[]{:S(2)}) collective-permute-start(f32[16,5,384]{2,0,1:T(8,128)S(1)} %get-tuple-element.16), channel_id=1, source_target_pairs={{0,12},{1,13},{2,14},{3,15},{4,8},{5,9},{6,10},{7,11},{8,4},{9,5},... | collective-permute-start | bytes 368648 | tf_op jit(solution)/shard_map/ppermute | solution.py:72
  128.1 0.1 compare_reduce_fusion.3
  128.2 5.1 %collective-permute-start.22 = (f32[16,5,384]{2,0,1:T(8,128)S(1)}, f32[16,5,384]{2,0,1:T(8,128)S(1)}, u32[]{:S(2)}, u32[]{:S(2)}) collective-permute-start(f32[16,5,384]{2,0,1:T(8,128)S(1)} %get-tuple-element.17), channel_id=1, source_target_pairs={{0,10},{1,11},{2,12},{3,13},{4,14},{5,15},{6,8},{7,9},{8,2},{9,3},... | collective-permute-start | bytes 368648 | tf_op jit(solution)/shard_map/ppermute | solution.py:72
  133.3 2.1 %collective-permute-start.21 = (f32[16,5,384]{2,0,1:T(8,128)S(1)}, f32[16,5,384]{2,0,1:T(8,128)S(1)}, u32[]{:S(2)}, u32[]{:S(2)}) collective-permute-start(f32[16,5,384]{2,0,1:T(8,128)S(1)} %get-tuple-element.18), channel_id=1, source_target_pairs={{0,8},{1,9},{2,10},{3,11},{4,12},{5,13},{6,14},{7,15},{8,0},{9,1},... | collective-permute-start | bytes 368648 | tf_op jit(solution)/shard_map/ppermute | solution.py:72
  135.5 3.9 %collective-permute-start.20 = (f32[16,5,384]{2,0,1:T(8,128)S(1)}, f32[16,5,384]{2,0,1:T(8,128)S(1)}, u32[]{:S(2)}, u32[]{:S(2)}) collective-permute-start(f32[16,5,384]{2,0,1:T(8,128)S(1)} %get-tuple-element.19), channel_id=1, source_target_pairs={{0,6},{1,7},{2,0},{3,1},{4,2},{5,3},{6,4},{7,5},{8,14},{9,15},{10,... | collective-permute-start | bytes 368648 | tf_op jit(solution)/shard_map/ppermute | solution.py:72
  139.4 3.3 %collective-permute-start.19 = (f32[16,5,384]{2,0,1:T(8,128)S(1)}, f32[16,5,384]{2,0,1:T(8,128)S(1)}, u32[]{:S(2)}, u32[]{:S(2)}) collective-permute-start(f32[16,5,384]{2,0,1:T(8,128)S(1)} %get-tuple-element.20), channel_id=1, source_target_pairs={{0,4},{1,5},{2,6},{3,7},{4,0},{5,1},{6,2},{7,3},{8,12},{9,13},{10,... | collective-permute-start | bytes 368648 | tf_op jit(solution)/shard_map/ppermute | solution.py:72
  142.7 1.9 %collective-permute-start.18 = (f32[16,5,384]{2,0,1:T(8,128)S(1)}, f32[16,5,384]{2,0,1:T(8,128)S(1)}, u32[]{:S(2)}, u32[]{:S(2)}) collective-permute-start(f32[16,5,384]{2,0,1:T(8,128)S(1)} %get-tuple-element.14), channel_id=1, source_target_pairs={{0,2},{1,3},{2,4},{3,5},{4,6},{5,7},{6,0},{7,1},{8,10},{9,11},{10,... | collective-permute-start | bytes 368648 | tf_op jit(solution)/shard_map/ppermute | solution.py:72
  144.7 1.8 %collective-permute-done.19 = f32[16,5,384]{2,0,1:T(8,128)S(1)} collective-permute-done((f32[16,5,384]{2,0,1:T(8,128)S(1)}, f32[16,5,384]{2,0,1:T(8,128)S(1)}, u32[]{:S(2)}, u32[]{:S(2)}) %collective-permute-start.19) | collective-permute-done | bytes 122912 | tf_op jit(solution)/shard_map/ppermute | solution.py:72
  146.5 4.0 %collective-permute-done.18 = f32[16,5,384]{2,0,1:T(8,128)S(1)} collective-permute-done((f32[16,5,384]{2,0,1:T(8,128)S(1)}, f32[16,5,384]{2,0,1:T(8,128)S(1)}, u32[]{:S(2)}, u32[]{:S(2)}) %collective-permute-start.18) | collective-permute-done | bytes 122912 | tf_op jit(solution)/shard_map/ppermute | solution.py:72
  150.5 0.1 fusion.23
  150.5 0.6 slice_multiply_fusion
  151.2 0.6 slice_multiply_fusion.1
  (44 shorter events, 0.5 us)
Async XLA Ops:
  0.6 89.0 %copy-start = (f32[384,768]{1,0:T(8,128)S(1)}, f32[384,768]{1,0:T(8,128)}, u32[]{:S(2)}) copy-start(f32[384,768]{1,0:T(8,128)} %param.9) | copy-start | bytes 3538948
  2.4 6.2 %collective-permute-start = (f32[8,3840]{1,0:T(8,128)S(1)}, f32[8,3840]{1,0:T(8,128)S(1)}, u32[]{:S(2)}, u32[]{:S(2)}) collective-permute-start(f32[8,3840]{1,0:T(8,128)S(1)} %bitcast.90), channel_id=1, source_target_pairs={{0,256},{16,272},{32,288},{48,304},{64,320},{80,336},{96,352},{112... | collective-permute-start | bytes 368648 | tf_op jit(solution)/shard_map/ppermute | solution.py:33
  8.7 15.5 %collective-permute-start.1 = (f32[2,8,3840]{2,1,0:T(8,128)S(1)}, f32[2,8,3840]{2,1,0:T(8,128)S(1)}, u32[]{:S(2)}, u32[]{:S(2)}) collective-permute-start(f32[2,8,3840]{2,1,0:T(8,128)S(1)} %maximum_select_fusion.1), channel_id=1, source_target_pairs={{0,240},{16,0},{32,16},{48,32},{64,48},{80,64},{96,80},{112,96},{1... | collective-permute-start | bytes 737288 | tf_op jit(solution)/shard_map/ppermute | solution.py:43
  20.5 9.0 %collective-permute-start.8 = (f32[2,8,3840]{2,1,0:T(8,128)S(1)}, f32[2,8,3840]{2,1,0:T(8,128)S(1)}, u32[]{:S(2)}, u32[]{:S(2)}) collective-permute-start(f32[2,8,3840]{2,1,0:T(8,128)S(1)} %maximum_select_fusion.1), channel_id=1, source_target_pairs={{0,16},{16,32},{32,48},{48,64},{64,80},{80,96},{96,112},{112,128},... | collective-permute-start | bytes 737288 | tf_op jit(solution)/shard_map/ppermute | solution.py:42
  24.2 8.9 %collective-permute-start.2 = (f32[2,8,3840]{2,1,0:T(8,128)S(1)}, f32[2,8,3840]{2,1,0:T(8,128)S(1)}, u32[]{:S(2)}, u32[]{:S(2)}) collective-permute-start(f32[2,8,3840]{2,1,0:T(8,128)S(1)} %collective-permute-done.1), channel_id=1, source_target_pairs={{0,240},{16,0},{32,16},{48,32},{64,48},{80,64},{96,80},{112,96},{1... | collective-permute-start | bytes 737288 | tf_op jit(solution)/shard_map/ppermute | solution.py:43
  29.5 8.2 %collective-permute-start.9 = (f32[2,8,3840]{2,1,0:T(8,128)S(1)}, f32[2,8,3840]{2,1,0:T(8,128)S(1)}, u32[]{:S(2)}, u32[]{:S(2)}) collective-permute-start(f32[2,8,3840]{2,1,0:T(8,128)S(1)} %collective-permute-done.8), channel_id=1, source_target_pairs={{0,16},{16,32},{32,48},{48,64},{64,80},{80,96},{96,112},{112,128},... | collective-permute-start | bytes 737288 | tf_op jit(solution)/shard_map/ppermute | solution.py:42
  33.1 8.0 %collective-permute-start.3 = (f32[2,8,3840]{2,1,0:T(8,128)S(1)}, f32[2,8,3840]{2,1,0:T(8,128)S(1)}, u32[]{:S(2)}, u32[]{:S(2)}) collective-permute-start(f32[2,8,3840]{2,1,0:T(8,128)S(1)} %collective-permute-done.2), channel_id=1, source_target_pairs={{0,240},{16,0},{32,16},{48,32},{64,48},{80,64},{96,80},{112,96},{1... | collective-permute-start | bytes 737288 | tf_op jit(solution)/shard_map/ppermute | solution.py:43
  37.6 8.2 %collective-permute-start.10 = (f32[2,8,3840]{2,1,0:T(8,128)S(1)}, f32[2,8,3840]{2,1,0:T(8,128)S(1)}, u32[]{:S(2)}, u32[]{:S(2)}) collective-permute-start(f32[2,8,3840]{2,1,0:T(8,128)S(1)} %collective-permute-done.9), channel_id=1, source_target_pairs={{0,16},{16,32},{32,48},{48,64},{64,80},{80,96},{96,112},{112,128},... | collective-permute-start | bytes 737288 | tf_op jit(solution)/shard_map/ppermute | solution.py:42
  41.0 7.9 %collective-permute-start.4 = (f32[2,8,3840]{2,1,0:T(8,128)S(1)}, f32[2,8,3840]{2,1,0:T(8,128)}, u32[]{:S(2)}, u32[]{:S(2)}) collective-permute-start(f32[2,8,3840]{2,1,0:T(8,128)S(1)} %collective-permute-done.3), channel_id=1, source_target_pairs={{0,240},{16,0},{32,16},{48,32},{64,48},{80,64},{96,80},{112,96},{1... | collective-permute-start | bytes 737288 | tf_op jit(solution)/shard_map/ppermute | solution.py:43
  45.8 8.2 %collective-permute-start.11 = (f32[2,8,3840]{2,1,0:T(8,128)S(1)}, f32[2,8,3840]{2,1,0:T(8,128)S(1)}, u32[]{:S(2)}, u32[]{:S(2)}) collective-permute-start(f32[2,8,3840]{2,1,0:T(8,128)S(1)} %collective-permute-done.10), channel_id=1, source_target_pairs={{0,16},{16,32},{32,48},{48,64},{64,80},{80,96},{96,112},{112,128},... | collective-permute-start | bytes 737288 | tf_op jit(solution)/shard_map/ppermute | solution.py:42
  48.9 8.6 %collective-permute-start.5 = (f32[2,8,3840]{2,1,0:T(8,128)}, f32[2,8,3840]{2,1,0:T(8,128)}, u32[]{:S(2)}, u32[]{:S(2)}) collective-permute-start(f32[2,8,3840]{2,1,0:T(8,128)} %collective-permute-done.4), channel_id=1, source_target_pairs={{0,240},{16,0},{32,16},{48,32},{64,48},{80,64},{96,80},{112,96},{1... | collective-permute-start | bytes 737288 | tf_op jit(solution)/shard_map/ppermute | solution.py:43
  54.0 8.4 %collective-permute-start.12 = (f32[2,8,3840]{2,1,0:T(8,128)S(1)}, f32[2,8,3840]{2,1,0:T(8,128)S(1)}, u32[]{:S(2)}, u32[]{:S(2)}) collective-permute-start(f32[2,8,3840]{2,1,0:T(8,128)S(1)} %collective-permute-done.11), channel_id=1, source_target_pairs={{0,16},{16,32},{32,48},{48,64},{64,80},{80,96},{96,112},{112,128},... | collective-permute-start | bytes 737288 | tf_op jit(solution)/shard_map/ppermute | solution.py:42
  57.5 9.0 %collective-permute-start.6 = (f32[2,8,3840]{2,1,0:T(8,128)}, f32[2,8,3840]{2,1,0:T(8,128)S(1)}, u32[]{:S(2)}, u32[]{:S(2)}) collective-permute-start(f32[2,8,3840]{2,1,0:T(8,128)} %collective-permute-done.5), channel_id=1, source_target_pairs={{0,240},{16,0},{32,16},{48,32},{64,48},{80,64},{96,80},{112,96},{1... | collective-permute-start | bytes 737288 | tf_op jit(solution)/shard_map/ppermute | solution.py:43
  62.5 9.0 %collective-permute-start.13 = (f32[2,8,3840]{2,1,0:T(8,128)S(1)}, f32[2,8,3840]{2,1,0:T(8,128)S(1)}, u32[]{:S(2)}, u32[]{:S(2)}) collective-permute-start(f32[2,8,3840]{2,1,0:T(8,128)S(1)} %collective-permute-done.12), channel_id=1, source_target_pairs={{0,16},{16,32},{32,48},{48,64},{64,80},{80,96},{96,112},{112,128},... | collective-permute-start | bytes 737288 | tf_op jit(solution)/shard_map/ppermute | solution.py:42
  66.5 10.0 %collective-permute-start.7 = (f32[2,8,3840]{2,1,0:T(8,128)S(1)}, f32[2,8,3840]{2,1,0:T(8,128)S(1)}, u32[]{:S(2)}, u32[]{:S(2)}) collective-permute-start(f32[2,8,3840]{2,1,0:T(8,128)S(1)} %collective-permute-done.6), channel_id=1, source_target_pairs={{0,240},{16,0},{32,16},{48,32},{64,48},{80,64},{96,80},{112,96},{1... | collective-permute-start | bytes 737288 | tf_op jit(solution)/shard_map/ppermute | solution.py:43
  71.5 10.1 %collective-permute-start.14 = (f32[2,8,3840]{2,1,0:T(8,128)S(1)}, f32[2,8,3840]{2,1,0:T(8,128)S(1)}, u32[]{:S(2)}, u32[]{:S(2)}) collective-permute-start(f32[2,8,3840]{2,1,0:T(8,128)S(1)} %collective-permute-done.13), channel_id=1, source_target_pairs={{0,16},{16,32},{32,48},{48,64},{64,80},{80,96},{96,112},{112,128},... | collective-permute-start | bytes 737288 | tf_op jit(solution)/shard_map/ppermute | solution.py:42
  76.4 7.8 %collective-permute-start.16 = (f32[2,8,1920]{2,1,0:T(8,128)S(1)}, f32[2,8,1920]{2,1,0:T(8,128)S(1)}, u32[]{:S(2)}, u32[]{:S(2)}) collective-permute-start(f32[2,8,1920]{2,1,0:T(8,128)S(1)} %slice.44), channel_id=1, source_target_pairs={{0,240},{16,0},{32,16},{48,32},{64,48},{80,64},{96,80},{112,96},{1... | collective-permute-start | bytes 368648 | tf_op jit(solution)/shard_map/ppermute | solution.py:48
  81.6 7.8 %collective-permute-start.15 = (f32[2,8,1920]{2,1,0:T(8,128)S(1)}, f32[2,8,1920]{2,1,0:T(8,128)S(1)}, u32[]{:S(2)}, u32[]{:S(2)}) collective-permute-start(f32[2,8,1920]{2,1,0:T(8,128)S(1)} %slice.43), channel_id=1, source_target_pairs={{0,16},{16,32},{32,48},{48,64},{64,80},{80,96},{96,112},{112,128},... | collective-permute-start | bytes 368648 | tf_op jit(solution)/shard_map/ppermute | solution.py:47
  96.7 1.3 copy-start.2
  101.3 1.3 copy-start.1
  101.3 26.8 %copy-start.3 = (s32[2,36]{1,0:T(2,128)S(1)}, s32[2,36]{1,0:T(2,128)}, u32[]{:S(2)}) copy-start(s32[2,36]{1,0:T(2,128)} %param.13) | copy-start | bytes 868
  102.7 14.7 %collective-permute-start.17 = (f32[2,4,16,5,384]{4,2,1,0,3:T(8,128)S(1)}, f32[2,4,16,5,384]{4,2,1,0,3:T(8,128)S(1)}, u32[]{:S(2)}, u32[]{:S(2)}) collective-permute-start(f32[2,4,16,5,384]{4,2,1,0,3:T(8,128)S(1)} %select_bitcast_fusion), channel_id=1, source_target_pairs={{0,1},{1,0},{2,3},{3,2},{4,5},{5,4},{6,7},{7,6},{8,9},{9,8},{10,11... | collective-permute-start | bytes 2949128 | tf_op jit(solution)/shard_map/ppermute | solution.py:61
  118.8 20.6 %collective-permute-start.24 = (f32[16,5,384]{2,0,1:T(8,128)S(1)}, f32[16,5,384]{2,0,1:T(8,128)S(1)}, u32[]{:S(2)}, u32[]{:S(2)}) collective-permute-start(f32[16,5,384]{2,0,1:T(8,128)S(1)} %get-tuple-element.15), channel_id=1, source_target_pairs={{0,14},{1,15},{2,8},{3,9},{4,10},{5,11},{6,12},{7,13},{8,6},{9,7},... | collective-permute-start | bytes 368648 | tf_op jit(solution)/shard_map/ppermute | solution.py:72
  125.9 16.8 %collective-permute-start.23 = (f32[16,5,384]{2,0,1:T(8,128)S(1)}, f32[16,5,384]{2,0,1:T(8,128)S(1)}, u32[]{:S(2)}, u32[]{:S(2)}) collective-permute-start(f32[16,5,384]{2,0,1:T(8,128)S(1)} %get-tuple-element.16), channel_id=1, source_target_pairs={{0,12},{1,13},{2,14},{3,15},{4,8},{5,9},{6,10},{7,11},{8,4},{9,5},... | collective-permute-start | bytes 368648 | tf_op jit(solution)/shard_map/ppermute | solution.py:72
  128.2 16.4 %collective-permute-start.22 = (f32[16,5,384]{2,0,1:T(8,128)S(1)}, f32[16,5,384]{2,0,1:T(8,128)S(1)}, u32[]{:S(2)}, u32[]{:S(2)}) collective-permute-start(f32[16,5,384]{2,0,1:T(8,128)S(1)} %get-tuple-element.17), channel_id=1, source_target_pairs={{0,10},{1,11},{2,12},{3,13},{4,14},{5,15},{6,8},{7,9},{8,2},{9,3},... | collective-permute-start | bytes 368648 | tf_op jit(solution)/shard_map/ppermute | solution.py:72
  133.3 11.3 %collective-permute-start.21 = (f32[16,5,384]{2,0,1:T(8,128)S(1)}, f32[16,5,384]{2,0,1:T(8,128)S(1)}, u32[]{:S(2)}, u32[]{:S(2)}) collective-permute-start(f32[16,5,384]{2,0,1:T(8,128)S(1)} %get-tuple-element.18), channel_id=1, source_target_pairs={{0,8},{1,9},{2,10},{3,11},{4,12},{5,13},{6,14},{7,15},{8,0},{9,1},... | collective-permute-start | bytes 368648 | tf_op jit(solution)/shard_map/ppermute | solution.py:72
  135.5 9.2 %collective-permute-start.20 = (f32[16,5,384]{2,0,1:T(8,128)S(1)}, f32[16,5,384]{2,0,1:T(8,128)S(1)}, u32[]{:S(2)}, u32[]{:S(2)}) collective-permute-start(f32[16,5,384]{2,0,1:T(8,128)S(1)} %get-tuple-element.19), channel_id=1, source_target_pairs={{0,6},{1,7},{2,0},{3,1},{4,2},{5,3},{6,4},{7,5},{8,14},{9,15},{10,... | collective-permute-start | bytes 368648 | tf_op jit(solution)/shard_map/ppermute | solution.py:72
  139.4 7.1 %collective-permute-start.19 = (f32[16,5,384]{2,0,1:T(8,128)S(1)}, f32[16,5,384]{2,0,1:T(8,128)S(1)}, u32[]{:S(2)}, u32[]{:S(2)}) collective-permute-start(f32[16,5,384]{2,0,1:T(8,128)S(1)} %get-tuple-element.20), channel_id=1, source_target_pairs={{0,4},{1,5},{2,6},{3,7},{4,0},{5,1},{6,2},{7,3},{8,12},{9,13},{10,... | collective-permute-start | bytes 368648 | tf_op jit(solution)/shard_map/ppermute | solution.py:72
  142.7 7.7 %collective-permute-start.18 = (f32[16,5,384]{2,0,1:T(8,128)S(1)}, f32[16,5,384]{2,0,1:T(8,128)S(1)}, u32[]{:S(2)}, u32[]{:S(2)}) collective-permute-start(f32[16,5,384]{2,0,1:T(8,128)S(1)} %get-tuple-element.14), channel_id=1, source_target_pairs={{0,2},{1,3},{2,4},{3,5},{4,6},{5,7},{6,0},{7,1},{8,10},{9,11},{10,... | collective-permute-start | bytes 368648 | tf_op jit(solution)/shard_map/ppermute | solution.py:72

commit v5 on v3

--- a/solution.py
+++ b/solution.py
@@ -8,6 +8,7 @@
 X_LO = 2
 X_HI = 2
 CORES = 2
+SC_MEMBERS = 2
 
 
 def tile_flags(block_lists, anchor, extent, tile_height):
@@ -91,7 +92,10 @@
     out_first = tile_flags(lists_first, row_anchor, local_rows, panel_width)
     out_second = tile_flags(lists_second, row_anchor, local_rows, panel_width)
     panels = jnp.concatenate([factors_first, factors_second], axis=0)
-    stacked = jnp.transpose(panels, (1, 0, 2)).reshape(share_rows, members * local_cols)
+    native = jnp.transpose(panels[:SC_MEMBERS], (1, 0, 2)).reshape(share_rows, SC_MEMBERS * local_cols)
+    native = lax.all_gather(native, "row", axis=0, tiled=True).reshape(panel_width, SC_MEMBERS, local_cols)
+    ring_members = members - SC_MEMBERS
+    stacked = jnp.transpose(panels[SC_MEMBERS:], (1, 0, 2)).reshape(share_rows, ring_members * local_cols)
     pieces, z = gather_rows(stacked, n_row)
     col_mask = jnp.concatenate(
         [
@@ -100,12 +104,16 @@
         ],
         axis=0,
     )
-    pieces = pieces.reshape(nz, X_LO, share_rows, members, local_cols) * col_mask
-    partial_value = jnp.einsum(
+    native = native * col_mask[:SC_MEMBERS]
+    pieces = pieces.reshape(nz, X_LO, share_rows, ring_members, local_cols) * col_mask[SC_MEMBERS:]
+    native_value = jnp.einsum(
+        "kmj,ij->kmi", native, anc_inv, precision=highest, preferred_element_type=jnp.float32
+    )
+    ring_value = jnp.einsum(
         "tlkmj,ij->ltkmi", pieces, anc_inv, precision=highest, preferred_element_type=jnp.float32
     )
-    partial_value = jnp.roll(partial_value, z, axis=1)
-    partial_value = partial_value.reshape(panel_width, members, local_rows)
+    ring_value = jnp.roll(ring_value, z, axis=1).reshape(panel_width, ring_members, local_rows)
+    partial_value = jnp.concatenate([native_value, ring_value], axis=1)
     first_partial = partial_value[:, :n_first]
     chosen = jnp.take(first_partial, parents, axis=1)
     chosen_mask = jnp.take(out_first, parents, axis=0)

time: 150 us -> 211 us (1.41)
  waiting for transfers between devices: 41.3 us -> 73.7 us
  between operations: 1.15 us -> 14.6 us
  starting transfers between devices: 83.3 us -> 93.1 us
  matrix products: 8.85 us -> 13.1 us
    all_gather x0 -> x1, waiting for transfers between devices: none -> 38.7 us  [local(): lax.all_gather(native, 'row', axis=0, tiled=True)]
    all_to_all x1, starting transfers between devices: 17.5 us -> 27.6 us  [local(): reduced = jnp.sum(lax.all_to_all(combined, 'col', 0, 0, tiled=True), axis=0)]
    dot_general x0 -> x1, matrix products: none -> 6.67 us  [local(): jnp.einsum('kmj,ij->kmi', native, anc_inv, precision=highest, preferred_e...]
    ppermute x7, waiting for transfers between devices: 6.07 us -> 0.56 us  [gather_rows(): bwd = lax.ppermute(bwd, 'row', down)]
    unnamed x21 -> x22, local copies, waits for them, and re-layouts: 4.46 us -> 0.2 us
    all_gather x0 -> x1, local copies, waits for them, and re-layouts: none -> 3.02 us  [local(): lax.all_gather(native, 'row', axis=0, tiled=True)]
    dot_general x1, matrix products: 6.32 us -> 3.88 us  [local(): jnp.einsum('tlkmj,ij->ltkmi', pieces, anc_inv, precision=highest, preferr...]
    ppermute x1, waiting for transfers between devices: 2.23 us -> 0.01 us  [gather_rows(): lax.ppermute(block, 'row', [(p, (p + nz) % n_row) for p in range(n_row)])]
  transfers between devices with their start and end apart: 18 -> 19, of which waited for: 11 -> 9; matrix products, arithmetic and copies ran while one was open for 4% -> 5% of each run, Pallas kernels for 0% -> 0%
where the time goes in v5:
time: 211 us; the launch traced here: 209 us
  starting transfers between devices  93.1 us (44%)
  waiting for transfers between devices  73.7 us (35%)
  between operations  14.6 us (7%)
  matrix products  13.1 us (6%)
  local copies, waits for them, and re-layouts  8.25 us (4%)
  other arithmetic  6.7 us (3%)
    ppermute x7, starting transfers between devices, gather_rows(): bwd = lax.ppermute(bwd, 'row', down)  40.8 us
    all_gather x1, waiting for transfers between devices, local(): lax.all_gather(native, 'row', axis=0, tiled=True)  38.7 us
    all_to_all x1, starting transfers between devices, local(): reduced = jnp.sum(lax.all_to_all(combined, 'col', 0, 0, tiled=True), axis=0)  27.6 us
    all_to_all x1, waiting for transfers between devices, local(): reduced = jnp.sum(lax.all_to_all(combined, 'col', 0, 0, tiled=True), axis=0)  26.9 us
    ppermute x7, starting transfers between devices, gather_rows(): fwd = lax.ppermute(fwd, 'row', up)  13.4 us
    dot_general x1, matrix products, local(): jnp.einsum('kmj,ij->kmi', native, anc_inv, precision=highest, preferred_e...  6.67 us
    ppermute x1, starting transfers between devices, gather_rows(): last_bwd = lax.ppermute(bwd[..., half:], 'row', down)  5.34 us
    ppermute x1, waiting for transfers between devices, gather_rows(): last_fwd = lax.ppermute(fwd[..., :half], 'row', up)  5.3 us
  transfers between devices with their start and end apart: 19, of which 9 were waited for; matrix products, arithmetic and copies ran while one was open for 5% of the time, Pallas kernels for 0%

profile of v5, /device:TPU:1, one launch (start us, length us, event | category | flops | bytes accessed | tf_op | source)
XLA Modules:
  0.0 209.4 jit_solution(17832674133509458173)
XLA Ops:
  7.2 0.0 copy-start
  7.2 0.0 all-gather.2.cloned.1.call-start
  7.2 0.9 pad_maximum_fusion.3
  8.1 3.9 %collective-permute-start = (f32[8,2304]{1,0:T(8,128)S(1)}, f32[8,2304]{1,0:T(8,128)S(1)}, u32[]{:S(2)}, u32[]{:S(2)}) collective-permute-start(f32[8,2304]{1,0:T(8,128)S(1)} %bitcast.53), channel_id=1, source_target_pairs={{0,256},{16,272},{32,288},{48,304},{64,320},{80,336},{96,352},{112... | collective-permute-start | bytes 221192 | tf_op jit(solution)/shard_map/ppermute | solution.py:34
  12.1 1.4 slice.30
  13.5 0.0 all-gather.2.cloned.1.call-update
  13.5 0.7 compare_select_fusion
  14.2 0.7 compare_and_fusion
  14.9 0.8 compare_reduce_fusion.1
  15.6 0.0 collective-permute-done
  15.7 11.1 %collective-permute-start.1 = (f32[2,8,2304]{2,1,0:T(8,128)S(1)}, f32[2,8,2304]{2,1,0:T(8,128)S(1)}, u32[]{:S(2)}, u32[]{:S(2)}) collective-permute-start(f32[2,8,2304]{2,1,0:T(8,128)S(1)} %maximum_select_fusion.1), channel_id=1, source_target_pairs={{0,240},{16,0},{32,16},{48,32},{64,48},{80,64},{96,80},{112,96},{1... | collective-permute-start | bytes 442376 | tf_op jit(solution)/shard_map/ppermute | solution.py:44
  26.8 1.9 collective-permute-start.8
  28.8 0.8 compare_reduce_fusion
  29.6 0.0 collective-permute-done.1
  29.6 4.7 %collective-permute-start.2 = (f32[2,8,2304]{2,1,0:T(8,128)S(1)}, f32[2,8,2304]{2,1,0:T(8,128)S(1)}, u32[]{:S(2)}, u32[]{:S(2)}) collective-permute-start(f32[2,8,2304]{2,1,0:T(8,128)S(1)} %collective-permute-done.1), channel_id=1, source_target_pairs={{0,240},{16,0},{32,16},{48,32},{64,48},{80,64},{96,80},{112,96},{1... | collective-permute-start | bytes 442376 | tf_op jit(solution)/shard_map/ppermute | solution.py:44
  34.3 0.0 collective-permute-done.8
  34.3 1.9 collective-permute-start.9
  36.2 0.8 compare_reduce_fusion.2
  37.1 0.0 copy-start.1
  37.1 0.6 gather_fusion
  37.7 0.0 collective-permute-done.2
  37.7 4.6 %collective-permute-start.3 = (f32[2,8,2304]{2,1,0:T(8,128)S(1)}, f32[2,8,2304]{2,1,0:T(8,128)S(1)}, u32[]{:S(2)}, u32[]{:S(2)}) collective-permute-start(f32[2,8,2304]{2,1,0:T(8,128)S(1)} %collective-permute-done.2), channel_id=1, source_target_pairs={{0,240},{16,0},{32,16},{48,32},{64,48},{80,64},{96,80},{112,96},{1... | collective-permute-start | bytes 442376 | tf_op jit(solution)/shard_map/ppermute | solution.py:44
  42.2 0.0 collective-permute-done.9
  42.3 1.9 collective-permute-start.10
  44.2 0.1 broadcast_select_fusion
  44.3 0.3 collective-permute-done.3
  44.6 5.0 %collective-permute-start.4 = (f32[2,8,2304]{2,1,0:T(8,128)S(1)}, f32[2,8,2304]{2,1,0:T(8,128)S(1)}, u32[]{:S(2)}, u32[]{:S(2)}) collective-permute-start(f32[2,8,2304]{2,1,0:T(8,128)S(1)} %collective-permute-done.3), channel_id=1, source_target_pairs={{0,240},{16,0},{32,16},{48,32},{64,48},{80,64},{96,80},{112,96},{1... | collective-permute-start | bytes 442376 | tf_op jit(solution)/shard_map/ppermute | solution.py:44
  49.6 0.4 collective-permute-done.10
  50.0 1.9 collective-permute-start.11
  52.0 0.0 collective-permute-done.4
  52.0 5.3 %collective-permute-start.5 = (f32[2,8,2304]{2,1,0:T(8,128)S(1)}, f32[2,8,2304]{2,1,0:T(8,128)S(1)}, u32[]{:S(2)}, u32[]{:S(2)}) collective-permute-start(f32[2,8,2304]{2,1,0:T(8,128)S(1)} %collective-permute-done.4), channel_id=1, source_target_pairs={{0,240},{16,0},{32,16},{48,32},{64,48},{80,64},{96,80},{112,96},{1... | collective-permute-start | bytes 442376 | tf_op jit(solution)/shard_map/ppermute | solution.py:44
  57.3 0.0 collective-permute-done.11
  57.3 1.9 collective-permute-start.12
  59.3 0.2 collective-permute-done.5
  59.5 5.0 %collective-permute-start.6 = (f32[2,8,2304]{2,1,0:T(8,128)S(1)}, f32[2,8,2304]{2,1,0:T(8,128)S(1)}, u32[]{:S(2)}, u32[]{:S(2)}) collective-permute-start(f32[2,8,2304]{2,1,0:T(8,128)S(1)} %collective-permute-done.5), channel_id=1, source_target_pairs={{0,240},{16,0},{32,16},{48,32},{64,48},{80,64},{96,80},{112,96},{1... | collective-permute-start | bytes 442376 | tf_op jit(solution)/shard_map/ppermute | solution.py:44
  64.5 0.5 collective-permute-done.12
  65.1 1.9 collective-permute-start.13
  67.0 0.0 collective-permute-done.6
  67.0 5.1 %collective-permute-start.7 = (f32[2,8,2304]{2,1,0:T(8,128)S(1)}, f32[2,8,2304]{2,1,0:T(8,128)S(1)}, u32[]{:S(2)}, u32[]{:S(2)}) collective-permute-start(f32[2,8,2304]{2,1,0:T(8,128)S(1)} %collective-permute-done.6), channel_id=1, source_target_pairs={{0,240},{16,0},{32,16},{48,32},{64,48},{80,64},{96,80},{112,96},{1... | collective-permute-start | bytes 442376 | tf_op jit(solution)/shard_map/ppermute | solution.py:44
  72.1 0.8 collective-permute-done.13
  72.9 1.9 collective-permute-start.14
  74.9 0.0 collective-permute-done.7
  74.9 5.3 %collective-permute-start.16 = (f32[2,8,1152]{2,1,0:T(8,128)S(1)}, f32[2,8,1152]{2,1,0:T(8,128)S(1)}, u32[]{:S(2)}, u32[]{:S(2)}) collective-permute-start(f32[2,8,1152]{2,1,0:T(8,128)S(1)} %slice.46), channel_id=1, source_target_pairs={{0,240},{16,0},{32,16},{48,32},{64,48},{80,64},{96,80},{112,96},{1... | collective-permute-start | bytes 221192 | tf_op jit(solution)/shard_map/ppermute | solution.py:49
  80.3 1.9 collective-permute-start.15
  82.2 0.4 collective-permute-done.16
  82.7 5.3 %collective-permute-done.15 = f32[2,8,1152]{2,1,0:T(8,128)S(1)} collective-permute-done((f32[2,8,1152]{2,1,0:T(8,128)S(1)}, f32[2,8,1152]{2,1,0:T(8,128)S(1)}, u32[]{:S(2)}, u32[]{:S(2)}) %collective-permute-start.15) | collective-permute-done | bytes 73760 | tf_op jit(solution)/shard_map/ppermute | solution.py:48
  88.2 3.9 %fusion.4 = f32[2,16,8,3,384]{4,2,3,0,1:T(8,128)S(1)} fusion(f32[16,2,8,3,768]{4,2,3,1,0:T(8,128)S(1)} %constant_dynamic-update-slice_fusion, f32[384,768]{1,0:T(8,128)S(1)} %copy-done, f32[3,768]{1,0:T(4,128)S(1)} %pad_maximum_fusion.4), kind=kOutput, calls=%fused_computation.9 | convolution fusion | flops 2718498816 | bytes 4727808 | tf_op jit(solution)/shard_map/tlkmj,ij->ltkmi/dot_general | solution.py:112
  92.0 0.2 fusion.9
  92.3 0.0 slice-start
  92.3 0.1 copy.21
  92.4 38.7 %all-gather.2.cloned.1.call-done = f32[256,1536]{1,0:T(8,128)} async-done(((f32[8,1536]{1,0:T(8,128)}), f32[256,1536]{1,0:T(8,128)}) %all-gather.2.cloned.1.call-update) | async-done | bytes 1572880 | tf_op jit(solution)/shard_map/all_gather | solution.py:96
  131.1 3.0 %copy.19 = f32[256,1536]{0,1:T(8,128)} copy(f32[256,1536]{1,0:T(8,128)} %all-gather.2.cloned.1.call-done) | data formatting | bytes 3145728 | tf_op jit(solution)/shard_map/all_gather | solution.py:96
  134.1 6.7 %fusion.2 = f32[256,2,384]{2,0,1:T(8,128)S(1)} fusion(f32[256,2,768]{0,2,1:T(8,128)} %bitcast.52, f32[384,768]{1,0:T(8,128)S(1)} %copy-done, f32[2,768]{1,0:T(2,128)S(1)} %slice-done), kind=kOutput, calls=%fused_computation.7 | convolution fusion | flops 1812332544 | bytes 3545088 | tf_op jit(solution)/shard_map/kmj,ij->kmi/dot_general | solution.py:109
  140.8 0.1 pad_maximum_fusion.1
  140.9 1.5 gather_fusion.1
  142.4 2.5 %fusion.8 = f32[256,2,384]{2,0,1:T(8,128)S(1)} fusion(f32[2,256,256]{2,1,0:T(8,128)} %param.13, f32[256,3,384]{2,0,1:T(8,128)S(1)} %bitcast.50, f32[2,256,384]{2,1,0:T(8,128)} %gather_fusion.1, f32[2,384]{1,0:T(2,128)S(1)} %broadcast_select_fusion, pred[2]{0:T(512)(128)(4,1)} %copy-done.3), kind=kOutput, calls=%fused_computation.12 | convolution fusion | flops 604569600 | bytes 2886658 | tf_op jit(solution)/shard_map/cqk,qci->kci/dot_general | solution.py:120
  144.9 0.1 pad_maximum_fusion
  145.0 1.4 copy.23
  146.5 27.6 %all-to-all-start = ((f32[16,16,5,384]{3,1,2,0:T(8,128)}), f32[16,16,5,384]{3,1,2,0:T(8,128)S(1)}, u32[]{:S(2)}, u32[]{:S(2)}) async-start(f32[16,16,5,384]{3,1,2,0:T(8,128)} %copy.23), calls=%async_computation | async-start | bytes 3932160 | tf_op jit(solution)/shard_map/all_to_all | solution.py:124
  174.1 0.1 compare_reduce_fusion.3
  174.2 26.9 %all-to-all-done = f32[16,16,5,384]{3,1,2,0:T(8,128)S(1)} async-done(((f32[16,16,5,384]{3,1,2,0:T(8,128)}), f32[16,16,5,384]{3,1,2,0:T(8,128)S(1)}, u32[]{:S(2)}, u32[]{:S(2)}) %all-to-all-start) | async-done | bytes 1966112 | tf_op jit(solution)/shard_map/all_to_all | solution.py:124
  201.2 0.1 reduce_sum.9
  201.3 0.6 slice_multiply_fusion
  201.9 0.6 slice_multiply_fusion.1
  (37 shorter events, 0.3 us)
Async XLA Ops:
  7.2 81.0 %copy-start = (f32[384,768]{1,0:T(8,128)S(1)}, f32[384,768]{1,0:T(8,128)}, u32[]{:S(2)}) copy-start(f32[384,768]{1,0:T(8,128)} %param.7) | copy-start | bytes 3538948
  7.2 123.9 %all-gather.2.cloned.1.call-start = ((), (), s32[]{:S(2)}) async-start(), calls=%async_computation.1 | async-start | bytes 1622016 | tf_op jit(solution)/shard_map/all_gather | solution.py:96
  8.1 7.5 %collective-permute-start = (f32[8,2304]{1,0:T(8,128)S(1)}, f32[8,2304]{1,0:T(8,128)S(1)}, u32[]{:S(2)}, u32[]{:S(2)}) collective-permute-start(f32[8,2304]{1,0:T(8,128)S(1)} %bitcast.53), channel_id=1, source_target_pairs={{0,256},{16,272},{32,288},{48,304},{64,320},{80,336},{96,352},{112... | collective-permute-start | bytes 221192 | tf_op jit(solution)/shard_map/ppermute | solution.py:34
  14.8 35.2 %copy-start.3 = (pred[2]{0:T(512)(128)(4,1)}, pred[2]{0:T(512)(128)(4,1)S(1)}, u32[]{:S(2)}) copy-start(pred[2]{0:T(512)(128)(4,1)S(1)} %compare_and_fusion) | copy-start | bytes 10
  15.7 13.9 %collective-permute-start.1 = (f32[2,8,2304]{2,1,0:T(8,128)S(1)}, f32[2,8,2304]{2,1,0:T(8,128)S(1)}, u32[]{:S(2)}, u32[]{:S(2)}) collective-permute-start(f32[2,8,2304]{2,1,0:T(8,128)S(1)} %maximum_select_fusion.1), channel_id=1, source_target_pairs={{0,240},{16,0},{32,16},{48,32},{64,48},{80,64},{96,80},{112,96},{1... | collective-permute-start | bytes 442376 | tf_op jit(solution)/shard_map/ppermute | solution.py:44
  26.8 7.5 %collective-permute-start.8 = (f32[2,8,2304]{2,1,0:T(8,128)S(1)}, f32[2,8,2304]{2,1,0:T(8,128)S(1)}, u32[]{:S(2)}, u32[]{:S(2)}) collective-permute-start(f32[2,8,2304]{2,1,0:T(8,128)S(1)} %maximum_select_fusion.1), channel_id=1, source_target_pairs={{0,16},{16,32},{32,48},{48,64},{64,80},{80,96},{96,112},{112,128},... | collective-permute-start | bytes 442376 | tf_op jit(solution)/shard_map/ppermute | solution.py:43
  29.6 8.1 %collective-permute-start.2 = (f32[2,8,2304]{2,1,0:T(8,128)S(1)}, f32[2,8,2304]{2,1,0:T(8,128)S(1)}, u32[]{:S(2)}, u32[]{:S(2)}) collective-permute-start(f32[2,8,2304]{2,1,0:T(8,128)S(1)} %collective-permute-done.1), channel_id=1, source_target_pairs={{0,240},{16,0},{32,16},{48,32},{64,48},{80,64},{96,80},{112,96},{1... | collective-permute-start | bytes 442376 | tf_op jit(solution)/shard_map/ppermute | solution.py:44
  34.3 7.9 %collective-permute-start.9 = (f32[2,8,2304]{2,1,0:T(8,128)S(1)}, f32[2,8,2304]{2,1,0:T(8,128)S(1)}, u32[]{:S(2)}, u32[]{:S(2)}) collective-permute-start(f32[2,8,2304]{2,1,0:T(8,128)S(1)} %collective-permute-done.8), channel_id=1, source_target_pairs={{0,16},{16,32},{32,48},{48,64},{64,80},{80,96},{96,112},{112,128},... | collective-permute-start | bytes 442376 | tf_op jit(solution)/shard_map/ppermute | solution.py:43
  37.1 51.0 %copy-start.1 = (f32[3,768]{1,0:T(4,128)}, f32[3,768]{1,0:T(4,128)S(1)}, u32[]{:S(2)}) copy-start(f32[3,768]{1,0:T(4,128)S(1)} %convert_element_type.21) | copy-start | bytes 27652
  37.7 6.9 %collective-permute-start.3 = (f32[2,8,2304]{2,1,0:T(8,128)S(1)}, f32[2,8,2304]{2,1,0:T(8,128)S(1)}, u32[]{:S(2)}, u32[]{:S(2)}) collective-permute-start(f32[2,8,2304]{2,1,0:T(8,128)S(1)} %collective-permute-done.2), channel_id=1, source_target_pairs={{0,240},{16,0},{32,16},{48,32},{64,48},{80,64},{96,80},{112,96},{1... | collective-permute-start | bytes 442376 | tf_op jit(solution)/shard_map/ppermute | solution.py:44
  42.3 7.7 %collective-permute-start.10 = (f32[2,8,2304]{2,1,0:T(8,128)S(1)}, f32[2,8,2304]{2,1,0:T(8,128)S(1)}, u32[]{:S(2)}, u32[]{:S(2)}) collective-permute-start(f32[2,8,2304]{2,1,0:T(8,128)S(1)} %collective-permute-done.9), channel_id=1, source_target_pairs={{0,16},{16,32},{32,48},{48,64},{64,80},{80,96},{96,112},{112,128},... | collective-permute-start | bytes 442376 | tf_op jit(solution)/shard_map/ppermute | solution.py:43
  44.6 7.4 %collective-permute-start.4 = (f32[2,8,2304]{2,1,0:T(8,128)S(1)}, f32[2,8,2304]{2,1,0:T(8,128)S(1)}, u32[]{:S(2)}, u32[]{:S(2)}) collective-permute-start(f32[2,8,2304]{2,1,0:T(8,128)S(1)} %collective-permute-done.3), channel_id=1, source_target_pairs={{0,240},{16,0},{32,16},{48,32},{64,48},{80,64},{96,80},{112,96},{1... | collective-permute-start | bytes 442376 | tf_op jit(solution)/shard_map/ppermute | solution.py:44
  50.0 7.3 %collective-permute-start.11 = (f32[2,8,2304]{2,1,0:T(8,128)S(1)}, f32[2,8,2304]{2,1,0:T(8,128)S(1)}, u32[]{:S(2)}, u32[]{:S(2)}) collective-permute-start(f32[2,8,2304]{2,1,0:T(8,128)S(1)} %collective-permute-done.10), channel_id=1, source_target_pairs={{0,16},{16,32},{32,48},{48,64},{64,80},{80,96},{96,112},{112,128},... | collective-permute-start | bytes 442376 | tf_op jit(solution)/shard_map/ppermute | solution.py:43
  52.0 7.5 %collective-permute-start.5 = (f32[2,8,2304]{2,1,0:T(8,128)S(1)}, f32[2,8,2304]{2,1,0:T(8,128)S(1)}, u32[]{:S(2)}, u32[]{:S(2)}) collective-permute-start(f32[2,8,2304]{2,1,0:T(8,128)S(1)} %collective-permute-done.4), channel_id=1, source_target_pairs={{0,240},{16,0},{32,16},{48,32},{64,48},{80,64},{96,80},{112,96},{1... | collective-permute-start | bytes 442376 | tf_op jit(solution)/shard_map/ppermute | solution.py:44
  57.3 7.8 %collective-permute-start.12 = (f32[2,8,2304]{2,1,0:T(8,128)S(1)}, f32[2,8,2304]{2,1,0:T(8,128)S(1)}, u32[]{:S(2)}, u32[]{:S(2)}) collective-permute-start(f32[2,8,2304]{2,1,0:T(8,128)S(1)} %collective-permute-done.11), channel_id=1, source_target_pairs={{0,16},{16,32},{32,48},{48,64},{64,80},{80,96},{96,112},{112,128},... | collective-permute-start | bytes 442376 | tf_op jit(solution)/shard_map/ppermute | solution.py:43
  59.5 7.5 %collective-permute-start.6 = (f32[2,8,2304]{2,1,0:T(8,128)S(1)}, f32[2,8,2304]{2,1,0:T(8,128)S(1)}, u32[]{:S(2)}, u32[]{:S(2)}) collective-permute-start(f32[2,8,2304]{2,1,0:T(8,128)S(1)} %collective-permute-done.5), channel_id=1, source_target_pairs={{0,240},{16,0},{32,16},{48,32},{64,48},{80,64},{96,80},{112,96},{1... | collective-permute-start | bytes 442376 | tf_op jit(solution)/shard_map/ppermute | solution.py:44
  65.1 7.9 %collective-permute-start.13 = (f32[2,8,2304]{2,1,0:T(8,128)S(1)}, f32[2,8,2304]{2,1,0:T(8,128)S(1)}, u32[]{:S(2)}, u32[]{:S(2)}) collective-permute-start(f32[2,8,2304]{2,1,0:T(8,128)S(1)} %collective-permute-done.12), channel_id=1, source_target_pairs={{0,16},{16,32},{32,48},{48,64},{64,80},{80,96},{96,112},{112,128},... | collective-permute-start | bytes 442376 | tf_op jit(solution)/shard_map/ppermute | solution.py:43
  67.0 7.9 %collective-permute-start.7 = (f32[2,8,2304]{2,1,0:T(8,128)S(1)}, f32[2,8,2304]{2,1,0:T(8,128)S(1)}, u32[]{:S(2)}, u32[]{:S(2)}) collective-permute-start(f32[2,8,2304]{2,1,0:T(8,128)S(1)} %collective-permute-done.6), channel_id=1, source_target_pairs={{0,240},{16,0},{32,16},{48,32},{64,48},{80,64},{96,80},{112,96},{1... | collective-permute-start | bytes 442376 | tf_op jit(solution)/shard_map/ppermute | solution.py:44
  72.9 7.3 %collective-permute-start.14 = (f32[2,8,2304]{2,1,0:T(8,128)S(1)}, f32[2,8,2304]{2,1,0:T(8,128)S(1)}, u32[]{:S(2)}, u32[]{:S(2)}) collective-permute-start(f32[2,8,2304]{2,1,0:T(8,128)S(1)} %collective-permute-done.13), channel_id=1, source_target_pairs={{0,16},{16,32},{32,48},{48,64},{64,80},{80,96},{96,112},{112,128},... | collective-permute-start | bytes 442376 | tf_op jit(solution)/shard_map/ppermute | solution.py:43
  74.9 7.7 %collective-permute-start.16 = (f32[2,8,1152]{2,1,0:T(8,128)S(1)}, f32[2,8,1152]{2,1,0:T(8,128)S(1)}, u32[]{:S(2)}, u32[]{:S(2)}) collective-permute-start(f32[2,8,1152]{2,1,0:T(8,128)S(1)} %slice.46), channel_id=1, source_target_pairs={{0,240},{16,0},{32,16},{48,32},{64,48},{80,64},{96,80},{112,96},{1... | collective-permute-start | bytes 221192 | tf_op jit(solution)/shard_map/ppermute | solution.py:49
  80.3 7.7 %collective-permute-start.15 = (f32[2,8,1152]{2,1,0:T(8,128)S(1)}, f32[2,8,1152]{2,1,0:T(8,128)S(1)}, u32[]{:S(2)}, u32[]{:S(2)}) collective-permute-start(f32[2,8,1152]{2,1,0:T(8,128)S(1)} %slice.45), channel_id=1, source_target_pairs={{0,16},{16,32},{32,48},{48,64},{64,80},{80,96},{96,112},{112,128},... | collective-permute-start | bytes 221192 | tf_op jit(solution)/shard_map/ppermute | solution.py:48
  92.3 41.9 %slice-start = ((f32[3,768]{1,0:T(4,128)}), f32[2,768]{1,0:T(2,128)S(1)}, s32[]{:S(2)}) async-start(f32[3,768]{1,0:T(4,128)} %copy-done.1), calls=%async_computation.2 | async-start | bytes 12288 | tf_op jit(solution)/shard_map/slice | solution.py:107
  146.5 27.6 %copy-start.2 = (s32[2,36]{1,0:T(2,128)S(1)}, s32[2,36]{1,0:T(2,128)}, u32[]{:S(2)}) copy-start(s32[2,36]{1,0:T(2,128)} %param.11) | copy-start | bytes 868
  146.5 54.7 %all-to-all-start = ((f32[16,16,5,384]{3,1,2,0:T(8,128)}), f32[16,16,5,384]{3,1,2,0:T(8,128)S(1)}, u32[]{:S(2)}, u32[]{:S(2)}) async-start(f32[16,16,5,384]{3,1,2,0:T(8,128)} %copy.23), calls=%async_computation | async-start | bytes 3932160 | tf_op jit(solution)/shard_map/all_to_all | solution.py:124
Sparse Core Ops, SparseCore 0:
  13.6 117.4 all-gather.1

commit v6 on v3

--- a/solution.py
+++ b/solution.py
@@ -32,21 +32,24 @@
     z = r % nz
     partner = lax.ppermute(block, "row", [(p, (p + nz) % n_row) for p in range(n_row)])
     pair = jnp.where(x_lo == 0, jnp.stack([block, partner]), jnp.stack([partner, block]))
-    up = shift_pairs(n_row, nz, 1, 1)
-    down = shift_pairs(n_row, nz, 1, -1)
     pieces = [None] * nz
     pieces[0] = pair
-    fwd = pair
-    bwd = pair
-    for t in range(1, nz // 2):
-        fwd = lax.ppermute(fwd, "row", up)
-        bwd = lax.ppermute(bwd, "row", down)
-        pieces[nz - t] = fwd
-        pieces[t] = bwd
+    steps = nz // 4
     half = pair.shape[-1] // 2
-    last_fwd = lax.ppermute(fwd[..., :half], "row", up)
-    last_bwd = lax.ppermute(bwd[..., half:], "row", down)
-    pieces[nz // 2] = jnp.concatenate([last_fwd, last_bwd], axis=-1)
+    lane_up = pair
+    lane_down = pair
+    for t in range(1, steps + 1):
+        pieces[nz - (2 * t - 1)] = lax.ppermute(lane_up, "row", shift_pairs(n_row, nz, 1, 1))
+        pieces[2 * t - 1] = lax.ppermute(lane_down, "row", shift_pairs(n_row, nz, 1, -1))
+        if t < steps:
+            lane_up = lax.ppermute(lane_up, "row", shift_pairs(n_row, nz, 1, 2))
+            lane_down = lax.ppermute(lane_down, "row", shift_pairs(n_row, nz, 1, -2))
+            pieces[nz - 2 * t] = lane_up
+            pieces[2 * t] = lane_down
+        else:
+            last_up = lax.ppermute(lane_up[..., :half], "row", shift_pairs(n_row, nz, 1, 2))
+            last_down = lax.ppermute(lane_down[..., half:], "row", shift_pairs(n_row, nz, 1, -2))
+            pieces[nz // 2] = jnp.concatenate([last_up, last_down], axis=-1)
     return jnp.stack(pieces), z
 
 

time: 150 us -> 147 us (0.980)
  local copies, waits for them, and re-layouts: 8.13 us -> 6.24 us
  waiting for transfers between devices: 41.3 us -> 39.6 us
    ppermute x16, starting transfers between devices: 61.9 us -> 67.8 us  [the longest x3 23.3 us: gather_rows(): lane_down = lax.ppermute(lane_down, 'row', shift_pairs(n_row, nz, 1, -2))]
    all_to_all x1, starting transfers between devices: 17.5 us -> 12.5 us  [local(): reduced = jnp.sum(lax.all_to_all(combined, 'col', 0, 0, tiled=True), axis=0)]
    ppermute x1, waiting for transfers between devices: 2.23 us -> 0.01 us  [gather_rows(): lax.ppermute(block, 'row', [(p, (p + nz) % n_row) for p in range(n_row)])]
    unnamed x21, local copies, waits for them, and re-layouts: 4.46 us -> 2.57 us
  transfers between devices with their start and end apart: 18 -> 18, of which waited for: 11 -> 6; matrix products, arithmetic and copies ran while one was open for 4% -> 3% of each run, Pallas kernels for 0% -> 0%
where the time goes in v6:
time: 147 us; the launch traced here: 146 us
  starting transfers between devices  84.3 us (57%)
  waiting for transfers between devices  39.6 us (27%)
  matrix products  9.03 us (6%)
  local copies, waits for them, and re-layouts  6.24 us (4%)
  other arithmetic  5.88 us (4%)
    all_to_all x1, waiting for transfers between devices, local(): reduced = jnp.sum(lax.all_to_all(combined, 'col', 0, 0, tiled=True), axis=0)  26.9 us
    ppermute x3, starting transfers between devices, gather_rows(): lane_down = lax.ppermute(lane_down, 'row', shift_pairs(n_row, nz, 1, -2))  23.3 us
    ppermute x4, starting transfers between devices, gather_rows(): lax.ppermute(lane_down, 'row', shift_pairs(n_row, nz, 1, -1))  16.4 us
    ppermute x4, starting transfers between devices, gather_rows(): lax.ppermute(lane_up, 'row', shift_pairs(n_row, nz, 1, 1))  14.3 us
    all_to_all x1, starting transfers between devices, local(): reduced = jnp.sum(lax.all_to_all(combined, 'col', 0, 0, tiled=True), axis=0)  12.5 us
    dot_general x1, matrix products, local(): jnp.einsum('tlkmj,ij->ltkmi', pieces, anc_inv, precision=highest, preferr...  6.5 us
    ppermute x1, starting transfers between devices, gather_rows(): lax.ppermute(lane_down[..., half:], 'row', shift_pairs(n_row, nz, 1, -2))  6.17 us
    ppermute x3, starting transfers between devices, gather_rows(): lane_up = lax.ppermute(lane_up, 'row', shift_pairs(n_row, nz, 1, 2))  5.76 us
  transfers between devices with their start and end apart: 18, of which 6 were waited for; matrix products, arithmetic and copies ran while one was open for 3% of the time, Pallas kernels for 0%

profile of v6, /device:TPU:1, one launch (start us, length us, event | category | flops | bytes accessed | tf_op | source)
XLA Modules:
  0.0 146.2 jit_solution(2884916021554006193)
XLA Ops:
  0.6 0.0 copy-start
  0.6 1.0 constant_dynamic-update-slice_fusion.1
  1.6 0.8 constant_dynamic-update-slice_fusion
  2.4 3.9 %collective-permute-start = (f32[8,3840]{1,0:T(8,128)S(1)}, f32[8,3840]{1,0:T(8,128)S(1)}, u32[]{:S(2)}, u32[]{:S(2)}) collective-permute-start(f32[8,3840]{1,0:T(8,128)S(1)} %bitcast.46), channel_id=1, source_target_pairs={{0,256},{16,272},{32,288},{48,304},{64,320},{80,336},{96,352},{112... | collective-permute-start | bytes 368648 | tf_op jit(solution)/shard_map/ppermute | solution.py:33
  6.4 0.7 compare_select_fusion
  7.0 0.7 compare_and_fusion
  7.7 0.8 compare_reduce_fusion.2
  8.5 0.6 gather_fusion
  9.1 0.1 broadcast_select_fusion
  9.2 0.0 collective-permute-done
  9.2 11.7 %collective-permute-start.2 = (f32[2,8,3840]{2,1,0:T(8,128)S(1)}, f32[2,8,3840]{2,1,0:T(8,128)S(1)}, u32[]{:S(2)}, u32[]{:S(2)}) collective-permute-start(f32[2,8,3840]{2,1,0:T(8,128)S(1)} %maximum_select_fusion.1), channel_id=1, source_target_pairs={{0,224},{16,240},{32,0},{48,16},{64,32},{80,48},{96,64},{112,80},{... | collective-permute-start | bytes 737288 | tf_op jit(solution)/shard_map/ppermute | solution.py:46
  20.9 1.9 %collective-permute-start.8 = (f32[2,8,3840]{2,1,0:T(8,128)S(1)}, f32[2,8,3840]{2,1,0:T(8,128)S(1)}, u32[]{:S(2)}, u32[]{:S(2)}) collective-permute-start(f32[2,8,3840]{2,1,0:T(8,128)S(1)} %maximum_select_fusion.1), channel_id=1, source_target_pairs={{0,32},{16,48},{32,64},{48,80},{64,96},{80,112},{96,128},{112,144}... | collective-permute-start | bytes 737288 | tf_op jit(solution)/shard_map/ppermute | solution.py:45
  22.9 0.8 compare_reduce_fusion
  23.7 5.0 %collective-permute-start.1 = (f32[2,8,3840]{2,1,0:T(8,128)S(1)}, f32[2,8,3840]{2,1,0:T(8,128)S(1)}, u32[]{:S(2)}, u32[]{:S(2)}) collective-permute-start(f32[2,8,3840]{2,1,0:T(8,128)S(1)} %maximum_select_fusion.1), channel_id=1, source_target_pairs={{0,240},{16,0},{32,16},{48,32},{64,48},{80,64},{96,80},{112,96},{1... | collective-permute-start | bytes 737288 | tf_op jit(solution)/shard_map/ppermute | solution.py:43
  28.7 0.8 compare_reduce_fusion.1
  29.5 0.2 collective-permute-done.2
  29.7 6.7 %collective-permute-start.4 = (f32[2,8,3840]{2,1,0:T(8,128)S(1)}, f32[2,8,3840]{2,1,0:T(8,128)S(1)}, u32[]{:S(2)}, u32[]{:S(2)}) collective-permute-start(f32[2,8,3840]{2,1,0:T(8,128)S(1)} %collective-permute-done.2), channel_id=1, source_target_pairs={{0,224},{16,240},{32,0},{48,16},{64,32},{80,48},{96,64},{112,80},{... | collective-permute-start | bytes 737288 | tf_op jit(solution)/shard_map/ppermute | solution.py:46
  36.4 0.0 collective-permute-done.8
  36.4 1.9 %collective-permute-start.9 = (f32[2,8,3840]{2,1,0:T(8,128)S(1)}, f32[2,8,3840]{2,1,0:T(8,128)S(1)}, u32[]{:S(2)}, u32[]{:S(2)}) collective-permute-start(f32[2,8,3840]{2,1,0:T(8,128)S(1)} %collective-permute-done.8), channel_id=1, source_target_pairs={{0,32},{16,48},{32,64},{48,80},{64,96},{80,112},{96,128},{112,144}... | collective-permute-start | bytes 737288 | tf_op jit(solution)/shard_map/ppermute | solution.py:45
  38.4 3.6 %collective-permute-start.16 = (f32[2,8,3840]{2,1,0:T(8,128)S(1)}, f32[2,8,3840]{2,1,0:T(8,128)S(1)}, u32[]{:S(2)}, u32[]{:S(2)}) collective-permute-start(f32[2,8,3840]{2,1,0:T(8,128)S(1)} %maximum_select_fusion.1), channel_id=1, source_target_pairs={{0,16},{16,32},{32,48},{48,64},{64,80},{80,96},{96,112},{112,128},... | collective-permute-start | bytes 737288 | tf_op jit(solution)/shard_map/ppermute | solution.py:42
  42.1 4.3 %collective-permute-start.3 = (f32[2,8,3840]{2,1,0:T(8,128)S(1)}, f32[2,8,3840]{2,1,0:T(8,128)S(1)}, u32[]{:S(2)}, u32[]{:S(2)}) collective-permute-start(f32[2,8,3840]{2,1,0:T(8,128)S(1)} %collective-permute-done.2), channel_id=1, source_target_pairs={{0,240},{16,0},{32,16},{48,32},{64,48},{80,64},{96,80},{112,96},{1... | collective-permute-start | bytes 737288 | tf_op jit(solution)/shard_map/ppermute | solution.py:43
  46.4 0.0 collective-permute-done.1
  46.4 0.0 collective-permute-done.4
  46.4 3.4 %collective-permute-start.5 = (f32[2,8,3840]{2,1,0:T(8,128)S(1)}, f32[2,8,3840]{2,1,0:T(8,128)S(1)}, u32[]{:S(2)}, u32[]{:S(2)}) collective-permute-start(f32[2,8,3840]{2,1,0:T(8,128)S(1)} %collective-permute-done.4), channel_id=1, source_target_pairs={{0,240},{16,0},{32,16},{48,32},{64,48},{80,64},{96,80},{112,96},{1... | collective-permute-start | bytes 737288 | tf_op jit(solution)/shard_map/ppermute | solution.py:43
  49.8 4.9 %collective-permute-start.6 = (f32[2,8,3840]{2,1,0:T(8,128)S(1)}, f32[2,8,3840]{2,1,0:T(8,128)S(1)}, u32[]{:S(2)}, u32[]{:S(2)}) collective-permute-start(f32[2,8,3840]{2,1,0:T(8,128)S(1)} %collective-permute-done.4), channel_id=1, source_target_pairs={{0,224},{16,240},{32,0},{48,16},{64,32},{80,48},{96,64},{112,80},{... | collective-permute-start | bytes 737288 | tf_op jit(solution)/shard_map/ppermute | solution.py:46
  54.7 0.0 collective-permute-done.9
  54.7 1.9 %collective-permute-start.10 = (f32[2,8,3840]{2,1,0:T(8,128)S(1)}, f32[2,8,3840]{2,1,0:T(8,128)S(1)}, u32[]{:S(2)}, u32[]{:S(2)}) collective-permute-start(f32[2,8,3840]{2,1,0:T(8,128)S(1)} %collective-permute-done.9), channel_id=1, source_target_pairs={{0,32},{16,48},{32,64},{48,80},{64,96},{80,112},{96,128},{112,144}... | collective-permute-start | bytes 737288 | tf_op jit(solution)/shard_map/ppermute | solution.py:45
  56.7 0.0 collective-permute-done.3
  56.7 3.4 %collective-permute-start.15 = (f32[2,8,3840]{2,1,0:T(8,128)S(1)}, f32[2,8,3840]{2,1,0:T(8,128)S(1)}, u32[]{:S(2)}, u32[]{:S(2)}) collective-permute-start(f32[2,8,3840]{2,1,0:T(8,128)S(1)} %collective-permute-done.8), channel_id=1, source_target_pairs={{0,16},{16,32},{32,48},{48,64},{64,80},{80,96},{96,112},{112,128},... | collective-permute-start | bytes 737288 | tf_op jit(solution)/shard_map/ppermute | solution.py:42
  60.1 5.2 %collective-permute-done.6 = f32[2,8,3840]{2,1,0:T(8,128)S(1)} collective-permute-done((f32[2,8,3840]{2,1,0:T(8,128)S(1)}, f32[2,8,3840]{2,1,0:T(8,128)S(1)}, u32[]{:S(2)}, u32[]{:S(2)}) %collective-permute-start.6) | collective-permute-done | bytes 245792 | tf_op jit(solution)/shard_map/ppermute | solution.py:46
  65.2 1.9 %collective-permute-start.14 = (f32[2,8,3840]{2,1,0:T(8,128)S(1)}, f32[2,8,3840]{2,1,0:T(8,128)S(1)}, u32[]{:S(2)}, u32[]{:S(2)}) collective-permute-start(f32[2,8,3840]{2,1,0:T(8,128)S(1)} %collective-permute-done.9), channel_id=1, source_target_pairs={{0,16},{16,32},{32,48},{48,64},{64,80},{80,96},{96,112},{112,128},... | collective-permute-start | bytes 737288 | tf_op jit(solution)/shard_map/ppermute | solution.py:42
  67.2 0.0 collective-permute-done.10
  67.2 6.2 %collective-permute-start.12 = (f32[2,8,1920]{2,1,0:T(8,128)S(1)}, f32[2,8,1920]{2,1,0:T(8,128)S(1)}, u32[]{:S(2)}, u32[]{:S(2)}) collective-permute-start(f32[2,8,1920]{2,1,0:T(8,128)S(1)} %slice.29), channel_id=1, source_target_pairs={{0,224},{16,240},{32,0},{48,16},{64,32},{80,48},{96,64},{112,80},{... | collective-permute-start | bytes 368648 | tf_op jit(solution)/shard_map/ppermute | solution.py:51
  73.4 0.0 collective-permute-done.5
  73.4 1.9 %collective-permute-start.11 = (f32[2,8,1920]{2,1,0:T(8,128)S(1)}, f32[2,8,1920]{2,1,0:T(8,128)S(1)}, u32[]{:S(2)}, u32[]{:S(2)}) collective-permute-start(f32[2,8,1920]{2,1,0:T(8,128)S(1)} %slice.28), channel_id=1, source_target_pairs={{0,32},{16,48},{32,64},{48,80},{64,96},{80,112},{96,128},{112,144}... | collective-permute-start | bytes 368648 | tf_op jit(solution)/shard_map/ppermute | solution.py:50
  75.4 1.3 collective-permute-done.12
  76.6 3.7 %collective-permute-start.7 = (f32[2,8,3840]{2,1,0:T(8,128)S(1)}, f32[2,8,3840]{2,1,0:T(8,128)S(1)}, u32[]{:S(2)}, u32[]{:S(2)}) collective-permute-start(f32[2,8,3840]{2,1,0:T(8,128)S(1)} %collective-permute-done.6), channel_id=1, source_target_pairs={{0,240},{16,0},{32,16},{48,32},{64,48},{80,64},{96,80},{112,96},{1... | collective-permute-start | bytes 737288 | tf_op jit(solution)/shard_map/ppermute | solution.py:43
  80.4 2.5 %collective-permute-done.11 = f32[2,8,1920]{2,1,0:T(8,128)S(1)} collective-permute-done((f32[2,8,1920]{2,1,0:T(8,128)S(1)}, f32[2,8,1920]{2,1,0:T(8,128)S(1)}, u32[]{:S(2)}, u32[]{:S(2)}) %collective-permute-start.11) | collective-permute-done | bytes 122912 | tf_op jit(solution)/shard_map/ppermute | solution.py:50
  82.9 5.4 %collective-permute-start.13 = (f32[2,8,3840]{2,1,0:T(8,128)S(1)}, f32[2,8,3840]{2,1,0:T(8,128)S(1)}, u32[]{:S(2)}, u32[]{:S(2)}) collective-permute-start(f32[2,8,3840]{2,1,0:T(8,128)S(1)} %collective-permute-done.10), channel_id=1, source_target_pairs={{0,16},{16,32},{32,48},{48,64},{64,80},{80,96},{96,112},{112,128},... | collective-permute-start | bytes 737288 | tf_op jit(solution)/shard_map/ppermute | solution.py:42
  88.3 0.0 collective-permute-done.7
  88.4 3.4 %collective-permute-done.13 = f32[2,8,3840]{2,1,0:T(8,128)S(1)} collective-permute-done((f32[2,8,3840]{2,1,0:T(8,128)S(1)}, f32[2,8,3840]{2,1,0:T(8,128)S(1)}, u32[]{:S(2)}, u32[]{:S(2)}) %collective-permute-start.13) | collective-permute-done | bytes 245792 | tf_op jit(solution)/shard_map/ppermute | solution.py:42
  91.9 0.0 collective-permute-done.14
  91.9 0.0 collective-permute-done.15
  92.0 0.0 collective-permute-done.16
  92.0 0.0 copy-done
  92.1 6.5 %fusion.4 = f32[2,16,8,5,384]{4,2,3,0,1:T(8,128)S(1)} fusion(f32[16,2,8,5,768]{4,2,3,1,0:T(8,128)S(1)} %constant_dynamic-update-slice_fusion.2, f32[5,768]{1,0:T(8,128)S(1)} %add_convert_fusion, f32[384,768]{1,0:T(8,128)S(1)} %copy-done), kind=kOutput, calls=%fused_computation.9 | convolution fusion | flops 4530831360 | bytes 7093248 | tf_op jit(solution)/shard_map/tlkmj,ij->ltkmi/dot_general | solution.py:107
  98.6 0.4 fusion.2
  99.0 0.2 copy.15
  99.1 0.0 copy-start.1
  99.1 1.3 copy-done.1
  100.4 0.1 slice.30
  100.5 0.6 gather_fusion.1
  101.1 2.5 %fusion.8 = f32[256,2,384]{2,0,1:T(8,128)S(1)} fusion(f32[2,256,256]{2,1,0:T(8,128)} %param.13, f32[256,5,384]{2,0,1:T(8,128)} %bitcast.43, f32[2,256,384]{2,1,0:T(8,128)S(1)} %gather_fusion.1, f32[2,384]{1,0:T(2,128)S(1)} %broadcast_select_fusion, pred[2]{0:T(512)(128)(4,1)S(1)} %compare_and_fusion), kind=kOutput, calls=%fused_computation.12 | convolution fusion | flops 604569600 | bytes 2886658 | tf_op jit(solution)/shard_map/cqk,qci->kci/dot_general | solution.py:115
  103.7 0.1 pad_maximum_fusion
  103.8 0.0 copy-start.2
  103.8 1.4 copy.17
  105.2 12.5 %all-to-all-start = ((f32[16,16,5,384]{3,1,2,0:T(8,128)}), f32[16,16,5,384]{3,1,2,0:T(8,128)S(1)}, u32[]{:S(2)}, u32[]{:S(2)}) async-start(f32[16,16,5,384]{3,1,2,0:T(8,128)} %copy.17), calls=%async_computation | async-start | bytes 3932160 | tf_op jit(solution)/shard_map/all_to_all | solution.py:119
  117.8 0.0 copy-done.2
  117.8 0.1 compare_reduce_fusion.3
  117.9 26.9 %all-to-all-done = f32[16,16,5,384]{3,1,2,0:T(8,128)S(1)} async-done(((f32[16,16,5,384]{3,1,2,0:T(8,128)}), f32[16,16,5,384]{3,1,2,0:T(8,128)S(1)}, u32[]{:S(2)}, u32[]{:S(2)}) %all-to-all-start) | async-done | bytes 1966112 | tf_op jit(solution)/shard_map/all_to_all | solution.py:119
  144.8 0.1 reduce_sum.9
  144.9 0.6 slice_multiply_fusion
  145.6 0.6 slice_multiply_fusion.1
  (27 shorter events, 0.4 us)
Async XLA Ops:
  0.6 91.4 %copy-start = (f32[384,768]{1,0:T(8,128)S(1)}, f32[384,768]{1,0:T(8,128)}, u32[]{:S(2)}) copy-start(f32[384,768]{1,0:T(8,128)} %param.7) | copy-start | bytes 3538948
  2.4 6.8 %collective-permute-start = (f32[8,3840]{1,0:T(8,128)S(1)}, f32[8,3840]{1,0:T(8,128)S(1)}, u32[]{:S(2)}, u32[]{:S(2)}) collective-permute-start(f32[8,3840]{1,0:T(8,128)S(1)} %bitcast.46), channel_id=1, source_target_pairs={{0,256},{16,272},{32,288},{48,304},{64,320},{80,336},{96,352},{112... | collective-permute-start | bytes 368648 | tf_op jit(solution)/shard_map/ppermute | solution.py:33
  9.2 20.5 %collective-permute-start.2 = (f32[2,8,3840]{2,1,0:T(8,128)S(1)}, f32[2,8,3840]{2,1,0:T(8,128)S(1)}, u32[]{:S(2)}, u32[]{:S(2)}) collective-permute-start(f32[2,8,3840]{2,1,0:T(8,128)S(1)} %maximum_select_fusion.1), channel_id=1, source_target_pairs={{0,224},{16,240},{32,0},{48,16},{64,32},{80,48},{96,64},{112,80},{... | collective-permute-start | bytes 737288 | tf_op jit(solution)/shard_map/ppermute | solution.py:46
  20.9 15.5 %collective-permute-start.8 = (f32[2,8,3840]{2,1,0:T(8,128)S(1)}, f32[2,8,3840]{2,1,0:T(8,128)S(1)}, u32[]{:S(2)}, u32[]{:S(2)}) collective-permute-start(f32[2,8,3840]{2,1,0:T(8,128)S(1)} %maximum_select_fusion.1), channel_id=1, source_target_pairs={{0,32},{16,48},{32,64},{48,80},{64,96},{80,112},{96,128},{112,144}... | collective-permute-start | bytes 737288 | tf_op jit(solution)/shard_map/ppermute | solution.py:45
  23.7 22.7 %collective-permute-start.1 = (f32[2,8,3840]{2,1,0:T(8,128)S(1)}, f32[2,8,3840]{2,1,0:T(8,128)S(1)}, u32[]{:S(2)}, u32[]{:S(2)}) collective-permute-start(f32[2,8,3840]{2,1,0:T(8,128)S(1)} %maximum_select_fusion.1), channel_id=1, source_target_pairs={{0,240},{16,0},{32,16},{48,32},{64,48},{80,64},{96,80},{112,96},{1... | collective-permute-start | bytes 737288 | tf_op jit(solution)/shard_map/ppermute | solution.py:43
  29.7 16.7 %collective-permute-start.4 = (f32[2,8,3840]{2,1,0:T(8,128)S(1)}, f32[2,8,3840]{2,1,0:T(8,128)S(1)}, u32[]{:S(2)}, u32[]{:S(2)}) collective-permute-start(f32[2,8,3840]{2,1,0:T(8,128)S(1)} %collective-permute-done.2), channel_id=1, source_target_pairs={{0,224},{16,240},{32,0},{48,16},{64,32},{80,48},{96,64},{112,80},{... | collective-permute-start | bytes 737288 | tf_op jit(solution)/shard_map/ppermute | solution.py:46
  36.4 18.2 %collective-permute-start.9 = (f32[2,8,3840]{2,1,0:T(8,128)S(1)}, f32[2,8,3840]{2,1,0:T(8,128)S(1)}, u32[]{:S(2)}, u32[]{:S(2)}) collective-permute-start(f32[2,8,3840]{2,1,0:T(8,128)S(1)} %collective-permute-done.8), channel_id=1, source_target_pairs={{0,32},{16,48},{32,64},{48,80},{64,96},{80,112},{96,128},{112,144}... | collective-permute-start | bytes 737288 | tf_op jit(solution)/shard_map/ppermute | solution.py:45
  38.4 53.6 %collective-permute-start.16 = (f32[2,8,3840]{2,1,0:T(8,128)S(1)}, f32[2,8,3840]{2,1,0:T(8,128)S(1)}, u32[]{:S(2)}, u32[]{:S(2)}) collective-permute-start(f32[2,8,3840]{2,1,0:T(8,128)S(1)} %maximum_select_fusion.1), channel_id=1, source_target_pairs={{0,16},{16,32},{32,48},{48,64},{64,80},{80,96},{96,112},{112,128},... | collective-permute-start | bytes 737288 | tf_op jit(solution)/shard_map/ppermute | solution.py:42
  42.1 14.6 %collective-permute-start.3 = (f32[2,8,3840]{2,1,0:T(8,128)S(1)}, f32[2,8,3840]{2,1,0:T(8,128)S(1)}, u32[]{:S(2)}, u32[]{:S(2)}) collective-permute-start(f32[2,8,3840]{2,1,0:T(8,128)S(1)} %collective-permute-done.2), channel_id=1, source_target_pairs={{0,240},{16,0},{32,16},{48,32},{64,48},{80,64},{96,80},{112,96},{1... | collective-permute-start | bytes 737288 | tf_op jit(solution)/shard_map/ppermute | solution.py:43
  46.4 27.0 %collective-permute-start.5 = (f32[2,8,3840]{2,1,0:T(8,128)S(1)}, f32[2,8,3840]{2,1,0:T(8,128)S(1)}, u32[]{:S(2)}, u32[]{:S(2)}) collective-permute-start(f32[2,8,3840]{2,1,0:T(8,128)S(1)} %collective-permute-done.4), channel_id=1, source_target_pairs={{0,240},{16,0},{32,16},{48,32},{64,48},{80,64},{96,80},{112,96},{1... | collective-permute-start | bytes 737288 | tf_op jit(solution)/shard_map/ppermute | solution.py:43
  49.8 15.4 %collective-permute-start.6 = (f32[2,8,3840]{2,1,0:T(8,128)S(1)}, f32[2,8,3840]{2,1,0:T(8,128)S(1)}, u32[]{:S(2)}, u32[]{:S(2)}) collective-permute-start(f32[2,8,3840]{2,1,0:T(8,128)S(1)} %collective-permute-done.4), channel_id=1, source_target_pairs={{0,224},{16,240},{32,0},{48,16},{64,32},{80,48},{96,64},{112,80},{... | collective-permute-start | bytes 737288 | tf_op jit(solution)/shard_map/ppermute | solution.py:46
  54.7 12.5 %collective-permute-start.10 = (f32[2,8,3840]{2,1,0:T(8,128)S(1)}, f32[2,8,3840]{2,1,0:T(8,128)S(1)}, u32[]{:S(2)}, u32[]{:S(2)}) collective-permute-start(f32[2,8,3840]{2,1,0:T(8,128)S(1)} %collective-permute-done.9), channel_id=1, source_target_pairs={{0,32},{16,48},{32,64},{48,80},{64,96},{80,112},{96,128},{112,144}... | collective-permute-start | bytes 737288 | tf_op jit(solution)/shard_map/ppermute | solution.py:45
  56.7 35.3 %collective-permute-start.15 = (f32[2,8,3840]{2,1,0:T(8,128)S(1)}, f32[2,8,3840]{2,1,0:T(8,128)S(1)}, u32[]{:S(2)}, u32[]{:S(2)}) collective-permute-start(f32[2,8,3840]{2,1,0:T(8,128)S(1)} %collective-permute-done.8), channel_id=1, source_target_pairs={{0,16},{16,32},{32,48},{48,64},{64,80},{80,96},{96,112},{112,128},... | collective-permute-start | bytes 737288 | tf_op jit(solution)/shard_map/ppermute | solution.py:42
  65.2 26.6 %collective-permute-start.14 = (f32[2,8,3840]{2,1,0:T(8,128)S(1)}, f32[2,8,3840]{2,1,0:T(8,128)S(1)}, u32[]{:S(2)}, u32[]{:S(2)}) collective-permute-start(f32[2,8,3840]{2,1,0:T(8,128)S(1)} %collective-permute-done.9), channel_id=1, source_target_pairs={{0,16},{16,32},{32,48},{48,64},{64,80},{80,96},{96,112},{112,128},... | collective-permute-start | bytes 737288 | tf_op jit(solution)/shard_map/ppermute | solution.py:42
  67.2 9.4 %collective-permute-start.12 = (f32[2,8,1920]{2,1,0:T(8,128)S(1)}, f32[2,8,1920]{2,1,0:T(8,128)S(1)}, u32[]{:S(2)}, u32[]{:S(2)}) collective-permute-start(f32[2,8,1920]{2,1,0:T(8,128)S(1)} %slice.29), channel_id=1, source_target_pairs={{0,224},{16,240},{32,0},{48,16},{64,32},{80,48},{96,64},{112,80},{... | collective-permute-start | bytes 368648 | tf_op jit(solution)/shard_map/ppermute | solution.py:51
  73.4 9.5 %collective-permute-start.11 = (f32[2,8,1920]{2,1,0:T(8,128)S(1)}, f32[2,8,1920]{2,1,0:T(8,128)S(1)}, u32[]{:S(2)}, u32[]{:S(2)}) collective-permute-start(f32[2,8,1920]{2,1,0:T(8,128)S(1)} %slice.28), channel_id=1, source_target_pairs={{0,32},{16,48},{32,64},{48,80},{64,96},{80,112},{96,128},{112,144}... | collective-permute-start | bytes 368648 | tf_op jit(solution)/shard_map/ppermute | solution.py:50
  76.6 11.7 %collective-permute-start.7 = (f32[2,8,3840]{2,1,0:T(8,128)S(1)}, f32[2,8,3840]{2,1,0:T(8,128)S(1)}, u32[]{:S(2)}, u32[]{:S(2)}) collective-permute-start(f32[2,8,3840]{2,1,0:T(8,128)S(1)} %collective-permute-done.6), channel_id=1, source_target_pairs={{0,240},{16,0},{32,16},{48,32},{64,48},{80,64},{96,80},{112,96},{1... | collective-permute-start | bytes 737288 | tf_op jit(solution)/shard_map/ppermute | solution.py:43
  82.9 8.9 %collective-permute-start.13 = (f32[2,8,3840]{2,1,0:T(8,128)S(1)}, f32[2,8,3840]{2,1,0:T(8,128)S(1)}, u32[]{:S(2)}, u32[]{:S(2)}) collective-permute-start(f32[2,8,3840]{2,1,0:T(8,128)S(1)} %collective-permute-done.10), channel_id=1, source_target_pairs={{0,16},{16,32},{32,48},{48,64},{64,80},{80,96},{96,112},{112,128},... | collective-permute-start | bytes 737288 | tf_op jit(solution)/shard_map/ppermute | solution.py:42
  99.1 1.3 copy-start.1
  103.8 14.0 %copy-start.2 = (s32[2,36]{1,0:T(2,128)S(1)}, s32[2,36]{1,0:T(2,128)}, u32[]{:S(2)}) copy-start(s32[2,36]{1,0:T(2,128)} %param.11) | copy-start | bytes 868
  105.2 39.6 %all-to-all-start = ((f32[16,16,5,384]{3,1,2,0:T(8,128)}), f32[16,16,5,384]{3,1,2,0:T(8,128)S(1)}, u32[]{:S(2)}, u32[]{:S(2)}) async-start(f32[16,16,5,384]{3,1,2,0:T(8,128)} %copy.17), calls=%async_computation | async-start | bytes 3932160 | tf_op jit(solution)/shard_map/all_to_all | solution.py:119

commit v7 on v6

--- a/solution.py
+++ b/solution.py
@@ -50,7 +50,7 @@
             last_up = lax.ppermute(lane_up[..., :half], "row", shift_pairs(n_row, nz, 1, 2))
             last_down = lax.ppermute(lane_down[..., half:], "row", shift_pairs(n_row, nz, 1, -2))
             pieces[nz // 2] = jnp.concatenate([last_up, last_down], axis=-1)
-    return jnp.stack(pieces), z
+    return pieces, z
 
 
 def reduce_cols(value, n_col):
@@ -103,10 +103,14 @@
         ],
         axis=0,
     )
-    pieces = pieces.reshape(nz, X_LO, share_rows, members, local_cols) * col_mask
-    partial_value = jnp.einsum(
-        "tlkmj,ij->ltkmi", pieces, anc_inv, precision=highest, preferred_element_type=jnp.float32
-    )
+
+    def apply_piece(piece):
+        piece = piece.reshape(X_LO, share_rows, members, local_cols) * col_mask
+        return jnp.einsum(
+            "lkmj,ij->lkmi", piece, anc_inv, precision=highest, preferred_element_type=jnp.float32
+        )
+
+    partial_value = jnp.stack([apply_piece(piece) for piece in pieces], axis=1)
     partial_value = jnp.roll(partial_value, z, axis=1)
     partial_value = partial_value.reshape(panel_width, members, local_rows)
     first_partial = partial_value[:, :n_first]

time: 147 us -> 161 us (1.095)
  matrix products: 9.03 us -> 22.1 us
  waiting for transfers between devices: 39.6 us -> 47.3 us
  starting transfers between devices: 84.3 us -> 77.5 us
    ppermute x3, starting transfers between devices: 23.3 us -> 9.83 us  [gather_rows(): lane_down = lax.ppermute(lane_down, 'row', shift_pairs(n_row, nz, 1, -2))]
    dot_general x1 -> x16, matrix products: 6.5 us -> 19.6 us  [apply_piece(): jnp.einsum('lkmj,ij->lkmi', piece, anc_inv, precision=highest, preferred_...]
    ppermute x3, waiting for transfers between devices: 0.01 us -> 11.8 us  [gather_rows(): lane_up = lax.ppermute(lane_up, 'row', shift_pairs(n_row, nz, 1, 2))]
    ppermute x4, starting transfers between devices: 16.4 us -> 25.8 us  [gather_rows(): lax.ppermute(lane_down, 'row', shift_pairs(n_row, nz, 1, -1))]
    ppermute x4, starting transfers between devices: 14.3 us -> 9.81 us  [gather_rows(): lax.ppermute(lane_up, 'row', shift_pairs(n_row, nz, 1, 1))]
    ppermute x3, starting transfers between devices: 5.76 us -> 8.71 us  [gather_rows(): lane_up = lax.ppermute(lane_up, 'row', shift_pairs(n_row, nz, 1, 2))]
    ppermute x1, waiting for transfers between devices: 2.55 us -> 0.2 us  [gather_rows(): lax.ppermute(lane_up[..., :half], 'row', shift_pairs(n_row, nz, 1, 2))]
    ppermute x4, waiting for transfers between devices: 3.43 us -> 1.53 us  [gather_rows(): lax.ppermute(lane_up, 'row', shift_pairs(n_row, nz, 1, 1))]
  transfers between devices with their start and end apart: 18 -> 18, of which waited for: 6 -> 7; matrix products, arithmetic and copies ran while one was open for 3% -> 14% of each run, Pallas kernels for 0% -> 0%
where the time goes in v7:
time: 161 us; the launch traced here: 160 us
  starting transfers between devices  77.5 us (48%)
  waiting for transfers between devices  47.3 us (29%)
  matrix products  22.1 us (14%)
  local copies, waits for them, and re-layouts  6.24 us (4%)
  other arithmetic  5.47 us (3%)
    all_to_all x1, waiting for transfers between devices, local(): reduced = jnp.sum(lax.all_to_all(combined, 'col', 0, 0, tiled=True), axis=0)  26.9 us
    ppermute x4, starting transfers between devices, gather_rows(): lax.ppermute(lane_down, 'row', shift_pairs(n_row, nz, 1, -1))  25.8 us
    dot_general x16, matrix products, apply_piece(): jnp.einsum('lkmj,ij->lkmi', piece, anc_inv, precision=highest, preferred_...  19.6 us
    all_to_all x1, starting transfers between devices, local(): reduced = jnp.sum(lax.all_to_all(combined, 'col', 0, 0, tiled=True), axis=0)  12.1 us
    ppermute x3, waiting for transfers between devices, gather_rows(): lane_up = lax.ppermute(lane_up, 'row', shift_pairs(n_row, nz, 1, 2))  11.8 us
    ppermute x3, starting transfers between devices, gather_rows(): lane_down = lax.ppermute(lane_down, 'row', shift_pairs(n_row, nz, 1, -2))  9.83 us
    ppermute x4, starting transfers between devices, gather_rows(): lax.ppermute(lane_up, 'row', shift_pairs(n_row, nz, 1, 1))  9.81 us
    ppermute x3, starting transfers between devices, gather_rows(): lane_up = lax.ppermute(lane_up, 'row', shift_pairs(n_row, nz, 1, 2))  8.71 us
  transfers between devices with their start and end apart: 18, of which 7 were waited for; matrix products, arithmetic and copies ran while one was open for 14% of the time, Pallas kernels for 0%

profile of v7, /device:TPU:1, one launch (start us, length us, event | category | flops | bytes accessed | tf_op | source)
XLA Modules:
  0.0 160.0 jit_solution(9095836918198550053)
XLA Ops:
  0.6 0.0 copy-start
  0.6 1.0 constant_dynamic-update-slice_fusion.1
  1.6 0.8 constant_dynamic-update-slice_fusion
  2.4 3.9 %collective-permute-start = (f32[8,3840]{1,0:T(8,128)S(1)}, f32[8,3840]{1,0:T(8,128)S(1)}, u32[]{:S(2)}, u32[]{:S(2)}) collective-permute-start(f32[8,3840]{1,0:T(8,128)S(1)} %bitcast.170), channel_id=1, source_target_pairs={{0,256},{16,272},{32,288},{48,304},{64,320},{80,336},{96,352},{112... | collective-permute-start | bytes 368648 | tf_op jit(solution)/shard_map/ppermute | solution.py:33
  6.4 0.7 compare_select_fusion
  7.0 0.7 compare_and_fusion
  7.7 0.8 compare_reduce_fusion
  8.6 0.8 compare_reduce_fusion.2
  9.4 0.6 gather_fusion
  9.9 0.1 broadcast_select_fusion
  10.0 0.8 compare_reduce_fusion.1
  10.9 11.1 %collective-permute-start.1 = (f32[2,8,3840]{2,1,0:T(8,128)S(1)}, f32[2,8,3840]{2,1,0:T(8,128)S(1)}, u32[]{:S(2)}, u32[]{:S(2)}) collective-permute-start(f32[2,8,3840]{2,1,0:T(8,128)S(1)} %maximum_select_fusion.1), channel_id=1, source_target_pairs={{0,240},{16,0},{32,16},{48,32},{64,48},{80,64},{96,80},{112,96},{1... | collective-permute-start | bytes 737288 | tf_op jit(solution)/shard_map/ppermute | solution.py:43
  22.0 3.1 %collective-permute-start.2 = (f32[2,8,3840]{2,1,0:T(8,128)S(1)}, f32[2,8,3840]{2,1,0:T(8,128)S(1)}, u32[]{:S(2)}, u32[]{:S(2)}) collective-permute-start(f32[2,8,3840]{2,1,0:T(8,128)S(1)} %maximum_select_fusion.1), channel_id=1, source_target_pairs={{0,224},{16,240},{32,0},{48,16},{64,32},{80,48},{96,64},{112,80},{... | collective-permute-start | bytes 737288 | tf_op jit(solution)/shard_map/ppermute | solution.py:46
  25.1 3.1 %collective-permute-start.8 = (f32[2,8,3840]{2,1,0:T(8,128)S(1)}, f32[2,8,3840]{2,1,0:T(8,128)S(1)}, u32[]{:S(2)}, u32[]{:S(2)}) collective-permute-start(f32[2,8,3840]{2,1,0:T(8,128)S(1)} %maximum_select_fusion.1), channel_id=1, source_target_pairs={{0,32},{16,48},{32,64},{48,80},{64,96},{80,112},{96,128},{112,144}... | collective-permute-start | bytes 737288 | tf_op jit(solution)/shard_map/ppermute | solution.py:45
  28.2 1.9 %collective-permute-start.16 = (f32[2,8,3840]{2,1,0:T(8,128)S(1)}, f32[2,8,3840]{2,1,0:T(8,128)S(1)}, u32[]{:S(2)}, u32[]{:S(2)}) collective-permute-start(f32[2,8,3840]{2,1,0:T(8,128)S(1)} %maximum_select_fusion.1), channel_id=1, source_target_pairs={{0,16},{16,32},{32,48},{48,64},{64,80},{80,96},{96,112},{112,128},... | collective-permute-start | bytes 737288 | tf_op jit(solution)/shard_map/ppermute | solution.py:42
  30.2 1.2 constant_dynamic-update-slice_fusion.33
  31.4 3.0 %collective-permute-done.2 = f32[2,8,3840]{2,1,0:T(8,128)S(1)} collective-permute-done((f32[2,8,3840]{2,1,0:T(8,128)S(1)}, f32[2,8,3840]{2,1,0:T(8,128)S(1)}, u32[]{:S(2)}, u32[]{:S(2)}) %collective-permute-start.2) | collective-permute-done | bytes 245792 | tf_op jit(solution)/shard_map/ppermute | solution.py:46
  34.4 6.4 %collective-permute-start.3 = (f32[2,8,3840]{2,1,0:T(8,128)S(1)}, f32[2,8,3840]{2,1,0:T(8,128)S(1)}, u32[]{:S(2)}, u32[]{:S(2)}) collective-permute-start(f32[2,8,3840]{2,1,0:T(8,128)S(1)} %collective-permute-done.2), channel_id=1, source_target_pairs={{0,240},{16,0},{32,16},{48,32},{64,48},{80,64},{96,80},{112,96},{1... | collective-permute-start | bytes 737288 | tf_op jit(solution)/shard_map/ppermute | solution.py:43
  40.8 4.2 %collective-permute-start.4 = (f32[2,8,3840]{2,1,0:T(8,128)S(1)}, f32[2,8,3840]{2,1,0:T(8,128)S(1)}, u32[]{:S(2)}, u32[]{:S(2)}) collective-permute-start(f32[2,8,3840]{2,1,0:T(8,128)S(1)} %collective-permute-done.2), channel_id=1, source_target_pairs={{0,224},{16,240},{32,0},{48,16},{64,32},{80,48},{96,64},{112,80},{... | collective-permute-start | bytes 737288 | tf_op jit(solution)/shard_map/ppermute | solution.py:46
  45.0 1.2 constant_dynamic-update-slice_fusion.32
  46.2 2.0 %collective-permute-start.9 = (f32[2,8,3840]{2,1,0:T(8,128)S(1)}, f32[2,8,3840]{2,1,0:T(8,128)S(1)}, u32[]{:S(2)}, u32[]{:S(2)}) collective-permute-start(f32[2,8,3840]{2,1,0:T(8,128)S(1)} %collective-permute-done.8), channel_id=1, source_target_pairs={{0,32},{16,48},{32,64},{48,80},{64,96},{80,112},{96,128},{112,144}... | collective-permute-start | bytes 737288 | tf_op jit(solution)/shard_map/ppermute | solution.py:45
  48.3 3.3 %collective-permute-start.15 = (f32[2,8,3840]{2,1,0:T(8,128)S(1)}, f32[2,8,3840]{2,1,0:T(8,128)S(1)}, u32[]{:S(2)}, u32[]{:S(2)}) collective-permute-start(f32[2,8,3840]{2,1,0:T(8,128)S(1)} %collective-permute-done.8), channel_id=1, source_target_pairs={{0,16},{16,32},{32,48},{48,64},{64,80},{80,96},{96,112},{112,128},... | collective-permute-start | bytes 737288 | tf_op jit(solution)/shard_map/ppermute | solution.py:42
  51.5 1.2 constant_dynamic-update-slice_fusion.31
  52.8 2.4 %collective-permute-done.4 = f32[2,8,3840]{2,1,0:T(8,128)S(1)} collective-permute-done((f32[2,8,3840]{2,1,0:T(8,128)S(1)}, f32[2,8,3840]{2,1,0:T(8,128)S(1)}, u32[]{:S(2)}, u32[]{:S(2)}) %collective-permute-start.4) | collective-permute-done | bytes 245792 | tf_op jit(solution)/shard_map/ppermute | solution.py:46
  55.2 5.1 %collective-permute-start.5 = (f32[2,8,3840]{2,1,0:T(8,128)S(1)}, f32[2,8,3840]{2,1,0:T(8,128)S(1)}, u32[]{:S(2)}, u32[]{:S(2)}) collective-permute-start(f32[2,8,3840]{2,1,0:T(8,128)S(1)} %collective-permute-done.4), channel_id=1, source_target_pairs={{0,240},{16,0},{32,16},{48,32},{64,48},{80,64},{96,80},{112,96},{1... | collective-permute-start | bytes 737288 | tf_op jit(solution)/shard_map/ppermute | solution.py:43
  60.2 2.6 %collective-permute-start.6 = (f32[2,8,3840]{2,1,0:T(8,128)S(1)}, f32[2,8,3840]{2,1,0:T(8,128)S(1)}, u32[]{:S(2)}, u32[]{:S(2)}) collective-permute-start(f32[2,8,3840]{2,1,0:T(8,128)S(1)} %collective-permute-done.4), channel_id=1, source_target_pairs={{0,224},{16,240},{32,0},{48,16},{64,32},{80,48},{96,64},{112,80},{... | collective-permute-start | bytes 737288 | tf_op jit(solution)/shard_map/ppermute | solution.py:46
  62.8 1.2 constant_dynamic-update-slice_fusion.30
  64.1 3.6 %collective-permute-start.10 = (f32[2,8,3840]{2,1,0:T(8,128)S(1)}, f32[2,8,3840]{2,1,0:T(8,128)S(1)}, u32[]{:S(2)}, u32[]{:S(2)}) collective-permute-start(f32[2,8,3840]{2,1,0:T(8,128)S(1)} %collective-permute-done.9), channel_id=1, source_target_pairs={{0,32},{16,48},{32,64},{48,80},{64,96},{80,112},{96,128},{112,144}... | collective-permute-start | bytes 737288 | tf_op jit(solution)/shard_map/ppermute | solution.py:45
  67.7 1.2 constant_dynamic-update-slice_fusion.29
  68.9 11.8 %collective-permute-done.10 = f32[2,8,3840]{2,1,0:T(8,128)S(1)} collective-permute-done((f32[2,8,3840]{2,1,0:T(8,128)S(1)}, f32[2,8,3840]{2,1,0:T(8,128)S(1)}, u32[]{:S(2)}, u32[]{:S(2)}) %collective-permute-start.10) | collective-permute-done | bytes 245792 | tf_op jit(solution)/shard_map/ppermute | solution.py:45
  80.7 1.9 %collective-permute-start.14 = (f32[2,8,3840]{2,1,0:T(8,128)S(1)}, f32[2,8,3840]{2,1,0:T(8,128)S(1)}, u32[]{:S(2)}, u32[]{:S(2)}) collective-permute-start(f32[2,8,3840]{2,1,0:T(8,128)S(1)} %collective-permute-done.9), channel_id=1, source_target_pairs={{0,16},{16,32},{32,48},{48,64},{64,80},{80,96},{96,112},{112,128},... | collective-permute-start | bytes 737288 | tf_op jit(solution)/shard_map/ppermute | solution.py:42
  82.7 1.9 %collective-permute-start.11 = (f32[2,8,1920]{2,1,0:T(8,128)S(1)}, f32[2,8,1920]{2,1,0:T(8,128)S(1)}, u32[]{:S(2)}, u32[]{:S(2)}) collective-permute-start(f32[2,8,1920]{2,1,0:T(8,128)S(1)} %slice.28), channel_id=1, source_target_pairs={{0,32},{16,48},{32,64},{48,80},{64,96},{80,112},{96,128},{112,144}... | collective-permute-start | bytes 368648 | tf_op jit(solution)/shard_map/ppermute | solution.py:50
  84.6 5.5 %collective-permute-start.12 = (f32[2,8,1920]{2,1,0:T(8,128)S(1)}, f32[2,8,1920]{2,1,0:T(8,128)S(1)}, u32[]{:S(2)}, u32[]{:S(2)}) collective-permute-start(f32[2,8,1920]{2,1,0:T(8,128)S(1)} %slice.29), channel_id=1, source_target_pairs={{0,224},{16,240},{32,0},{48,16},{64,32},{80,48},{96,64},{112,80},{... | collective-permute-start | bytes 368648 | tf_op jit(solution)/shard_map/ppermute | solution.py:51
  90.1 1.2 constant_dynamic-update-slice_fusion.28
  91.3 1.2 constant_dynamic-update-slice_fusion.27
  92.6 0.2 collective-permute-done.11
  92.8 3.2 %collective-permute-start.7 = (f32[2,8,3840]{2,1,0:T(8,128)S(1)}, f32[2,8,3840]{2,1,0:T(8,128)S(1)}, u32[]{:S(2)}, u32[]{:S(2)}) collective-permute-start(f32[2,8,3840]{2,1,0:T(8,128)S(1)} %collective-permute-done.6), channel_id=1, source_target_pairs={{0,240},{16,0},{32,16},{48,32},{64,48},{80,64},{96,80},{112,96},{1... | collective-permute-start | bytes 737288 | tf_op jit(solution)/shard_map/ppermute | solution.py:43
  96.0 2.7 %collective-permute-start.13 = (f32[2,8,3840]{2,1,0:T(8,128)S(1)}, f32[2,8,3840]{2,1,0:T(8,128)S(1)}, u32[]{:S(2)}, u32[]{:S(2)}) collective-permute-start(f32[2,8,3840]{2,1,0:T(8,128)S(1)} %collective-permute-done.10), channel_id=1, source_target_pairs={{0,16},{16,32},{32,48},{48,64},{64,80},{80,96},{96,112},{112,128},... | collective-permute-start | bytes 737288 | tf_op jit(solution)/shard_map/ppermute | solution.py:42
  98.7 1.4 collective-permute-done.7
  100.1 1.2 constant_dynamic-update-slice_fusion.26
  101.4 1.2 constant_dynamic-update-slice_fusion.25
  102.6 1.5 collective-permute-done.13
  104.1 1.2 constant_dynamic-update-slice_fusion.24
  105.3 1.2 constant_dynamic-update-slice_fusion.23
  106.6 1.2 constant_dynamic-update-slice_fusion.22
  107.8 1.2 constant_dynamic-update-slice_fusion.21
  109.1 1.2 constant_dynamic-update-slice_fusion.20
  110.3 1.2 constant_dynamic-update-slice_fusion.19
  111.5 1.2 constant_dynamic-update-slice_fusion.18
  113.1 0.1 constant_dynamic-slice_fusion
  113.2 0.2 copy.15
  113.4 1.3 copy-done.1
  114.7 0.1 slice.30
  114.7 0.6 gather_fusion.1
  115.3 2.5 %fusion.1 = f32[256,2,384]{2,0,1:T(8,128)S(1)} fusion(f32[2,256,256]{2,1,0:T(8,128)} %param.13, f32[256,5,384]{2,0,1:T(8,128)} %bitcast.167, f32[2,256,384]{2,1,0:T(8,128)S(1)} %gather_fusion.1, f32[2,384]{1,0:T(2,128)S(1)} %broadcast_select_fusion, pred[2]{0:T(512)(128)(4,1)S(1)} %compare_and_fusion), kind=kOutput, calls=%fused_computation.5 | convolution fusion | flops 604569600 | bytes 2886658 | tf_op jit(solution)/shard_map/cqk,qci->kci/dot_general | solution.py:119
  117.9 0.1 pad_maximum_fusion
  118.0 0.0 copy-start.2
  118.0 1.4 copy.17
  119.5 12.1 %all-to-all-start = ((f32[16,16,5,384]{3,1,2,0:T(8,128)}), f32[16,16,5,384]{3,1,2,0:T(8,128)S(1)}, u32[]{:S(2)}, u32[]{:S(2)}) async-start(f32[16,16,5,384]{3,1,2,0:T(8,128)} %copy.17), calls=%async_computation | async-start | bytes 3932160 | tf_op jit(solution)/shard_map/all_to_all | solution.py:123
  131.5 0.1 compare_reduce_fusion.3
  131.7 26.9 %all-to-all-done = f32[16,16,5,384]{3,1,2,0:T(8,128)S(1)} async-done(((f32[16,16,5,384]{3,1,2,0:T(8,128)}), f32[16,16,5,384]{3,1,2,0:T(8,128)S(1)}, u32[]{:S(2)}, u32[]{:S(2)}) %all-to-all-start) | async-done | bytes 1966112 | tf_op jit(solution)/shard_map/all_to_all | solution.py:123
  158.6 0.1 reduce_sum.9
  158.7 0.6 slice_multiply_fusion
  159.3 0.6 slice_multiply_fusion.1
  (41 shorter events, 0.3 us)
Async XLA Ops:
  0.6 29.5 %copy-start = (f32[384,768]{1,0:T(8,128)S(1)}, f32[384,768]{1,0:T(8,128)}, u32[]{:S(2)}) copy-start(f32[384,768]{1,0:T(8,128)} %param.7) | copy-start | bytes 3538948
  2.4 8.4 %collective-permute-start = (f32[8,3840]{1,0:T(8,128)S(1)}, f32[8,3840]{1,0:T(8,128)S(1)}, u32[]{:S(2)}, u32[]{:S(2)}) collective-permute-start(f32[8,3840]{1,0:T(8,128)S(1)} %bitcast.170), channel_id=1, source_target_pairs={{0,256},{16,272},{32,288},{48,304},{64,320},{80,336},{96,352},{112... | collective-permute-start | bytes 368648 | tf_op jit(solution)/shard_map/ppermute | solution.py:33
  10.9 34.1 %collective-permute-start.1 = (f32[2,8,3840]{2,1,0:T(8,128)S(1)}, f32[2,8,3840]{2,1,0:T(8,128)S(1)}, u32[]{:S(2)}, u32[]{:S(2)}) collective-permute-start(f32[2,8,3840]{2,1,0:T(8,128)S(1)} %maximum_select_fusion.1), channel_id=1, source_target_pairs={{0,240},{16,0},{32,16},{48,32},{64,48},{80,64},{96,80},{112,96},{1... | collective-permute-start | bytes 737288 | tf_op jit(solution)/shard_map/ppermute | solution.py:43
  22.0 12.3 %collective-permute-start.2 = (f32[2,8,3840]{2,1,0:T(8,128)S(1)}, f32[2,8,3840]{2,1,0:T(8,128)S(1)}, u32[]{:S(2)}, u32[]{:S(2)}) collective-permute-start(f32[2,8,3840]{2,1,0:T(8,128)S(1)} %maximum_select_fusion.1), channel_id=1, source_target_pairs={{0,224},{16,240},{32,0},{48,16},{64,32},{80,48},{96,64},{112,80},{... | collective-permute-start | bytes 737288 | tf_op jit(solution)/shard_map/ppermute | solution.py:46
  25.1 21.1 %collective-permute-start.8 = (f32[2,8,3840]{2,1,0:T(8,128)S(1)}, f32[2,8,3840]{2,1,0:T(8,128)S(1)}, u32[]{:S(2)}, u32[]{:S(2)}) collective-permute-start(f32[2,8,3840]{2,1,0:T(8,128)S(1)} %maximum_select_fusion.1), channel_id=1, source_target_pairs={{0,32},{16,48},{32,64},{48,80},{64,96},{80,112},{96,128},{112,144}... | collective-permute-start | bytes 737288 | tf_op jit(solution)/shard_map/ppermute | solution.py:45
  28.2 83.3 %collective-permute-start.16 = (f32[2,8,3840]{2,1,0:T(8,128)S(1)}, f32[2,8,3840]{2,1,0:T(8,128)S(1)}, u32[]{:S(2)}, u32[]{:S(2)}) collective-permute-start(f32[2,8,3840]{2,1,0:T(8,128)S(1)} %maximum_select_fusion.1), channel_id=1, source_target_pairs={{0,16},{16,32},{32,48},{48,64},{64,80},{80,96},{96,112},{112,128},... | collective-permute-start | bytes 737288 | tf_op jit(solution)/shard_map/ppermute | solution.py:42
  34.4 25.9 %collective-permute-start.3 = (f32[2,8,3840]{2,1,0:T(8,128)S(1)}, f32[2,8,3840]{2,1,0:T(8,128)S(1)}, u32[]{:S(2)}, u32[]{:S(2)}) collective-permute-start(f32[2,8,3840]{2,1,0:T(8,128)S(1)} %collective-permute-done.2), channel_id=1, source_target_pairs={{0,240},{16,0},{32,16},{48,32},{64,48},{80,64},{96,80},{112,96},{1... | collective-permute-start | bytes 737288 | tf_op jit(solution)/shard_map/ppermute | solution.py:43
  40.8 14.4 %collective-permute-start.4 = (f32[2,8,3840]{2,1,0:T(8,128)S(1)}, f32[2,8,3840]{2,1,0:T(8,128)S(1)}, u32[]{:S(2)}, u32[]{:S(2)}) collective-permute-start(f32[2,8,3840]{2,1,0:T(8,128)S(1)} %collective-permute-done.2), channel_id=1, source_target_pairs={{0,224},{16,240},{32,0},{48,16},{64,32},{80,48},{96,64},{112,80},{... | collective-permute-start | bytes 737288 | tf_op jit(solution)/shard_map/ppermute | solution.py:46
  46.2 17.8 %collective-permute-start.9 = (f32[2,8,3840]{2,1,0:T(8,128)S(1)}, f32[2,8,3840]{2,1,0:T(8,128)S(1)}, u32[]{:S(2)}, u32[]{:S(2)}) collective-permute-start(f32[2,8,3840]{2,1,0:T(8,128)S(1)} %collective-permute-done.8), channel_id=1, source_target_pairs={{0,32},{16,48},{32,64},{48,80},{64,96},{80,112},{96,128},{112,144}... | collective-permute-start | bytes 737288 | tf_op jit(solution)/shard_map/ppermute | solution.py:45
  48.3 60.8 %collective-permute-start.15 = (f32[2,8,3840]{2,1,0:T(8,128)S(1)}, f32[2,8,3840]{2,1,0:T(8,128)S(1)}, u32[]{:S(2)}, u32[]{:S(2)}) collective-permute-start(f32[2,8,3840]{2,1,0:T(8,128)S(1)} %collective-permute-done.8), channel_id=1, source_target_pairs={{0,16},{16,32},{32,48},{48,64},{64,80},{80,96},{96,112},{112,128},... | collective-permute-start | bytes 737288 | tf_op jit(solution)/shard_map/ppermute | solution.py:42
  55.2 29.5 %collective-permute-start.5 = (f32[2,8,3840]{2,1,0:T(8,128)S(1)}, f32[2,8,3840]{2,1,0:T(8,128)S(1)}, u32[]{:S(2)}, u32[]{:S(2)}) collective-permute-start(f32[2,8,3840]{2,1,0:T(8,128)S(1)} %collective-permute-done.4), channel_id=1, source_target_pairs={{0,240},{16,0},{32,16},{48,32},{64,48},{80,64},{96,80},{112,96},{1... | collective-permute-start | bytes 737288 | tf_op jit(solution)/shard_map/ppermute | solution.py:43
  60.2 22.4 %collective-permute-start.6 = (f32[2,8,3840]{2,1,0:T(8,128)S(1)}, f32[2,8,3840]{2,1,0:T(8,128)S(1)}, u32[]{:S(2)}, u32[]{:S(2)}) collective-permute-start(f32[2,8,3840]{2,1,0:T(8,128)S(1)} %collective-permute-done.4), channel_id=1, source_target_pairs={{0,224},{16,240},{32,0},{48,16},{64,32},{80,48},{96,64},{112,80},{... | collective-permute-start | bytes 737288 | tf_op jit(solution)/shard_map/ppermute | solution.py:46
  64.1 16.7 %collective-permute-start.10 = (f32[2,8,3840]{2,1,0:T(8,128)S(1)}, f32[2,8,3840]{2,1,0:T(8,128)S(1)}, u32[]{:S(2)}, u32[]{:S(2)}) collective-permute-start(f32[2,8,3840]{2,1,0:T(8,128)S(1)} %collective-permute-done.9), channel_id=1, source_target_pairs={{0,32},{16,48},{32,64},{48,80},{64,96},{80,112},{96,128},{112,144}... | collective-permute-start | bytes 737288 | tf_op jit(solution)/shard_map/ppermute | solution.py:45
  80.7 25.8 %collective-permute-start.14 = (f32[2,8,3840]{2,1,0:T(8,128)S(1)}, f32[2,8,3840]{2,1,0:T(8,128)S(1)}, u32[]{:S(2)}, u32[]{:S(2)}) collective-permute-start(f32[2,8,3840]{2,1,0:T(8,128)S(1)} %collective-permute-done.9), channel_id=1, source_target_pairs={{0,16},{16,32},{32,48},{48,64},{64,80},{80,96},{96,112},{112,128},... | collective-permute-start | bytes 737288 | tf_op jit(solution)/shard_map/ppermute | solution.py:42
  82.7 10.1 %collective-permute-start.11 = (f32[2,8,1920]{2,1,0:T(8,128)S(1)}, f32[2,8,1920]{2,1,0:T(8,128)S(1)}, u32[]{:S(2)}, u32[]{:S(2)}) collective-permute-start(f32[2,8,1920]{2,1,0:T(8,128)S(1)} %slice.28), channel_id=1, source_target_pairs={{0,32},{16,48},{32,64},{48,80},{64,96},{80,112},{96,128},{112,144}... | collective-permute-start | bytes 368648 | tf_op jit(solution)/shard_map/ppermute | solution.py:50
  84.6 11.3 %collective-permute-start.12 = (f32[2,8,1920]{2,1,0:T(8,128)S(1)}, f32[2,8,1920]{2,1,0:T(8,128)S(1)}, u32[]{:S(2)}, u32[]{:S(2)}) collective-permute-start(f32[2,8,1920]{2,1,0:T(8,128)S(1)} %slice.29), channel_id=1, source_target_pairs={{0,224},{16,240},{32,0},{48,16},{64,32},{80,48},{96,64},{112,80},{... | collective-permute-start | bytes 368648 | tf_op jit(solution)/shard_map/ppermute | solution.py:51
  92.8 7.4 %collective-permute-start.7 = (f32[2,8,3840]{2,1,0:T(8,128)S(1)}, f32[2,8,3840]{2,1,0:T(8,128)S(1)}, u32[]{:S(2)}, u32[]{:S(2)}) collective-permute-start(f32[2,8,3840]{2,1,0:T(8,128)S(1)} %collective-permute-done.6), channel_id=1, source_target_pairs={{0,240},{16,0},{32,16},{48,32},{64,48},{80,64},{96,80},{112,96},{1... | collective-permute-start | bytes 737288 | tf_op jit(solution)/shard_map/ppermute | solution.py:43
  96.0 8.2 %collective-permute-start.13 = (f32[2,8,3840]{2,1,0:T(8,128)S(1)}, f32[2,8,3840]{2,1,0:T(8,128)S(1)}, u32[]{:S(2)}, u32[]{:S(2)}) collective-permute-start(f32[2,8,3840]{2,1,0:T(8,128)S(1)} %collective-permute-done.10), channel_id=1, source_target_pairs={{0,16},{16,32},{32,48},{48,64},{64,80},{80,96},{96,112},{112,128},... | collective-permute-start | bytes 737288 | tf_op jit(solution)/shard_map/ppermute | solution.py:42
  113.4 1.3 copy-start.1
  118.0 13.5 %copy-start.2 = (s32[2,36]{1,0:T(2,128)S(1)}, s32[2,36]{1,0:T(2,128)}, u32[]{:S(2)}) copy-start(s32[2,36]{1,0:T(2,128)} %param.11) | copy-start | bytes 868
  119.5 39.1 %all-to-all-start = ((f32[16,16,5,384]{3,1,2,0:T(8,128)}), f32[16,16,5,384]{3,1,2,0:T(8,128)S(1)}, u32[]{:S(2)}, u32[]{:S(2)}) async-start(f32[16,16,5,384]{3,1,2,0:T(8,128)} %copy.17), calls=%async_computation | async-start | bytes 3932160 | tf_op jit(solution)/shard_map/all_to_all | solution.py:123

commit v8 on v7

--- a/solution.py
+++ b/solution.py
@@ -104,13 +104,19 @@
         axis=0,
     )
 
-    def apply_piece(piece):
-        piece = piece.reshape(X_LO, share_rows, members, local_cols) * col_mask
+    def apply_pieces(offsets):
+        block = jnp.stack([pieces[t] for t in offsets]).reshape(
+            len(offsets), X_LO, share_rows, members, local_cols
+        )
         return jnp.einsum(
-            "lkmj,ij->lkmi", piece, anc_inv, precision=highest, preferred_element_type=jnp.float32
+            "tlkmj,ij->ltkmi", block * col_mask, anc_inv, precision=highest, preferred_element_type=jnp.float32
         )
 
-    partial_value = jnp.stack([apply_piece(piece) for piece in pieces], axis=1)
+    late = [nz // 2 - 1, nz // 2, nz // 2 + 1]
+    early = [t for t in range(nz) if t not in late]
+    products = jnp.concatenate([apply_pieces(early), apply_pieces(late)], axis=1)
+    order = early + late
+    partial_value = jnp.take(products, jnp.array([order.index(t) for t in range(nz)]), axis=1)
     partial_value = jnp.roll(partial_value, z, axis=1)
     partial_value = partial_value.reshape(panel_width, members, local_rows)
     first_partial = partial_value[:, :n_first]

time: 161 us -> 151 us (0.938)
  matrix products: 22.1 us -> 9.11 us
  waiting for transfers between devices: 47.3 us -> 36.7 us
  starting transfers between devices: 77.5 us -> 87 us
  other arithmetic: 5.47 us -> 8.16 us
  local copies, waits for them, and re-layouts: 6.24 us -> 8.17 us
    dot_general x16 -> x2, matrix products: 19.6 us -> 6.59 us  [apply_pieces(): jnp.einsum('tlkmj,ij->ltkmi', block * col_mask, anc_inv, precision=highes...]
    ppermute x3, starting transfers between devices: 9.83 us -> 22.4 us  [gather_rows(): lane_down = lax.ppermute(lane_down, 'row', shift_pairs(n_row, nz, 1, -2))]
    ppermute x4, starting transfers between devices: 25.8 us -> 15.5 us  [gather_rows(): lax.ppermute(lane_down, 'row', shift_pairs(n_row, nz, 1, -1))]
    ppermute x3, waiting for transfers between devices: 11.8 us -> 3.76 us  [gather_rows(): lane_up = lax.ppermute(lane_up, 'row', shift_pairs(n_row, nz, 1, 2))]
    ppermute x4, starting transfers between devices: 9.81 us -> 17.2 us  [gather_rows(): lax.ppermute(lane_up, 'row', shift_pairs(n_row, nz, 1, 1))]
    ppermute x3, waiting for transfers between devices: 5.38 us -> 0.21 us  [gather_rows(): lane_down = lax.ppermute(lane_down, 'row', shift_pairs(n_row, nz, 1, -2))]
    ppermute x3, starting transfers between devices: 8.71 us -> 6.05 us  [gather_rows(): lane_up = lax.ppermute(lane_up, 'row', shift_pairs(n_row, nz, 1, 2))]
    ppermute x4, waiting for transfers between devices: 1.53 us -> 4.16 us  [gather_rows(): lax.ppermute(lane_up, 'row', shift_pairs(n_row, nz, 1, 1))]
  transfers between devices with their start and end apart: 18 -> 18, of which waited for: 7 -> 6; matrix products, arithmetic and copies ran while one was open for 14% -> 7% of each run, Pallas kernels for 0% -> 0%
where the time goes in v8:
time: 151 us; the launch traced here: 150 us
  starting transfers between devices  87 us (58%)
  waiting for transfers between devices  36.7 us (24%)
  matrix products  9.11 us (6%)
  local copies, waits for them, and re-layouts  8.17 us (5%)
  other arithmetic  8.16 us (5%)
    all_to_all x1, waiting for transfers between devices, local(): reduced = jnp.sum(lax.all_to_all(combined, 'col', 0, 0, tiled=True), axis=0)  26.9 us
    ppermute x3, starting transfers between devices, gather_rows(): lane_down = lax.ppermute(lane_down, 'row', shift_pairs(n_row, nz, 1, -2))  22.4 us
    ppermute x4, starting transfers between devices, gather_rows(): lax.ppermute(lane_up, 'row', shift_pairs(n_row, nz, 1, 1))  17.2 us
    ppermute x4, starting transfers between devices, gather_rows(): lax.ppermute(lane_down, 'row', shift_pairs(n_row, nz, 1, -1))  15.5 us
    all_to_all x1, starting transfers between devices, local(): reduced = jnp.sum(lax.all_to_all(combined, 'col', 0, 0, tiled=True), axis=0)  14.6 us
    dot_general x2, matrix products, apply_pieces(): jnp.einsum('tlkmj,ij->ltkmi', block * col_mask, anc_inv, precision=highes...  6.59 us
    ppermute x3, starting transfers between devices, gather_rows(): lane_up = lax.ppermute(lane_up, 'row', shift_pairs(n_row, nz, 1, 2))  6.05 us
    ppermute x1, starting transfers between devices, gather_rows(): lax.ppermute(lane_down[..., half:], 'row', shift_pairs(n_row, nz, 1, -2))  5.39 us
  transfers between devices with their start and end apart: 18, of which 6 were waited for; matrix products, arithmetic and copies ran while one was open for 7% of the time, Pallas kernels for 0%

profile of v8, /device:TPU:1, one launch (start us, length us, event | category | flops | bytes accessed | tf_op | source)
XLA Modules:
  0.0 150.3 jit_solution(1916431554766616911)
XLA Ops:
  0.6 0.0 copy-start
  0.6 1.0 constant_dynamic-update-slice_fusion.1
  1.6 0.8 constant_dynamic-update-slice_fusion
  2.4 3.9 %collective-permute-start = (f32[8,3840]{1,0:T(8,128)S(1)}, f32[8,3840]{1,0:T(8,128)S(1)}, u32[]{:S(2)}, u32[]{:S(2)}) collective-permute-start(f32[8,3840]{1,0:T(8,128)S(1)} %bitcast.52), channel_id=1, source_target_pairs={{0,256},{16,272},{32,288},{48,304},{64,320},{80,336},{96,352},{112... | collective-permute-start | bytes 368648 | tf_op jit(solution)/shard_map/ppermute | solution.py:33
  6.4 0.7 compare_select_fusion
  7.0 0.7 compare_and_fusion
  7.7 0.8 compare_reduce_fusion.2
  8.5 0.6 gather_fusion.1
  9.1 0.1 broadcast_select_fusion
  9.2 0.0 collective-permute-done
  9.2 11.7 %collective-permute-start.2 = (f32[2,8,3840]{2,1,0:T(8,128)S(1)}, f32[2,8,3840]{2,1,0:T(8,128)S(1)}, u32[]{:S(2)}, u32[]{:S(2)}) collective-permute-start(f32[2,8,3840]{2,1,0:T(8,128)S(1)} %maximum_select_fusion.1), channel_id=1, source_target_pairs={{0,224},{16,240},{32,0},{48,16},{64,32},{80,48},{96,64},{112,80},{... | collective-permute-start | bytes 737288 | tf_op jit(solution)/shard_map/ppermute | solution.py:46
  20.9 1.9 %collective-permute-start.7 = (f32[2,8,3840]{2,1,0:T(8,128)S(1)}, f32[2,8,3840]{2,1,0:T(8,128)S(1)}, u32[]{:S(2)}, u32[]{:S(2)}) collective-permute-start(f32[2,8,3840]{2,1,0:T(8,128)S(1)} %maximum_select_fusion.1), channel_id=1, source_target_pairs={{0,32},{16,48},{32,64},{48,80},{64,96},{80,112},{96,128},{112,144}... | collective-permute-start | bytes 737288 | tf_op jit(solution)/shard_map/ppermute | solution.py:45
  22.9 0.8 compare_reduce_fusion.1
  23.7 0.8 compare_reduce_fusion
  24.5 5.0 %collective-permute-start.1 = (f32[2,8,3840]{2,1,0:T(8,128)S(1)}, f32[2,8,3840]{2,1,0:T(8,128)S(1)}, u32[]{:S(2)}, u32[]{:S(2)}) collective-permute-start(f32[2,8,3840]{2,1,0:T(8,128)S(1)} %maximum_select_fusion.1), channel_id=1, source_target_pairs={{0,240},{16,0},{32,16},{48,32},{64,48},{80,64},{96,80},{112,96},{1... | collective-permute-start | bytes 737288 | tf_op jit(solution)/shard_map/ppermute | solution.py:43
  29.5 0.2 collective-permute-done.2
  29.7 6.7 %collective-permute-start.4 = (f32[2,8,3840]{2,1,0:T(8,128)S(1)}, f32[2,8,3840]{2,1,0:T(8,128)S(1)}, u32[]{:S(2)}, u32[]{:S(2)}) collective-permute-start(f32[2,8,3840]{2,1,0:T(8,128)S(1)} %collective-permute-done.2), channel_id=1, source_target_pairs={{0,224},{16,240},{32,0},{48,16},{64,32},{80,48},{96,64},{112,80},{... | collective-permute-start | bytes 737288 | tf_op jit(solution)/shard_map/ppermute | solution.py:46
  36.4 0.0 collective-permute-done.7
  36.4 1.9 %collective-permute-start.8 = (f32[2,8,3840]{2,1,0:T(8,128)S(1)}, f32[2,8,3840]{2,1,0:T(8,128)S(1)}, u32[]{:S(2)}, u32[]{:S(2)}) collective-permute-start(f32[2,8,3840]{2,1,0:T(8,128)S(1)} %collective-permute-done.7), channel_id=1, source_target_pairs={{0,32},{16,48},{32,64},{48,80},{64,96},{80,112},{96,128},{112,144}... | collective-permute-start | bytes 737288 | tf_op jit(solution)/shard_map/ppermute | solution.py:45
  38.4 0.7 pad_clamp_fusion.1
  39.0 3.6 %collective-permute-start.12 = (f32[2,8,3840]{2,1,0:T(8,128)S(1)}, f32[2,8,3840]{2,1,0:T(8,128)S(1)}, u32[]{:S(2)}, u32[]{:S(2)}) collective-permute-start(f32[2,8,3840]{2,1,0:T(8,128)S(1)} %maximum_select_fusion.1), channel_id=1, source_target_pairs={{0,16},{16,32},{32,48},{48,64},{64,80},{80,96},{96,112},{112,128},... | collective-permute-start | bytes 737288 | tf_op jit(solution)/shard_map/ppermute | solution.py:42
  42.7 4.3 %collective-permute-start.3 = (f32[2,8,3840]{2,1,0:T(8,128)S(1)}, f32[2,8,3840]{2,1,0:T(8,128)S(1)}, u32[]{:S(2)}, u32[]{:S(2)}) collective-permute-start(f32[2,8,3840]{2,1,0:T(8,128)S(1)} %collective-permute-done.2), channel_id=1, source_target_pairs={{0,240},{16,0},{32,16},{48,32},{64,48},{80,64},{96,80},{112,96},{1... | collective-permute-start | bytes 737288 | tf_op jit(solution)/shard_map/ppermute | solution.py:43
  47.0 0.0 collective-permute-done.1
  47.0 0.0 collective-permute-done.4
  47.0 3.4 %collective-permute-start.5 = (f32[2,8,3840]{2,1,0:T(8,128)S(1)}, f32[2,8,3840]{2,1,0:T(8,128)S(1)}, u32[]{:S(2)}, u32[]{:S(2)}) collective-permute-start(f32[2,8,3840]{2,1,0:T(8,128)S(1)} %collective-permute-done.4), channel_id=1, source_target_pairs={{0,240},{16,0},{32,16},{48,32},{64,48},{80,64},{96,80},{112,96},{1... | collective-permute-start | bytes 737288 | tf_op jit(solution)/shard_map/ppermute | solution.py:43
  50.4 4.0 %collective-permute-start.6 = (f32[2,8,3840]{2,1,0:T(8,128)S(1)}, f32[2,8,3840]{2,1,0:T(8,128)S(1)}, u32[]{:S(2)}, u32[]{:S(2)}) collective-permute-start(f32[2,8,3840]{2,1,0:T(8,128)S(1)} %collective-permute-done.4), channel_id=1, source_target_pairs={{0,224},{16,240},{32,0},{48,16},{64,32},{80,48},{96,64},{112,80},{... | collective-permute-start | bytes 737288 | tf_op jit(solution)/shard_map/ppermute | solution.py:46
  54.4 0.0 collective-permute-done.8
  54.4 2.2 %collective-permute-start.9 = (f32[2,8,3840]{2,1,0:T(8,128)S(1)}, f32[2,8,3840]{2,1,0:T(8,128)S(1)}, u32[]{:S(2)}, u32[]{:S(2)}) collective-permute-start(f32[2,8,3840]{2,1,0:T(8,128)S(1)} %collective-permute-done.8), channel_id=1, source_target_pairs={{0,32},{16,48},{32,64},{48,80},{64,96},{80,112},{96,128},{112,144}... | collective-permute-start | bytes 737288 | tf_op jit(solution)/shard_map/ppermute | solution.py:45
  56.6 0.0 collective-permute-done.3
  56.7 3.1 %collective-permute-start.11 = (f32[2,8,3840]{2,1,0:T(8,128)S(1)}, f32[2,8,3840]{2,1,0:T(8,128)S(1)}, u32[]{:S(2)}, u32[]{:S(2)}) collective-permute-start(f32[2,8,3840]{2,1,0:T(8,128)S(1)} %collective-permute-done.7), channel_id=1, source_target_pairs={{0,16},{16,32},{32,48},{48,64},{64,80},{80,96},{96,112},{112,128},... | collective-permute-start | bytes 737288 | tf_op jit(solution)/shard_map/ppermute | solution.py:42
  59.8 3.8 %collective-permute-done.9 = f32[2,8,3840]{2,1,0:T(8,128)S(1)} collective-permute-done((f32[2,8,3840]{2,1,0:T(8,128)S(1)}, f32[2,8,3840]{2,1,0:T(8,128)S(1)}, u32[]{:S(2)}, u32[]{:S(2)}) %collective-permute-start.9) | collective-permute-done | bytes 245792 | tf_op jit(solution)/shard_map/ppermute | solution.py:45
  63.6 8.0 %collective-permute-start.10 = (f32[2,8,3840]{2,1,0:T(8,128)S(1)}, f32[2,8,3840]{2,1,0:T(8,128)S(1)}, u32[]{:S(2)}, u32[]{:S(2)}) collective-permute-start(f32[2,8,3840]{2,1,0:T(8,128)S(1)} %collective-permute-done.8), channel_id=1, source_target_pairs={{0,16},{16,32},{32,48},{48,64},{64,80},{80,96},{96,112},{112,128},... | collective-permute-start | bytes 737288 | tf_op jit(solution)/shard_map/ppermute | solution.py:42
  71.6 0.0 collective-permute-done.6
  71.6 2.0 %collective-permute-start.14 = (f32[2,8,1920]{2,1,0:T(8,128)S(1)}, f32[2,8,1920]{2,1,0:T(8,128)S(1)}, u32[]{:S(2)}, u32[]{:S(2)}) collective-permute-start(f32[2,8,1920]{2,1,0:T(8,128)S(1)} %slice.30), channel_id=1, source_target_pairs={{0,32},{16,48},{32,64},{48,80},{64,96},{80,112},{96,128},{112,144}... | collective-permute-start | bytes 368648 | tf_op jit(solution)/shard_map/ppermute | solution.py:50
  73.6 0.0 collective-permute-done.5
  73.6 5.4 %collective-permute-start.15 = (f32[2,8,1920]{2,1,0:T(8,128)S(1)}, f32[2,8,1920]{2,1,0:T(8,128)S(1)}, u32[]{:S(2)}, u32[]{:S(2)}) collective-permute-start(f32[2,8,1920]{2,1,0:T(8,128)S(1)} %slice.31), channel_id=1, source_target_pairs={{0,224},{16,240},{32,0},{48,16},{64,32},{80,48},{96,64},{112,80},{... | collective-permute-start | bytes 368648 | tf_op jit(solution)/shard_map/ppermute | solution.py:51
  79.1 0.1 collective-permute-done.10
  79.3 0.0 collective-permute-done.11
  79.4 0.0 collective-permute-done.12
  79.4 5.2 %fusion.4 = f32[2,13,8,5,384]{4,2,3,0,1:T(8,128)S(1)} fusion(f32[13,2,8,5,768]{4,2,3,1,0:T(8,128)S(1)} %constant_dynamic-update-slice_fusion.2, f32[5,768]{1,0:T(8,128)S(1)} %add_convert_fusion, f32[384,768]{1,0:T(8,128)S(1)} %copy-done), kind=kOutput, calls=%fused_computation.11 | convolution fusion | flops 3681300480 | bytes 5987328 | tf_op jit(solution)/shard_map/tlkmj,ij->ltkmi/dot_general | solution.py:111
  84.6 2.8 %collective-permute-start.13 = (f32[2,8,3840]{2,1,0:T(8,128)S(1)}, f32[2,8,3840]{2,1,0:T(8,128)S(1)}, u32[]{:S(2)}, u32[]{:S(2)}) collective-permute-start(f32[2,8,3840]{2,1,0:T(8,128)S(1)} %collective-permute-done.6), channel_id=1, source_target_pairs={{0,240},{16,0},{32,16},{48,32},{64,48},{80,64},{96,80},{112,96},{1... | collective-permute-start | bytes 737288 | tf_op jit(solution)/shard_map/ppermute | solution.py:43
  87.4 2.5 %collective-permute-start.16 = (f32[2,8,3840]{2,1,0:T(8,128)S(1)}, f32[2,8,3840]{2,1,0:T(8,128)S(1)}, u32[]{:S(2)}, u32[]{:S(2)}) collective-permute-start(f32[2,8,3840]{2,1,0:T(8,128)S(1)} %collective-permute-done.9), channel_id=1, source_target_pairs={{0,16},{16,32},{32,48},{48,64},{64,80},{80,96},{96,112},{112,128},... | collective-permute-start | bytes 737288 | tf_op jit(solution)/shard_map/ppermute | solution.py:42
  89.9 0.0 collective-permute-done.14
  89.9 0.0 collective-permute-done.15
  89.9 1.6 %collective-permute-done.13 = f32[2,8,3840]{2,1,0:T(8,128)S(1)} collective-permute-done((f32[2,8,3840]{2,1,0:T(8,128)S(1)}, f32[2,8,3840]{2,1,0:T(8,128)S(1)}, u32[]{:S(2)}, u32[]{:S(2)}) %collective-permute-start.13) | collective-permute-done | bytes 245792 | tf_op jit(solution)/shard_map/ppermute | solution.py:43
  91.5 4.0 %collective-permute-done.16 = f32[2,8,3840]{2,1,0:T(8,128)S(1)} collective-permute-done((f32[2,8,3840]{2,1,0:T(8,128)S(1)}, f32[2,8,3840]{2,1,0:T(8,128)S(1)}, u32[]{:S(2)}, u32[]{:S(2)}) %collective-permute-start.16) | collective-permute-done | bytes 245792 | tf_op jit(solution)/shard_map/ppermute | solution.py:42
  95.6 1.4 convolution_bitcast_fusion
  97.0 0.1 pad_maximum_fusion
  97.1 2.0 %gather_fusion = f32[16,2,8,5,384]{4,2,3,1,0:T(8,128)} fusion(f32[2,16,8,5,384]{4,2,3,0,1:T(8,128)S(1)} %pad_maximum_fusion, s32[1024]{0:T(1024)S(1)} %pad_clamp_fusion.1), kind=kCustom, calls=%fused_computation | custom fusion | bytes 3932224 | tf_op jit(solution)/shard_map/jit(_take)/gather | solution.py:119
  99.1 1.9 %fusion.2 = f32[2,16,8,5,384]{4,2,3,0,1:T(8,128)S(1)} fusion(s32[]{:T(128)S(6)} %select_n.102, f32[2,16,8,5,384]{4,2,3,0,1:T(8,128)} %bitcast.47), kind=kLoop, calls=%fused_computation.7 | loop fusion | flops 491520 | bytes 3932164 | tf_op jit(solution)/shard_map/jit(_roll_dynamic)/concatenate | solution.py:120
  101.0 0.2 copy.16
  101.1 1.3 copy-done.1
  102.4 0.1 slice.32
  102.5 0.6 gather_fusion.2
  103.1 2.5 %fusion.8 = f32[256,2,384]{2,0,1:T(8,128)S(1)} fusion(f32[2,256,256]{2,1,0:T(8,128)} %param.14, f32[256,5,384]{2,0,1:T(8,128)} %bitcast.49, f32[2,256,384]{2,1,0:T(8,128)S(1)} %gather_fusion.2, f32[2,384]{1,0:T(2,128)S(1)} %broadcast_select_fusion, pred[2]{0:T(512)(128)(4,1)S(1)} %compare_and_fusion), kind=kOutput, calls=%fused_computation.14 | convolution fusion | flops 604569600 | bytes 2886658 | tf_op jit(solution)/shard_map/cqk,qci->kci/dot_general | solution.py:125
  105.7 0.1 pad_maximum_fusion.1
  105.8 0.0 copy-start.2
  105.8 1.4 copy.18
  107.2 14.6 %all-to-all-start = ((f32[16,16,5,384]{3,1,2,0:T(8,128)}), f32[16,16,5,384]{3,1,2,0:T(8,128)S(1)}, u32[]{:S(2)}, u32[]{:S(2)}) async-start(f32[16,16,5,384]{3,1,2,0:T(8,128)} %copy.18), calls=%async_computation | async-start | bytes 3932160 | tf_op jit(solution)/shard_map/all_to_all | solution.py:129
  121.9 0.1 compare_reduce_fusion.3
  122.0 26.9 %all-to-all-done = f32[16,16,5,384]{3,1,2,0:T(8,128)S(1)} async-done(((f32[16,16,5,384]{3,1,2,0:T(8,128)}), f32[16,16,5,384]{3,1,2,0:T(8,128)S(1)}, u32[]{:S(2)}, u32[]{:S(2)}) %all-to-all-start) | async-done | bytes 1966112 | tf_op jit(solution)/shard_map/all_to_all | solution.py:129
  148.9 0.1 reduce_sum.9
  149.0 0.6 slice_multiply_fusion
  149.7 0.6 slice_multiply_fusion.1
  (27 shorter events, 0.4 us)
Async XLA Ops:
  0.6 78.8 %copy-start = (f32[384,768]{1,0:T(8,128)S(1)}, f32[384,768]{1,0:T(8,128)}, u32[]{:S(2)}) copy-start(f32[384,768]{1,0:T(8,128)} %param.8) | copy-start | bytes 3538948
  2.4 6.8 %collective-permute-start = (f32[8,3840]{1,0:T(8,128)S(1)}, f32[8,3840]{1,0:T(8,128)S(1)}, u32[]{:S(2)}, u32[]{:S(2)}) collective-permute-start(f32[8,3840]{1,0:T(8,128)S(1)} %bitcast.52), channel_id=1, source_target_pairs={{0,256},{16,272},{32,288},{48,304},{64,320},{80,336},{96,352},{112... | collective-permute-start | bytes 368648 | tf_op jit(solution)/shard_map/ppermute | solution.py:33
  9.2 20.5 %collective-permute-start.2 = (f32[2,8,3840]{2,1,0:T(8,128)S(1)}, f32[2,8,3840]{2,1,0:T(8,128)S(1)}, u32[]{:S(2)}, u32[]{:S(2)}) collective-permute-start(f32[2,8,3840]{2,1,0:T(8,128)S(1)} %maximum_select_fusion.1), channel_id=1, source_target_pairs={{0,224},{16,240},{32,0},{48,16},{64,32},{80,48},{96,64},{112,80},{... | collective-permute-start | bytes 737288 | tf_op jit(solution)/shard_map/ppermute | solution.py:46
  20.9 15.5 %collective-permute-start.7 = (f32[2,8,3840]{2,1,0:T(8,128)S(1)}, f32[2,8,3840]{2,1,0:T(8,128)S(1)}, u32[]{:S(2)}, u32[]{:S(2)}) collective-permute-start(f32[2,8,3840]{2,1,0:T(8,128)S(1)} %maximum_select_fusion.1), channel_id=1, source_target_pairs={{0,32},{16,48},{32,64},{48,80},{64,96},{80,112},{96,128},{112,144}... | collective-permute-start | bytes 737288 | tf_op jit(solution)/shard_map/ppermute | solution.py:45
  24.5 22.5 %collective-permute-start.1 = (f32[2,8,3840]{2,1,0:T(8,128)S(1)}, f32[2,8,3840]{2,1,0:T(8,128)S(1)}, u32[]{:S(2)}, u32[]{:S(2)}) collective-permute-start(f32[2,8,3840]{2,1,0:T(8,128)S(1)} %maximum_select_fusion.1), channel_id=1, source_target_pairs={{0,240},{16,0},{32,16},{48,32},{64,48},{80,64},{96,80},{112,96},{1... | collective-permute-start | bytes 737288 | tf_op jit(solution)/shard_map/ppermute | solution.py:43
  29.7 17.3 %collective-permute-start.4 = (f32[2,8,3840]{2,1,0:T(8,128)S(1)}, f32[2,8,3840]{2,1,0:T(8,128)S(1)}, u32[]{:S(2)}, u32[]{:S(2)}) collective-permute-start(f32[2,8,3840]{2,1,0:T(8,128)S(1)} %collective-permute-done.2), channel_id=1, source_target_pairs={{0,224},{16,240},{32,0},{48,16},{64,32},{80,48},{96,64},{112,80},{... | collective-permute-start | bytes 737288 | tf_op jit(solution)/shard_map/ppermute | solution.py:46
  36.4 18.0 %collective-permute-start.8 = (f32[2,8,3840]{2,1,0:T(8,128)S(1)}, f32[2,8,3840]{2,1,0:T(8,128)S(1)}, u32[]{:S(2)}, u32[]{:S(2)}) collective-permute-start(f32[2,8,3840]{2,1,0:T(8,128)S(1)} %collective-permute-done.7), channel_id=1, source_target_pairs={{0,32},{16,48},{32,64},{48,80},{64,96},{80,112},{96,128},{112,144}... | collective-permute-start | bytes 737288 | tf_op jit(solution)/shard_map/ppermute | solution.py:45
  39.0 40.3 %collective-permute-start.12 = (f32[2,8,3840]{2,1,0:T(8,128)S(1)}, f32[2,8,3840]{2,1,0:T(8,128)S(1)}, u32[]{:S(2)}, u32[]{:S(2)}) collective-permute-start(f32[2,8,3840]{2,1,0:T(8,128)S(1)} %maximum_select_fusion.1), channel_id=1, source_target_pairs={{0,16},{16,32},{32,48},{48,64},{64,80},{80,96},{96,112},{112,128},... | collective-permute-start | bytes 737288 | tf_op jit(solution)/shard_map/ppermute | solution.py:42
  42.7 14.0 %collective-permute-start.3 = (f32[2,8,3840]{2,1,0:T(8,128)S(1)}, f32[2,8,3840]{2,1,0:T(8,128)S(1)}, u32[]{:S(2)}, u32[]{:S(2)}) collective-permute-start(f32[2,8,3840]{2,1,0:T(8,128)S(1)} %collective-permute-done.2), channel_id=1, source_target_pairs={{0,240},{16,0},{32,16},{48,32},{64,48},{80,64},{96,80},{112,96},{1... | collective-permute-start | bytes 737288 | tf_op jit(solution)/shard_map/ppermute | solution.py:43
  47.0 26.6 %collective-permute-start.5 = (f32[2,8,3840]{2,1,0:T(8,128)S(1)}, f32[2,8,3840]{2,1,0:T(8,128)S(1)}, u32[]{:S(2)}, u32[]{:S(2)}) collective-permute-start(f32[2,8,3840]{2,1,0:T(8,128)S(1)} %collective-permute-done.4), channel_id=1, source_target_pairs={{0,240},{16,0},{32,16},{48,32},{64,48},{80,64},{96,80},{112,96},{1... | collective-permute-start | bytes 737288 | tf_op jit(solution)/shard_map/ppermute | solution.py:43
  50.4 21.2 %collective-permute-start.6 = (f32[2,8,3840]{2,1,0:T(8,128)S(1)}, f32[2,8,3840]{2,1,0:T(8,128)S(1)}, u32[]{:S(2)}, u32[]{:S(2)}) collective-permute-start(f32[2,8,3840]{2,1,0:T(8,128)S(1)} %collective-permute-done.4), channel_id=1, source_target_pairs={{0,224},{16,240},{32,0},{48,16},{64,32},{80,48},{96,64},{112,80},{... | collective-permute-start | bytes 737288 | tf_op jit(solution)/shard_map/ppermute | solution.py:46
  54.4 9.1 %collective-permute-start.9 = (f32[2,8,3840]{2,1,0:T(8,128)S(1)}, f32[2,8,3840]{2,1,0:T(8,128)S(1)}, u32[]{:S(2)}, u32[]{:S(2)}) collective-permute-start(f32[2,8,3840]{2,1,0:T(8,128)S(1)} %collective-permute-done.8), channel_id=1, source_target_pairs={{0,32},{16,48},{32,64},{48,80},{64,96},{80,112},{96,128},{112,144}... | collective-permute-start | bytes 737288 | tf_op jit(solution)/shard_map/ppermute | solution.py:45
  56.7 22.7 %collective-permute-start.11 = (f32[2,8,3840]{2,1,0:T(8,128)S(1)}, f32[2,8,3840]{2,1,0:T(8,128)S(1)}, u32[]{:S(2)}, u32[]{:S(2)}) collective-permute-start(f32[2,8,3840]{2,1,0:T(8,128)S(1)} %collective-permute-done.7), channel_id=1, source_target_pairs={{0,16},{16,32},{32,48},{48,64},{64,80},{80,96},{96,112},{112,128},... | collective-permute-start | bytes 737288 | tf_op jit(solution)/shard_map/ppermute | solution.py:42
  63.6 15.7 %collective-permute-start.10 = (f32[2,8,3840]{2,1,0:T(8,128)S(1)}, f32[2,8,3840]{2,1,0:T(8,128)S(1)}, u32[]{:S(2)}, u32[]{:S(2)}) collective-permute-start(f32[2,8,3840]{2,1,0:T(8,128)S(1)} %collective-permute-done.8), channel_id=1, source_target_pairs={{0,16},{16,32},{32,48},{48,64},{64,80},{80,96},{96,112},{112,128},... | collective-permute-start | bytes 737288 | tf_op jit(solution)/shard_map/ppermute | solution.py:42
  71.6 18.3 %collective-permute-start.14 = (f32[2,8,1920]{2,1,0:T(8,128)S(1)}, f32[2,8,1920]{2,1,0:T(8,128)S(1)}, u32[]{:S(2)}, u32[]{:S(2)}) collective-permute-start(f32[2,8,1920]{2,1,0:T(8,128)S(1)} %slice.30), channel_id=1, source_target_pairs={{0,32},{16,48},{32,64},{48,80},{64,96},{80,112},{96,128},{112,144}... | collective-permute-start | bytes 368648 | tf_op jit(solution)/shard_map/ppermute | solution.py:50
  73.6 16.3 %collective-permute-start.15 = (f32[2,8,1920]{2,1,0:T(8,128)S(1)}, f32[2,8,1920]{2,1,0:T(8,128)S(1)}, u32[]{:S(2)}, u32[]{:S(2)}) collective-permute-start(f32[2,8,1920]{2,1,0:T(8,128)S(1)} %slice.31), channel_id=1, source_target_pairs={{0,224},{16,240},{32,0},{48,16},{64,32},{80,48},{96,64},{112,80},{... | collective-permute-start | bytes 368648 | tf_op jit(solution)/shard_map/ppermute | solution.py:51
  84.6 6.9 %collective-permute-start.13 = (f32[2,8,3840]{2,1,0:T(8,128)S(1)}, f32[2,8,3840]{2,1,0:T(8,128)S(1)}, u32[]{:S(2)}, u32[]{:S(2)}) collective-permute-start(f32[2,8,3840]{2,1,0:T(8,128)S(1)} %collective-permute-done.6), channel_id=1, source_target_pairs={{0,240},{16,0},{32,16},{48,32},{64,48},{80,64},{96,80},{112,96},{1... | collective-permute-start | bytes 737288 | tf_op jit(solution)/shard_map/ppermute | solution.py:43
  87.4 8.2 %collective-permute-start.16 = (f32[2,8,3840]{2,1,0:T(8,128)S(1)}, f32[2,8,3840]{2,1,0:T(8,128)S(1)}, u32[]{:S(2)}, u32[]{:S(2)}) collective-permute-start(f32[2,8,3840]{2,1,0:T(8,128)S(1)} %collective-permute-done.9), channel_id=1, source_target_pairs={{0,16},{16,32},{32,48},{48,64},{64,80},{80,96},{96,112},{112,128},... | collective-permute-start | bytes 737288 | tf_op jit(solution)/shard_map/ppermute | solution.py:42
  101.1 1.3 copy-start.1
  105.8 16.1 %copy-start.2 = (s32[2,36]{1,0:T(2,128)S(1)}, s32[2,36]{1,0:T(2,128)}, u32[]{:S(2)}) copy-start(s32[2,36]{1,0:T(2,128)} %param.12) | copy-start | bytes 868
  107.2 41.7 %all-to-all-start = ((f32[16,16,5,384]{3,1,2,0:T(8,128)}), f32[16,16,5,384]{3,1,2,0:T(8,128)S(1)}, u32[]{:S(2)}, u32[]{:S(2)}) async-start(f32[16,16,5,384]{3,1,2,0:T(8,128)} %copy.18), calls=%async_computation | async-start | bytes 3932160 | tf_op jit(solution)/shard_map/all_to_all | solution.py:129

commit v9 on v6

--- a/solution.py
+++ b/solution.py
@@ -3,7 +3,7 @@
 from jax import lax
 from jax.sharding import PartitionSpec as P
 
-highest = lax.Precision.HIGHEST
+high = lax.Precision.HIGH
 
 X_LO = 2
 X_HI = 2
@@ -94,8 +94,7 @@
     out_first = tile_flags(lists_first, row_anchor, local_rows, panel_width)
     out_second = tile_flags(lists_second, row_anchor, local_rows, panel_width)
     panels = jnp.concatenate([factors_first, factors_second], axis=0)
-    stacked = jnp.transpose(panels, (1, 0, 2)).reshape(share_rows, members * local_cols)
-    pieces, z = gather_rows(stacked, n_row)
+    pieces, z = gather_rows(panels, n_row)
     col_mask = jnp.concatenate(
         [
             tile_flags(lists_first, col_anchor, local_cols, panel_width),
@@ -103,16 +102,16 @@
         ],
         axis=0,
     )
-    pieces = pieces.reshape(nz, X_LO, share_rows, members, local_cols) * col_mask
+    pieces = pieces * col_mask[None, None, :, None, :]
     partial_value = jnp.einsum(
-        "tlkmj,ij->ltkmi", pieces, anc_inv, precision=highest, preferred_element_type=jnp.float32
+        "tlmkj,ij->ltkmi", pieces, anc_inv, precision=high, preferred_element_type=jnp.float32
     )
     partial_value = jnp.roll(partial_value, z, axis=1)
     partial_value = partial_value.reshape(panel_width, members, local_rows)
     first_partial = partial_value[:, :n_first]
     chosen = jnp.take(first_partial, parents, axis=1)
     chosen_mask = jnp.take(out_first, parents, axis=0)
-    coupling = jnp.einsum("cqk,qci->kci", parent_link, chosen, precision=highest)
+    coupling = jnp.einsum("cqk,qci->kci", parent_link, chosen, precision=high)
     second_partial = partial_value[:, n_first:] - chosen_mask[None, :, :] * coupling
     combined = jnp.concatenate([first_partial, second_partial], axis=1)
     combined = combined.reshape(n_col, panel_width // n_col, members, local_rows)

time: 147 us -> 151 us (1.027)
  waiting for transfers between devices: 39.6 us -> 52.3 us
  starting transfers between devices: 84.3 us -> 79.1 us
  matrix products: 9.03 us -> 5.32 us
    ppermute x3, starting transfers between devices: 23.3 us -> 9.83 us  [gather_rows(): lane_down = lax.ppermute(lane_down, 'row', shift_pairs(n_row, nz, 1, -2))]
    ppermute x3, waiting for transfers between devices: 5.37 us -> 14.2 us  [gather_rows(): lane_down = lax.ppermute(lane_down, 'row', shift_pairs(n_row, nz, 1, -2))]
    ppermute x4, starting transfers between devices: 16.4 us -> 24.5 us  [gather_rows(): lax.ppermute(lane_down, 'row', shift_pairs(n_row, nz, 1, -1))]
    ppermute x4, waiting for transfers between devices: 0.01 us -> 4.97 us  [gather_rows(): lax.ppermute(lane_down, 'row', shift_pairs(n_row, nz, 1, -1))]
    dot_general x2, matrix products: 9.03 us -> 5.32 us  [the longest x1 3.31 us: local(): jnp.einsum('tlmkj,ij->ltkmi', pieces, anc_inv, precision=high, preferred_...]
    ppermute x4, starting transfers between devices: 14.3 us -> 10.7 us  [gather_rows(): lax.ppermute(lane_up, 'row', shift_pairs(n_row, nz, 1, 1))]
    ppermute x3, starting transfers between devices: 5.76 us -> 8.71 us  [gather_rows(): lane_up = lax.ppermute(lane_up, 'row', shift_pairs(n_row, nz, 1, 2))]
    ppermute x1, waiting for transfers between devices: 2.55 us -> 0.01 us  [gather_rows(): lax.ppermute(lane_up[..., :half], 'row', shift_pairs(n_row, nz, 1, 2))]
  transfers between devices with their start and end apart: 18 -> 18, of which waited for: 6 -> 8; matrix products, arithmetic and copies ran while one was open for 3% -> 3% of each run, Pallas kernels for 0% -> 0%
where the time goes in v9:
time: 151 us; the launch traced here: 150 us
  starting transfers between devices  79.1 us (52%)
  waiting for transfers between devices  52.3 us (35%)
  local copies, waits for them, and re-layouts  6.22 us (4%)
  other arithmetic  5.89 us (4%)
  matrix products  5.32 us (4%)
    all_to_all x1, waiting for transfers between devices, local(): reduced = jnp.sum(lax.all_to_all(combined, 'col', 0, 0, tiled=True), axis=0)  26.9 us
    ppermute x4, starting transfers between devices, gather_rows(): lax.ppermute(lane_down, 'row', shift_pairs(n_row, nz, 1, -1))  24.5 us
    ppermute x3, waiting for transfers between devices, gather_rows(): lane_down = lax.ppermute(lane_down, 'row', shift_pairs(n_row, nz, 1, -2))  14.2 us
    all_to_all x1, starting transfers between devices, local(): reduced = jnp.sum(lax.all_to_all(combined, 'col', 0, 0, tiled=True), axis=0)  13.4 us
    ppermute x4, starting transfers between devices, gather_rows(): lax.ppermute(lane_up, 'row', shift_pairs(n_row, nz, 1, 1))  10.7 us
    ppermute x3, starting transfers between devices, gather_rows(): lane_down = lax.ppermute(lane_down, 'row', shift_pairs(n_row, nz, 1, -2))  9.83 us
    ppermute x3, starting transfers between devices, gather_rows(): lane_up = lax.ppermute(lane_up, 'row', shift_pairs(n_row, nz, 1, 2))  8.71 us
    ppermute x1, starting transfers between devices, gather_rows(): lax.ppermute(lane_down[..., half:], 'row', shift_pairs(n_row, nz, 1, -2))  6.08 us
  transfers between devices with their start and end apart: 18, of which 8 were waited for; matrix products, arithmetic and copies ran while one was open for 3% of the time, Pallas kernels for 0%

profile of v9, /device:TPU:1, one launch (start us, length us, event | category | flops | bytes accessed | tf_op | source)
XLA Modules:
  0.0 150.0 jit_solution(18415245905227865683)
XLA Ops:
  0.6 0.0 copy-start
  0.6 1.0 constant_dynamic-update-slice_fusion.1
  1.6 0.8 constant_dynamic-update-slice_fusion
  2.4 3.9 %collective-permute-start = (f32[5,8,768]{2,1,0:T(8,128)S(1)}, f32[5,8,768]{2,1,0:T(8,128)S(1)}, u32[]{:S(2)}, u32[]{:S(2)}) collective-permute-start(f32[5,8,768]{2,1,0:T(8,128)S(1)} %constant_dynamic-update-slice_fusion), channel_id=1, source_target_pairs={{0,256},{16,272},{32,288},{48,304},{64,320},{80,336},{96,352},{112... | collective-permute-start | bytes 368648 | tf_op jit(solution)/shard_map/ppermute | solution.py:33
  6.4 0.7 compare_select_fusion
  7.0 0.7 compare_and_fusion
  7.7 0.8 compare_reduce_fusion.2
  8.5 0.6 gather_fusion
  9.1 0.1 broadcast_select_fusion
  9.2 0.8 compare_reduce_fusion
  10.0 0.0 collective-permute-done
  10.1 11.1 %collective-permute-start.1 = (f32[2,5,8,768]{3,2,1,0:T(8,128)S(1)}, f32[2,5,8,768]{3,2,1,0:T(8,128)S(1)}, u32[]{:S(2)}, u32[]{:S(2)}) collective-permute-start(f32[2,5,8,768]{3,2,1,0:T(8,128)S(1)} %maximum_select_fusion.1), channel_id=1, source_target_pairs={{0,240},{16,0},{32,16},{48,32},{64,48},{80,64},{96,80},{112,96},{1... | collective-permute-start | bytes 737288 | tf_op jit(solution)/shard_map/ppermute | solution.py:43
  21.2 3.1 %collective-permute-start.2 = (f32[2,5,8,768]{3,2,1,0:T(8,128)S(1)}, f32[2,5,8,768]{3,2,1,0:T(8,128)S(1)}, u32[]{:S(2)}, u32[]{:S(2)}) collective-permute-start(f32[2,5,8,768]{3,2,1,0:T(8,128)S(1)} %maximum_select_fusion.1), channel_id=1, source_target_pairs={{0,224},{16,240},{32,0},{48,16},{64,32},{80,48},{96,64},{112,80},{... | collective-permute-start | bytes 737288 | tf_op jit(solution)/shard_map/ppermute | solution.py:46
  24.3 3.1 %collective-permute-start.8 = (f32[2,5,8,768]{3,2,1,0:T(8,128)S(1)}, f32[2,5,8,768]{3,2,1,0:T(8,128)S(1)}, u32[]{:S(2)}, u32[]{:S(2)}) collective-permute-start(f32[2,5,8,768]{3,2,1,0:T(8,128)S(1)} %maximum_select_fusion.1), channel_id=1, source_target_pairs={{0,32},{16,48},{32,64},{48,80},{64,96},{80,112},{96,128},{112,144}... | collective-permute-start | bytes 737288 | tf_op jit(solution)/shard_map/ppermute | solution.py:45
  27.4 0.8 compare_reduce_fusion.1
  28.2 1.9 %collective-permute-start.16 = (f32[2,5,8,768]{3,2,1,0:T(8,128)S(1)}, f32[2,5,8,768]{3,2,1,0:T(8,128)S(1)}, u32[]{:S(2)}, u32[]{:S(2)}) collective-permute-start(f32[2,5,8,768]{3,2,1,0:T(8,128)S(1)} %maximum_select_fusion.1), channel_id=1, source_target_pairs={{0,16},{16,32},{32,48},{48,64},{64,80},{80,96},{96,112},{112,128},... | collective-permute-start | bytes 737288 | tf_op jit(solution)/shard_map/ppermute | solution.py:42
  30.2 3.3 %collective-permute-done.2 = f32[2,5,8,768]{3,2,1,0:T(8,128)S(1)} collective-permute-done((f32[2,5,8,768]{3,2,1,0:T(8,128)S(1)}, f32[2,5,8,768]{3,2,1,0:T(8,128)S(1)}, u32[]{:S(2)}, u32[]{:S(2)}) %collective-permute-start.2) | collective-permute-done | bytes 245792 | tf_op jit(solution)/shard_map/ppermute | solution.py:46
  33.5 6.4 %collective-permute-start.3 = (f32[2,5,8,768]{3,2,1,0:T(8,128)S(1)}, f32[2,5,8,768]{3,2,1,0:T(8,128)S(1)}, u32[]{:S(2)}, u32[]{:S(2)}) collective-permute-start(f32[2,5,8,768]{3,2,1,0:T(8,128)S(1)} %collective-permute-done.2), channel_id=1, source_target_pairs={{0,240},{16,0},{32,16},{48,32},{64,48},{80,64},{96,80},{112,96},{1... | collective-permute-start | bytes 737288 | tf_op jit(solution)/shard_map/ppermute | solution.py:43
  40.0 4.2 %collective-permute-start.4 = (f32[2,5,8,768]{3,2,1,0:T(8,128)S(1)}, f32[2,5,8,768]{3,2,1,0:T(8,128)S(1)}, u32[]{:S(2)}, u32[]{:S(2)}) collective-permute-start(f32[2,5,8,768]{3,2,1,0:T(8,128)S(1)} %collective-permute-done.2), channel_id=1, source_target_pairs={{0,224},{16,240},{32,0},{48,16},{64,32},{80,48},{96,64},{112,80},{... | collective-permute-start | bytes 737288 | tf_op jit(solution)/shard_map/ppermute | solution.py:46
  44.1 0.0 collective-permute-done.8
  44.2 2.0 %collective-permute-start.9 = (f32[2,5,8,768]{3,2,1,0:T(8,128)S(1)}, f32[2,5,8,768]{3,2,1,0:T(8,128)S(1)}, u32[]{:S(2)}, u32[]{:S(2)}) collective-permute-start(f32[2,5,8,768]{3,2,1,0:T(8,128)S(1)} %collective-permute-done.8), channel_id=1, source_target_pairs={{0,32},{16,48},{32,64},{48,80},{64,96},{80,112},{96,128},{112,144}... | collective-permute-start | bytes 737288 | tf_op jit(solution)/shard_map/ppermute | solution.py:45
  46.2 0.0 collective-permute-done.1
  46.2 3.3 %collective-permute-start.15 = (f32[2,5,8,768]{3,2,1,0:T(8,128)S(1)}, f32[2,5,8,768]{3,2,1,0:T(8,128)S(1)}, u32[]{:S(2)}, u32[]{:S(2)}) collective-permute-start(f32[2,5,8,768]{3,2,1,0:T(8,128)S(1)} %collective-permute-done.8), channel_id=1, source_target_pairs={{0,16},{16,32},{32,48},{48,64},{64,80},{80,96},{96,112},{112,128},... | collective-permute-start | bytes 737288 | tf_op jit(solution)/shard_map/ppermute | solution.py:42
  49.5 4.8 %collective-permute-done.4 = f32[2,5,8,768]{3,2,1,0:T(8,128)S(1)} collective-permute-done((f32[2,5,8,768]{3,2,1,0:T(8,128)S(1)}, f32[2,5,8,768]{3,2,1,0:T(8,128)S(1)}, u32[]{:S(2)}, u32[]{:S(2)}) %collective-permute-start.4) | collective-permute-done | bytes 245792 | tf_op jit(solution)/shard_map/ppermute | solution.py:46
  54.3 5.1 %collective-permute-start.5 = (f32[2,5,8,768]{3,2,1,0:T(8,128)S(1)}, f32[2,5,8,768]{3,2,1,0:T(8,128)S(1)}, u32[]{:S(2)}, u32[]{:S(2)}) collective-permute-start(f32[2,5,8,768]{3,2,1,0:T(8,128)S(1)} %collective-permute-done.4), channel_id=1, source_target_pairs={{0,240},{16,0},{32,16},{48,32},{64,48},{80,64},{96,80},{112,96},{1... | collective-permute-start | bytes 737288 | tf_op jit(solution)/shard_map/ppermute | solution.py:43
  59.4 0.0 collective-permute-done.3
  59.4 2.6 %collective-permute-start.6 = (f32[2,5,8,768]{3,2,1,0:T(8,128)S(1)}, f32[2,5,8,768]{3,2,1,0:T(8,128)S(1)}, u32[]{:S(2)}, u32[]{:S(2)}) collective-permute-start(f32[2,5,8,768]{3,2,1,0:T(8,128)S(1)} %collective-permute-done.4), channel_id=1, source_target_pairs={{0,224},{16,240},{32,0},{48,16},{64,32},{80,48},{96,64},{112,80},{... | collective-permute-start | bytes 737288 | tf_op jit(solution)/shard_map/ppermute | solution.py:46
  62.0 0.0 collective-permute-done.9
  62.0 3.6 %collective-permute-start.10 = (f32[2,5,8,768]{3,2,1,0:T(8,128)S(1)}, f32[2,5,8,768]{3,2,1,0:T(8,128)S(1)}, u32[]{:S(2)}, u32[]{:S(2)}) collective-permute-start(f32[2,5,8,768]{3,2,1,0:T(8,128)S(1)} %collective-permute-done.9), channel_id=1, source_target_pairs={{0,32},{16,48},{32,64},{48,80},{64,96},{80,112},{96,128},{112,144}... | collective-permute-start | bytes 737288 | tf_op jit(solution)/shard_map/ppermute | solution.py:45
  65.7 6.0 %collective-permute-done.6 = f32[2,5,8,768]{3,2,1,0:T(8,128)S(1)} collective-permute-done((f32[2,5,8,768]{3,2,1,0:T(8,128)S(1)}, f32[2,5,8,768]{3,2,1,0:T(8,128)S(1)}, u32[]{:S(2)}, u32[]{:S(2)}) %collective-permute-start.6) | collective-permute-done | bytes 245792 | tf_op jit(solution)/shard_map/ppermute | solution.py:46
  71.7 6.1 %collective-permute-start.12 = (f32[2,5,8,384]{3,2,1,0:T(8,128)S(1)}, f32[2,5,8,384]{3,2,1,0:T(8,128)S(1)}, u32[]{:S(2)}, u32[]{:S(2)}) collective-permute-start(f32[2,5,8,384]{3,2,1,0:T(8,128)S(1)} %slice.29), channel_id=1, source_target_pairs={{0,224},{16,240},{32,0},{48,16},{64,32},{80,48},{96,64},{112,80},{... | collective-permute-start | bytes 368648 | tf_op jit(solution)/shard_map/ppermute | solution.py:51
  77.8 0.8 collective-permute-done.10
  78.7 1.9 %collective-permute-start.11 = (f32[2,5,8,384]{3,2,1,0:T(8,128)S(1)}, f32[2,5,8,384]{3,2,1,0:T(8,128)S(1)}, u32[]{:S(2)}, u32[]{:S(2)}) collective-permute-start(f32[2,5,8,384]{3,2,1,0:T(8,128)S(1)} %slice.28), channel_id=1, source_target_pairs={{0,32},{16,48},{32,64},{48,80},{64,96},{80,112},{96,128},{112,144}... | collective-permute-start | bytes 368648 | tf_op jit(solution)/shard_map/ppermute | solution.py:50
  80.6 0.0 collective-permute-done.5
  80.6 1.9 %collective-permute-start.7 = (f32[2,5,8,768]{3,2,1,0:T(8,128)S(1)}, f32[2,5,8,768]{3,2,1,0:T(8,128)S(1)}, u32[]{:S(2)}, u32[]{:S(2)}) collective-permute-start(f32[2,5,8,768]{3,2,1,0:T(8,128)S(1)} %collective-permute-done.6), channel_id=1, source_target_pairs={{0,240},{16,0},{32,16},{48,32},{64,48},{80,64},{96,80},{112,96},{1... | collective-permute-start | bytes 737288 | tf_op jit(solution)/shard_map/ppermute | solution.py:43
  82.6 5.0 %collective-permute-done.7 = f32[2,5,8,768]{3,2,1,0:T(8,128)S(1)} collective-permute-done((f32[2,5,8,768]{3,2,1,0:T(8,128)S(1)}, f32[2,5,8,768]{3,2,1,0:T(8,128)S(1)}, u32[]{:S(2)}, u32[]{:S(2)}) %collective-permute-start.7) | collective-permute-done | bytes 245792 | tf_op jit(solution)/shard_map/ppermute | solution.py:43
  87.6 2.1 %collective-permute-start.13 = (f32[2,5,8,768]{3,2,1,0:T(8,128)S(1)}, f32[2,5,8,768]{3,2,1,0:T(8,128)S(1)}, u32[]{:S(2)}, u32[]{:S(2)}) collective-permute-start(f32[2,5,8,768]{3,2,1,0:T(8,128)S(1)} %collective-permute-done.10), channel_id=1, source_target_pairs={{0,16},{16,32},{32,48},{48,64},{64,80},{80,96},{96,112},{112,128},... | collective-permute-start | bytes 737288 | tf_op jit(solution)/shard_map/ppermute | solution.py:42
  89.7 0.0 collective-permute-done.12
  89.7 3.4 %collective-permute-start.14 = (f32[2,5,8,768]{3,2,1,0:T(8,128)S(1)}, f32[2,5,8,768]{3,2,1,0:T(8,128)S(1)}, u32[]{:S(2)}, u32[]{:S(2)}) collective-permute-start(f32[2,5,8,768]{3,2,1,0:T(8,128)S(1)} %collective-permute-done.9), channel_id=1, source_target_pairs={{0,16},{16,32},{32,48},{48,64},{64,80},{80,96},{96,112},{112,128},... | collective-permute-start | bytes 737288 | tf_op jit(solution)/shard_map/ppermute | solution.py:42
  93.1 0.0 collective-permute-done.11
  93.1 2.8 %collective-permute-done.13 = f32[2,5,8,768]{3,2,1,0:T(8,128)S(1)} collective-permute-done((f32[2,5,8,768]{3,2,1,0:T(8,128)S(1)}, f32[2,5,8,768]{3,2,1,0:T(8,128)S(1)}, u32[]{:S(2)}, u32[]{:S(2)}) %collective-permute-start.13) | collective-permute-done | bytes 245792 | tf_op jit(solution)/shard_map/ppermute | solution.py:42
  95.9 2.6 %collective-permute-done.14 = f32[2,5,8,768]{3,2,1,0:T(8,128)S(1)} collective-permute-done((f32[2,5,8,768]{3,2,1,0:T(8,128)S(1)}, f32[2,5,8,768]{3,2,1,0:T(8,128)S(1)}, u32[]{:S(2)}, u32[]{:S(2)}) %collective-permute-start.14) | collective-permute-done | bytes 245792 | tf_op jit(solution)/shard_map/ppermute | solution.py:42
  98.6 0.0 collective-permute-done.15
  98.6 0.0 collective-permute-done.16
  98.7 0.0 copy-done
  98.7 3.3 %fusion.4 = f32[2,16,8,5,384]{4,2,3,0,1:T(8,128)S(1)} fusion(f32[16,2,5,8,768]{4,3,2,1,0:T(8,128)S(1)} %bitcast_dynamic-update-slice_fusion, f32[5,768]{1,0:T(8,128)S(1)} %add_convert_fusion, f32[384,768]{1,0:T(8,128)S(1)} %copy-done), kind=kOutput, calls=%fused_computation.9 | convolution fusion | flops 2265907200 | bytes 7093248 | tf_op jit(solution)/shard_map/tlmkj,ij->ltkmi/dot_general | solution.py:106
  102.0 0.4 fusion.2
  102.4 0.2 copy.15
  102.6 0.0 copy-start.1
  102.6 1.3 copy-done.1
  103.9 0.1 slice.30
  104.0 0.6 gather_fusion.1
  104.6 2.0 %fusion.8 = f32[256,2,384]{2,0,1:T(8,128)S(1)} fusion(f32[2,256,256]{2,1,0:T(8,128)} %param.13, f32[256,5,384]{2,0,1:T(8,128)} %bitcast.55, f32[2,256,384]{2,1,0:T(8,128)S(1)} %gather_fusion.1, f32[2,384]{1,0:T(2,128)S(1)} %broadcast_select_fusion, pred[2]{0:T(512)(128)(4,1)S(1)} %compare_and_fusion), kind=kOutput, calls=%fused_computation.12 | convolution fusion | flops 302579712 | bytes 2886658 | tf_op jit(solution)/shard_map/cqk,qci->kci/dot_general | solution.py:114
  106.6 0.1 pad_maximum_fusion
  106.7 0.0 copy-start.2
  106.7 1.4 copy.17
  108.2 13.4 %all-to-all-start = ((f32[16,16,5,384]{3,1,2,0:T(8,128)}), f32[16,16,5,384]{3,1,2,0:T(8,128)S(1)}, u32[]{:S(2)}, u32[]{:S(2)}) async-start(f32[16,16,5,384]{3,1,2,0:T(8,128)} %copy.17), calls=%async_computation | async-start | bytes 3932160 | tf_op jit(solution)/shard_map/all_to_all | solution.py:118
  121.6 0.0 copy-done.2
  121.6 0.1 compare_reduce_fusion.3
  121.7 26.9 %all-to-all-done = f32[16,16,5,384]{3,1,2,0:T(8,128)S(1)} async-done(((f32[16,16,5,384]{3,1,2,0:T(8,128)}), f32[16,16,5,384]{3,1,2,0:T(8,128)S(1)}, u32[]{:S(2)}, u32[]{:S(2)}) %all-to-all-start) | async-done | bytes 1966112 | tf_op jit(solution)/shard_map/all_to_all | solution.py:118
  148.6 0.1 reduce_sum.9
  148.7 0.6 slice_multiply_fusion
  149.4 0.6 slice_multiply_fusion.1
  (26 shorter events, 0.4 us)
Async XLA Ops:
  0.6 98.1 %copy-start = (f32[384,768]{1,0:T(8,128)S(1)}, f32[384,768]{1,0:T(8,128)}, u32[]{:S(2)}) copy-start(f32[384,768]{1,0:T(8,128)} %param.7) | copy-start | bytes 3538948
  2.4 7.6 %collective-permute-start = (f32[5,8,768]{2,1,0:T(8,128)S(1)}, f32[5,8,768]{2,1,0:T(8,128)S(1)}, u32[]{:S(2)}, u32[]{:S(2)}) collective-permute-start(f32[5,8,768]{2,1,0:T(8,128)S(1)} %constant_dynamic-update-slice_fusion), channel_id=1, source_target_pairs={{0,256},{16,272},{32,288},{48,304},{64,320},{80,336},{96,352},{112... | collective-permute-start | bytes 368648 | tf_op jit(solution)/shard_map/ppermute | solution.py:33
  10.1 36.1 %collective-permute-start.1 = (f32[2,5,8,768]{3,2,1,0:T(8,128)S(1)}, f32[2,5,8,768]{3,2,1,0:T(8,128)S(1)}, u32[]{:S(2)}, u32[]{:S(2)}) collective-permute-start(f32[2,5,8,768]{3,2,1,0:T(8,128)S(1)} %maximum_select_fusion.1), channel_id=1, source_target_pairs={{0,240},{16,0},{32,16},{48,32},{64,48},{80,64},{96,80},{112,96},{1... | collective-permute-start | bytes 737288 | tf_op jit(solution)/shard_map/ppermute | solution.py:43
  21.2 12.3 %collective-permute-start.2 = (f32[2,5,8,768]{3,2,1,0:T(8,128)S(1)}, f32[2,5,8,768]{3,2,1,0:T(8,128)S(1)}, u32[]{:S(2)}, u32[]{:S(2)}) collective-permute-start(f32[2,5,8,768]{3,2,1,0:T(8,128)S(1)} %maximum_select_fusion.1), channel_id=1, source_target_pairs={{0,224},{16,240},{32,0},{48,16},{64,32},{80,48},{96,64},{112,80},{... | collective-permute-start | bytes 737288 | tf_op jit(solution)/shard_map/ppermute | solution.py:46
  24.3 19.9 %collective-permute-start.8 = (f32[2,5,8,768]{3,2,1,0:T(8,128)S(1)}, f32[2,5,8,768]{3,2,1,0:T(8,128)S(1)}, u32[]{:S(2)}, u32[]{:S(2)}) collective-permute-start(f32[2,5,8,768]{3,2,1,0:T(8,128)S(1)} %maximum_select_fusion.1), channel_id=1, source_target_pairs={{0,32},{16,48},{32,64},{48,80},{64,96},{80,112},{96,128},{112,144}... | collective-permute-start | bytes 737288 | tf_op jit(solution)/shard_map/ppermute | solution.py:45
  28.2 70.4 %collective-permute-start.16 = (f32[2,5,8,768]{3,2,1,0:T(8,128)S(1)}, f32[2,5,8,768]{3,2,1,0:T(8,128)S(1)}, u32[]{:S(2)}, u32[]{:S(2)}) collective-permute-start(f32[2,5,8,768]{3,2,1,0:T(8,128)S(1)} %maximum_select_fusion.1), channel_id=1, source_target_pairs={{0,16},{16,32},{32,48},{48,64},{64,80},{80,96},{96,112},{112,128},... | collective-permute-start | bytes 737288 | tf_op jit(solution)/shard_map/ppermute | solution.py:42
  33.5 25.9 %collective-permute-start.3 = (f32[2,5,8,768]{3,2,1,0:T(8,128)S(1)}, f32[2,5,8,768]{3,2,1,0:T(8,128)S(1)}, u32[]{:S(2)}, u32[]{:S(2)}) collective-permute-start(f32[2,5,8,768]{3,2,1,0:T(8,128)S(1)} %collective-permute-done.2), channel_id=1, source_target_pairs={{0,240},{16,0},{32,16},{48,32},{64,48},{80,64},{96,80},{112,96},{1... | collective-permute-start | bytes 737288 | tf_op jit(solution)/shard_map/ppermute | solution.py:43
  40.0 14.4 %collective-permute-start.4 = (f32[2,5,8,768]{3,2,1,0:T(8,128)S(1)}, f32[2,5,8,768]{3,2,1,0:T(8,128)S(1)}, u32[]{:S(2)}, u32[]{:S(2)}) collective-permute-start(f32[2,5,8,768]{3,2,1,0:T(8,128)S(1)} %collective-permute-done.2), channel_id=1, source_target_pairs={{0,224},{16,240},{32,0},{48,16},{64,32},{80,48},{96,64},{112,80},{... | collective-permute-start | bytes 737288 | tf_op jit(solution)/shard_map/ppermute | solution.py:46
  44.2 17.8 %collective-permute-start.9 = (f32[2,5,8,768]{3,2,1,0:T(8,128)S(1)}, f32[2,5,8,768]{3,2,1,0:T(8,128)S(1)}, u32[]{:S(2)}, u32[]{:S(2)}) collective-permute-start(f32[2,5,8,768]{3,2,1,0:T(8,128)S(1)} %collective-permute-done.8), channel_id=1, source_target_pairs={{0,32},{16,48},{32,64},{48,80},{64,96},{80,112},{96,128},{112,144}... | collective-permute-start | bytes 737288 | tf_op jit(solution)/shard_map/ppermute | solution.py:45
  46.2 52.4 %collective-permute-start.15 = (f32[2,5,8,768]{3,2,1,0:T(8,128)S(1)}, f32[2,5,8,768]{3,2,1,0:T(8,128)S(1)}, u32[]{:S(2)}, u32[]{:S(2)}) collective-permute-start(f32[2,5,8,768]{3,2,1,0:T(8,128)S(1)} %collective-permute-done.8), channel_id=1, source_target_pairs={{0,16},{16,32},{32,48},{48,64},{64,80},{80,96},{96,112},{112,128},... | collective-permute-start | bytes 737288 | tf_op jit(solution)/shard_map/ppermute | solution.py:42
  54.3 26.3 %collective-permute-start.5 = (f32[2,5,8,768]{3,2,1,0:T(8,128)S(1)}, f32[2,5,8,768]{3,2,1,0:T(8,128)S(1)}, u32[]{:S(2)}, u32[]{:S(2)}) collective-permute-start(f32[2,5,8,768]{3,2,1,0:T(8,128)S(1)} %collective-permute-done.4), channel_id=1, source_target_pairs={{0,240},{16,0},{32,16},{48,32},{64,48},{80,64},{96,80},{112,96},{1... | collective-permute-start | bytes 737288 | tf_op jit(solution)/shard_map/ppermute | solution.py:43
  59.4 12.3 %collective-permute-start.6 = (f32[2,5,8,768]{3,2,1,0:T(8,128)S(1)}, f32[2,5,8,768]{3,2,1,0:T(8,128)S(1)}, u32[]{:S(2)}, u32[]{:S(2)}) collective-permute-start(f32[2,5,8,768]{3,2,1,0:T(8,128)S(1)} %collective-permute-done.4), channel_id=1, source_target_pairs={{0,224},{16,240},{32,0},{48,16},{64,32},{80,48},{96,64},{112,80},{... | collective-permute-start | bytes 737288 | tf_op jit(solution)/shard_map/ppermute | solution.py:46
  62.0 16.7 %collective-permute-start.10 = (f32[2,5,8,768]{3,2,1,0:T(8,128)S(1)}, f32[2,5,8,768]{3,2,1,0:T(8,128)S(1)}, u32[]{:S(2)}, u32[]{:S(2)}) collective-permute-start(f32[2,5,8,768]{3,2,1,0:T(8,128)S(1)} %collective-permute-done.9), channel_id=1, source_target_pairs={{0,32},{16,48},{32,64},{48,80},{64,96},{80,112},{96,128},{112,144}... | collective-permute-start | bytes 737288 | tf_op jit(solution)/shard_map/ppermute | solution.py:45
  71.7 18.0 %collective-permute-start.12 = (f32[2,5,8,384]{3,2,1,0:T(8,128)S(1)}, f32[2,5,8,384]{3,2,1,0:T(8,128)S(1)}, u32[]{:S(2)}, u32[]{:S(2)}) collective-permute-start(f32[2,5,8,384]{3,2,1,0:T(8,128)S(1)} %slice.29), channel_id=1, source_target_pairs={{0,224},{16,240},{32,0},{48,16},{64,32},{80,48},{96,64},{112,80},{... | collective-permute-start | bytes 368648 | tf_op jit(solution)/shard_map/ppermute | solution.py:51
  78.7 14.4 %collective-permute-start.11 = (f32[2,5,8,384]{3,2,1,0:T(8,128)S(1)}, f32[2,5,8,384]{3,2,1,0:T(8,128)S(1)}, u32[]{:S(2)}, u32[]{:S(2)}) collective-permute-start(f32[2,5,8,384]{3,2,1,0:T(8,128)S(1)} %slice.28), channel_id=1, source_target_pairs={{0,32},{16,48},{32,64},{48,80},{64,96},{80,112},{96,128},{112,144}... | collective-permute-start | bytes 368648 | tf_op jit(solution)/shard_map/ppermute | solution.py:50
  80.6 6.9 %collective-permute-start.7 = (f32[2,5,8,768]{3,2,1,0:T(8,128)S(1)}, f32[2,5,8,768]{3,2,1,0:T(8,128)S(1)}, u32[]{:S(2)}, u32[]{:S(2)}) collective-permute-start(f32[2,5,8,768]{3,2,1,0:T(8,128)S(1)} %collective-permute-done.6), channel_id=1, source_target_pairs={{0,240},{16,0},{32,16},{48,32},{64,48},{80,64},{96,80},{112,96},{1... | collective-permute-start | bytes 737288 | tf_op jit(solution)/shard_map/ppermute | solution.py:43
  87.6 8.3 %collective-permute-start.13 = (f32[2,5,8,768]{3,2,1,0:T(8,128)S(1)}, f32[2,5,8,768]{3,2,1,0:T(8,128)S(1)}, u32[]{:S(2)}, u32[]{:S(2)}) collective-permute-start(f32[2,5,8,768]{3,2,1,0:T(8,128)S(1)} %collective-permute-done.10), channel_id=1, source_target_pairs={{0,16},{16,32},{32,48},{48,64},{64,80},{80,96},{96,112},{112,128},... | collective-permute-start | bytes 737288 | tf_op jit(solution)/shard_map/ppermute | solution.py:42
  89.7 8.8 %collective-permute-start.14 = (f32[2,5,8,768]{3,2,1,0:T(8,128)S(1)}, f32[2,5,8,768]{3,2,1,0:T(8,128)S(1)}, u32[]{:S(2)}, u32[]{:S(2)}) collective-permute-start(f32[2,5,8,768]{3,2,1,0:T(8,128)S(1)} %collective-permute-done.9), channel_id=1, source_target_pairs={{0,16},{16,32},{32,48},{48,64},{64,80},{80,96},{96,112},{112,128},... | collective-permute-start | bytes 737288 | tf_op jit(solution)/shard_map/ppermute | solution.py:42
  102.6 1.3 copy-start.1
  106.7 14.8 %copy-start.2 = (s32[2,36]{1,0:T(2,128)S(1)}, s32[2,36]{1,0:T(2,128)}, u32[]{:S(2)}) copy-start(s32[2,36]{1,0:T(2,128)} %param.11) | copy-start | bytes 868
  108.2 40.5 %all-to-all-start = ((f32[16,16,5,384]{3,1,2,0:T(8,128)}), f32[16,16,5,384]{3,1,2,0:T(8,128)S(1)}, u32[]{:S(2)}, u32[]{:S(2)}) async-start(f32[16,16,5,384]{3,1,2,0:T(8,128)} %copy.17), calls=%async_computation | async-start | bytes 3932160 | tf_op jit(solution)/shard_map/all_to_all | solution.py:118

commit v10 on v6

--- a/solution.py
+++ b/solution.py
@@ -3,7 +3,7 @@
 from jax import lax
 from jax.sharding import PartitionSpec as P
 
-highest = lax.Precision.HIGHEST
+high = lax.Precision.HIGH
 
 X_LO = 2
 X_HI = 2
@@ -105,14 +105,14 @@
     )
     pieces = pieces.reshape(nz, X_LO, share_rows, members, local_cols) * col_mask
     partial_value = jnp.einsum(
-        "tlkmj,ij->ltkmi", pieces, anc_inv, precision=highest, preferred_element_type=jnp.float32
+        "tlkmj,ij->ltkmi", pieces, anc_inv, precision=high, preferred_element_type=jnp.float32
     )
     partial_value = jnp.roll(partial_value, z, axis=1)
     partial_value = partial_value.reshape(panel_width, members, local_rows)
     first_partial = partial_value[:, :n_first]
     chosen = jnp.take(first_partial, parents, axis=1)
     chosen_mask = jnp.take(out_first, parents, axis=0)
-    coupling = jnp.einsum("cqk,qci->kci", parent_link, chosen, precision=highest)
+    coupling = jnp.einsum("cqk,qci->kci", parent_link, chosen, precision=high)
     second_partial = partial_value[:, n_first:] - chosen_mask[None, :, :] * coupling
     combined = jnp.concatenate([first_partial, second_partial], axis=1)
     combined = combined.reshape(n_col, panel_width // n_col, members, local_rows)

time: 147 us -> 144 us (0.980)
  matrix products: 9.03 us -> 5.33 us
    dot_general x2, matrix products: 9.03 us -> 5.33 us  [the longest x1 3.32 us: local(): jnp.einsum('tlkmj,ij->ltkmi', pieces, anc_inv, precision=high, preferred_...]
where the time goes in v10:
time: 144 us; the launch traced here: 143 us
  starting transfers between devices  84.3 us (59%)
  waiting for transfers between devices  39.6 us (28%)
  local copies, waits for them, and re-layouts  6.24 us (4%)
  other arithmetic  5.88 us (4%)
  matrix products  5.33 us (4%)
    all_to_all x1, waiting for transfers between devices, local(): reduced = jnp.sum(lax.all_to_all(combined, 'col', 0, 0, tiled=True), axis=0)  26.9 us
    ppermute x3, starting transfers between devices, gather_rows(): lane_down = lax.ppermute(lane_down, 'row', shift_pairs(n_row, nz, 1, -2))  23.3 us
    ppermute x4, starting transfers between devices, gather_rows(): lax.ppermute(lane_down, 'row', shift_pairs(n_row, nz, 1, -1))  16.4 us
    ppermute x4, starting transfers between devices, gather_rows(): lax.ppermute(lane_up, 'row', shift_pairs(n_row, nz, 1, 1))  14.3 us
    all_to_all x1, starting transfers between devices, local(): reduced = jnp.sum(lax.all_to_all(combined, 'col', 0, 0, tiled=True), axis=0)  12.5 us
    ppermute x1, starting transfers between devices, gather_rows(): lax.ppermute(lane_down[..., half:], 'row', shift_pairs(n_row, nz, 1, -2))  6.17 us
    ppermute x3, starting transfers between devices, gather_rows(): lane_up = lax.ppermute(lane_up, 'row', shift_pairs(n_row, nz, 1, 2))  5.76 us
    ppermute x3, waiting for transfers between devices, gather_rows(): lane_down = lax.ppermute(lane_down, 'row', shift_pairs(n_row, nz, 1, -2))  5.37 us
  transfers between devices with their start and end apart: 18, of which 6 were waited for; matrix products, arithmetic and copies ran while one was open for 3% of the time, Pallas kernels for 0%

profile of v10, /device:TPU:1, one launch (start us, length us, event | category | flops | bytes accessed | tf_op | source)
XLA Modules:
  0.0 142.5 jit_solution(14427211694655633635)
XLA Ops:
  0.6 0.0 copy-start
  0.6 1.0 constant_dynamic-update-slice_fusion.1
  1.6 0.8 constant_dynamic-update-slice_fusion
  2.4 3.9 %collective-permute-start = (f32[8,3840]{1,0:T(8,128)S(1)}, f32[8,3840]{1,0:T(8,128)S(1)}, u32[]{:S(2)}, u32[]{:S(2)}) collective-permute-start(f32[8,3840]{1,0:T(8,128)S(1)} %bitcast.46), channel_id=1, source_target_pairs={{0,256},{16,272},{32,288},{48,304},{64,320},{80,336},{96,352},{112... | collective-permute-start | bytes 368648 | tf_op jit(solution)/shard_map/ppermute | solution.py:33
  6.4 0.7 compare_select_fusion
  7.0 0.7 compare_and_fusion
  7.7 0.8 compare_reduce_fusion.2
  8.5 0.6 gather_fusion
  9.1 0.1 broadcast_select_fusion
  9.2 0.0 collective-permute-done
  9.2 11.7 %collective-permute-start.2 = (f32[2,8,3840]{2,1,0:T(8,128)S(1)}, f32[2,8,3840]{2,1,0:T(8,128)S(1)}, u32[]{:S(2)}, u32[]{:S(2)}) collective-permute-start(f32[2,8,3840]{2,1,0:T(8,128)S(1)} %maximum_select_fusion.1), channel_id=1, source_target_pairs={{0,224},{16,240},{32,0},{48,16},{64,32},{80,48},{96,64},{112,80},{... | collective-permute-start | bytes 737288 | tf_op jit(solution)/shard_map/ppermute | solution.py:46
  20.9 1.9 %collective-permute-start.8 = (f32[2,8,3840]{2,1,0:T(8,128)S(1)}, f32[2,8,3840]{2,1,0:T(8,128)S(1)}, u32[]{:S(2)}, u32[]{:S(2)}) collective-permute-start(f32[2,8,3840]{2,1,0:T(8,128)S(1)} %maximum_select_fusion.1), channel_id=1, source_target_pairs={{0,32},{16,48},{32,64},{48,80},{64,96},{80,112},{96,128},{112,144}... | collective-permute-start | bytes 737288 | tf_op jit(solution)/shard_map/ppermute | solution.py:45
  22.9 0.8 compare_reduce_fusion
  23.7 5.0 %collective-permute-start.1 = (f32[2,8,3840]{2,1,0:T(8,128)S(1)}, f32[2,8,3840]{2,1,0:T(8,128)S(1)}, u32[]{:S(2)}, u32[]{:S(2)}) collective-permute-start(f32[2,8,3840]{2,1,0:T(8,128)S(1)} %maximum_select_fusion.1), channel_id=1, source_target_pairs={{0,240},{16,0},{32,16},{48,32},{64,48},{80,64},{96,80},{112,96},{1... | collective-permute-start | bytes 737288 | tf_op jit(solution)/shard_map/ppermute | solution.py:43
  28.7 0.8 compare_reduce_fusion.1
  29.5 0.2 collective-permute-done.2
  29.7 6.7 %collective-permute-start.4 = (f32[2,8,3840]{2,1,0:T(8,128)S(1)}, f32[2,8,3840]{2,1,0:T(8,128)S(1)}, u32[]{:S(2)}, u32[]{:S(2)}) collective-permute-start(f32[2,8,3840]{2,1,0:T(8,128)S(1)} %collective-permute-done.2), channel_id=1, source_target_pairs={{0,224},{16,240},{32,0},{48,16},{64,32},{80,48},{96,64},{112,80},{... | collective-permute-start | bytes 737288 | tf_op jit(solution)/shard_map/ppermute | solution.py:46
  36.4 0.0 collective-permute-done.8
  36.4 1.9 %collective-permute-start.9 = (f32[2,8,3840]{2,1,0:T(8,128)S(1)}, f32[2,8,3840]{2,1,0:T(8,128)S(1)}, u32[]{:S(2)}, u32[]{:S(2)}) collective-permute-start(f32[2,8,3840]{2,1,0:T(8,128)S(1)} %collective-permute-done.8), channel_id=1, source_target_pairs={{0,32},{16,48},{32,64},{48,80},{64,96},{80,112},{96,128},{112,144}... | collective-permute-start | bytes 737288 | tf_op jit(solution)/shard_map/ppermute | solution.py:45
  38.4 3.6 %collective-permute-start.16 = (f32[2,8,3840]{2,1,0:T(8,128)S(1)}, f32[2,8,3840]{2,1,0:T(8,128)S(1)}, u32[]{:S(2)}, u32[]{:S(2)}) collective-permute-start(f32[2,8,3840]{2,1,0:T(8,128)S(1)} %maximum_select_fusion.1), channel_id=1, source_target_pairs={{0,16},{16,32},{32,48},{48,64},{64,80},{80,96},{96,112},{112,128},... | collective-permute-start | bytes 737288 | tf_op jit(solution)/shard_map/ppermute | solution.py:42
  42.1 4.3 %collective-permute-start.3 = (f32[2,8,3840]{2,1,0:T(8,128)S(1)}, f32[2,8,3840]{2,1,0:T(8,128)S(1)}, u32[]{:S(2)}, u32[]{:S(2)}) collective-permute-start(f32[2,8,3840]{2,1,0:T(8,128)S(1)} %collective-permute-done.2), channel_id=1, source_target_pairs={{0,240},{16,0},{32,16},{48,32},{64,48},{80,64},{96,80},{112,96},{1... | collective-permute-start | bytes 737288 | tf_op jit(solution)/shard_map/ppermute | solution.py:43
  46.4 0.0 collective-permute-done.1
  46.4 0.0 collective-permute-done.4
  46.4 3.4 %collective-permute-start.5 = (f32[2,8,3840]{2,1,0:T(8,128)S(1)}, f32[2,8,3840]{2,1,0:T(8,128)S(1)}, u32[]{:S(2)}, u32[]{:S(2)}) collective-permute-start(f32[2,8,3840]{2,1,0:T(8,128)S(1)} %collective-permute-done.4), channel_id=1, source_target_pairs={{0,240},{16,0},{32,16},{48,32},{64,48},{80,64},{96,80},{112,96},{1... | collective-permute-start | bytes 737288 | tf_op jit(solution)/shard_map/ppermute | solution.py:43
  49.8 4.9 %collective-permute-start.6 = (f32[2,8,3840]{2,1,0:T(8,128)S(1)}, f32[2,8,3840]{2,1,0:T(8,128)S(1)}, u32[]{:S(2)}, u32[]{:S(2)}) collective-permute-start(f32[2,8,3840]{2,1,0:T(8,128)S(1)} %collective-permute-done.4), channel_id=1, source_target_pairs={{0,224},{16,240},{32,0},{48,16},{64,32},{80,48},{96,64},{112,80},{... | collective-permute-start | bytes 737288 | tf_op jit(solution)/shard_map/ppermute | solution.py:46
  54.7 0.0 collective-permute-done.9
  54.7 1.9 %collective-permute-start.10 = (f32[2,8,3840]{2,1,0:T(8,128)S(1)}, f32[2,8,3840]{2,1,0:T(8,128)S(1)}, u32[]{:S(2)}, u32[]{:S(2)}) collective-permute-start(f32[2,8,3840]{2,1,0:T(8,128)S(1)} %collective-permute-done.9), channel_id=1, source_target_pairs={{0,32},{16,48},{32,64},{48,80},{64,96},{80,112},{96,128},{112,144}... | collective-permute-start | bytes 737288 | tf_op jit(solution)/shard_map/ppermute | solution.py:45
  56.7 0.0 collective-permute-done.3
  56.7 3.4 %collective-permute-start.15 = (f32[2,8,3840]{2,1,0:T(8,128)S(1)}, f32[2,8,3840]{2,1,0:T(8,128)S(1)}, u32[]{:S(2)}, u32[]{:S(2)}) collective-permute-start(f32[2,8,3840]{2,1,0:T(8,128)S(1)} %collective-permute-done.8), channel_id=1, source_target_pairs={{0,16},{16,32},{32,48},{48,64},{64,80},{80,96},{96,112},{112,128},... | collective-permute-start | bytes 737288 | tf_op jit(solution)/shard_map/ppermute | solution.py:42
  60.1 5.2 %collective-permute-done.6 = f32[2,8,3840]{2,1,0:T(8,128)S(1)} collective-permute-done((f32[2,8,3840]{2,1,0:T(8,128)S(1)}, f32[2,8,3840]{2,1,0:T(8,128)S(1)}, u32[]{:S(2)}, u32[]{:S(2)}) %collective-permute-start.6) | collective-permute-done | bytes 245792 | tf_op jit(solution)/shard_map/ppermute | solution.py:46
  65.2 1.9 %collective-permute-start.14 = (f32[2,8,3840]{2,1,0:T(8,128)S(1)}, f32[2,8,3840]{2,1,0:T(8,128)S(1)}, u32[]{:S(2)}, u32[]{:S(2)}) collective-permute-start(f32[2,8,3840]{2,1,0:T(8,128)S(1)} %collective-permute-done.9), channel_id=1, source_target_pairs={{0,16},{16,32},{32,48},{48,64},{64,80},{80,96},{96,112},{112,128},... | collective-permute-start | bytes 737288 | tf_op jit(solution)/shard_map/ppermute | solution.py:42
  67.2 0.0 collective-permute-done.10
  67.2 6.2 %collective-permute-start.12 = (f32[2,8,1920]{2,1,0:T(8,128)S(1)}, f32[2,8,1920]{2,1,0:T(8,128)S(1)}, u32[]{:S(2)}, u32[]{:S(2)}) collective-permute-start(f32[2,8,1920]{2,1,0:T(8,128)S(1)} %slice.29), channel_id=1, source_target_pairs={{0,224},{16,240},{32,0},{48,16},{64,32},{80,48},{96,64},{112,80},{... | collective-permute-start | bytes 368648 | tf_op jit(solution)/shard_map/ppermute | solution.py:51
  73.4 0.0 collective-permute-done.5
  73.4 1.9 %collective-permute-start.11 = (f32[2,8,1920]{2,1,0:T(8,128)S(1)}, f32[2,8,1920]{2,1,0:T(8,128)S(1)}, u32[]{:S(2)}, u32[]{:S(2)}) collective-permute-start(f32[2,8,1920]{2,1,0:T(8,128)S(1)} %slice.28), channel_id=1, source_target_pairs={{0,32},{16,48},{32,64},{48,80},{64,96},{80,112},{96,128},{112,144}... | collective-permute-start | bytes 368648 | tf_op jit(solution)/shard_map/ppermute | solution.py:50
  75.4 1.3 collective-permute-done.12
  76.6 3.7 %collective-permute-start.7 = (f32[2,8,3840]{2,1,0:T(8,128)S(1)}, f32[2,8,3840]{2,1,0:T(8,128)S(1)}, u32[]{:S(2)}, u32[]{:S(2)}) collective-permute-start(f32[2,8,3840]{2,1,0:T(8,128)S(1)} %collective-permute-done.6), channel_id=1, source_target_pairs={{0,240},{16,0},{32,16},{48,32},{64,48},{80,64},{96,80},{112,96},{1... | collective-permute-start | bytes 737288 | tf_op jit(solution)/shard_map/ppermute | solution.py:43
  80.4 2.5 %collective-permute-done.11 = f32[2,8,1920]{2,1,0:T(8,128)S(1)} collective-permute-done((f32[2,8,1920]{2,1,0:T(8,128)S(1)}, f32[2,8,1920]{2,1,0:T(8,128)S(1)}, u32[]{:S(2)}, u32[]{:S(2)}) %collective-permute-start.11) | collective-permute-done | bytes 122912 | tf_op jit(solution)/shard_map/ppermute | solution.py:50
  82.9 5.4 %collective-permute-start.13 = (f32[2,8,3840]{2,1,0:T(8,128)S(1)}, f32[2,8,3840]{2,1,0:T(8,128)S(1)}, u32[]{:S(2)}, u32[]{:S(2)}) collective-permute-start(f32[2,8,3840]{2,1,0:T(8,128)S(1)} %collective-permute-done.10), channel_id=1, source_target_pairs={{0,16},{16,32},{32,48},{48,64},{64,80},{80,96},{96,112},{112,128},... | collective-permute-start | bytes 737288 | tf_op jit(solution)/shard_map/ppermute | solution.py:42
  88.3 0.0 collective-permute-done.7
  88.4 3.4 %collective-permute-done.13 = f32[2,8,3840]{2,1,0:T(8,128)S(1)} collective-permute-done((f32[2,8,3840]{2,1,0:T(8,128)S(1)}, f32[2,8,3840]{2,1,0:T(8,128)S(1)}, u32[]{:S(2)}, u32[]{:S(2)}) %collective-permute-start.13) | collective-permute-done | bytes 245792 | tf_op jit(solution)/shard_map/ppermute | solution.py:42
  91.9 0.0 collective-permute-done.14
  91.9 0.0 collective-permute-done.15
  92.0 0.0 collective-permute-done.16
  92.0 0.0 copy-done
  92.1 3.3 %fusion.4 = f32[2,16,8,5,384]{4,2,3,0,1:T(8,128)S(1)} fusion(f32[16,2,8,5,768]{4,2,3,1,0:T(8,128)S(1)} %constant_dynamic-update-slice_fusion.2, f32[5,768]{1,0:T(8,128)S(1)} %add_convert_fusion, f32[384,768]{1,0:T(8,128)S(1)} %copy-done), kind=kOutput, calls=%fused_computation.9 | convolution fusion | flops 2265907200 | bytes 7093248 | tf_op jit(solution)/shard_map/tlkmj,ij->ltkmi/dot_general | solution.py:107
  95.4 0.4 fusion.2
  95.8 0.2 copy.15
  95.9 0.0 copy-start.1
  95.9 1.3 copy-done.1
  97.2 0.1 slice.30
  97.3 0.6 gather_fusion.1
  97.9 2.0 %fusion.8 = f32[256,2,384]{2,0,1:T(8,128)S(1)} fusion(f32[2,256,256]{2,1,0:T(8,128)} %param.13, f32[256,5,384]{2,0,1:T(8,128)} %bitcast.43, f32[2,256,384]{2,1,0:T(8,128)S(1)} %gather_fusion.1, f32[2,384]{1,0:T(2,128)S(1)} %broadcast_select_fusion, pred[2]{0:T(512)(128)(4,1)S(1)} %compare_and_fusion), kind=kOutput, calls=%fused_computation.12 | convolution fusion | flops 302579712 | bytes 2886658 | tf_op jit(solution)/shard_map/cqk,qci->kci/dot_general | solution.py:115
  100.0 0.1 pad_maximum_fusion
  100.1 0.0 copy-start.2
  100.1 1.4 %copy.17 = f32[16,16,5,384]{3,1,2,0:T(8,128)} copy(f32[16,16,5,384]{3,1,0,2:T(8,128)S(1)} %bitcast.44) | data formatting | bytes 3932160 | tf_op jit(solution)/shard_map/reshape | solution.py:118
  101.5 12.5 %all-to-all-start = ((f32[16,16,5,384]{3,1,2,0:T(8,128)}), f32[16,16,5,384]{3,1,2,0:T(8,128)S(1)}, u32[]{:S(2)}, u32[]{:S(2)}) async-start(f32[16,16,5,384]{3,1,2,0:T(8,128)} %copy.17), calls=%async_computation | async-start | bytes 3932160 | tf_op jit(solution)/shard_map/all_to_all | solution.py:119
  114.1 0.0 copy-done.2
  114.1 0.1 compare_reduce_fusion.3
  114.2 26.9 %all-to-all-done = f32[16,16,5,384]{3,1,2,0:T(8,128)S(1)} async-done(((f32[16,16,5,384]{3,1,2,0:T(8,128)}), f32[16,16,5,384]{3,1,2,0:T(8,128)S(1)}, u32[]{:S(2)}, u32[]{:S(2)}) %all-to-all-start) | async-done | bytes 1966112 | tf_op jit(solution)/shard_map/all_to_all | solution.py:119
  141.1 0.1 reduce_sum.9
  141.2 0.6 slice_multiply_fusion
  141.9 0.6 slice_multiply_fusion.1
  (27 shorter events, 0.4 us)
Async XLA Ops:
  0.6 91.4 %copy-start = (f32[384,768]{1,0:T(8,128)S(1)}, f32[384,768]{1,0:T(8,128)}, u32[]{:S(2)}) copy-start(f32[384,768]{1,0:T(8,128)} %param.7) | copy-start | bytes 3538948
  2.4 6.8 %collective-permute-start = (f32[8,3840]{1,0:T(8,128)S(1)}, f32[8,3840]{1,0:T(8,128)S(1)}, u32[]{:S(2)}, u32[]{:S(2)}) collective-permute-start(f32[8,3840]{1,0:T(8,128)S(1)} %bitcast.46), channel_id=1, source_target_pairs={{0,256},{16,272},{32,288},{48,304},{64,320},{80,336},{96,352},{112... | collective-permute-start | bytes 368648 | tf_op jit(solution)/shard_map/ppermute | solution.py:33
  9.2 20.5 %collective-permute-start.2 = (f32[2,8,3840]{2,1,0:T(8,128)S(1)}, f32[2,8,3840]{2,1,0:T(8,128)S(1)}, u32[]{:S(2)}, u32[]{:S(2)}) collective-permute-start(f32[2,8,3840]{2,1,0:T(8,128)S(1)} %maximum_select_fusion.1), channel_id=1, source_target_pairs={{0,224},{16,240},{32,0},{48,16},{64,32},{80,48},{96,64},{112,80},{... | collective-permute-start | bytes 737288 | tf_op jit(solution)/shard_map/ppermute | solution.py:46
  20.9 15.5 %collective-permute-start.8 = (f32[2,8,3840]{2,1,0:T(8,128)S(1)}, f32[2,8,3840]{2,1,0:T(8,128)S(1)}, u32[]{:S(2)}, u32[]{:S(2)}) collective-permute-start(f32[2,8,3840]{2,1,0:T(8,128)S(1)} %maximum_select_fusion.1), channel_id=1, source_target_pairs={{0,32},{16,48},{32,64},{48,80},{64,96},{80,112},{96,128},{112,144}... | collective-permute-start | bytes 737288 | tf_op jit(solution)/shard_map/ppermute | solution.py:45
  23.7 22.7 %collective-permute-start.1 = (f32[2,8,3840]{2,1,0:T(8,128)S(1)}, f32[2,8,3840]{2,1,0:T(8,128)S(1)}, u32[]{:S(2)}, u32[]{:S(2)}) collective-permute-start(f32[2,8,3840]{2,1,0:T(8,128)S(1)} %maximum_select_fusion.1), channel_id=1, source_target_pairs={{0,240},{16,0},{32,16},{48,32},{64,48},{80,64},{96,80},{112,96},{1... | collective-permute-start | bytes 737288 | tf_op jit(solution)/shard_map/ppermute | solution.py:43
  29.7 16.7 %collective-permute-start.4 = (f32[2,8,3840]{2,1,0:T(8,128)S(1)}, f32[2,8,3840]{2,1,0:T(8,128)S(1)}, u32[]{:S(2)}, u32[]{:S(2)}) collective-permute-start(f32[2,8,3840]{2,1,0:T(8,128)S(1)} %collective-permute-done.2), channel_id=1, source_target_pairs={{0,224},{16,240},{32,0},{48,16},{64,32},{80,48},{96,64},{112,80},{... | collective-permute-start | bytes 737288 | tf_op jit(solution)/shard_map/ppermute | solution.py:46
  36.4 18.2 %collective-permute-start.9 = (f32[2,8,3840]{2,1,0:T(8,128)S(1)}, f32[2,8,3840]{2,1,0:T(8,128)S(1)}, u32[]{:S(2)}, u32[]{:S(2)}) collective-permute-start(f32[2,8,3840]{2,1,0:T(8,128)S(1)} %collective-permute-done.8), channel_id=1, source_target_pairs={{0,32},{16,48},{32,64},{48,80},{64,96},{80,112},{96,128},{112,144}... | collective-permute-start | bytes 737288 | tf_op jit(solution)/shard_map/ppermute | solution.py:45
  38.4 53.6 %collective-permute-start.16 = (f32[2,8,3840]{2,1,0:T(8,128)S(1)}, f32[2,8,3840]{2,1,0:T(8,128)S(1)}, u32[]{:S(2)}, u32[]{:S(2)}) collective-permute-start(f32[2,8,3840]{2,1,0:T(8,128)S(1)} %maximum_select_fusion.1), channel_id=1, source_target_pairs={{0,16},{16,32},{32,48},{48,64},{64,80},{80,96},{96,112},{112,128},... | collective-permute-start | bytes 737288 | tf_op jit(solution)/shard_map/ppermute | solution.py:42
  42.1 14.6 %collective-permute-start.3 = (f32[2,8,3840]{2,1,0:T(8,128)S(1)}, f32[2,8,3840]{2,1,0:T(8,128)S(1)}, u32[]{:S(2)}, u32[]{:S(2)}) collective-permute-start(f32[2,8,3840]{2,1,0:T(8,128)S(1)} %collective-permute-done.2), channel_id=1, source_target_pairs={{0,240},{16,0},{32,16},{48,32},{64,48},{80,64},{96,80},{112,96},{1... | collective-permute-start | bytes 737288 | tf_op jit(solution)/shard_map/ppermute | solution.py:43
  46.4 27.0 %collective-permute-start.5 = (f32[2,8,3840]{2,1,0:T(8,128)S(1)}, f32[2,8,3840]{2,1,0:T(8,128)S(1)}, u32[]{:S(2)}, u32[]{:S(2)}) collective-permute-start(f32[2,8,3840]{2,1,0:T(8,128)S(1)} %collective-permute-done.4), channel_id=1, source_target_pairs={{0,240},{16,0},{32,16},{48,32},{64,48},{80,64},{96,80},{112,96},{1... | collective-permute-start | bytes 737288 | tf_op jit(solution)/shard_map/ppermute | solution.py:43
  49.8 15.4 %collective-permute-start.6 = (f32[2,8,3840]{2,1,0:T(8,128)S(1)}, f32[2,8,3840]{2,1,0:T(8,128)S(1)}, u32[]{:S(2)}, u32[]{:S(2)}) collective-permute-start(f32[2,8,3840]{2,1,0:T(8,128)S(1)} %collective-permute-done.4), channel_id=1, source_target_pairs={{0,224},{16,240},{32,0},{48,16},{64,32},{80,48},{96,64},{112,80},{... | collective-permute-start | bytes 737288 | tf_op jit(solution)/shard_map/ppermute | solution.py:46
  54.7 12.5 %collective-permute-start.10 = (f32[2,8,3840]{2,1,0:T(8,128)S(1)}, f32[2,8,3840]{2,1,0:T(8,128)S(1)}, u32[]{:S(2)}, u32[]{:S(2)}) collective-permute-start(f32[2,8,3840]{2,1,0:T(8,128)S(1)} %collective-permute-done.9), channel_id=1, source_target_pairs={{0,32},{16,48},{32,64},{48,80},{64,96},{80,112},{96,128},{112,144}... | collective-permute-start | bytes 737288 | tf_op jit(solution)/shard_map/ppermute | solution.py:45
  56.7 35.3 %collective-permute-start.15 = (f32[2,8,3840]{2,1,0:T(8,128)S(1)}, f32[2,8,3840]{2,1,0:T(8,128)S(1)}, u32[]{:S(2)}, u32[]{:S(2)}) collective-permute-start(f32[2,8,3840]{2,1,0:T(8,128)S(1)} %collective-permute-done.8), channel_id=1, source_target_pairs={{0,16},{16,32},{32,48},{48,64},{64,80},{80,96},{96,112},{112,128},... | collective-permute-start | bytes 737288 | tf_op jit(solution)/shard_map/ppermute | solution.py:42
  65.2 26.6 %collective-permute-start.14 = (f32[2,8,3840]{2,1,0:T(8,128)S(1)}, f32[2,8,3840]{2,1,0:T(8,128)S(1)}, u32[]{:S(2)}, u32[]{:S(2)}) collective-permute-start(f32[2,8,3840]{2,1,0:T(8,128)S(1)} %collective-permute-done.9), channel_id=1, source_target_pairs={{0,16},{16,32},{32,48},{48,64},{64,80},{80,96},{96,112},{112,128},... | collective-permute-start | bytes 737288 | tf_op jit(solution)/shard_map/ppermute | solution.py:42
  67.2 9.4 %collective-permute-start.12 = (f32[2,8,1920]{2,1,0:T(8,128)S(1)}, f32[2,8,1920]{2,1,0:T(8,128)S(1)}, u32[]{:S(2)}, u32[]{:S(2)}) collective-permute-start(f32[2,8,1920]{2,1,0:T(8,128)S(1)} %slice.29), channel_id=1, source_target_pairs={{0,224},{16,240},{32,0},{48,16},{64,32},{80,48},{96,64},{112,80},{... | collective-permute-start | bytes 368648 | tf_op jit(solution)/shard_map/ppermute | solution.py:51
  73.4 9.5 %collective-permute-start.11 = (f32[2,8,1920]{2,1,0:T(8,128)S(1)}, f32[2,8,1920]{2,1,0:T(8,128)S(1)}, u32[]{:S(2)}, u32[]{:S(2)}) collective-permute-start(f32[2,8,1920]{2,1,0:T(8,128)S(1)} %slice.28), channel_id=1, source_target_pairs={{0,32},{16,48},{32,64},{48,80},{64,96},{80,112},{96,128},{112,144}... | collective-permute-start | bytes 368648 | tf_op jit(solution)/shard_map/ppermute | solution.py:50
  76.6 11.7 %collective-permute-start.7 = (f32[2,8,3840]{2,1,0:T(8,128)S(1)}, f32[2,8,3840]{2,1,0:T(8,128)S(1)}, u32[]{:S(2)}, u32[]{:S(2)}) collective-permute-start(f32[2,8,3840]{2,1,0:T(8,128)S(1)} %collective-permute-done.6), channel_id=1, source_target_pairs={{0,240},{16,0},{32,16},{48,32},{64,48},{80,64},{96,80},{112,96},{1... | collective-permute-start | bytes 737288 | tf_op jit(solution)/shard_map/ppermute | solution.py:43
  82.9 8.9 %collective-permute-start.13 = (f32[2,8,3840]{2,1,0:T(8,128)S(1)}, f32[2,8,3840]{2,1,0:T(8,128)S(1)}, u32[]{:S(2)}, u32[]{:S(2)}) collective-permute-start(f32[2,8,3840]{2,1,0:T(8,128)S(1)} %collective-permute-done.10), channel_id=1, source_target_pairs={{0,16},{16,32},{32,48},{48,64},{64,80},{80,96},{96,112},{112,128},... | collective-permute-start | bytes 737288 | tf_op jit(solution)/shard_map/ppermute | solution.py:42
  95.9 1.3 copy-start.1
  100.1 14.0 %copy-start.2 = (s32[2,36]{1,0:T(2,128)S(1)}, s32[2,36]{1,0:T(2,128)}, u32[]{:S(2)}) copy-start(s32[2,36]{1,0:T(2,128)} %param.11) | copy-start | bytes 868
  101.5 39.6 %all-to-all-start = ((f32[16,16,5,384]{3,1,2,0:T(8,128)}), f32[16,16,5,384]{3,1,2,0:T(8,128)S(1)}, u32[]{:S(2)}, u32[]{:S(2)}) async-start(f32[16,16,5,384]{3,1,2,0:T(8,128)} %copy.17), calls=%async_computation | async-start | bytes 3932160 | tf_op jit(solution)/shard_map/all_to_all | solution.py:119

commit v11 on v10

--- a/solution.py
+++ b/solution.py
@@ -79,6 +79,23 @@
     return keep + lax.ppermute(send, "col", [(p, (p + half) % n_col) for p in range(n_col)])
 
 
+def reduce_cols_a2a(value, n_col):
+    chips = n_col // CORES
+    rows = value.shape[0] // n_col
+    core = lax.axis_index("col") % CORES
+    value = value.reshape(chips, CORES, rows, *value.shape[1:])
+    partner_pairs = [(p, p ^ 1) for p in range(n_col)]
+    send = jnp.take(value, 1 - core, axis=1)
+    summed = jnp.take(value, core, axis=1) + lax.ppermute(send, "col", partner_pairs)
+    half = rows // CORES
+    summed = summed.reshape(n_col, half, *value.shape[3:])
+    received = lax.all_to_all(summed, "col", 0, 0, tiled=True)
+    totals = jnp.sum(received.reshape(chips, CORES, half, *value.shape[3:]), axis=0)
+    own = jnp.take(totals, core, axis=0)
+    other = lax.ppermute(jnp.take(totals, 1 - core, axis=0), "col", partner_pairs)
+    return jnp.where(core == 0, jnp.concatenate([own, other]), jnp.concatenate([other, own]))
+
+
 def local(anc_inv, factors_first, factors_second, lists_first, lists_second, parents, parent_link):
     n_row = lax.axis_size("row")
     n_col = lax.axis_size("col")
@@ -115,8 +132,7 @@
     coupling = jnp.einsum("cqk,qci->kci", parent_link, chosen, precision=high)
     second_partial = partial_value[:, n_first:] - chosen_mask[None, :, :] * coupling
     combined = jnp.concatenate([first_partial, second_partial], axis=1)
-    combined = combined.reshape(n_col, panel_width // n_col, members, local_rows)
-    reduced = jnp.sum(lax.all_to_all(combined, "col", 0, 0, tiled=True), axis=0)
+    reduced = reduce_cols_a2a(combined, n_col)
     reduced = jnp.transpose(reduced, (1, 0, 2))
     first_cols = -out_first[:, None, :] * reduced[:n_first]
     second_cols = -out_second[:, None, :] * reduced[n_first:]

time: 144 us -> 143 us (level)
  waiting for transfers between devices: 39.6 us -> 32 us
  starting transfers between devices: 84.3 us -> 89.4 us
    all_to_all x1, waiting for transfers between devices: 26.9 us -> 16.4 us  [reduce_cols_a2a(): received = lax.all_to_all(summed, 'col', 0, 0, tiled=True)]
    ppermute x0 -> x2, starting transfers between devices: none -> 10.3 us  [the longest x1 7.48 us: reduce_cols_a2a(): lax.ppermute(send, 'col', partner_pairs)]
    all_to_all x1, starting transfers between devices: 12.5 us -> 7.29 us  [reduce_cols_a2a(): received = lax.all_to_all(summed, 'col', 0, 0, tiled=True)]
    ppermute x0 -> x2, waiting for transfers between devices: none -> 3.01 us  [the longest x1 2.16 us: reduce_cols_a2a(): lax.ppermute(send, 'col', partner_pairs)]
    unnamed x21 -> x23, local copies, waits for them, and re-layouts: 2.57 us -> 3.85 us
  transfers between devices with their start and end apart: 18 -> 20, of which waited for: 6 -> 8; matrix products, arithmetic and copies ran while one was open for 3% -> 3% of each run, Pallas kernels for 0% -> 0%
where the time goes in v11:
time: 143 us; the launch traced here: 142 us
  starting transfers between devices  89.4 us (63%)
  waiting for transfers between devices  32 us (22%)
  other arithmetic  7.28 us (5%)
  local copies, waits for them, and re-layouts  7.09 us (5%)
  matrix products  5.33 us (4%)
    ppermute x3, starting transfers between devices, gather_rows(): lane_down = lax.ppermute(lane_down, 'row', shift_pairs(n_row, nz, 1, -2))  23.3 us
    ppermute x4, starting transfers between devices, gather_rows(): lax.ppermute(lane_down, 'row', shift_pairs(n_row, nz, 1, -1))  16.5 us
    all_to_all x1, waiting for transfers between devices, reduce_cols_a2a(): received = lax.all_to_all(summed, 'col', 0, 0, tiled=True)  16.4 us
    ppermute x4, starting transfers between devices, gather_rows(): lax.ppermute(lane_up, 'row', shift_pairs(n_row, nz, 1, 1))  14.3 us
    ppermute x1, starting transfers between devices, reduce_cols_a2a(): lax.ppermute(send, 'col', partner_pairs)  7.48 us
    all_to_all x1, starting transfers between devices, reduce_cols_a2a(): received = lax.all_to_all(summed, 'col', 0, 0, tiled=True)  7.29 us
    ppermute x1, starting transfers between devices, gather_rows(): lax.ppermute(lane_down[..., half:], 'row', shift_pairs(n_row, nz, 1, -2))  6.13 us
    ppermute x3, starting transfers between devices, gather_rows(): lane_up = lax.ppermute(lane_up, 'row', shift_pairs(n_row, nz, 1, 2))  5.76 us
  transfers between devices with their start and end apart: 20, of which 8 were waited for; matrix products, arithmetic and copies ran while one was open for 3% of the time, Pallas kernels for 0%

profile of v11, /device:TPU:1, one launch (start us, length us, event | category | flops | bytes accessed | tf_op | source)
XLA Modules:
  0.0 142.4 jit_solution(16565661578931708903)
XLA Ops:
  0.6 0.0 copy-start
  0.6 1.0 constant_dynamic-update-slice_fusion.1
  1.6 0.8 constant_dynamic-update-slice_fusion
  2.4 3.9 %collective-permute-start = (f32[8,3840]{1,0:T(8,128)S(1)}, f32[8,3840]{1,0:T(8,128)S(1)}, u32[]{:S(2)}, u32[]{:S(2)}) collective-permute-start(f32[8,3840]{1,0:T(8,128)S(1)} %bitcast.79), channel_id=1, source_target_pairs={{0,256},{16,272},{32,288},{48,304},{64,320},{80,336},{96,352},{112... | collective-permute-start | bytes 368648 | tf_op jit(solution)/shard_map/ppermute | solution.py:33
  6.4 0.7 compare_select_fusion
  7.0 0.7 compare_and_fusion
  7.7 0.8 compare_reduce_fusion.2
  8.5 0.6 gather_fusion
  9.1 0.1 broadcast_select_fusion
  9.2 0.0 collective-permute-done
  9.2 11.7 %collective-permute-start.2 = (f32[2,8,3840]{2,1,0:T(8,128)S(1)}, f32[2,8,3840]{2,1,0:T(8,128)S(1)}, u32[]{:S(2)}, u32[]{:S(2)}) collective-permute-start(f32[2,8,3840]{2,1,0:T(8,128)S(1)} %maximum_select_fusion.1), channel_id=1, source_target_pairs={{0,224},{16,240},{32,0},{48,16},{64,32},{80,48},{96,64},{112,80},{... | collective-permute-start | bytes 737288 | tf_op jit(solution)/shard_map/ppermute | solution.py:46
  20.9 1.9 %collective-permute-start.8 = (f32[2,8,3840]{2,1,0:T(8,128)S(1)}, f32[2,8,3840]{2,1,0:T(8,128)S(1)}, u32[]{:S(2)}, u32[]{:S(2)}) collective-permute-start(f32[2,8,3840]{2,1,0:T(8,128)S(1)} %maximum_select_fusion.1), channel_id=1, source_target_pairs={{0,32},{16,48},{32,64},{48,80},{64,96},{80,112},{96,128},{112,144}... | collective-permute-start | bytes 737288 | tf_op jit(solution)/shard_map/ppermute | solution.py:45
  22.9 0.8 compare_reduce_fusion
  23.7 5.0 %collective-permute-start.1 = (f32[2,8,3840]{2,1,0:T(8,128)S(1)}, f32[2,8,3840]{2,1,0:T(8,128)S(1)}, u32[]{:S(2)}, u32[]{:S(2)}) collective-permute-start(f32[2,8,3840]{2,1,0:T(8,128)S(1)} %maximum_select_fusion.1), channel_id=1, source_target_pairs={{0,240},{16,0},{32,16},{48,32},{64,48},{80,64},{96,80},{112,96},{1... | collective-permute-start | bytes 737288 | tf_op jit(solution)/shard_map/ppermute | solution.py:43
  28.7 0.8 compare_reduce_fusion.1
  29.5 0.2 collective-permute-done.2
  29.7 6.7 %collective-permute-start.4 = (f32[2,8,3840]{2,1,0:T(8,128)S(1)}, f32[2,8,3840]{2,1,0:T(8,128)S(1)}, u32[]{:S(2)}, u32[]{:S(2)}) collective-permute-start(f32[2,8,3840]{2,1,0:T(8,128)S(1)} %collective-permute-done.2), channel_id=1, source_target_pairs={{0,224},{16,240},{32,0},{48,16},{64,32},{80,48},{96,64},{112,80},{... | collective-permute-start | bytes 737288 | tf_op jit(solution)/shard_map/ppermute | solution.py:46
  36.4 0.0 collective-permute-done.8
  36.4 1.9 %collective-permute-start.9 = (f32[2,8,3840]{2,1,0:T(8,128)S(1)}, f32[2,8,3840]{2,1,0:T(8,128)S(1)}, u32[]{:S(2)}, u32[]{:S(2)}) collective-permute-start(f32[2,8,3840]{2,1,0:T(8,128)S(1)} %collective-permute-done.8), channel_id=1, source_target_pairs={{0,32},{16,48},{32,64},{48,80},{64,96},{80,112},{96,128},{112,144}... | collective-permute-start | bytes 737288 | tf_op jit(solution)/shard_map/ppermute | solution.py:45
  38.5 3.6 %collective-permute-start.16 = (f32[2,8,3840]{2,1,0:T(8,128)S(1)}, f32[2,8,3840]{2,1,0:T(8,128)S(1)}, u32[]{:S(2)}, u32[]{:S(2)}) collective-permute-start(f32[2,8,3840]{2,1,0:T(8,128)S(1)} %maximum_select_fusion.1), channel_id=1, source_target_pairs={{0,16},{16,32},{32,48},{48,64},{64,80},{80,96},{96,112},{112,128},... | collective-permute-start | bytes 737288 | tf_op jit(solution)/shard_map/ppermute | solution.py:42
  42.1 4.3 %collective-permute-start.3 = (f32[2,8,3840]{2,1,0:T(8,128)S(1)}, f32[2,8,3840]{2,1,0:T(8,128)S(1)}, u32[]{:S(2)}, u32[]{:S(2)}) collective-permute-start(f32[2,8,3840]{2,1,0:T(8,128)S(1)} %collective-permute-done.2), channel_id=1, source_target_pairs={{0,240},{16,0},{32,16},{48,32},{64,48},{80,64},{96,80},{112,96},{1... | collective-permute-start | bytes 737288 | tf_op jit(solution)/shard_map/ppermute | solution.py:43
  46.4 0.0 collective-permute-done.1
  46.5 0.0 collective-permute-done.4
  46.5 3.4 %collective-permute-start.5 = (f32[2,8,3840]{2,1,0:T(8,128)S(1)}, f32[2,8,3840]{2,1,0:T(8,128)S(1)}, u32[]{:S(2)}, u32[]{:S(2)}) collective-permute-start(f32[2,8,3840]{2,1,0:T(8,128)S(1)} %collective-permute-done.4), channel_id=1, source_target_pairs={{0,240},{16,0},{32,16},{48,32},{64,48},{80,64},{96,80},{112,96},{1... | collective-permute-start | bytes 737288 | tf_op jit(solution)/shard_map/ppermute | solution.py:43
  49.8 4.9 %collective-permute-start.6 = (f32[2,8,3840]{2,1,0:T(8,128)S(1)}, f32[2,8,3840]{2,1,0:T(8,128)S(1)}, u32[]{:S(2)}, u32[]{:S(2)}) collective-permute-start(f32[2,8,3840]{2,1,0:T(8,128)S(1)} %collective-permute-done.4), channel_id=1, source_target_pairs={{0,224},{16,240},{32,0},{48,16},{64,32},{80,48},{96,64},{112,80},{... | collective-permute-start | bytes 737288 | tf_op jit(solution)/shard_map/ppermute | solution.py:46
  54.7 0.0 collective-permute-done.9
  54.7 1.9 %collective-permute-start.10 = (f32[2,8,3840]{2,1,0:T(8,128)S(1)}, f32[2,8,3840]{2,1,0:T(8,128)S(1)}, u32[]{:S(2)}, u32[]{:S(2)}) collective-permute-start(f32[2,8,3840]{2,1,0:T(8,128)S(1)} %collective-permute-done.9), channel_id=1, source_target_pairs={{0,32},{16,48},{32,64},{48,80},{64,96},{80,112},{96,128},{112,144}... | collective-permute-start | bytes 737288 | tf_op jit(solution)/shard_map/ppermute | solution.py:45
  56.7 0.0 collective-permute-done.3
  56.7 3.4 %collective-permute-start.15 = (f32[2,8,3840]{2,1,0:T(8,128)S(1)}, f32[2,8,3840]{2,1,0:T(8,128)S(1)}, u32[]{:S(2)}, u32[]{:S(2)}) collective-permute-start(f32[2,8,3840]{2,1,0:T(8,128)S(1)} %collective-permute-done.8), channel_id=1, source_target_pairs={{0,16},{16,32},{32,48},{48,64},{64,80},{80,96},{96,112},{112,128},... | collective-permute-start | bytes 737288 | tf_op jit(solution)/shard_map/ppermute | solution.py:42
  60.1 5.2 %collective-permute-done.6 = f32[2,8,3840]{2,1,0:T(8,128)S(1)} collective-permute-done((f32[2,8,3840]{2,1,0:T(8,128)S(1)}, f32[2,8,3840]{2,1,0:T(8,128)S(1)}, u32[]{:S(2)}, u32[]{:S(2)}) %collective-permute-start.6) | collective-permute-done | bytes 245792 | tf_op jit(solution)/shard_map/ppermute | solution.py:46
  65.3 1.9 %collective-permute-start.14 = (f32[2,8,3840]{2,1,0:T(8,128)S(1)}, f32[2,8,3840]{2,1,0:T(8,128)S(1)}, u32[]{:S(2)}, u32[]{:S(2)}) collective-permute-start(f32[2,8,3840]{2,1,0:T(8,128)S(1)} %collective-permute-done.9), channel_id=1, source_target_pairs={{0,16},{16,32},{32,48},{48,64},{64,80},{80,96},{96,112},{112,128},... | collective-permute-start | bytes 737288 | tf_op jit(solution)/shard_map/ppermute | solution.py:42
  67.2 0.0 collective-permute-done.10
  67.2 6.1 %collective-permute-start.12 = (f32[2,8,1920]{2,1,0:T(8,128)S(1)}, f32[2,8,1920]{2,1,0:T(8,128)S(1)}, u32[]{:S(2)}, u32[]{:S(2)}) collective-permute-start(f32[2,8,1920]{2,1,0:T(8,128)S(1)} %slice.53), channel_id=1, source_target_pairs={{0,224},{16,240},{32,0},{48,16},{64,32},{80,48},{96,64},{112,80},{... | collective-permute-start | bytes 368648 | tf_op jit(solution)/shard_map/ppermute | solution.py:51
  73.4 0.0 collective-permute-done.5
  73.4 1.9 %collective-permute-start.11 = (f32[2,8,1920]{2,1,0:T(8,128)S(1)}, f32[2,8,1920]{2,1,0:T(8,128)S(1)}, u32[]{:S(2)}, u32[]{:S(2)}) collective-permute-start(f32[2,8,1920]{2,1,0:T(8,128)S(1)} %slice.52), channel_id=1, source_target_pairs={{0,32},{16,48},{32,64},{48,80},{64,96},{80,112},{96,128},{112,144}... | collective-permute-start | bytes 368648 | tf_op jit(solution)/shard_map/ppermute | solution.py:50
  75.4 1.2 collective-permute-done.12
  76.6 3.8 %collective-permute-start.7 = (f32[2,8,3840]{2,1,0:T(8,128)S(1)}, f32[2,8,3840]{2,1,0:T(8,128)S(1)}, u32[]{:S(2)}, u32[]{:S(2)}) collective-permute-start(f32[2,8,3840]{2,1,0:T(8,128)S(1)} %collective-permute-done.6), channel_id=1, source_target_pairs={{0,240},{16,0},{32,16},{48,32},{64,48},{80,64},{96,80},{112,96},{1... | collective-permute-start | bytes 737288 | tf_op jit(solution)/shard_map/ppermute | solution.py:43
  80.4 2.5 %collective-permute-done.11 = f32[2,8,1920]{2,1,0:T(8,128)S(1)} collective-permute-done((f32[2,8,1920]{2,1,0:T(8,128)S(1)}, f32[2,8,1920]{2,1,0:T(8,128)S(1)}, u32[]{:S(2)}, u32[]{:S(2)}) %collective-permute-start.11) | collective-permute-done | bytes 122912 | tf_op jit(solution)/shard_map/ppermute | solution.py:50
  82.9 5.4 %collective-permute-start.13 = (f32[2,8,3840]{2,1,0:T(8,128)S(1)}, f32[2,8,3840]{2,1,0:T(8,128)S(1)}, u32[]{:S(2)}, u32[]{:S(2)}) collective-permute-start(f32[2,8,3840]{2,1,0:T(8,128)S(1)} %collective-permute-done.10), channel_id=1, source_target_pairs={{0,16},{16,32},{32,48},{48,64},{64,80},{80,96},{96,112},{112,128},... | collective-permute-start | bytes 737288 | tf_op jit(solution)/shard_map/ppermute | solution.py:42
  88.4 0.0 collective-permute-done.7
  88.4 3.4 %collective-permute-done.13 = f32[2,8,3840]{2,1,0:T(8,128)S(1)} collective-permute-done((f32[2,8,3840]{2,1,0:T(8,128)S(1)}, f32[2,8,3840]{2,1,0:T(8,128)S(1)}, u32[]{:S(2)}, u32[]{:S(2)}) %collective-permute-start.13) | collective-permute-done | bytes 245792 | tf_op jit(solution)/shard_map/ppermute | solution.py:42
  92.1 3.3 %fusion.4 = f32[2,16,8,5,384]{4,2,3,0,1:T(8,128)S(1)} fusion(f32[16,2,8,5,768]{4,2,3,1,0:T(8,128)S(1)} %constant_dynamic-update-slice_fusion.2, f32[5,768]{1,0:T(8,128)S(1)} %add_convert_fusion, f32[384,768]{1,0:T(8,128)S(1)} %copy-done), kind=kOutput, calls=%fused_computation.9 | convolution fusion | flops 2265907200 | bytes 7093248 | tf_op jit(solution)/shard_map/tlkmj,ij->ltkmi/dot_general | solution.py:124
  95.4 0.4 fusion.2
  95.8 0.2 copy.26
  96.0 1.3 copy-done.1
  97.3 0.1 slice.54
  97.4 0.6 gather_fusion.1
  98.0 2.0 %fusion.8 = f32[256,2,384]{2,0,1:T(8,128)S(1)} fusion(f32[2,256,256]{2,1,0:T(8,128)} %param.17, f32[256,5,384]{2,0,1:T(8,128)} %bitcast.73, f32[2,256,384]{2,1,0:T(8,128)S(1)} %gather_fusion.1, f32[2,384]{1,0:T(2,128)S(1)} %broadcast_select_fusion, pred[2]{0:T(512)(128)(4,1)S(1)} %compare_and_fusion), kind=kOutput, calls=%fused_computation.12 | convolution fusion | flops 302579712 | bytes 2886658 | tf_op jit(solution)/shard_map/cqk,qci->kci/dot_general | solution.py:132
  100.0 0.1 pad_maximum_fusion
  100.1 1.3 copy-done.2
  101.4 0.1 fusion.10
  101.5 0.0 copy-start.3
  101.5 7.5 %collective-permute-start.17 = (f32[8,16,5,384]{3,1,0,2:T(8,128)S(1)}, f32[8,16,5,384]{3,1,0,2:T(8,128)S(1)}, u32[]{:S(2)}, u32[]{:S(2)}) collective-permute-start(f32[8,16,5,384]{3,1,0,2:T(8,128)S(1)} %fusion.10), channel_id=1, source_target_pairs={{0,1},{1,0},{2,3},{3,2},{4,5},{5,4},{6,7},{7,6},{8,9},{9,8},{10,11... | collective-permute-start | bytes 2949128 | tf_op jit(solution)/shard_map/ppermute | solution.py:89
  109.0 2.2 %collective-permute-done.17 = f32[8,16,5,384]{3,1,0,2:T(8,128)S(1)} collective-permute-done((f32[8,16,5,384]{3,1,0,2:T(8,128)S(1)}, f32[8,16,5,384]{3,1,0,2:T(8,128)S(1)}, u32[]{:S(2)}, u32[]{:S(2)}) %collective-permute-start.17) | collective-permute-done | bytes 983072 | tf_op jit(solution)/shard_map/ppermute | solution.py:89
  111.2 1.3 fusion.12
  112.5 1.0 copy.30
  113.5 7.3 %all-to-all-start = ((f32[16,8,5,384]{3,1,2,0:T(8,128)}), f32[16,8,5,384]{3,1,2,0:T(8,128)S(1)}, u32[]{:S(2)}, u32[]{:S(2)}) async-start(f32[16,8,5,384]{3,1,2,0:T(8,128)} %copy.30), calls=%async_computation | async-start | bytes 1966080 | tf_op jit(solution)/shard_map/all_to_all | solution.py:92
  120.8 0.1 compare_reduce_fusion.3
  120.9 16.4 %all-to-all-done = f32[16,8,5,384]{3,1,2,0:T(8,128)S(1)} async-done(((f32[16,8,5,384]{3,1,2,0:T(8,128)}), f32[16,8,5,384]{3,1,2,0:T(8,128)S(1)}, u32[]{:S(2)}, u32[]{:S(2)}) %all-to-all-start) | async-done | bytes 983072 | tf_op jit(solution)/shard_map/all_to_all | solution.py:92
  137.3 0.1 reduce_sum.9
  137.4 2.8 %collective-permute-start.18 = (f32[8,5,384]{2,0,1:T(8,128)S(1)}, f32[8,5,384]{2,0,1:T(8,128)S(1)}, u32[]{:S(2)}, u32[]{:S(2)}) collective-permute-start(f32[8,5,384]{2,0,1:T(8,128)S(1)} %fusion.19), channel_id=1, source_target_pairs={{0,1},{1,0},{2,3},{3,2},{4,5},{5,4},{6,7},{7,6},{8,9},{9,8},{10,11... | collective-permute-start | bytes 184328 | tf_op jit(solution)/shard_map/ppermute | solution.py:95
  140.2 0.9 collective-permute-done.18
  141.1 0.6 slice_multiply_fusion
  141.7 0.6 slice_multiply_fusion.1
  (37 shorter events, 0.5 us)
Async XLA Ops:
  0.6 91.5 %copy-start = (f32[384,768]{1,0:T(8,128)S(1)}, f32[384,768]{1,0:T(8,128)}, u32[]{:S(2)}) copy-start(f32[384,768]{1,0:T(8,128)} %param.11) | copy-start | bytes 3538948
  2.4 6.8 %collective-permute-start = (f32[8,3840]{1,0:T(8,128)S(1)}, f32[8,3840]{1,0:T(8,128)S(1)}, u32[]{:S(2)}, u32[]{:S(2)}) collective-permute-start(f32[8,3840]{1,0:T(8,128)S(1)} %bitcast.79), channel_id=1, source_target_pairs={{0,256},{16,272},{32,288},{48,304},{64,320},{80,336},{96,352},{112... | collective-permute-start | bytes 368648 | tf_op jit(solution)/shard_map/ppermute | solution.py:33
  9.2 20.5 %collective-permute-start.2 = (f32[2,8,3840]{2,1,0:T(8,128)S(1)}, f32[2,8,3840]{2,1,0:T(8,128)S(1)}, u32[]{:S(2)}, u32[]{:S(2)}) collective-permute-start(f32[2,8,3840]{2,1,0:T(8,128)S(1)} %maximum_select_fusion.1), channel_id=1, source_target_pairs={{0,224},{16,240},{32,0},{48,16},{64,32},{80,48},{96,64},{112,80},{... | collective-permute-start | bytes 737288 | tf_op jit(solution)/shard_map/ppermute | solution.py:46
  20.9 15.5 %collective-permute-start.8 = (f32[2,8,3840]{2,1,0:T(8,128)S(1)}, f32[2,8,3840]{2,1,0:T(8,128)S(1)}, u32[]{:S(2)}, u32[]{:S(2)}) collective-permute-start(f32[2,8,3840]{2,1,0:T(8,128)S(1)} %maximum_select_fusion.1), channel_id=1, source_target_pairs={{0,32},{16,48},{32,64},{48,80},{64,96},{80,112},{96,128},{112,144}... | collective-permute-start | bytes 737288 | tf_op jit(solution)/shard_map/ppermute | solution.py:45
  23.7 22.7 %collective-permute-start.1 = (f32[2,8,3840]{2,1,0:T(8,128)S(1)}, f32[2,8,3840]{2,1,0:T(8,128)S(1)}, u32[]{:S(2)}, u32[]{:S(2)}) collective-permute-start(f32[2,8,3840]{2,1,0:T(8,128)S(1)} %maximum_select_fusion.1), channel_id=1, source_target_pairs={{0,240},{16,0},{32,16},{48,32},{64,48},{80,64},{96,80},{112,96},{1... | collective-permute-start | bytes 737288 | tf_op jit(solution)/shard_map/ppermute | solution.py:43
  29.7 16.7 %collective-permute-start.4 = (f32[2,8,3840]{2,1,0:T(8,128)S(1)}, f32[2,8,3840]{2,1,0:T(8,128)S(1)}, u32[]{:S(2)}, u32[]{:S(2)}) collective-permute-start(f32[2,8,3840]{2,1,0:T(8,128)S(1)} %collective-permute-done.2), channel_id=1, source_target_pairs={{0,224},{16,240},{32,0},{48,16},{64,32},{80,48},{96,64},{112,80},{... | collective-permute-start | bytes 737288 | tf_op jit(solution)/shard_map/ppermute | solution.py:46
  36.4 18.2 %collective-permute-start.9 = (f32[2,8,3840]{2,1,0:T(8,128)S(1)}, f32[2,8,3840]{2,1,0:T(8,128)S(1)}, u32[]{:S(2)}, u32[]{:S(2)}) collective-permute-start(f32[2,8,3840]{2,1,0:T(8,128)S(1)} %collective-permute-done.8), channel_id=1, source_target_pairs={{0,32},{16,48},{32,64},{48,80},{64,96},{80,112},{96,128},{112,144}... | collective-permute-start | bytes 737288 | tf_op jit(solution)/shard_map/ppermute | solution.py:45
  38.5 53.6 %collective-permute-start.16 = (f32[2,8,3840]{2,1,0:T(8,128)S(1)}, f32[2,8,3840]{2,1,0:T(8,128)S(1)}, u32[]{:S(2)}, u32[]{:S(2)}) collective-permute-start(f32[2,8,3840]{2,1,0:T(8,128)S(1)} %maximum_select_fusion.1), channel_id=1, source_target_pairs={{0,16},{16,32},{32,48},{48,64},{64,80},{80,96},{96,112},{112,128},... | collective-permute-start | bytes 737288 | tf_op jit(solution)/shard_map/ppermute | solution.py:42
  42.1 14.6 %collective-permute-start.3 = (f32[2,8,3840]{2,1,0:T(8,128)S(1)}, f32[2,8,3840]{2,1,0:T(8,128)S(1)}, u32[]{:S(2)}, u32[]{:S(2)}) collective-permute-start(f32[2,8,3840]{2,1,0:T(8,128)S(1)} %collective-permute-done.2), channel_id=1, source_target_pairs={{0,240},{16,0},{32,16},{48,32},{64,48},{80,64},{96,80},{112,96},{1... | collective-permute-start | bytes 737288 | tf_op jit(solution)/shard_map/ppermute | solution.py:43
  46.5 26.9 %collective-permute-start.5 = (f32[2,8,3840]{2,1,0:T(8,128)S(1)}, f32[2,8,3840]{2,1,0:T(8,128)S(1)}, u32[]{:S(2)}, u32[]{:S(2)}) collective-permute-start(f32[2,8,3840]{2,1,0:T(8,128)S(1)} %collective-permute-done.4), channel_id=1, source_target_pairs={{0,240},{16,0},{32,16},{48,32},{64,48},{80,64},{96,80},{112,96},{1... | collective-permute-start | bytes 737288 | tf_op jit(solution)/shard_map/ppermute | solution.py:43
  49.8 15.5 %collective-permute-start.6 = (f32[2,8,3840]{2,1,0:T(8,128)S(1)}, f32[2,8,3840]{2,1,0:T(8,128)S(1)}, u32[]{:S(2)}, u32[]{:S(2)}) collective-permute-start(f32[2,8,3840]{2,1,0:T(8,128)S(1)} %collective-permute-done.4), channel_id=1, source_target_pairs={{0,224},{16,240},{32,0},{48,16},{64,32},{80,48},{96,64},{112,80},{... | collective-permute-start | bytes 737288 | tf_op jit(solution)/shard_map/ppermute | solution.py:46
  54.7 12.5 %collective-permute-start.10 = (f32[2,8,3840]{2,1,0:T(8,128)S(1)}, f32[2,8,3840]{2,1,0:T(8,128)S(1)}, u32[]{:S(2)}, u32[]{:S(2)}) collective-permute-start(f32[2,8,3840]{2,1,0:T(8,128)S(1)} %collective-permute-done.9), channel_id=1, source_target_pairs={{0,32},{16,48},{32,64},{48,80},{64,96},{80,112},{96,128},{112,144}... | collective-permute-start | bytes 737288 | tf_op jit(solution)/shard_map/ppermute | solution.py:45
  56.7 35.3 %collective-permute-start.15 = (f32[2,8,3840]{2,1,0:T(8,128)S(1)}, f32[2,8,3840]{2,1,0:T(8,128)S(1)}, u32[]{:S(2)}, u32[]{:S(2)}) collective-permute-start(f32[2,8,3840]{2,1,0:T(8,128)S(1)} %collective-permute-done.8), channel_id=1, source_target_pairs={{0,16},{16,32},{32,48},{48,64},{64,80},{80,96},{96,112},{112,128},... | collective-permute-start | bytes 737288 | tf_op jit(solution)/shard_map/ppermute | solution.py:42
  65.3 26.6 %collective-permute-start.14 = (f32[2,8,3840]{2,1,0:T(8,128)S(1)}, f32[2,8,3840]{2,1,0:T(8,128)S(1)}, u32[]{:S(2)}, u32[]{:S(2)}) collective-permute-start(f32[2,8,3840]{2,1,0:T(8,128)S(1)} %collective-permute-done.9), channel_id=1, source_target_pairs={{0,16},{16,32},{32,48},{48,64},{64,80},{80,96},{96,112},{112,128},... | collective-permute-start | bytes 737288 | tf_op jit(solution)/shard_map/ppermute | solution.py:42
  67.2 9.4 %collective-permute-start.12 = (f32[2,8,1920]{2,1,0:T(8,128)S(1)}, f32[2,8,1920]{2,1,0:T(8,128)S(1)}, u32[]{:S(2)}, u32[]{:S(2)}) collective-permute-start(f32[2,8,1920]{2,1,0:T(8,128)S(1)} %slice.53), channel_id=1, source_target_pairs={{0,224},{16,240},{32,0},{48,16},{64,32},{80,48},{96,64},{112,80},{... | collective-permute-start | bytes 368648 | tf_op jit(solution)/shard_map/ppermute | solution.py:51
  73.4 9.5 %collective-permute-start.11 = (f32[2,8,1920]{2,1,0:T(8,128)S(1)}, f32[2,8,1920]{2,1,0:T(8,128)S(1)}, u32[]{:S(2)}, u32[]{:S(2)}) collective-permute-start(f32[2,8,1920]{2,1,0:T(8,128)S(1)} %slice.52), channel_id=1, source_target_pairs={{0,32},{16,48},{32,64},{48,80},{64,96},{80,112},{96,128},{112,144}... | collective-permute-start | bytes 368648 | tf_op jit(solution)/shard_map/ppermute | solution.py:50
  76.6 11.7 %collective-permute-start.7 = (f32[2,8,3840]{2,1,0:T(8,128)S(1)}, f32[2,8,3840]{2,1,0:T(8,128)S(1)}, u32[]{:S(2)}, u32[]{:S(2)}) collective-permute-start(f32[2,8,3840]{2,1,0:T(8,128)S(1)} %collective-permute-done.6), channel_id=1, source_target_pairs={{0,240},{16,0},{32,16},{48,32},{64,48},{80,64},{96,80},{112,96},{1... | collective-permute-start | bytes 737288 | tf_op jit(solution)/shard_map/ppermute | solution.py:43
  82.9 9.0 %collective-permute-start.13 = (f32[2,8,3840]{2,1,0:T(8,128)S(1)}, f32[2,8,3840]{2,1,0:T(8,128)S(1)}, u32[]{:S(2)}, u32[]{:S(2)}) collective-permute-start(f32[2,8,3840]{2,1,0:T(8,128)S(1)} %collective-permute-done.10), channel_id=1, source_target_pairs={{0,16},{16,32},{32,48},{48,64},{64,80},{80,96},{96,112},{112,128},... | collective-permute-start | bytes 737288 | tf_op jit(solution)/shard_map/ppermute | solution.py:42
  96.0 1.3 copy-start.1
  100.1 1.3 copy-start.2
  101.5 19.3 %copy-start.3 = (s32[2,36]{1,0:T(2,128)S(1)}, s32[2,36]{1,0:T(2,128)}, u32[]{:S(2)}) copy-start(s32[2,36]{1,0:T(2,128)} %param.15) | copy-start | bytes 868
  101.5 9.7 %collective-permute-start.17 = (f32[8,16,5,384]{3,1,0,2:T(8,128)S(1)}, f32[8,16,5,384]{3,1,0,2:T(8,128)S(1)}, u32[]{:S(2)}, u32[]{:S(2)}) collective-permute-start(f32[8,16,5,384]{3,1,0,2:T(8,128)S(1)} %fusion.10), channel_id=1, source_target_pairs={{0,1},{1,0},{2,3},{3,2},{4,5},{5,4},{6,7},{7,6},{8,9},{9,8},{10,11... | collective-permute-start | bytes 2949128 | tf_op jit(solution)/shard_map/ppermute | solution.py:89
  113.5 23.8 %all-to-all-start = ((f32[16,8,5,384]{3,1,2,0:T(8,128)}), f32[16,8,5,384]{3,1,2,0:T(8,128)S(1)}, u32[]{:S(2)}, u32[]{:S(2)}) async-start(f32[16,8,5,384]{3,1,2,0:T(8,128)} %copy.30), calls=%async_computation | async-start | bytes 1966080 | tf_op jit(solution)/shard_map/all_to_all | solution.py:92
  137.4 3.7 %collective-permute-start.18 = (f32[8,5,384]{2,0,1:T(8,128)S(1)}, f32[8,5,384]{2,0,1:T(8,128)S(1)}, u32[]{:S(2)}, u32[]{:S(2)}) collective-permute-start(f32[8,5,384]{2,0,1:T(8,128)S(1)} %fusion.19), channel_id=1, source_target_pairs={{0,1},{1,0},{2,3},{3,2},{4,5},{5,4},{6,7},{7,6},{8,9},{9,8},{10,11... | collective-permute-start | bytes 184328 | tf_op jit(solution)/shard_map/ppermute | solution.py:95

commit v12 on v11

--- a/solution.py
+++ b/solution.py
@@ -87,13 +87,9 @@
     partner_pairs = [(p, p ^ 1) for p in range(n_col)]
     send = jnp.take(value, 1 - core, axis=1)
     summed = jnp.take(value, core, axis=1) + lax.ppermute(send, "col", partner_pairs)
-    half = rows // CORES
-    summed = summed.reshape(n_col, half, *value.shape[3:])
-    received = lax.all_to_all(summed, "col", 0, 0, tiled=True)
-    totals = jnp.sum(received.reshape(chips, CORES, half, *value.shape[3:]), axis=0)
-    own = jnp.take(totals, core, axis=0)
-    other = lax.ppermute(jnp.take(totals, 1 - core, axis=0), "col", partner_pairs)
-    return jnp.where(core == 0, jnp.concatenate([own, other]), jnp.concatenate([other, own]))
+    groups = [list(range(e, n_col, CORES)) for e in range(CORES)]
+    received = lax.all_to_all(summed, "col", 0, 0, tiled=True, axis_index_groups=groups)
+    return jnp.sum(received, axis=0)
 
 
 def local(anc_inv, factors_first, factors_second, lists_first, lists_second, parents, parent_link):

time: 143 us -> 135 us (0.944)
  starting transfers between devices: 89.4 us -> 85.9 us
  waiting for transfers between devices: 32 us -> 28.7 us
  local copies, waits for them, and re-layouts: 7.09 us -> 4.95 us
    ppermute x1 -> x0, starting transfers between devices: 2.8 us -> none  [reduce_cols_a2a(): lax.ppermute(jnp.take(totals, 1 - core, axis=0), 'col', partner_pairs)]
    all_to_all x1, waiting for transfers between devices: 16.4 us -> 13.7 us  [reduce_cols_a2a(): lax.all_to_all(summed, 'col', 0, 0, tiled=True, axis_index_groups=groups)]
    unnamed x23 -> x21, local copies, waits for them, and re-layouts: 3.85 us -> 2.56 us
  transfers between devices with their start and end apart: 20 -> 19, of which waited for: 8 -> 7; matrix products, arithmetic and copies ran while one was open for 3% -> 4% of each run, Pallas kernels for 0% -> 0%
where the time goes in v12:
time: 135 us; the launch traced here: 134 us
  starting transfers between devices  85.9 us (64%)
  waiting for transfers between devices  28.7 us (21%)
  other arithmetic  7.92 us (6%)
  matrix products  5.33 us (4%)
  local copies, waits for them, and re-layouts  4.95 us (4%)
    ppermute x3, starting transfers between devices, gather_rows(): lane_down = lax.ppermute(lane_down, 'row', shift_pairs(n_row, nz, 1, -2))  23.3 us
    ppermute x4, starting transfers between devices, gather_rows(): lax.ppermute(lane_down, 'row', shift_pairs(n_row, nz, 1, -1))  16.5 us
    ppermute x4, starting transfers between devices, gather_rows(): lax.ppermute(lane_up, 'row', shift_pairs(n_row, nz, 1, 1))  14.3 us
    all_to_all x1, waiting for transfers between devices, reduce_cols_a2a(): lax.all_to_all(summed, 'col', 0, 0, tiled=True, axis_index_groups=groups)  13.7 us
    ppermute x1, starting transfers between devices, reduce_cols_a2a(): lax.ppermute(send, 'col', partner_pairs)  7.45 us
    all_to_all x1, starting transfers between devices, reduce_cols_a2a(): lax.all_to_all(summed, 'col', 0, 0, tiled=True, axis_index_groups=groups)  6.63 us
    ppermute x1, starting transfers between devices, gather_rows(): lax.ppermute(lane_down[..., half:], 'row', shift_pairs(n_row, nz, 1, -2))  6.12 us
    ppermute x3, starting transfers between devices, gather_rows(): lane_up = lax.ppermute(lane_up, 'row', shift_pairs(n_row, nz, 1, 2))  5.76 us
  transfers between devices with their start and end apart: 19, of which 7 were waited for; matrix products, arithmetic and copies ran while one was open for 4% of the time, Pallas kernels for 0%

profile of v12, /device:TPU:1, one launch (start us, length us, event | category | flops | bytes accessed | tf_op | source)
XLA Modules:
  0.0 134.0 jit_solution(18385526852652934674)
XLA Ops:
  0.6 0.0 copy-start
  0.6 1.0 constant_dynamic-update-slice_fusion.1
  1.6 0.8 constant_dynamic-update-slice_fusion
  2.4 3.9 %collective-permute-start = (f32[8,3840]{1,0:T(8,128)S(1)}, f32[8,3840]{1,0:T(8,128)S(1)}, u32[]{:S(2)}, u32[]{:S(2)}) collective-permute-start(f32[8,3840]{1,0:T(8,128)S(1)} %bitcast.52), channel_id=1, source_target_pairs={{0,256},{16,272},{32,288},{48,304},{64,320},{80,336},{96,352},{112... | collective-permute-start | bytes 368648 | tf_op jit(solution)/shard_map/ppermute | solution.py:33
  6.4 0.7 compare_select_fusion
  7.0 0.7 compare_and_fusion
  7.7 0.8 compare_reduce_fusion.2
  8.5 0.6 gather_fusion
  9.1 0.1 broadcast_select_fusion
  9.2 0.0 collective-permute-done
  9.2 11.7 %collective-permute-start.2 = (f32[2,8,3840]{2,1,0:T(8,128)S(1)}, f32[2,8,3840]{2,1,0:T(8,128)S(1)}, u32[]{:S(2)}, u32[]{:S(2)}) collective-permute-start(f32[2,8,3840]{2,1,0:T(8,128)S(1)} %maximum_select_fusion.1), channel_id=1, source_target_pairs={{0,224},{16,240},{32,0},{48,16},{64,32},{80,48},{96,64},{112,80},{... | collective-permute-start | bytes 737288 | tf_op jit(solution)/shard_map/ppermute | solution.py:46
  20.9 1.9 %collective-permute-start.8 = (f32[2,8,3840]{2,1,0:T(8,128)S(1)}, f32[2,8,3840]{2,1,0:T(8,128)S(1)}, u32[]{:S(2)}, u32[]{:S(2)}) collective-permute-start(f32[2,8,3840]{2,1,0:T(8,128)S(1)} %maximum_select_fusion.1), channel_id=1, source_target_pairs={{0,32},{16,48},{32,64},{48,80},{64,96},{80,112},{96,128},{112,144}... | collective-permute-start | bytes 737288 | tf_op jit(solution)/shard_map/ppermute | solution.py:45
  22.9 0.8 compare_reduce_fusion
  23.7 5.0 %collective-permute-start.1 = (f32[2,8,3840]{2,1,0:T(8,128)S(1)}, f32[2,8,3840]{2,1,0:T(8,128)S(1)}, u32[]{:S(2)}, u32[]{:S(2)}) collective-permute-start(f32[2,8,3840]{2,1,0:T(8,128)S(1)} %maximum_select_fusion.1), channel_id=1, source_target_pairs={{0,240},{16,0},{32,16},{48,32},{64,48},{80,64},{96,80},{112,96},{1... | collective-permute-start | bytes 737288 | tf_op jit(solution)/shard_map/ppermute | solution.py:43
  28.7 0.8 compare_reduce_fusion.1
  29.5 0.2 collective-permute-done.2
  29.7 6.7 %collective-permute-start.4 = (f32[2,8,3840]{2,1,0:T(8,128)S(1)}, f32[2,8,3840]{2,1,0:T(8,128)S(1)}, u32[]{:S(2)}, u32[]{:S(2)}) collective-permute-start(f32[2,8,3840]{2,1,0:T(8,128)S(1)} %collective-permute-done.2), channel_id=1, source_target_pairs={{0,224},{16,240},{32,0},{48,16},{64,32},{80,48},{96,64},{112,80},{... | collective-permute-start | bytes 737288 | tf_op jit(solution)/shard_map/ppermute | solution.py:46
  36.4 0.0 collective-permute-done.8
  36.4 1.9 %collective-permute-start.9 = (f32[2,8,3840]{2,1,0:T(8,128)S(1)}, f32[2,8,3840]{2,1,0:T(8,128)S(1)}, u32[]{:S(2)}, u32[]{:S(2)}) collective-permute-start(f32[2,8,3840]{2,1,0:T(8,128)S(1)} %collective-permute-done.8), channel_id=1, source_target_pairs={{0,32},{16,48},{32,64},{48,80},{64,96},{80,112},{96,128},{112,144}... | collective-permute-start | bytes 737288 | tf_op jit(solution)/shard_map/ppermute | solution.py:45
  38.5 3.6 %collective-permute-start.16 = (f32[2,8,3840]{2,1,0:T(8,128)S(1)}, f32[2,8,3840]{2,1,0:T(8,128)S(1)}, u32[]{:S(2)}, u32[]{:S(2)}) collective-permute-start(f32[2,8,3840]{2,1,0:T(8,128)S(1)} %maximum_select_fusion.1), channel_id=1, source_target_pairs={{0,16},{16,32},{32,48},{48,64},{64,80},{80,96},{96,112},{112,128},... | collective-permute-start | bytes 737288 | tf_op jit(solution)/shard_map/ppermute | solution.py:42
  42.1 4.3 %collective-permute-start.3 = (f32[2,8,3840]{2,1,0:T(8,128)S(1)}, f32[2,8,3840]{2,1,0:T(8,128)S(1)}, u32[]{:S(2)}, u32[]{:S(2)}) collective-permute-start(f32[2,8,3840]{2,1,0:T(8,128)S(1)} %collective-permute-done.2), channel_id=1, source_target_pairs={{0,240},{16,0},{32,16},{48,32},{64,48},{80,64},{96,80},{112,96},{1... | collective-permute-start | bytes 737288 | tf_op jit(solution)/shard_map/ppermute | solution.py:43
  46.4 0.0 collective-permute-done.1
  46.5 0.0 collective-permute-done.4
  46.5 3.4 %collective-permute-start.5 = (f32[2,8,3840]{2,1,0:T(8,128)S(1)}, f32[2,8,3840]{2,1,0:T(8,128)S(1)}, u32[]{:S(2)}, u32[]{:S(2)}) collective-permute-start(f32[2,8,3840]{2,1,0:T(8,128)S(1)} %collective-permute-done.4), channel_id=1, source_target_pairs={{0,240},{16,0},{32,16},{48,32},{64,48},{80,64},{96,80},{112,96},{1... | collective-permute-start | bytes 737288 | tf_op jit(solution)/shard_map/ppermute | solution.py:43
  49.8 4.8 %collective-permute-start.6 = (f32[2,8,3840]{2,1,0:T(8,128)S(1)}, f32[2,8,3840]{2,1,0:T(8,128)S(1)}, u32[]{:S(2)}, u32[]{:S(2)}) collective-permute-start(f32[2,8,3840]{2,1,0:T(8,128)S(1)} %collective-permute-done.4), channel_id=1, source_target_pairs={{0,224},{16,240},{32,0},{48,16},{64,32},{80,48},{96,64},{112,80},{... | collective-permute-start | bytes 737288 | tf_op jit(solution)/shard_map/ppermute | solution.py:46
  54.7 0.0 collective-permute-done.9
  54.7 1.9 %collective-permute-start.10 = (f32[2,8,3840]{2,1,0:T(8,128)S(1)}, f32[2,8,3840]{2,1,0:T(8,128)S(1)}, u32[]{:S(2)}, u32[]{:S(2)}) collective-permute-start(f32[2,8,3840]{2,1,0:T(8,128)S(1)} %collective-permute-done.9), channel_id=1, source_target_pairs={{0,32},{16,48},{32,64},{48,80},{64,96},{80,112},{96,128},{112,144}... | collective-permute-start | bytes 737288 | tf_op jit(solution)/shard_map/ppermute | solution.py:45
  56.7 0.0 collective-permute-done.3
  56.7 3.4 %collective-permute-start.15 = (f32[2,8,3840]{2,1,0:T(8,128)S(1)}, f32[2,8,3840]{2,1,0:T(8,128)S(1)}, u32[]{:S(2)}, u32[]{:S(2)}) collective-permute-start(f32[2,8,3840]{2,1,0:T(8,128)S(1)} %collective-permute-done.8), channel_id=1, source_target_pairs={{0,16},{16,32},{32,48},{48,64},{64,80},{80,96},{96,112},{112,128},... | collective-permute-start | bytes 737288 | tf_op jit(solution)/shard_map/ppermute | solution.py:42
  60.1 5.2 %collective-permute-done.6 = f32[2,8,3840]{2,1,0:T(8,128)S(1)} collective-permute-done((f32[2,8,3840]{2,1,0:T(8,128)S(1)}, f32[2,8,3840]{2,1,0:T(8,128)S(1)}, u32[]{:S(2)}, u32[]{:S(2)}) %collective-permute-start.6) | collective-permute-done | bytes 245792 | tf_op jit(solution)/shard_map/ppermute | solution.py:46
  65.3 1.9 %collective-permute-start.14 = (f32[2,8,3840]{2,1,0:T(8,128)S(1)}, f32[2,8,3840]{2,1,0:T(8,128)S(1)}, u32[]{:S(2)}, u32[]{:S(2)}) collective-permute-start(f32[2,8,3840]{2,1,0:T(8,128)S(1)} %collective-permute-done.9), channel_id=1, source_target_pairs={{0,16},{16,32},{32,48},{48,64},{64,80},{80,96},{96,112},{112,128},... | collective-permute-start | bytes 737288 | tf_op jit(solution)/shard_map/ppermute | solution.py:42
  67.2 0.0 collective-permute-done.10
  67.2 6.1 %collective-permute-start.12 = (f32[2,8,1920]{2,1,0:T(8,128)S(1)}, f32[2,8,1920]{2,1,0:T(8,128)S(1)}, u32[]{:S(2)}, u32[]{:S(2)}) collective-permute-start(f32[2,8,1920]{2,1,0:T(8,128)S(1)} %slice.42), channel_id=1, source_target_pairs={{0,224},{16,240},{32,0},{48,16},{64,32},{80,48},{96,64},{112,80},{... | collective-permute-start | bytes 368648 | tf_op jit(solution)/shard_map/ppermute | solution.py:51
  73.4 0.0 collective-permute-done.5
  73.4 1.9 %collective-permute-start.11 = (f32[2,8,1920]{2,1,0:T(8,128)S(1)}, f32[2,8,1920]{2,1,0:T(8,128)S(1)}, u32[]{:S(2)}, u32[]{:S(2)}) collective-permute-start(f32[2,8,1920]{2,1,0:T(8,128)S(1)} %slice.41), channel_id=1, source_target_pairs={{0,32},{16,48},{32,64},{48,80},{64,96},{80,112},{96,128},{112,144}... | collective-permute-start | bytes 368648 | tf_op jit(solution)/shard_map/ppermute | solution.py:50
  75.4 1.2 collective-permute-done.12
  76.6 3.8 %collective-permute-start.7 = (f32[2,8,3840]{2,1,0:T(8,128)S(1)}, f32[2,8,3840]{2,1,0:T(8,128)S(1)}, u32[]{:S(2)}, u32[]{:S(2)}) collective-permute-start(f32[2,8,3840]{2,1,0:T(8,128)S(1)} %collective-permute-done.6), channel_id=1, source_target_pairs={{0,240},{16,0},{32,16},{48,32},{64,48},{80,64},{96,80},{112,96},{1... | collective-permute-start | bytes 737288 | tf_op jit(solution)/shard_map/ppermute | solution.py:43
  80.4 2.5 %collective-permute-done.11 = f32[2,8,1920]{2,1,0:T(8,128)S(1)} collective-permute-done((f32[2,8,1920]{2,1,0:T(8,128)S(1)}, f32[2,8,1920]{2,1,0:T(8,128)S(1)}, u32[]{:S(2)}, u32[]{:S(2)}) %collective-permute-start.11) | collective-permute-done | bytes 122912 | tf_op jit(solution)/shard_map/ppermute | solution.py:50
  82.9 5.4 %collective-permute-start.13 = (f32[2,8,3840]{2,1,0:T(8,128)S(1)}, f32[2,8,3840]{2,1,0:T(8,128)S(1)}, u32[]{:S(2)}, u32[]{:S(2)}) collective-permute-start(f32[2,8,3840]{2,1,0:T(8,128)S(1)} %collective-permute-done.10), channel_id=1, source_target_pairs={{0,16},{16,32},{32,48},{48,64},{64,80},{80,96},{96,112},{112,128},... | collective-permute-start | bytes 737288 | tf_op jit(solution)/shard_map/ppermute | solution.py:42
  88.4 0.0 collective-permute-done.7
  88.4 3.5 %collective-permute-done.13 = f32[2,8,3840]{2,1,0:T(8,128)S(1)} collective-permute-done((f32[2,8,3840]{2,1,0:T(8,128)S(1)}, f32[2,8,3840]{2,1,0:T(8,128)S(1)}, u32[]{:S(2)}, u32[]{:S(2)}) %collective-permute-start.13) | collective-permute-done | bytes 245792 | tf_op jit(solution)/shard_map/ppermute | solution.py:42
  91.9 0.0 collective-permute-done.14
  92.0 0.0 collective-permute-done.15
  92.1 0.0 collective-permute-done.16
  92.1 3.3 %fusion.4 = f32[2,16,8,5,384]{4,2,3,0,1:T(8,128)S(1)} fusion(f32[16,2,8,5,768]{4,2,3,1,0:T(8,128)S(1)} %constant_dynamic-update-slice_fusion.2, f32[5,768]{1,0:T(8,128)S(1)} %add_convert_fusion, f32[384,768]{1,0:T(8,128)S(1)} %copy-done), kind=kOutput, calls=%fused_computation.9 | convolution fusion | flops 2265907200 | bytes 7093248 | tf_op jit(solution)/shard_map/tlkmj,ij->ltkmi/dot_general | solution.py:120
  95.4 0.4 fusion.2
  95.8 0.2 copy.18
  96.0 1.3 copy-done.1
  97.3 0.1 slice.43
  97.4 0.6 gather_fusion.1
  98.0 2.0 %fusion.8 = f32[256,2,384]{2,0,1:T(8,128)S(1)} fusion(f32[2,256,256]{2,1,0:T(8,128)} %param.15, f32[256,5,384]{2,0,1:T(8,128)} %bitcast.49, f32[2,256,384]{2,1,0:T(8,128)S(1)} %gather_fusion.1, f32[2,384]{1,0:T(2,128)S(1)} %broadcast_select_fusion, pred[2]{0:T(512)(128)(4,1)S(1)} %compare_and_fusion), kind=kOutput, calls=%fused_computation.12 | convolution fusion | flops 302579712 | bytes 2886658 | tf_op jit(solution)/shard_map/cqk,qci->kci/dot_general | solution.py:128
  100.0 0.1 pad_maximum_fusion
  100.1 0.2 constant_dynamic-slice_fusion.1
  100.3 0.0 copy-start.2
  100.3 1.0 fusion.10
  101.3 7.4 %collective-permute-start.17 = (f32[8,16,5,384]{3,1,2,0:T(8,128)}, f32[8,16,5,384]{3,1,2,0:T(8,128)S(1)}, u32[]{:S(2)}, u32[]{:S(2)}) collective-permute-start(f32[8,16,5,384]{3,1,2,0:T(8,128)} %fusion.10), channel_id=1, source_target_pairs={{0,1},{1,0},{2,3},{3,2},{4,5},{5,4},{6,7},{7,6},{8,9},{9,8},{10,11... | collective-permute-start | bytes 2949128 | tf_op jit(solution)/shard_map/ppermute | solution.py:89
  108.8 2.4 %collective-permute-done.17 = f32[8,16,5,384]{3,1,2,0:T(8,128)S(1)} collective-permute-done((f32[8,16,5,384]{3,1,2,0:T(8,128)}, f32[8,16,5,384]{3,1,2,0:T(8,128)S(1)}, u32[]{:S(2)}, u32[]{:S(2)}) %collective-permute-start.17) | collective-permute-done | bytes 983072 | tf_op jit(solution)/shard_map/ppermute | solution.py:89
  111.2 1.1 fusion.12
  112.2 6.6 %all-to-all-start = ((f32[8,16,5,384]{3,1,2,0:T(8,128)}), f32[8,16,5,384]{3,1,2,0:T(8,128)S(1)}, u32[]{:S(2)}, u32[]{:S(2)}) async-start(f32[8,16,5,384]{3,1,2,0:T(8,128)} %fusion.12), calls=%async_computation | async-start | bytes 1966080 | tf_op jit(solution)/shard_map/all_to_all | solution.py:91
  118.9 0.1 compare_reduce_fusion.3
  119.0 13.7 %all-to-all-done = f32[8,16,5,384]{3,1,2,0:T(8,128)S(1)} async-done(((f32[8,16,5,384]{3,1,2,0:T(8,128)}), f32[8,16,5,384]{3,1,2,0:T(8,128)S(1)}, u32[]{:S(2)}, u32[]{:S(2)}) %all-to-all-start) | async-done | bytes 983072 | tf_op jit(solution)/shard_map/all_to_all | solution.py:91
  132.7 0.1 reduce_sum.9
  132.7 0.6 slice_multiply_fusion
  133.4 0.6 slice_multiply_fusion.1
  (30 shorter events, 0.4 us)
Async XLA Ops:
  0.6 91.5 %copy-start = (f32[384,768]{1,0:T(8,128)S(1)}, f32[384,768]{1,0:T(8,128)}, u32[]{:S(2)}) copy-start(f32[384,768]{1,0:T(8,128)} %param.9) | copy-start | bytes 3538948
  2.4 6.8 %collective-permute-start = (f32[8,3840]{1,0:T(8,128)S(1)}, f32[8,3840]{1,0:T(8,128)S(1)}, u32[]{:S(2)}, u32[]{:S(2)}) collective-permute-start(f32[8,3840]{1,0:T(8,128)S(1)} %bitcast.52), channel_id=1, source_target_pairs={{0,256},{16,272},{32,288},{48,304},{64,320},{80,336},{96,352},{112... | collective-permute-start | bytes 368648 | tf_op jit(solution)/shard_map/ppermute | solution.py:33
  9.2 20.5 %collective-permute-start.2 = (f32[2,8,3840]{2,1,0:T(8,128)S(1)}, f32[2,8,3840]{2,1,0:T(8,128)S(1)}, u32[]{:S(2)}, u32[]{:S(2)}) collective-permute-start(f32[2,8,3840]{2,1,0:T(8,128)S(1)} %maximum_select_fusion.1), channel_id=1, source_target_pairs={{0,224},{16,240},{32,0},{48,16},{64,32},{80,48},{96,64},{112,80},{... | collective-permute-start | bytes 737288 | tf_op jit(solution)/shard_map/ppermute | solution.py:46
  20.9 15.5 %collective-permute-start.8 = (f32[2,8,3840]{2,1,0:T(8,128)S(1)}, f32[2,8,3840]{2,1,0:T(8,128)S(1)}, u32[]{:S(2)}, u32[]{:S(2)}) collective-permute-start(f32[2,8,3840]{2,1,0:T(8,128)S(1)} %maximum_select_fusion.1), channel_id=1, source_target_pairs={{0,32},{16,48},{32,64},{48,80},{64,96},{80,112},{96,128},{112,144}... | collective-permute-start | bytes 737288 | tf_op jit(solution)/shard_map/ppermute | solution.py:45
  23.7 22.7 %collective-permute-start.1 = (f32[2,8,3840]{2,1,0:T(8,128)S(1)}, f32[2,8,3840]{2,1,0:T(8,128)S(1)}, u32[]{:S(2)}, u32[]{:S(2)}) collective-permute-start(f32[2,8,3840]{2,1,0:T(8,128)S(1)} %maximum_select_fusion.1), channel_id=1, source_target_pairs={{0,240},{16,0},{32,16},{48,32},{64,48},{80,64},{96,80},{112,96},{1... | collective-permute-start | bytes 737288 | tf_op jit(solution)/shard_map/ppermute | solution.py:43
  29.7 16.7 %collective-permute-start.4 = (f32[2,8,3840]{2,1,0:T(8,128)S(1)}, f32[2,8,3840]{2,1,0:T(8,128)S(1)}, u32[]{:S(2)}, u32[]{:S(2)}) collective-permute-start(f32[2,8,3840]{2,1,0:T(8,128)S(1)} %collective-permute-done.2), channel_id=1, source_target_pairs={{0,224},{16,240},{32,0},{48,16},{64,32},{80,48},{96,64},{112,80},{... | collective-permute-start | bytes 737288 | tf_op jit(solution)/shard_map/ppermute | solution.py:46
  36.4 18.2 %collective-permute-start.9 = (f32[2,8,3840]{2,1,0:T(8,128)S(1)}, f32[2,8,3840]{2,1,0:T(8,128)S(1)}, u32[]{:S(2)}, u32[]{:S(2)}) collective-permute-start(f32[2,8,3840]{2,1,0:T(8,128)S(1)} %collective-permute-done.8), channel_id=1, source_target_pairs={{0,32},{16,48},{32,64},{48,80},{64,96},{80,112},{96,128},{112,144}... | collective-permute-start | bytes 737288 | tf_op jit(solution)/shard_map/ppermute | solution.py:45
  38.5 53.6 %collective-permute-start.16 = (f32[2,8,3840]{2,1,0:T(8,128)S(1)}, f32[2,8,3840]{2,1,0:T(8,128)S(1)}, u32[]{:S(2)}, u32[]{:S(2)}) collective-permute-start(f32[2,8,3840]{2,1,0:T(8,128)S(1)} %maximum_select_fusion.1), channel_id=1, source_target_pairs={{0,16},{16,32},{32,48},{48,64},{64,80},{80,96},{96,112},{112,128},... | collective-permute-start | bytes 737288 | tf_op jit(solution)/shard_map/ppermute | solution.py:42
  42.1 14.6 %collective-permute-start.3 = (f32[2,8,3840]{2,1,0:T(8,128)S(1)}, f32[2,8,3840]{2,1,0:T(8,128)S(1)}, u32[]{:S(2)}, u32[]{:S(2)}) collective-permute-start(f32[2,8,3840]{2,1,0:T(8,128)S(1)} %collective-permute-done.2), channel_id=1, source_target_pairs={{0,240},{16,0},{32,16},{48,32},{64,48},{80,64},{96,80},{112,96},{1... | collective-permute-start | bytes 737288 | tf_op jit(solution)/shard_map/ppermute | solution.py:43
  46.5 26.9 %collective-permute-start.5 = (f32[2,8,3840]{2,1,0:T(8,128)S(1)}, f32[2,8,3840]{2,1,0:T(8,128)S(1)}, u32[]{:S(2)}, u32[]{:S(2)}) collective-permute-start(f32[2,8,3840]{2,1,0:T(8,128)S(1)} %collective-permute-done.4), channel_id=1, source_target_pairs={{0,240},{16,0},{32,16},{48,32},{64,48},{80,64},{96,80},{112,96},{1... | collective-permute-start | bytes 737288 | tf_op jit(solution)/shard_map/ppermute | solution.py:43
  49.8 15.5 %collective-permute-start.6 = (f32[2,8,3840]{2,1,0:T(8,128)S(1)}, f32[2,8,3840]{2,1,0:T(8,128)S(1)}, u32[]{:S(2)}, u32[]{:S(2)}) collective-permute-start(f32[2,8,3840]{2,1,0:T(8,128)S(1)} %collective-permute-done.4), channel_id=1, source_target_pairs={{0,224},{16,240},{32,0},{48,16},{64,32},{80,48},{96,64},{112,80},{... | collective-permute-start | bytes 737288 | tf_op jit(solution)/shard_map/ppermute | solution.py:46
  54.7 12.5 %collective-permute-start.10 = (f32[2,8,3840]{2,1,0:T(8,128)S(1)}, f32[2,8,3840]{2,1,0:T(8,128)S(1)}, u32[]{:S(2)}, u32[]{:S(2)}) collective-permute-start(f32[2,8,3840]{2,1,0:T(8,128)S(1)} %collective-permute-done.9), channel_id=1, source_target_pairs={{0,32},{16,48},{32,64},{48,80},{64,96},{80,112},{96,128},{112,144}... | collective-permute-start | bytes 737288 | tf_op jit(solution)/shard_map/ppermute | solution.py:45
  56.7 35.3 %collective-permute-start.15 = (f32[2,8,3840]{2,1,0:T(8,128)S(1)}, f32[2,8,3840]{2,1,0:T(8,128)S(1)}, u32[]{:S(2)}, u32[]{:S(2)}) collective-permute-start(f32[2,8,3840]{2,1,0:T(8,128)S(1)} %collective-permute-done.8), channel_id=1, source_target_pairs={{0,16},{16,32},{32,48},{48,64},{64,80},{80,96},{96,112},{112,128},... | collective-permute-start | bytes 737288 | tf_op jit(solution)/shard_map/ppermute | solution.py:42
  65.3 26.6 %collective-permute-start.14 = (f32[2,8,3840]{2,1,0:T(8,128)S(1)}, f32[2,8,3840]{2,1,0:T(8,128)S(1)}, u32[]{:S(2)}, u32[]{:S(2)}) collective-permute-start(f32[2,8,3840]{2,1,0:T(8,128)S(1)} %collective-permute-done.9), channel_id=1, source_target_pairs={{0,16},{16,32},{32,48},{48,64},{64,80},{80,96},{96,112},{112,128},... | collective-permute-start | bytes 737288 | tf_op jit(solution)/shard_map/ppermute | solution.py:42
  67.2 9.4 %collective-permute-start.12 = (f32[2,8,1920]{2,1,0:T(8,128)S(1)}, f32[2,8,1920]{2,1,0:T(8,128)S(1)}, u32[]{:S(2)}, u32[]{:S(2)}) collective-permute-start(f32[2,8,1920]{2,1,0:T(8,128)S(1)} %slice.42), channel_id=1, source_target_pairs={{0,224},{16,240},{32,0},{48,16},{64,32},{80,48},{96,64},{112,80},{... | collective-permute-start | bytes 368648 | tf_op jit(solution)/shard_map/ppermute | solution.py:51
  73.4 9.5 %collective-permute-start.11 = (f32[2,8,1920]{2,1,0:T(8,128)S(1)}, f32[2,8,1920]{2,1,0:T(8,128)S(1)}, u32[]{:S(2)}, u32[]{:S(2)}) collective-permute-start(f32[2,8,1920]{2,1,0:T(8,128)S(1)} %slice.41), channel_id=1, source_target_pairs={{0,32},{16,48},{32,64},{48,80},{64,96},{80,112},{96,128},{112,144}... | collective-permute-start | bytes 368648 | tf_op jit(solution)/shard_map/ppermute | solution.py:50
  76.6 11.8 %collective-permute-start.7 = (f32[2,8,3840]{2,1,0:T(8,128)S(1)}, f32[2,8,3840]{2,1,0:T(8,128)S(1)}, u32[]{:S(2)}, u32[]{:S(2)}) collective-permute-start(f32[2,8,3840]{2,1,0:T(8,128)S(1)} %collective-permute-done.6), channel_id=1, source_target_pairs={{0,240},{16,0},{32,16},{48,32},{64,48},{80,64},{96,80},{112,96},{1... | collective-permute-start | bytes 737288 | tf_op jit(solution)/shard_map/ppermute | solution.py:43
  82.9 9.0 %collective-permute-start.13 = (f32[2,8,3840]{2,1,0:T(8,128)S(1)}, f32[2,8,3840]{2,1,0:T(8,128)S(1)}, u32[]{:S(2)}, u32[]{:S(2)}) collective-permute-start(f32[2,8,3840]{2,1,0:T(8,128)S(1)} %collective-permute-done.10), channel_id=1, source_target_pairs={{0,16},{16,32},{32,48},{48,64},{64,80},{80,96},{96,112},{112,128},... | collective-permute-start | bytes 737288 | tf_op jit(solution)/shard_map/ppermute | solution.py:42
  96.0 1.3 copy-start.1
  100.3 18.6 %copy-start.2 = (s32[2,36]{1,0:T(2,128)S(1)}, s32[2,36]{1,0:T(2,128)}, u32[]{:S(2)}) copy-start(s32[2,36]{1,0:T(2,128)} %param.13) | copy-start | bytes 868
  101.3 9.8 %collective-permute-start.17 = (f32[8,16,5,384]{3,1,2,0:T(8,128)}, f32[8,16,5,384]{3,1,2,0:T(8,128)S(1)}, u32[]{:S(2)}, u32[]{:S(2)}) collective-permute-start(f32[8,16,5,384]{3,1,2,0:T(8,128)} %fusion.10), channel_id=1, source_target_pairs={{0,1},{1,0},{2,3},{3,2},{4,5},{5,4},{6,7},{7,6},{8,9},{9,8},{10,11... | collective-permute-start | bytes 2949128 | tf_op jit(solution)/shard_map/ppermute | solution.py:89
  112.2 20.4 %all-to-all-start = ((f32[8,16,5,384]{3,1,2,0:T(8,128)}), f32[8,16,5,384]{3,1,2,0:T(8,128)S(1)}, u32[]{:S(2)}, u32[]{:S(2)}) async-start(f32[8,16,5,384]{3,1,2,0:T(8,128)} %fusion.12), calls=%async_computation | async-start | bytes 1966080 | tf_op jit(solution)/shard_map/all_to_all | solution.py:91

commit v13 on v12

--- a/solution.py
+++ b/solution.py
@@ -35,21 +35,16 @@
     pieces = [None] * nz
     pieces[0] = pair
     steps = nz // 4
-    half = pair.shape[-1] // 2
     lane_up = pair
     lane_down = pair
     for t in range(1, steps + 1):
         pieces[nz - (2 * t - 1)] = lax.ppermute(lane_up, "row", shift_pairs(n_row, nz, 1, 1))
         pieces[2 * t - 1] = lax.ppermute(lane_down, "row", shift_pairs(n_row, nz, 1, -1))
+        lane_up = lax.ppermute(lane_up, "row", shift_pairs(n_row, nz, 1, 2))
+        pieces[nz - 2 * t] = lane_up
         if t < steps:
-            lane_up = lax.ppermute(lane_up, "row", shift_pairs(n_row, nz, 1, 2))
             lane_down = lax.ppermute(lane_down, "row", shift_pairs(n_row, nz, 1, -2))
-            pieces[nz - 2 * t] = lane_up
             pieces[2 * t] = lane_down
-        else:
-            last_up = lax.ppermute(lane_up[..., :half], "row", shift_pairs(n_row, nz, 1, 2))
-            last_down = lax.ppermute(lane_down[..., half:], "row", shift_pairs(n_row, nz, 1, -2))
-            pieces[nz // 2] = jnp.concatenate([last_up, last_down], axis=-1)
     return jnp.stack(pieces), z
 
 

time: 135 us -> 136 us (level)
  waiting for transfers between devices: 28.7 us -> 42.7 us
  starting transfers between devices: 85.9 us -> 72.9 us
    ppermute x3 -> x4, waiting for transfers between devices: 0.01 us -> 11.1 us  [gather_rows(): lane_up = lax.ppermute(lane_up, 'row', shift_pairs(n_row, nz, 1, 2))]
    ppermute x4, waiting for transfers between devices: 3.46 us -> 12.5 us  [gather_rows(): lax.ppermute(lane_up, 'row', shift_pairs(n_row, nz, 1, 1))]
    ppermute x2 -> x0, starting transfers between devices: 8.04 us -> none  [the longest x1 6.12 us: gather_rows(): lax.ppermute(lane_down[..., half:], 'row', shift_pairs(n_row, nz, 1, -2))]
    ppermute x1, starting transfers between devices: 7.45 us -> 3.49 us  [reduce_cols_a2a(): lax.ppermute(send, 'col', partner_pairs)]
    ppermute x2 -> x0, waiting for transfers between devices: 3.75 us -> none  [the longest x1 2.51 us: gather_rows(): lax.ppermute(lane_up[..., :half], 'row', shift_pairs(n_row, nz, 1, 2))]
    ppermute x4, starting transfers between devices: 16.5 us -> 13.5 us  [gather_rows(): lax.ppermute(lane_down, 'row', shift_pairs(n_row, nz, 1, -1))]
    ppermute x3, waiting for transfers between devices: 5.42 us -> 2.96 us  [gather_rows(): lane_down = lax.ppermute(lane_down, 'row', shift_pairs(n_row, nz, 1, -2))]
    ppermute x3 -> x4, starting transfers between devices: 5.76 us -> 7.66 us  [gather_rows(): lane_up = lax.ppermute(lane_up, 'row', shift_pairs(n_row, nz, 1, 2))]
  transfers between devices with their start and end apart: 19 -> 18, of which waited for: 7 -> 9; matrix products, arithmetic and copies ran while one was open for 4% -> 4% of each run, Pallas kernels for 0% -> 0%
where the time goes in v13:
time: 136 us; the launch traced here: 135 us
  starting transfers between devices  72.9 us (54%)
  waiting for transfers between devices  42.7 us (31%)
  other arithmetic  7.89 us (6%)
  matrix products  5.33 us (4%)
  local copies, waits for them, and re-layouts  4.94 us (4%)
    ppermute x3, starting transfers between devices, gather_rows(): lane_down = lax.ppermute(lane_down, 'row', shift_pairs(n_row, nz, 1, -2))  24.8 us
    all_to_all x1, waiting for transfers between devices, reduce_cols_a2a(): lax.all_to_all(summed, 'col', 0, 0, tiled=True, axis_index_groups=groups)  13.7 us
    ppermute x4, starting transfers between devices, gather_rows(): lax.ppermute(lane_down, 'row', shift_pairs(n_row, nz, 1, -1))  13.5 us
    ppermute x4, starting transfers between devices, gather_rows(): lax.ppermute(lane_up, 'row', shift_pairs(n_row, nz, 1, 1))  13.2 us
    ppermute x4, waiting for transfers between devices, gather_rows(): lax.ppermute(lane_up, 'row', shift_pairs(n_row, nz, 1, 1))  12.5 us
    ppermute x4, waiting for transfers between devices, gather_rows(): lane_up = lax.ppermute(lane_up, 'row', shift_pairs(n_row, nz, 1, 2))  11.1 us
    ppermute x4, starting transfers between devices, gather_rows(): lane_up = lax.ppermute(lane_up, 'row', shift_pairs(n_row, nz, 1, 2))  7.66 us
    all_to_all x1, starting transfers between devices, reduce_cols_a2a(): lax.all_to_all(summed, 'col', 0, 0, tiled=True, axis_index_groups=groups)  6.29 us
  transfers between devices with their start and end apart: 18, of which 9 were waited for; matrix products, arithmetic and copies ran while one was open for 4% of the time, Pallas kernels for 0%

profile of v13, /device:TPU:1, one launch (start us, length us, event | category | flops | bytes accessed | tf_op | source)
XLA Modules:
  0.0 134.9 jit_solution(7022230702387283752)
XLA Ops:
  0.6 0.0 copy-start
  0.6 1.0 constant_dynamic-update-slice_fusion.1
  1.6 0.8 constant_dynamic-update-slice_fusion
  2.4 3.9 %collective-permute-start = (f32[8,3840]{1,0:T(8,128)S(1)}, f32[8,3840]{1,0:T(8,128)S(1)}, u32[]{:S(2)}, u32[]{:S(2)}) collective-permute-start(f32[8,3840]{1,0:T(8,128)S(1)} %bitcast.51), channel_id=1, source_target_pairs={{0,256},{16,272},{32,288},{48,304},{64,320},{80,336},{96,352},{112... | collective-permute-start | bytes 368648 | tf_op jit(solution)/shard_map/ppermute | solution.py:33
  6.4 0.7 compare_select_fusion
  7.1 0.8 compare_reduce_fusion.2
  7.9 0.6 gather_fusion
  8.4 0.7 compare_and_fusion
  9.1 0.0 collective-permute-done
  9.1 11.8 %collective-permute-start.2 = (f32[2,8,3840]{2,1,0:T(8,128)S(1)}, f32[2,8,3840]{2,1,0:T(8,128)S(1)}, u32[]{:S(2)}, u32[]{:S(2)}) collective-permute-start(f32[2,8,3840]{2,1,0:T(8,128)S(1)} %maximum_select_fusion.1), channel_id=1, source_target_pairs={{0,224},{16,240},{32,0},{48,16},{64,32},{80,48},{96,64},{112,80},{... | collective-permute-start | bytes 737288 | tf_op jit(solution)/shard_map/ppermute | solution.py:46
  20.9 0.1 broadcast_select_fusion
  21.0 1.9 %collective-permute-start.8 = (f32[2,8,3840]{2,1,0:T(8,128)S(1)}, f32[2,8,3840]{2,1,0:T(8,128)S(1)}, u32[]{:S(2)}, u32[]{:S(2)}) collective-permute-start(f32[2,8,3840]{2,1,0:T(8,128)S(1)} %maximum_select_fusion.1), channel_id=1, source_target_pairs={{0,32},{16,48},{32,64},{48,80},{64,96},{80,112},{96,128},{112,144}... | collective-permute-start | bytes 737288 | tf_op jit(solution)/shard_map/ppermute | solution.py:43
  22.9 0.8 compare_reduce_fusion
  23.8 5.0 %collective-permute-start.1 = (f32[2,8,3840]{2,1,0:T(8,128)S(1)}, f32[2,8,3840]{2,1,0:T(8,128)S(1)}, u32[]{:S(2)}, u32[]{:S(2)}) collective-permute-start(f32[2,8,3840]{2,1,0:T(8,128)S(1)} %maximum_select_fusion.1), channel_id=1, source_target_pairs={{0,240},{16,0},{32,16},{48,32},{64,48},{80,64},{96,80},{112,96},{1... | collective-permute-start | bytes 737288 | tf_op jit(solution)/shard_map/ppermute | solution.py:42
  28.8 0.9 collective-permute-done.2
  29.7 6.7 %collective-permute-start.4 = (f32[2,8,3840]{2,1,0:T(8,128)S(1)}, f32[2,8,3840]{2,1,0:T(8,128)S(1)}, u32[]{:S(2)}, u32[]{:S(2)}) collective-permute-start(f32[2,8,3840]{2,1,0:T(8,128)S(1)} %collective-permute-done.2), channel_id=1, source_target_pairs={{0,224},{16,240},{32,0},{48,16},{64,32},{80,48},{96,64},{112,80},{... | collective-permute-start | bytes 737288 | tf_op jit(solution)/shard_map/ppermute | solution.py:46
  36.4 0.8 compare_reduce_fusion.1
  37.2 0.0 collective-permute-done.8
  37.2 1.9 %collective-permute-start.9 = (f32[2,8,3840]{2,1,0:T(8,128)S(1)}, f32[2,8,3840]{2,1,0:T(8,128)S(1)}, u32[]{:S(2)}, u32[]{:S(2)}) collective-permute-start(f32[2,8,3840]{2,1,0:T(8,128)S(1)} %collective-permute-done.8), channel_id=1, source_target_pairs={{0,32},{16,48},{32,64},{48,80},{64,96},{80,112},{96,128},{112,144}... | collective-permute-start | bytes 737288 | tf_op jit(solution)/shard_map/ppermute | solution.py:43
  39.2 2.9 %collective-permute-start.15 = (f32[2,8,3840]{2,1,0:T(8,128)S(1)}, f32[2,8,3840]{2,1,0:T(8,128)S(1)}, u32[]{:S(2)}, u32[]{:S(2)}) collective-permute-start(f32[2,8,3840]{2,1,0:T(8,128)S(1)} %maximum_select_fusion.1), channel_id=1, source_target_pairs={{0,16},{16,32},{32,48},{48,64},{64,80},{80,96},{96,112},{112,128},... | collective-permute-start | bytes 737288 | tf_op jit(solution)/shard_map/ppermute | solution.py:41
  42.1 4.3 %collective-permute-start.3 = (f32[2,8,3840]{2,1,0:T(8,128)S(1)}, f32[2,8,3840]{2,1,0:T(8,128)S(1)}, u32[]{:S(2)}, u32[]{:S(2)}) collective-permute-start(f32[2,8,3840]{2,1,0:T(8,128)S(1)} %collective-permute-done.2), channel_id=1, source_target_pairs={{0,240},{16,0},{32,16},{48,32},{64,48},{80,64},{96,80},{112,96},{1... | collective-permute-start | bytes 737288 | tf_op jit(solution)/shard_map/ppermute | solution.py:42
  46.5 0.0 collective-permute-done.4
  46.5 6.3 %collective-permute-start.6 = (f32[2,8,3840]{2,1,0:T(8,128)S(1)}, f32[2,8,3840]{2,1,0:T(8,128)S(1)}, u32[]{:S(2)}, u32[]{:S(2)}) collective-permute-start(f32[2,8,3840]{2,1,0:T(8,128)S(1)} %collective-permute-done.4), channel_id=1, source_target_pairs={{0,224},{16,240},{32,0},{48,16},{64,32},{80,48},{96,64},{112,80},{... | collective-permute-start | bytes 737288 | tf_op jit(solution)/shard_map/ppermute | solution.py:46
  52.8 0.0 collective-permute-done.1
  52.8 1.9 %collective-permute-start.5 = (f32[2,8,3840]{2,1,0:T(8,128)S(1)}, f32[2,8,3840]{2,1,0:T(8,128)S(1)}, u32[]{:S(2)}, u32[]{:S(2)}) collective-permute-start(f32[2,8,3840]{2,1,0:T(8,128)S(1)} %collective-permute-done.4), channel_id=1, source_target_pairs={{0,240},{16,0},{32,16},{48,32},{64,48},{80,64},{96,80},{112,96},{1... | collective-permute-start | bytes 737288 | tf_op jit(solution)/shard_map/ppermute | solution.py:42
  54.7 0.0 collective-permute-done.9
  54.7 1.9 %collective-permute-start.10 = (f32[2,8,3840]{2,1,0:T(8,128)S(1)}, f32[2,8,3840]{2,1,0:T(8,128)S(1)}, u32[]{:S(2)}, u32[]{:S(2)}) collective-permute-start(f32[2,8,3840]{2,1,0:T(8,128)S(1)} %collective-permute-done.9), channel_id=1, source_target_pairs={{0,32},{16,48},{32,64},{48,80},{64,96},{80,112},{96,128},{112,144}... | collective-permute-start | bytes 737288 | tf_op jit(solution)/shard_map/ppermute | solution.py:43
  56.7 0.0 collective-permute-done.3
  56.7 3.4 %collective-permute-start.14 = (f32[2,8,3840]{2,1,0:T(8,128)S(1)}, f32[2,8,3840]{2,1,0:T(8,128)S(1)}, u32[]{:S(2)}, u32[]{:S(2)}) collective-permute-start(f32[2,8,3840]{2,1,0:T(8,128)S(1)} %collective-permute-done.8), channel_id=1, source_target_pairs={{0,16},{16,32},{32,48},{48,64},{64,80},{80,96},{96,112},{112,128},... | collective-permute-start | bytes 737288 | tf_op jit(solution)/shard_map/ppermute | solution.py:41
  60.1 2.0 %collective-permute-done.6 = f32[2,8,3840]{2,1,0:T(8,128)S(1)} collective-permute-done((f32[2,8,3840]{2,1,0:T(8,128)S(1)}, f32[2,8,3840]{2,1,0:T(8,128)S(1)}, u32[]{:S(2)}, u32[]{:S(2)}) %collective-permute-start.6) | collective-permute-done | bytes 245792 | tf_op jit(solution)/shard_map/ppermute | solution.py:46
  62.1 2.3 %collective-permute-start.7 = (f32[2,8,3840]{2,1,0:T(8,128)S(1)}, f32[2,8,3840]{2,1,0:T(8,128)S(1)}, u32[]{:S(2)}, u32[]{:S(2)}) collective-permute-start(f32[2,8,3840]{2,1,0:T(8,128)S(1)} %collective-permute-done.6), channel_id=1, source_target_pairs={{0,240},{16,0},{32,16},{48,32},{64,48},{80,64},{96,80},{112,96},{1... | collective-permute-start | bytes 737288 | tf_op jit(solution)/shard_map/ppermute | solution.py:42
  64.4 2.0 %collective-permute-done.10 = f32[2,8,3840]{2,1,0:T(8,128)S(1)} collective-permute-done((f32[2,8,3840]{2,1,0:T(8,128)S(1)}, f32[2,8,3840]{2,1,0:T(8,128)S(1)}, u32[]{:S(2)}, u32[]{:S(2)}) %collective-permute-start.10) | collective-permute-done | bytes 245792 | tf_op jit(solution)/shard_map/ppermute | solution.py:43
  66.5 1.9 %collective-permute-start.11 = (f32[2,8,3840]{2,1,0:T(8,128)S(1)}, f32[2,8,3840]{2,1,0:T(8,128)S(1)}, u32[]{:S(2)}, u32[]{:S(2)}) collective-permute-start(f32[2,8,3840]{2,1,0:T(8,128)S(1)} %collective-permute-done.10), channel_id=1, source_target_pairs={{0,32},{16,48},{32,64},{48,80},{64,96},{80,112},{96,128},{112,144}... | collective-permute-start | bytes 737288 | tf_op jit(solution)/shard_map/ppermute | solution.py:43
  68.4 0.1 collective-permute-done.5
  68.5 5.0 %collective-permute-start.12 = (f32[2,8,3840]{2,1,0:T(8,128)S(1)}, f32[2,8,3840]{2,1,0:T(8,128)S(1)}, u32[]{:S(2)}, u32[]{:S(2)}) collective-permute-start(f32[2,8,3840]{2,1,0:T(8,128)S(1)} %collective-permute-done.10), channel_id=1, source_target_pairs={{0,16},{16,32},{32,48},{48,64},{64,80},{80,96},{96,112},{112,128},... | collective-permute-start | bytes 737288 | tf_op jit(solution)/shard_map/ppermute | solution.py:41
  73.6 0.0 collective-permute-done.7
  73.6 1.9 %collective-permute-start.13 = (f32[2,8,3840]{2,1,0:T(8,128)S(1)}, f32[2,8,3840]{2,1,0:T(8,128)S(1)}, u32[]{:S(2)}, u32[]{:S(2)}) collective-permute-start(f32[2,8,3840]{2,1,0:T(8,128)S(1)} %collective-permute-done.9), channel_id=1, source_target_pairs={{0,16},{16,32},{32,48},{48,64},{64,80},{80,96},{96,112},{112,128},... | collective-permute-start | bytes 737288 | tf_op jit(solution)/shard_map/ppermute | solution.py:41
  75.6 9.0 %collective-permute-done.11 = f32[2,8,3840]{2,1,0:T(8,128)S(1)} collective-permute-done((f32[2,8,3840]{2,1,0:T(8,128)S(1)}, f32[2,8,3840]{2,1,0:T(8,128)S(1)}, u32[]{:S(2)}, u32[]{:S(2)}) %collective-permute-start.11) | collective-permute-done | bytes 245792 | tf_op jit(solution)/shard_map/ppermute | solution.py:43
  84.6 7.2 %collective-permute-done.12 = f32[2,8,3840]{2,1,0:T(8,128)S(1)} collective-permute-done((f32[2,8,3840]{2,1,0:T(8,128)S(1)}, f32[2,8,3840]{2,1,0:T(8,128)S(1)}, u32[]{:S(2)}, u32[]{:S(2)}) %collective-permute-start.12) | collective-permute-done | bytes 245792 | tf_op jit(solution)/shard_map/ppermute | solution.py:41
  91.9 5.2 %collective-permute-done.13 = f32[2,8,3840]{2,1,0:T(8,128)S(1)} collective-permute-done((f32[2,8,3840]{2,1,0:T(8,128)S(1)}, f32[2,8,3840]{2,1,0:T(8,128)S(1)}, u32[]{:S(2)}, u32[]{:S(2)}) %collective-permute-start.13) | collective-permute-done | bytes 245792 | tf_op jit(solution)/shard_map/ppermute | solution.py:41
  97.2 0.0 collective-permute-done.14
  97.3 0.0 collective-permute-done.15
  97.3 0.0 copy-done
  97.3 3.3 %fusion.4 = f32[2,16,8,5,384]{4,2,3,0,1:T(8,128)S(1)} fusion(f32[16,2,8,5,768]{4,2,3,1,0:T(8,128)S(1)} %constant_dynamic-update-slice_fusion.2, f32[5,768]{1,0:T(8,128)S(1)} %add_convert_fusion, f32[384,768]{1,0:T(8,128)S(1)} %copy-done), kind=kOutput, calls=%fused_computation.9 | convolution fusion | flops 2265907200 | bytes 7093248 | tf_op jit(solution)/shard_map/tlkmj,ij->ltkmi/dot_general | solution.py:115
  100.6 0.4 fusion.2
  101.0 0.2 copy.18
  101.2 0.0 copy-start.1
  101.2 1.3 copy-done.1
  102.5 0.1 slice.33
  102.6 0.6 gather_fusion.1
  103.2 2.0 %fusion.8 = f32[256,2,384]{2,0,1:T(8,128)S(1)} fusion(f32[2,256,256]{2,1,0:T(8,128)} %param.15, f32[256,5,384]{2,0,1:T(8,128)} %bitcast.49, f32[2,256,384]{2,1,0:T(8,128)S(1)} %gather_fusion.1, f32[2,384]{1,0:T(2,128)S(1)} %broadcast_select_fusion, pred[2]{0:T(512)(128)(4,1)S(1)} %compare_and_fusion), kind=kOutput, calls=%fused_computation.12 | convolution fusion | flops 302579712 | bytes 2886658 | tf_op jit(solution)/shard_map/cqk,qci->kci/dot_general | solution.py:123
  105.2 0.1 pad_maximum_fusion
  105.3 0.2 constant_dynamic-slice_fusion.1
  105.5 0.0 copy-start.2
  105.5 1.0 fusion.10
  106.5 3.5 %collective-permute-start.16 = (f32[8,16,5,384]{3,1,2,0:T(8,128)}, f32[8,16,5,384]{3,1,2,0:T(8,128)S(1)}, u32[]{:S(2)}, u32[]{:S(2)}) collective-permute-start(f32[8,16,5,384]{3,1,2,0:T(8,128)} %fusion.10), channel_id=1, source_target_pairs={{0,1},{1,0},{2,3},{3,2},{4,5},{5,4},{6,7},{7,6},{8,9},{9,8},{10,11... | collective-permute-start | bytes 2949128 | tf_op jit(solution)/shard_map/ppermute | solution.py:84
  110.0 2.4 %collective-permute-done.16 = f32[8,16,5,384]{3,1,2,0:T(8,128)S(1)} collective-permute-done((f32[8,16,5,384]{3,1,2,0:T(8,128)}, f32[8,16,5,384]{3,1,2,0:T(8,128)S(1)}, u32[]{:S(2)}, u32[]{:S(2)}) %collective-permute-start.16) | collective-permute-done | bytes 983072 | tf_op jit(solution)/shard_map/ppermute | solution.py:84
  112.4 1.1 fusion.12
  113.5 6.3 %all-to-all-start = ((f32[8,16,5,384]{3,1,2,0:T(8,128)}), f32[8,16,5,384]{3,1,2,0:T(8,128)S(1)}, u32[]{:S(2)}, u32[]{:S(2)}) async-start(f32[8,16,5,384]{3,1,2,0:T(8,128)} %fusion.12), calls=%async_computation | async-start | bytes 1966080 | tf_op jit(solution)/shard_map/all_to_all | solution.py:86
  119.8 0.1 compare_reduce_fusion.3
  119.9 13.7 %all-to-all-done = f32[8,16,5,384]{3,1,2,0:T(8,128)S(1)} async-done(((f32[8,16,5,384]{3,1,2,0:T(8,128)}), f32[8,16,5,384]{3,1,2,0:T(8,128)S(1)}, u32[]{:S(2)}, u32[]{:S(2)}) %all-to-all-start) | async-done | bytes 983072 | tf_op jit(solution)/shard_map/all_to_all | solution.py:86
  133.6 0.1 reduce_sum.9
  133.6 0.6 slice_multiply_fusion
  134.3 0.6 slice_multiply_fusion.1
  (25 shorter events, 0.4 us)
Async XLA Ops:
  0.6 96.7 %copy-start = (f32[384,768]{1,0:T(8,128)S(1)}, f32[384,768]{1,0:T(8,128)}, u32[]{:S(2)}) copy-start(f32[384,768]{1,0:T(8,128)} %param.9) | copy-start | bytes 3538948
  2.4 6.7 %collective-permute-start = (f32[8,3840]{1,0:T(8,128)S(1)}, f32[8,3840]{1,0:T(8,128)S(1)}, u32[]{:S(2)}, u32[]{:S(2)}) collective-permute-start(f32[8,3840]{1,0:T(8,128)S(1)} %bitcast.51), channel_id=1, source_target_pairs={{0,256},{16,272},{32,288},{48,304},{64,320},{80,336},{96,352},{112... | collective-permute-start | bytes 368648 | tf_op jit(solution)/shard_map/ppermute | solution.py:33
  9.1 20.6 %collective-permute-start.2 = (f32[2,8,3840]{2,1,0:T(8,128)S(1)}, f32[2,8,3840]{2,1,0:T(8,128)S(1)}, u32[]{:S(2)}, u32[]{:S(2)}) collective-permute-start(f32[2,8,3840]{2,1,0:T(8,128)S(1)} %maximum_select_fusion.1), channel_id=1, source_target_pairs={{0,224},{16,240},{32,0},{48,16},{64,32},{80,48},{96,64},{112,80},{... | collective-permute-start | bytes 737288 | tf_op jit(solution)/shard_map/ppermute | solution.py:46
  21.0 16.2 %collective-permute-start.8 = (f32[2,8,3840]{2,1,0:T(8,128)S(1)}, f32[2,8,3840]{2,1,0:T(8,128)S(1)}, u32[]{:S(2)}, u32[]{:S(2)}) collective-permute-start(f32[2,8,3840]{2,1,0:T(8,128)S(1)} %maximum_select_fusion.1), channel_id=1, source_target_pairs={{0,32},{16,48},{32,64},{48,80},{64,96},{80,112},{96,128},{112,144}... | collective-permute-start | bytes 737288 | tf_op jit(solution)/shard_map/ppermute | solution.py:43
  23.8 29.0 %collective-permute-start.1 = (f32[2,8,3840]{2,1,0:T(8,128)S(1)}, f32[2,8,3840]{2,1,0:T(8,128)S(1)}, u32[]{:S(2)}, u32[]{:S(2)}) collective-permute-start(f32[2,8,3840]{2,1,0:T(8,128)S(1)} %maximum_select_fusion.1), channel_id=1, source_target_pairs={{0,240},{16,0},{32,16},{48,32},{64,48},{80,64},{96,80},{112,96},{1... | collective-permute-start | bytes 737288 | tf_op jit(solution)/shard_map/ppermute | solution.py:42
  29.7 16.8 %collective-permute-start.4 = (f32[2,8,3840]{2,1,0:T(8,128)S(1)}, f32[2,8,3840]{2,1,0:T(8,128)S(1)}, u32[]{:S(2)}, u32[]{:S(2)}) collective-permute-start(f32[2,8,3840]{2,1,0:T(8,128)S(1)} %collective-permute-done.2), channel_id=1, source_target_pairs={{0,224},{16,240},{32,0},{48,16},{64,32},{80,48},{96,64},{112,80},{... | collective-permute-start | bytes 737288 | tf_op jit(solution)/shard_map/ppermute | solution.py:46
  37.2 17.5 %collective-permute-start.9 = (f32[2,8,3840]{2,1,0:T(8,128)S(1)}, f32[2,8,3840]{2,1,0:T(8,128)S(1)}, u32[]{:S(2)}, u32[]{:S(2)}) collective-permute-start(f32[2,8,3840]{2,1,0:T(8,128)S(1)} %collective-permute-done.8), channel_id=1, source_target_pairs={{0,32},{16,48},{32,64},{48,80},{64,96},{80,112},{96,128},{112,144}... | collective-permute-start | bytes 737288 | tf_op jit(solution)/shard_map/ppermute | solution.py:43
  39.2 58.0 %collective-permute-start.15 = (f32[2,8,3840]{2,1,0:T(8,128)S(1)}, f32[2,8,3840]{2,1,0:T(8,128)S(1)}, u32[]{:S(2)}, u32[]{:S(2)}) collective-permute-start(f32[2,8,3840]{2,1,0:T(8,128)S(1)} %maximum_select_fusion.1), channel_id=1, source_target_pairs={{0,16},{16,32},{32,48},{48,64},{64,80},{80,96},{96,112},{112,128},... | collective-permute-start | bytes 737288 | tf_op jit(solution)/shard_map/ppermute | solution.py:41
  42.1 14.6 %collective-permute-start.3 = (f32[2,8,3840]{2,1,0:T(8,128)S(1)}, f32[2,8,3840]{2,1,0:T(8,128)S(1)}, u32[]{:S(2)}, u32[]{:S(2)}) collective-permute-start(f32[2,8,3840]{2,1,0:T(8,128)S(1)} %collective-permute-done.2), channel_id=1, source_target_pairs={{0,240},{16,0},{32,16},{48,32},{64,48},{80,64},{96,80},{112,96},{1... | collective-permute-start | bytes 737288 | tf_op jit(solution)/shard_map/ppermute | solution.py:42
  46.5 15.6 %collective-permute-start.6 = (f32[2,8,3840]{2,1,0:T(8,128)S(1)}, f32[2,8,3840]{2,1,0:T(8,128)S(1)}, u32[]{:S(2)}, u32[]{:S(2)}) collective-permute-start(f32[2,8,3840]{2,1,0:T(8,128)S(1)} %collective-permute-done.4), channel_id=1, source_target_pairs={{0,224},{16,240},{32,0},{48,16},{64,32},{80,48},{96,64},{112,80},{... | collective-permute-start | bytes 737288 | tf_op jit(solution)/shard_map/ppermute | solution.py:46
  52.8 15.7 %collective-permute-start.5 = (f32[2,8,3840]{2,1,0:T(8,128)S(1)}, f32[2,8,3840]{2,1,0:T(8,128)S(1)}, u32[]{:S(2)}, u32[]{:S(2)}) collective-permute-start(f32[2,8,3840]{2,1,0:T(8,128)S(1)} %collective-permute-done.4), channel_id=1, source_target_pairs={{0,240},{16,0},{32,16},{48,32},{64,48},{80,64},{96,80},{112,96},{1... | collective-permute-start | bytes 737288 | tf_op jit(solution)/shard_map/ppermute | solution.py:42
  54.7 11.8 %collective-permute-start.10 = (f32[2,8,3840]{2,1,0:T(8,128)S(1)}, f32[2,8,3840]{2,1,0:T(8,128)S(1)}, u32[]{:S(2)}, u32[]{:S(2)}) collective-permute-start(f32[2,8,3840]{2,1,0:T(8,128)S(1)} %collective-permute-done.9), channel_id=1, source_target_pairs={{0,32},{16,48},{32,64},{48,80},{64,96},{80,112},{96,128},{112,144}... | collective-permute-start | bytes 737288 | tf_op jit(solution)/shard_map/ppermute | solution.py:43
  56.7 40.5 %collective-permute-start.14 = (f32[2,8,3840]{2,1,0:T(8,128)S(1)}, f32[2,8,3840]{2,1,0:T(8,128)S(1)}, u32[]{:S(2)}, u32[]{:S(2)}) collective-permute-start(f32[2,8,3840]{2,1,0:T(8,128)S(1)} %collective-permute-done.8), channel_id=1, source_target_pairs={{0,16},{16,32},{32,48},{48,64},{64,80},{80,96},{96,112},{112,128},... | collective-permute-start | bytes 737288 | tf_op jit(solution)/shard_map/ppermute | solution.py:41
  62.1 11.5 %collective-permute-start.7 = (f32[2,8,3840]{2,1,0:T(8,128)S(1)}, f32[2,8,3840]{2,1,0:T(8,128)S(1)}, u32[]{:S(2)}, u32[]{:S(2)}) collective-permute-start(f32[2,8,3840]{2,1,0:T(8,128)S(1)} %collective-permute-done.6), channel_id=1, source_target_pairs={{0,240},{16,0},{32,16},{48,32},{64,48},{80,64},{96,80},{112,96},{1... | collective-permute-start | bytes 737288 | tf_op jit(solution)/shard_map/ppermute | solution.py:42
  66.5 18.1 %collective-permute-start.11 = (f32[2,8,3840]{2,1,0:T(8,128)S(1)}, f32[2,8,3840]{2,1,0:T(8,128)S(1)}, u32[]{:S(2)}, u32[]{:S(2)}) collective-permute-start(f32[2,8,3840]{2,1,0:T(8,128)S(1)} %collective-permute-done.10), channel_id=1, source_target_pairs={{0,32},{16,48},{32,64},{48,80},{64,96},{80,112},{96,128},{112,144}... | collective-permute-start | bytes 737288 | tf_op jit(solution)/shard_map/ppermute | solution.py:43
  68.5 23.3 %collective-permute-start.12 = (f32[2,8,3840]{2,1,0:T(8,128)S(1)}, f32[2,8,3840]{2,1,0:T(8,128)S(1)}, u32[]{:S(2)}, u32[]{:S(2)}) collective-permute-start(f32[2,8,3840]{2,1,0:T(8,128)S(1)} %collective-permute-done.10), channel_id=1, source_target_pairs={{0,16},{16,32},{32,48},{48,64},{64,80},{80,96},{96,112},{112,128},... | collective-permute-start | bytes 737288 | tf_op jit(solution)/shard_map/ppermute | solution.py:41
  73.6 23.5 %collective-permute-start.13 = (f32[2,8,3840]{2,1,0:T(8,128)S(1)}, f32[2,8,3840]{2,1,0:T(8,128)S(1)}, u32[]{:S(2)}, u32[]{:S(2)}) collective-permute-start(f32[2,8,3840]{2,1,0:T(8,128)S(1)} %collective-permute-done.9), channel_id=1, source_target_pairs={{0,16},{16,32},{32,48},{48,64},{64,80},{80,96},{96,112},{112,128},... | collective-permute-start | bytes 737288 | tf_op jit(solution)/shard_map/ppermute | solution.py:41
  101.2 1.3 copy-start.1
  105.5 14.3 %copy-start.2 = (s32[2,36]{1,0:T(2,128)S(1)}, s32[2,36]{1,0:T(2,128)}, u32[]{:S(2)}) copy-start(s32[2,36]{1,0:T(2,128)} %param.13) | copy-start | bytes 868
  106.5 5.9 %collective-permute-start.16 = (f32[8,16,5,384]{3,1,2,0:T(8,128)}, f32[8,16,5,384]{3,1,2,0:T(8,128)S(1)}, u32[]{:S(2)}, u32[]{:S(2)}) collective-permute-start(f32[8,16,5,384]{3,1,2,0:T(8,128)} %fusion.10), channel_id=1, source_target_pairs={{0,1},{1,0},{2,3},{3,2},{4,5},{5,4},{6,7},{7,6},{8,9},{9,8},{10,11... | collective-permute-start | bytes 2949128 | tf_op jit(solution)/shard_map/ppermute | solution.py:84
  113.5 20.1 %all-to-all-start = ((f32[8,16,5,384]{3,1,2,0:T(8,128)}), f32[8,16,5,384]{3,1,2,0:T(8,128)S(1)}, u32[]{:S(2)}, u32[]{:S(2)}) async-start(f32[8,16,5,384]{3,1,2,0:T(8,128)} %fusion.12), calls=%async_computation | async-start | bytes 1966080 | tf_op jit(solution)/shard_map/all_to_all | solution.py:86

commit v14 on v12

--- a/solution.py
+++ b/solution.py
@@ -50,7 +50,10 @@
             last_up = lax.ppermute(lane_up[..., :half], "row", shift_pairs(n_row, nz, 1, 2))
             last_down = lax.ppermute(lane_down[..., half:], "row", shift_pairs(n_row, nz, 1, -2))
             pieces[nz // 2] = jnp.concatenate([last_up, last_down], axis=-1)
-    return jnp.stack(pieces), z
+    gathered = jnp.zeros((nz,) + pair.shape, pair.dtype)
+    for t, piece in enumerate(pieces):
+        gathered = lax.dynamic_update_index_in_dim(gathered, piece, (z + t) % nz, 0)
+    return gathered
 
 
 def reduce_cols(value, n_col):
@@ -108,7 +111,7 @@
     out_second = tile_flags(lists_second, row_anchor, local_rows, panel_width)
     panels = jnp.concatenate([factors_first, factors_second], axis=0)
     stacked = jnp.transpose(panels, (1, 0, 2)).reshape(share_rows, members * local_cols)
-    pieces, z = gather_rows(stacked, n_row)
+    pieces = gather_rows(stacked, n_row)
     col_mask = jnp.concatenate(
         [
             tile_flags(lists_first, col_anchor, local_cols, panel_width),
@@ -120,7 +123,6 @@
     partial_value = jnp.einsum(
         "tlkmj,ij->ltkmi", pieces, anc_inv, precision=high, preferred_element_type=jnp.float32
     )
-    partial_value = jnp.roll(partial_value, z, axis=1)
     partial_value = partial_value.reshape(panel_width, members, local_rows)
     first_partial = partial_value[:, :n_first]
     chosen = jnp.take(first_partial, parents, axis=1)

time: 135 us -> 146 us (1.081)
  waiting for transfers between devices: 28.7 us -> 45.7 us
  starting transfers between devices: 85.9 us -> 79.5 us
    ppermute x3, starting transfers between devices: 23.3 us -> 9.83 us  [gather_rows(): lane_down = lax.ppermute(lane_down, 'row', shift_pairs(n_row, nz, 1, -2))]
    ppermute x3, waiting for transfers between devices: 0.01 us -> 13 us  [gather_rows(): lane_up = lax.ppermute(lane_up, 'row', shift_pairs(n_row, nz, 1, 2))]
    ppermute x4, starting transfers between devices: 16.5 us -> 27.2 us  [gather_rows(): lax.ppermute(lane_down, 'row', shift_pairs(n_row, nz, 1, -1))]
    ppermute x4, starting transfers between devices: 14.3 us -> 10.2 us  [gather_rows(): lax.ppermute(lane_up, 'row', shift_pairs(n_row, nz, 1, 1))]
    ppermute x3, waiting for transfers between devices: 5.42 us -> 8.6 us  [gather_rows(): lane_down = lax.ppermute(lane_down, 'row', shift_pairs(n_row, nz, 1, -2))]
    ppermute x4, waiting for transfers between devices: 0.01 us -> 3.05 us  [gather_rows(): lax.ppermute(lane_down, 'row', shift_pairs(n_row, nz, 1, -1))]
    ppermute x3, starting transfers between devices: 5.76 us -> 8.71 us  [gather_rows(): lane_up = lax.ppermute(lane_up, 'row', shift_pairs(n_row, nz, 1, 2))]
    ppermute x1, waiting for transfers between devices: 2.51 us -> 0.01 us  [gather_rows(): lax.ppermute(lane_up[..., :half], 'row', shift_pairs(n_row, nz, 1, 2))]
where the time goes in v14:
time: 146 us; the launch traced here: 145 us
  starting transfers between devices  79.5 us (54%)
  waiting for transfers between devices  45.7 us (31%)
  other arithmetic  7.54 us (5%)
  local copies, waits for them, and re-layouts  5.37 us (4%)
  matrix products  5.22 us (4%)
  between operations  1.53 us (1%)
    ppermute x4, starting transfers between devices, gather_rows(): lax.ppermute(lane_down, 'row', shift_pairs(n_row, nz, 1, -1))  27.2 us
    all_to_all x1, waiting for transfers between devices, reduce_cols_a2a(): lax.all_to_all(summed, 'col', 0, 0, tiled=True, axis_index_groups=groups)  13.7 us
    ppermute x3, waiting for transfers between devices, gather_rows(): lane_up = lax.ppermute(lane_up, 'row', shift_pairs(n_row, nz, 1, 2))  13 us
    ppermute x4, starting transfers between devices, gather_rows(): lax.ppermute(lane_up, 'row', shift_pairs(n_row, nz, 1, 1))  10.2 us
    ppermute x3, starting transfers between devices, gather_rows(): lane_down = lax.ppermute(lane_down, 'row', shift_pairs(n_row, nz, 1, -2))  9.83 us
    ppermute x3, starting transfers between devices, gather_rows(): lane_up = lax.ppermute(lane_up, 'row', shift_pairs(n_row, nz, 1, 2))  8.71 us
    ppermute x3, waiting for transfers between devices, gather_rows(): lane_down = lax.ppermute(lane_down, 'row', shift_pairs(n_row, nz, 1, -2))  8.6 us
    all_to_all x1, starting transfers between devices, reduce_cols_a2a(): lax.all_to_all(summed, 'col', 0, 0, tiled=True, axis_index_groups=groups)  6.36 us
  transfers between devices with their start and end apart: 19, of which 7 were waited for; matrix products, arithmetic and copies ran while one was open for 4% of the time, Pallas kernels for 0%

profile of v14, /device:TPU:1, one launch (start us, length us, event | category | flops | bytes accessed | tf_op | source)
XLA Modules:
  0.0 144.9 jit_solution(14530119825921710391)
XLA Ops:
  0.6 0.0 copy-start
  0.6 1.0 constant_dynamic-update-slice_fusion.1
  1.6 0.8 constant_dynamic-update-slice_fusion
  2.4 3.9 %collective-permute-start = (f32[8,3840]{1,0:T(8,128)S(1)}, f32[8,3840]{1,0:T(8,128)S(1)}, u32[]{:S(2)}, u32[]{:S(2)}) collective-permute-start(f32[8,3840]{1,0:T(8,128)S(1)} %bitcast.70), channel_id=1, source_target_pairs={{0,256},{16,272},{32,288},{48,304},{64,320},{80,336},{96,352},{112... | collective-permute-start | bytes 368648 | tf_op jit(solution)/shard_map/ppermute | solution.py:33
  6.5 0.7 compare_select_fusion
  7.2 0.7 compare_and_fusion
  7.8 0.8 compare_reduce_fusion
  8.6 0.8 compare_reduce_fusion.1
  9.5 0.8 compare_reduce_fusion.2
  10.3 0.6 gather_fusion
  10.8 0.1 broadcast_select_fusion
  11.2 0.0 collective-permute-done
  11.2 11.1 %collective-permute-start.1 = (f32[2,8,3840]{2,1,0:T(8,128)S(1)}, f32[2,8,3840]{2,1,0:T(8,128)S(1)}, u32[]{:S(2)}, u32[]{:S(2)}) collective-permute-start(f32[2,8,3840]{2,1,0:T(8,128)S(1)} %maximum_select_fusion.1), channel_id=1, source_target_pairs={{0,240},{16,0},{32,16},{48,32},{64,48},{80,64},{96,80},{112,96},{1... | collective-permute-start | bytes 737288 | tf_op jit(solution)/shard_map/ppermute | solution.py:43
  22.3 3.1 %collective-permute-start.2 = (f32[2,8,3840]{2,1,0:T(8,128)S(1)}, f32[2,8,3840]{2,1,0:T(8,128)S(1)}, u32[]{:S(2)}, u32[]{:S(2)}) collective-permute-start(f32[2,8,3840]{2,1,0:T(8,128)S(1)} %maximum_select_fusion.1), channel_id=1, source_target_pairs={{0,224},{16,240},{32,0},{48,16},{64,32},{80,48},{96,64},{112,80},{... | collective-permute-start | bytes 737288 | tf_op jit(solution)/shard_map/ppermute | solution.py:46
  25.4 3.1 %collective-permute-start.8 = (f32[2,8,3840]{2,1,0:T(8,128)S(1)}, f32[2,8,3840]{2,1,0:T(8,128)S(1)}, u32[]{:S(2)}, u32[]{:S(2)}) collective-permute-start(f32[2,8,3840]{2,1,0:T(8,128)S(1)} %maximum_select_fusion.1), channel_id=1, source_target_pairs={{0,32},{16,48},{32,64},{48,80},{64,96},{80,112},{96,128},{112,144}... | collective-permute-start | bytes 737288 | tf_op jit(solution)/shard_map/ppermute | solution.py:45
  28.5 1.9 %collective-permute-start.16 = (f32[2,8,3840]{2,1,0:T(8,128)S(1)}, f32[2,8,3840]{2,1,0:T(8,128)S(1)}, u32[]{:S(2)}, u32[]{:S(2)}) collective-permute-start(f32[2,8,3840]{2,1,0:T(8,128)S(1)} %maximum_select_fusion.1), channel_id=1, source_target_pairs={{0,16},{16,32},{32,48},{48,64},{64,80},{80,96},{96,112},{112,128},... | collective-permute-start | bytes 737288 | tf_op jit(solution)/shard_map/ppermute | solution.py:42
  30.5 0.4 broadcast_in_dim.93
  30.9 3.8 %collective-permute-done.2 = f32[2,8,3840]{2,1,0:T(8,128)S(1)} collective-permute-done((f32[2,8,3840]{2,1,0:T(8,128)S(1)}, f32[2,8,3840]{2,1,0:T(8,128)S(1)}, u32[]{:S(2)}, u32[]{:S(2)}) %collective-permute-start.2) | collective-permute-done | bytes 245792 | tf_op jit(solution)/shard_map/ppermute | solution.py:46
  34.7 6.4 %collective-permute-start.3 = (f32[2,8,3840]{2,1,0:T(8,128)S(1)}, f32[2,8,3840]{2,1,0:T(8,128)S(1)}, u32[]{:S(2)}, u32[]{:S(2)}) collective-permute-start(f32[2,8,3840]{2,1,0:T(8,128)S(1)} %collective-permute-done.2), channel_id=1, source_target_pairs={{0,240},{16,0},{32,16},{48,32},{64,48},{80,64},{96,80},{112,96},{1... | collective-permute-start | bytes 737288 | tf_op jit(solution)/shard_map/ppermute | solution.py:43
  41.1 4.2 %collective-permute-start.4 = (f32[2,8,3840]{2,1,0:T(8,128)S(1)}, f32[2,8,3840]{2,1,0:T(8,128)S(1)}, u32[]{:S(2)}, u32[]{:S(2)}) collective-permute-start(f32[2,8,3840]{2,1,0:T(8,128)S(1)} %collective-permute-done.2), channel_id=1, source_target_pairs={{0,224},{16,240},{32,0},{48,16},{64,32},{80,48},{96,64},{112,80},{... | collective-permute-start | bytes 737288 | tf_op jit(solution)/shard_map/ppermute | solution.py:46
  45.3 0.0 collective-permute-done.8
  45.3 2.0 %collective-permute-start.9 = (f32[2,8,3840]{2,1,0:T(8,128)S(1)}, f32[2,8,3840]{2,1,0:T(8,128)S(1)}, u32[]{:S(2)}, u32[]{:S(2)}) collective-permute-start(f32[2,8,3840]{2,1,0:T(8,128)S(1)} %collective-permute-done.8), channel_id=1, source_target_pairs={{0,32},{16,48},{32,64},{48,80},{64,96},{80,112},{96,128},{112,144}... | collective-permute-start | bytes 737288 | tf_op jit(solution)/shard_map/ppermute | solution.py:45
  47.3 0.0 collective-permute-done.1
  47.3 3.3 %collective-permute-start.15 = (f32[2,8,3840]{2,1,0:T(8,128)S(1)}, f32[2,8,3840]{2,1,0:T(8,128)S(1)}, u32[]{:S(2)}, u32[]{:S(2)}) collective-permute-start(f32[2,8,3840]{2,1,0:T(8,128)S(1)} %collective-permute-done.8), channel_id=1, source_target_pairs={{0,16},{16,32},{32,48},{48,64},{64,80},{80,96},{96,112},{112,128},... | collective-permute-start | bytes 737288 | tf_op jit(solution)/shard_map/ppermute | solution.py:42
  50.7 4.8 %collective-permute-done.4 = f32[2,8,3840]{2,1,0:T(8,128)S(1)} collective-permute-done((f32[2,8,3840]{2,1,0:T(8,128)S(1)}, f32[2,8,3840]{2,1,0:T(8,128)S(1)}, u32[]{:S(2)}, u32[]{:S(2)}) %collective-permute-start.4) | collective-permute-done | bytes 245792 | tf_op jit(solution)/shard_map/ppermute | solution.py:46
  55.5 5.1 %collective-permute-start.5 = (f32[2,8,3840]{2,1,0:T(8,128)S(1)}, f32[2,8,3840]{2,1,0:T(8,128)S(1)}, u32[]{:S(2)}, u32[]{:S(2)}) collective-permute-start(f32[2,8,3840]{2,1,0:T(8,128)S(1)} %collective-permute-done.4), channel_id=1, source_target_pairs={{0,240},{16,0},{32,16},{48,32},{64,48},{80,64},{96,80},{112,96},{1... | collective-permute-start | bytes 737288 | tf_op jit(solution)/shard_map/ppermute | solution.py:43
  60.5 0.0 collective-permute-done.3
  60.6 2.6 %collective-permute-start.6 = (f32[2,8,3840]{2,1,0:T(8,128)S(1)}, f32[2,8,3840]{2,1,0:T(8,128)S(1)}, u32[]{:S(2)}, u32[]{:S(2)}) collective-permute-start(f32[2,8,3840]{2,1,0:T(8,128)S(1)} %collective-permute-done.4), channel_id=1, source_target_pairs={{0,224},{16,240},{32,0},{48,16},{64,32},{80,48},{96,64},{112,80},{... | collective-permute-start | bytes 737288 | tf_op jit(solution)/shard_map/ppermute | solution.py:46
  63.1 0.0 collective-permute-done.9
  63.1 3.6 %collective-permute-start.10 = (f32[2,8,3840]{2,1,0:T(8,128)S(1)}, f32[2,8,3840]{2,1,0:T(8,128)S(1)}, u32[]{:S(2)}, u32[]{:S(2)}) collective-permute-start(f32[2,8,3840]{2,1,0:T(8,128)S(1)} %collective-permute-done.9), channel_id=1, source_target_pairs={{0,32},{16,48},{32,64},{48,80},{64,96},{80,112},{96,128},{112,144}... | collective-permute-start | bytes 737288 | tf_op jit(solution)/shard_map/ppermute | solution.py:45
  66.8 13.0 %collective-permute-done.10 = f32[2,8,3840]{2,1,0:T(8,128)S(1)} collective-permute-done((f32[2,8,3840]{2,1,0:T(8,128)S(1)}, f32[2,8,3840]{2,1,0:T(8,128)S(1)}, u32[]{:S(2)}, u32[]{:S(2)}) %collective-permute-start.10) | collective-permute-done | bytes 245792 | tf_op jit(solution)/shard_map/ppermute | solution.py:45
  79.8 1.9 %collective-permute-start.14 = (f32[2,8,3840]{2,1,0:T(8,128)S(1)}, f32[2,8,3840]{2,1,0:T(8,128)S(1)}, u32[]{:S(2)}, u32[]{:S(2)}) collective-permute-start(f32[2,8,3840]{2,1,0:T(8,128)S(1)} %collective-permute-done.9), channel_id=1, source_target_pairs={{0,16},{16,32},{32,48},{48,64},{64,80},{80,96},{96,112},{112,128},... | collective-permute-start | bytes 737288 | tf_op jit(solution)/shard_map/ppermute | solution.py:42
  81.7 0.0 collective-permute-done.5
  81.7 1.9 %collective-permute-start.11 = (f32[2,8,1920]{2,1,0:T(8,128)S(1)}, f32[2,8,1920]{2,1,0:T(8,128)S(1)}, u32[]{:S(2)}, u32[]{:S(2)}) collective-permute-start(f32[2,8,1920]{2,1,0:T(8,128)S(1)} %slice.41), channel_id=1, source_target_pairs={{0,32},{16,48},{32,64},{48,80},{64,96},{80,112},{96,128},{112,144}... | collective-permute-start | bytes 368648 | tf_op jit(solution)/shard_map/ppermute | solution.py:50
  83.7 0.0 collective-permute-done.6
  83.7 4.6 %collective-permute-start.7 = (f32[2,8,3840]{2,1,0:T(8,128)S(1)}, f32[2,8,3840]{2,1,0:T(8,128)S(1)}, u32[]{:S(2)}, u32[]{:S(2)}) collective-permute-start(f32[2,8,3840]{2,1,0:T(8,128)S(1)} %collective-permute-done.6), channel_id=1, source_target_pairs={{0,240},{16,0},{32,16},{48,32},{64,48},{80,64},{96,80},{112,96},{1... | collective-permute-start | bytes 737288 | tf_op jit(solution)/shard_map/ppermute | solution.py:43
  88.3 3.0 %collective-permute-done.7 = f32[2,8,3840]{2,1,0:T(8,128)S(1)} collective-permute-done((f32[2,8,3840]{2,1,0:T(8,128)S(1)}, f32[2,8,3840]{2,1,0:T(8,128)S(1)}, u32[]{:S(2)}, u32[]{:S(2)}) %collective-permute-start.7) | collective-permute-done | bytes 245792 | tf_op jit(solution)/shard_map/ppermute | solution.py:43
  91.4 5.2 %collective-permute-start.12 = (f32[2,8,1920]{2,1,0:T(8,128)S(1)}, f32[2,8,1920]{2,1,0:T(8,128)S(1)}, u32[]{:S(2)}, u32[]{:S(2)}) collective-permute-start(f32[2,8,1920]{2,1,0:T(8,128)S(1)} %slice.42), channel_id=1, source_target_pairs={{0,224},{16,240},{32,0},{48,16},{64,32},{80,48},{96,64},{112,80},{... | collective-permute-start | bytes 368648 | tf_op jit(solution)/shard_map/ppermute | solution.py:51
  96.6 0.0 collective-permute-done.11
  96.6 3.1 %collective-permute-start.13 = (f32[2,8,3840]{2,1,0:T(8,128)S(1)}, f32[2,8,3840]{2,1,0:T(8,128)S(1)}, u32[]{:S(2)}, u32[]{:S(2)}) collective-permute-start(f32[2,8,3840]{2,1,0:T(8,128)S(1)} %collective-permute-done.10), channel_id=1, source_target_pairs={{0,16},{16,32},{32,48},{48,64},{64,80},{80,96},{96,112},{112,128},... | collective-permute-start | bytes 737288 | tf_op jit(solution)/shard_map/ppermute | solution.py:42
  99.7 0.0 collective-permute-done.12
  99.7 5.0 %collective-permute-done.13 = f32[2,8,3840]{2,1,0:T(8,128)S(1)} collective-permute-done((f32[2,8,3840]{2,1,0:T(8,128)S(1)}, f32[2,8,3840]{2,1,0:T(8,128)S(1)}, u32[]{:S(2)}, u32[]{:S(2)}) %collective-permute-start.13) | collective-permute-done | bytes 245792 | tf_op jit(solution)/shard_map/ppermute | solution.py:42
  104.8 0.0 collective-permute-done.14
  104.9 0.0 collective-permute-done.15
  105.0 0.0 collective-permute-done.16
  105.0 3.2 %fusion.3 = f32[2,16,8,5,384]{4,2,3,0,1:T(8,128)S(1)} fusion(f32[16,2,8,5,768]{4,2,3,1,0:T(8,128)S(1)} %bitcast.66, f32[5,768]{1,0:T(8,128)S(1)} %add_convert_fusion, f32[384,768]{1,0:T(8,128)S(1)} %copy-done), kind=kOutput, calls=%fused_computation.6 | convolution fusion | flops 2265907200 | bytes 7093248 | tf_op jit(solution)/shard_map/tlkmj,ij->ltkmi/dot_general | solution.py:123
  108.2 0.2 copy.18
  108.4 1.3 copy-done.1
  109.7 0.1 slice.43
  109.8 0.6 gather_fusion.1
  110.4 2.0 %fusion.7 = f32[256,2,384]{2,0,1:T(8,128)S(1)} fusion(f32[2,256,256]{2,1,0:T(8,128)} %param.15, f32[256,5,384]{2,0,1:T(8,128)} %bitcast.68, f32[2,256,384]{2,1,0:T(8,128)S(1)} %gather_fusion.1, f32[2,384]{1,0:T(2,128)S(1)} %broadcast_select_fusion, pred[2]{0:T(512)(128)(4,1)S(1)} %compare_and_fusion), kind=kOutput, calls=%fused_computation.9 | convolution fusion | flops 302579712 | bytes 2886658 | tf_op jit(solution)/shard_map/cqk,qci->kci/dot_general | solution.py:130
  112.4 0.1 pad_maximum_fusion
  112.5 0.2 constant_dynamic-slice_fusion.1
  112.7 0.0 copy-start.2
  112.7 1.0 fusion.9
  113.7 6.2 %collective-permute-start.17 = (f32[8,16,5,384]{3,1,2,0:T(8,128)}, f32[8,16,5,384]{3,1,2,0:T(8,128)S(1)}, u32[]{:S(2)}, u32[]{:S(2)}) collective-permute-start(f32[8,16,5,384]{3,1,2,0:T(8,128)} %fusion.9), channel_id=1, source_target_pairs={{0,1},{1,0},{2,3},{3,2},{4,5},{5,4},{6,7},{7,6},{8,9},{9,8},{10,11... | collective-permute-start | bytes 2949128 | tf_op jit(solution)/shard_map/ppermute | solution.py:92
  119.9 2.4 %collective-permute-done.17 = f32[8,16,5,384]{3,1,2,0:T(8,128)S(1)} collective-permute-done((f32[8,16,5,384]{3,1,2,0:T(8,128)}, f32[8,16,5,384]{3,1,2,0:T(8,128)S(1)}, u32[]{:S(2)}, u32[]{:S(2)}) %collective-permute-start.17) | collective-permute-done | bytes 983072 | tf_op jit(solution)/shard_map/ppermute | solution.py:92
  122.3 1.1 fusion.11
  123.4 6.4 %all-to-all-start = ((f32[8,16,5,384]{3,1,2,0:T(8,128)}), f32[8,16,5,384]{3,1,2,0:T(8,128)S(1)}, u32[]{:S(2)}, u32[]{:S(2)}) async-start(f32[8,16,5,384]{3,1,2,0:T(8,128)} %fusion.11), calls=%async_computation | async-start | bytes 1966080 | tf_op jit(solution)/shard_map/all_to_all | solution.py:94
  129.7 0.1 compare_reduce_fusion.3
  129.9 13.7 %all-to-all-done = f32[8,16,5,384]{3,1,2,0:T(8,128)S(1)} async-done(((f32[8,16,5,384]{3,1,2,0:T(8,128)}), f32[8,16,5,384]{3,1,2,0:T(8,128)S(1)}, u32[]{:S(2)}, u32[]{:S(2)}) %all-to-all-start) | async-done | bytes 983072 | tf_op jit(solution)/shard_map/all_to_all | solution.py:94
  143.6 0.1 reduce_sum.9
  143.6 0.6 slice_multiply_fusion
  144.3 0.6 slice_multiply_fusion.1
  (29 shorter events, 0.5 us)
Async XLA Ops:
  0.6 104.4 %copy-start = (f32[384,768]{1,0:T(8,128)S(1)}, f32[384,768]{1,0:T(8,128)}, u32[]{:S(2)}) copy-start(f32[384,768]{1,0:T(8,128)} %param.9) | copy-start | bytes 3538948
  2.4 8.7 %collective-permute-start = (f32[8,3840]{1,0:T(8,128)S(1)}, f32[8,3840]{1,0:T(8,128)S(1)}, u32[]{:S(2)}, u32[]{:S(2)}) collective-permute-start(f32[8,3840]{1,0:T(8,128)S(1)} %bitcast.70), channel_id=1, source_target_pairs={{0,256},{16,272},{32,288},{48,304},{64,320},{80,336},{96,352},{112... | collective-permute-start | bytes 368648 | tf_op jit(solution)/shard_map/ppermute | solution.py:33
  11.2 36.1 %collective-permute-start.1 = (f32[2,8,3840]{2,1,0:T(8,128)S(1)}, f32[2,8,3840]{2,1,0:T(8,128)S(1)}, u32[]{:S(2)}, u32[]{:S(2)}) collective-permute-start(f32[2,8,3840]{2,1,0:T(8,128)S(1)} %maximum_select_fusion.1), channel_id=1, source_target_pairs={{0,240},{16,0},{32,16},{48,32},{64,48},{80,64},{96,80},{112,96},{1... | collective-permute-start | bytes 737288 | tf_op jit(solution)/shard_map/ppermute | solution.py:43
  22.3 12.3 %collective-permute-start.2 = (f32[2,8,3840]{2,1,0:T(8,128)S(1)}, f32[2,8,3840]{2,1,0:T(8,128)S(1)}, u32[]{:S(2)}, u32[]{:S(2)}) collective-permute-start(f32[2,8,3840]{2,1,0:T(8,128)S(1)} %maximum_select_fusion.1), channel_id=1, source_target_pairs={{0,224},{16,240},{32,0},{48,16},{64,32},{80,48},{96,64},{112,80},{... | collective-permute-start | bytes 737288 | tf_op jit(solution)/shard_map/ppermute | solution.py:46
  25.4 19.9 %collective-permute-start.8 = (f32[2,8,3840]{2,1,0:T(8,128)S(1)}, f32[2,8,3840]{2,1,0:T(8,128)S(1)}, u32[]{:S(2)}, u32[]{:S(2)}) collective-permute-start(f32[2,8,3840]{2,1,0:T(8,128)S(1)} %maximum_select_fusion.1), channel_id=1, source_target_pairs={{0,32},{16,48},{32,64},{48,80},{64,96},{80,112},{96,128},{112,144}... | collective-permute-start | bytes 737288 | tf_op jit(solution)/shard_map/ppermute | solution.py:45
  28.5 76.4 %collective-permute-start.16 = (f32[2,8,3840]{2,1,0:T(8,128)S(1)}, f32[2,8,3840]{2,1,0:T(8,128)S(1)}, u32[]{:S(2)}, u32[]{:S(2)}) collective-permute-start(f32[2,8,3840]{2,1,0:T(8,128)S(1)} %maximum_select_fusion.1), channel_id=1, source_target_pairs={{0,16},{16,32},{32,48},{48,64},{64,80},{80,96},{96,112},{112,128},... | collective-permute-start | bytes 737288 | tf_op jit(solution)/shard_map/ppermute | solution.py:42
  34.7 25.9 %collective-permute-start.3 = (f32[2,8,3840]{2,1,0:T(8,128)S(1)}, f32[2,8,3840]{2,1,0:T(8,128)S(1)}, u32[]{:S(2)}, u32[]{:S(2)}) collective-permute-start(f32[2,8,3840]{2,1,0:T(8,128)S(1)} %collective-permute-done.2), channel_id=1, source_target_pairs={{0,240},{16,0},{32,16},{48,32},{64,48},{80,64},{96,80},{112,96},{1... | collective-permute-start | bytes 737288 | tf_op jit(solution)/shard_map/ppermute | solution.py:43
  41.1 14.4 %collective-permute-start.4 = (f32[2,8,3840]{2,1,0:T(8,128)S(1)}, f32[2,8,3840]{2,1,0:T(8,128)S(1)}, u32[]{:S(2)}, u32[]{:S(2)}) collective-permute-start(f32[2,8,3840]{2,1,0:T(8,128)S(1)} %collective-permute-done.2), channel_id=1, source_target_pairs={{0,224},{16,240},{32,0},{48,16},{64,32},{80,48},{96,64},{112,80},{... | collective-permute-start | bytes 737288 | tf_op jit(solution)/shard_map/ppermute | solution.py:46
  45.3 17.8 %collective-permute-start.9 = (f32[2,8,3840]{2,1,0:T(8,128)S(1)}, f32[2,8,3840]{2,1,0:T(8,128)S(1)}, u32[]{:S(2)}, u32[]{:S(2)}) collective-permute-start(f32[2,8,3840]{2,1,0:T(8,128)S(1)} %collective-permute-done.8), channel_id=1, source_target_pairs={{0,32},{16,48},{32,64},{48,80},{64,96},{80,112},{96,128},{112,144}... | collective-permute-start | bytes 737288 | tf_op jit(solution)/shard_map/ppermute | solution.py:45
  47.3 57.6 %collective-permute-start.15 = (f32[2,8,3840]{2,1,0:T(8,128)S(1)}, f32[2,8,3840]{2,1,0:T(8,128)S(1)}, u32[]{:S(2)}, u32[]{:S(2)}) collective-permute-start(f32[2,8,3840]{2,1,0:T(8,128)S(1)} %collective-permute-done.8), channel_id=1, source_target_pairs={{0,16},{16,32},{32,48},{48,64},{64,80},{80,96},{96,112},{112,128},... | collective-permute-start | bytes 737288 | tf_op jit(solution)/shard_map/ppermute | solution.py:42
  55.5 26.3 %collective-permute-start.5 = (f32[2,8,3840]{2,1,0:T(8,128)S(1)}, f32[2,8,3840]{2,1,0:T(8,128)S(1)}, u32[]{:S(2)}, u32[]{:S(2)}) collective-permute-start(f32[2,8,3840]{2,1,0:T(8,128)S(1)} %collective-permute-done.4), channel_id=1, source_target_pairs={{0,240},{16,0},{32,16},{48,32},{64,48},{80,64},{96,80},{112,96},{1... | collective-permute-start | bytes 737288 | tf_op jit(solution)/shard_map/ppermute | solution.py:43
  60.6 23.1 %collective-permute-start.6 = (f32[2,8,3840]{2,1,0:T(8,128)S(1)}, f32[2,8,3840]{2,1,0:T(8,128)S(1)}, u32[]{:S(2)}, u32[]{:S(2)}) collective-permute-start(f32[2,8,3840]{2,1,0:T(8,128)S(1)} %collective-permute-done.4), channel_id=1, source_target_pairs={{0,224},{16,240},{32,0},{48,16},{64,32},{80,48},{96,64},{112,80},{... | collective-permute-start | bytes 737288 | tf_op jit(solution)/shard_map/ppermute | solution.py:46
  63.1 16.7 %collective-permute-start.10 = (f32[2,8,3840]{2,1,0:T(8,128)S(1)}, f32[2,8,3840]{2,1,0:T(8,128)S(1)}, u32[]{:S(2)}, u32[]{:S(2)}) collective-permute-start(f32[2,8,3840]{2,1,0:T(8,128)S(1)} %collective-permute-done.9), channel_id=1, source_target_pairs={{0,32},{16,48},{32,64},{48,80},{64,96},{80,112},{96,128},{112,144}... | collective-permute-start | bytes 737288 | tf_op jit(solution)/shard_map/ppermute | solution.py:45
  79.8 25.0 %collective-permute-start.14 = (f32[2,8,3840]{2,1,0:T(8,128)S(1)}, f32[2,8,3840]{2,1,0:T(8,128)S(1)}, u32[]{:S(2)}, u32[]{:S(2)}) collective-permute-start(f32[2,8,3840]{2,1,0:T(8,128)S(1)} %collective-permute-done.9), channel_id=1, source_target_pairs={{0,16},{16,32},{32,48},{48,64},{64,80},{80,96},{96,112},{112,128},... | collective-permute-start | bytes 737288 | tf_op jit(solution)/shard_map/ppermute | solution.py:42
  81.7 14.9 %collective-permute-start.11 = (f32[2,8,1920]{2,1,0:T(8,128)S(1)}, f32[2,8,1920]{2,1,0:T(8,128)S(1)}, u32[]{:S(2)}, u32[]{:S(2)}) collective-permute-start(f32[2,8,1920]{2,1,0:T(8,128)S(1)} %slice.41), channel_id=1, source_target_pairs={{0,32},{16,48},{32,64},{48,80},{64,96},{80,112},{96,128},{112,144}... | collective-permute-start | bytes 368648 | tf_op jit(solution)/shard_map/ppermute | solution.py:50
  83.7 7.7 %collective-permute-start.7 = (f32[2,8,3840]{2,1,0:T(8,128)S(1)}, f32[2,8,3840]{2,1,0:T(8,128)S(1)}, u32[]{:S(2)}, u32[]{:S(2)}) collective-permute-start(f32[2,8,3840]{2,1,0:T(8,128)S(1)} %collective-permute-done.6), channel_id=1, source_target_pairs={{0,240},{16,0},{32,16},{48,32},{64,48},{80,64},{96,80},{112,96},{1... | collective-permute-start | bytes 737288 | tf_op jit(solution)/shard_map/ppermute | solution.py:43
  91.4 8.3 %collective-permute-start.12 = (f32[2,8,1920]{2,1,0:T(8,128)S(1)}, f32[2,8,1920]{2,1,0:T(8,128)S(1)}, u32[]{:S(2)}, u32[]{:S(2)}) collective-permute-start(f32[2,8,1920]{2,1,0:T(8,128)S(1)} %slice.42), channel_id=1, source_target_pairs={{0,224},{16,240},{32,0},{48,16},{64,32},{80,48},{96,64},{112,80},{... | collective-permute-start | bytes 368648 | tf_op jit(solution)/shard_map/ppermute | solution.py:51
  96.6 8.2 %collective-permute-start.13 = (f32[2,8,3840]{2,1,0:T(8,128)S(1)}, f32[2,8,3840]{2,1,0:T(8,128)S(1)}, u32[]{:S(2)}, u32[]{:S(2)}) collective-permute-start(f32[2,8,3840]{2,1,0:T(8,128)S(1)} %collective-permute-done.10), channel_id=1, source_target_pairs={{0,16},{16,32},{32,48},{48,64},{64,80},{80,96},{96,112},{112,128},... | collective-permute-start | bytes 737288 | tf_op jit(solution)/shard_map/ppermute | solution.py:42
  108.4 1.3 copy-start.1
  112.7 17.0 %copy-start.2 = (s32[2,36]{1,0:T(2,128)S(1)}, s32[2,36]{1,0:T(2,128)}, u32[]{:S(2)}) copy-start(s32[2,36]{1,0:T(2,128)} %param.13) | copy-start | bytes 868
  113.7 8.6 %collective-permute-start.17 = (f32[8,16,5,384]{3,1,2,0:T(8,128)}, f32[8,16,5,384]{3,1,2,0:T(8,128)S(1)}, u32[]{:S(2)}, u32[]{:S(2)}) collective-permute-start(f32[8,16,5,384]{3,1,2,0:T(8,128)} %fusion.9), channel_id=1, source_target_pairs={{0,1},{1,0},{2,3},{3,2},{4,5},{5,4},{6,7},{7,6},{8,9},{9,8},{10,11... | collective-permute-start | bytes 2949128 | tf_op jit(solution)/shard_map/ppermute | solution.py:92
  123.4 20.2 %all-to-all-start = ((f32[8,16,5,384]{3,1,2,0:T(8,128)}), f32[8,16,5,384]{3,1,2,0:T(8,128)S(1)}, u32[]{:S(2)}, u32[]{:S(2)}) async-start(f32[8,16,5,384]{3,1,2,0:T(8,128)} %fusion.11), calls=%async_computation | async-start | bytes 1966080 | tf_op jit(solution)/shard_map/all_to_all | solution.py:94

commit v15 on v12

--- a/solution.py
+++ b/solution.py
@@ -31,7 +31,7 @@
     x_lo = r // nz
     z = r % nz
     partner = lax.ppermute(block, "row", [(p, (p + nz) % n_row) for p in range(n_row)])
-    pair = jnp.where(x_lo == 0, jnp.stack([block, partner]), jnp.stack([partner, block]))
+    pair = jnp.stack([block, partner])
     pieces = [None] * nz
     pieces[0] = pair
     steps = nz // 4
@@ -50,7 +50,7 @@
             last_up = lax.ppermute(lane_up[..., :half], "row", shift_pairs(n_row, nz, 1, 2))
             last_down = lax.ppermute(lane_down[..., half:], "row", shift_pairs(n_row, nz, 1, -2))
             pieces[nz // 2] = jnp.concatenate([last_up, last_down], axis=-1)
-    return jnp.stack(pieces), z
+    return jnp.stack(pieces), z, x_lo
 
 
 def reduce_cols(value, n_col):
@@ -108,7 +108,7 @@
     out_second = tile_flags(lists_second, row_anchor, local_rows, panel_width)
     panels = jnp.concatenate([factors_first, factors_second], axis=0)
     stacked = jnp.transpose(panels, (1, 0, 2)).reshape(share_rows, members * local_cols)
-    pieces, z = gather_rows(stacked, n_row)
+    pieces, z, x_lo = gather_rows(stacked, n_row)
     col_mask = jnp.concatenate(
         [
             tile_flags(lists_first, col_anchor, local_cols, panel_width),
@@ -120,7 +120,11 @@
     partial_value = jnp.einsum(
         "tlkmj,ij->ltkmi", pieces, anc_inv, precision=high, preferred_element_type=jnp.float32
     )
-    partial_value = jnp.roll(partial_value, z, axis=1)
+    source = jnp.arange(X_LO * nz)
+    slot = (source // nz) ^ x_lo
+    offset = (source % nz - z) % nz
+    partial_value = partial_value.reshape(X_LO * nz, *partial_value.shape[2:])
+    partial_value = jnp.take(partial_value, slot * nz + offset, axis=0)
     partial_value = partial_value.reshape(panel_width, members, local_rows)
     first_partial = partial_value[:, :n_first]
     chosen = jnp.take(first_partial, parents, axis=1)

time: 135 us -> 141 us (1.044)
  local copies, waits for them, and re-layouts: 4.95 us -> 7.07 us
  starting transfers between devices: 85.9 us -> 87.6 us
  other arithmetic: 7.92 us -> 9.35 us
    ppermute x3, waiting for transfers between devices: 5.42 us -> 0.21 us  [gather_rows(): lane_down = lax.ppermute(lane_down, 'row', shift_pairs(n_row, nz, 1, -2))]
    ppermute x4, starting transfers between devices: 14.3 us -> 18.2 us  [gather_rows(): lax.ppermute(lane_up, 'row', shift_pairs(n_row, nz, 1, 1))]
    ppermute x3, waiting for transfers between devices: 0.01 us -> 3.76 us  [gather_rows(): lane_up = lax.ppermute(lane_up, 'row', shift_pairs(n_row, nz, 1, 2))]
    ppermute x1, waiting for transfers between devices: 2.51 us -> 4.54 us  [gather_rows(): lax.ppermute(lane_up[..., :half], 'row', shift_pairs(n_row, nz, 1, 2))]
    ppermute x4, waiting for transfers between devices: 0.01 us -> 2.01 us  [gather_rows(): lax.ppermute(lane_down, 'row', shift_pairs(n_row, nz, 1, -1))]
    gather x0 -> x1, local copies, waits for them, and re-layouts: none -> 1.97 us  [local(): partial_value = jnp.take(partial_value, slot * nz + offset, axis=0)]
    ppermute x4, starting transfers between devices: 16.5 us -> 14.6 us  [gather_rows(): lax.ppermute(lane_down, 'row', shift_pairs(n_row, nz, 1, -1))]
    select_n x1 -> x2, other arithmetic: 0.02 us -> 1.79 us  [local(): partial_value = jnp.take(partial_value, slot * nz + offset, axis=0)]
where the time goes in v15:
time: 141 us; the launch traced here: 140 us
  starting transfers between devices  87.6 us (62%)
  waiting for transfers between devices  29.3 us (21%)
  other arithmetic  9.35 us (7%)
  local copies, waits for them, and re-layouts  7.07 us (5%)
  matrix products  5.33 us (4%)
    ppermute x3, starting transfers between devices, gather_rows(): lane_down = lax.ppermute(lane_down, 'row', shift_pairs(n_row, nz, 1, -2))  22.8 us
    ppermute x4, starting transfers between devices, gather_rows(): lax.ppermute(lane_up, 'row', shift_pairs(n_row, nz, 1, 1))  18.2 us
    ppermute x4, starting transfers between devices, gather_rows(): lax.ppermute(lane_down, 'row', shift_pairs(n_row, nz, 1, -1))  14.6 us
    all_to_all x1, waiting for transfers between devices, reduce_cols_a2a(): lax.all_to_all(summed, 'col', 0, 0, tiled=True, axis_index_groups=groups)  13.7 us
    ppermute x1, starting transfers between devices, reduce_cols_a2a(): lax.ppermute(send, 'col', partner_pairs)  8.65 us
    all_to_all x1, starting transfers between devices, reduce_cols_a2a(): lax.all_to_all(summed, 'col', 0, 0, tiled=True, axis_index_groups=groups)  6.35 us
    ppermute x3, starting transfers between devices, gather_rows(): lane_up = lax.ppermute(lane_up, 'row', shift_pairs(n_row, nz, 1, 2))  5.76 us
    ppermute x1, starting transfers between devices, gather_rows(): lax.ppermute(lane_down[..., half:], 'row', shift_pairs(n_row, nz, 1, -2))  5.47 us
  transfers between devices with their start and end apart: 19, of which 7 were waited for; matrix products, arithmetic and copies ran while one was open for 4% of the time, Pallas kernels for 0%

profile of v15, /device:TPU:1, one launch (start us, length us, event | category | flops | bytes accessed | tf_op | source)
XLA Modules:
  0.0 139.9 jit_solution(1448708019997337982)
XLA Ops:
  0.6 0.0 copy-start
  0.6 1.0 constant_dynamic-update-slice_fusion.1
  1.6 0.8 constant_dynamic-update-slice_fusion
  2.4 3.9 %collective-permute-start = (f32[8,3840]{1,0:T(8,128)S(1)}, f32[8,3840]{1,0:T(8,128)S(1)}, u32[]{:S(2)}, u32[]{:S(2)}) collective-permute-start(f32[8,3840]{1,0:T(8,128)S(1)} %bitcast.55), channel_id=1, source_target_pairs={{0,256},{16,272},{32,288},{48,304},{64,320},{80,336},{96,352},{112... | collective-permute-start | bytes 368648 | tf_op jit(solution)/shard_map/ppermute | solution.py:33
  6.4 0.7 compare_select_fusion
  7.1 0.7 compare_and_fusion
  7.7 0.8 compare_reduce_fusion.2
  8.6 0.6 gather_fusion.1
  9.1 0.1 broadcast_select_fusion
  9.2 0.0 collective-permute-done
  9.3 11.7 %collective-permute-start.2 = (f32[2,8,3840]{2,1,0:T(8,128)S(1)}, f32[2,8,3840]{2,1,0:T(8,128)S(1)}, u32[]{:S(2)}, u32[]{:S(2)}) collective-permute-start(f32[2,8,3840]{2,1,0:T(8,128)S(1)} %pad_maximum_fusion.1), channel_id=1, source_target_pairs={{0,224},{16,240},{32,0},{48,16},{64,32},{80,48},{96,64},{112,80},{... | collective-permute-start | bytes 737288 | tf_op jit(solution)/shard_map/ppermute | solution.py:46
  20.9 1.9 %collective-permute-start.8 = (f32[2,8,3840]{2,1,0:T(8,128)S(1)}, f32[2,8,3840]{2,1,0:T(8,128)S(1)}, u32[]{:S(2)}, u32[]{:S(2)}) collective-permute-start(f32[2,8,3840]{2,1,0:T(8,128)S(1)} %pad_maximum_fusion.1), channel_id=1, source_target_pairs={{0,32},{16,48},{32,64},{48,80},{64,96},{80,112},{96,128},{112,144}... | collective-permute-start | bytes 737288 | tf_op jit(solution)/shard_map/ppermute | solution.py:45
  22.9 0.8 compare_reduce_fusion.1
  23.7 0.8 compare_reduce_fusion
  24.5 5.0 %collective-permute-start.1 = (f32[2,8,3840]{2,1,0:T(8,128)S(1)}, f32[2,8,3840]{2,1,0:T(8,128)S(1)}, u32[]{:S(2)}, u32[]{:S(2)}) collective-permute-start(f32[2,8,3840]{2,1,0:T(8,128)S(1)} %pad_maximum_fusion.1), channel_id=1, source_target_pairs={{0,240},{16,0},{32,16},{48,32},{64,48},{80,64},{96,80},{112,96},{1... | collective-permute-start | bytes 737288 | tf_op jit(solution)/shard_map/ppermute | solution.py:43
  29.5 0.2 collective-permute-done.2
  29.7 6.7 %collective-permute-start.4 = (f32[2,8,3840]{2,1,0:T(8,128)S(1)}, f32[2,8,3840]{2,1,0:T(8,128)S(1)}, u32[]{:S(2)}, u32[]{:S(2)}) collective-permute-start(f32[2,8,3840]{2,1,0:T(8,128)S(1)} %collective-permute-done.2), channel_id=1, source_target_pairs={{0,224},{16,240},{32,0},{48,16},{64,32},{80,48},{96,64},{112,80},{... | collective-permute-start | bytes 737288 | tf_op jit(solution)/shard_map/ppermute | solution.py:46
  36.4 0.0 collective-permute-done.8
  36.4 1.9 %collective-permute-start.9 = (f32[2,8,3840]{2,1,0:T(8,128)S(1)}, f32[2,8,3840]{2,1,0:T(8,128)S(1)}, u32[]{:S(2)}, u32[]{:S(2)}) collective-permute-start(f32[2,8,3840]{2,1,0:T(8,128)S(1)} %collective-permute-done.8), channel_id=1, source_target_pairs={{0,32},{16,48},{32,64},{48,80},{64,96},{80,112},{96,128},{112,144}... | collective-permute-start | bytes 737288 | tf_op jit(solution)/shard_map/ppermute | solution.py:45
  38.4 0.1 broadcast_in_dim.57
  38.5 0.1 broadcast_in_dim.58
  38.6 3.6 %collective-permute-start.16 = (f32[2,8,3840]{2,1,0:T(8,128)S(1)}, f32[2,8,3840]{2,1,0:T(8,128)S(1)}, u32[]{:S(2)}, u32[]{:S(2)}) collective-permute-start(f32[2,8,3840]{2,1,0:T(8,128)S(1)} %pad_maximum_fusion.1), channel_id=1, source_target_pairs={{0,16},{16,32},{32,48},{48,64},{64,80},{80,96},{96,112},{112,128},... | collective-permute-start | bytes 737288 | tf_op jit(solution)/shard_map/ppermute | solution.py:42
  42.2 4.3 %collective-permute-start.3 = (f32[2,8,3840]{2,1,0:T(8,128)S(1)}, f32[2,8,3840]{2,1,0:T(8,128)S(1)}, u32[]{:S(2)}, u32[]{:S(2)}) collective-permute-start(f32[2,8,3840]{2,1,0:T(8,128)S(1)} %collective-permute-done.2), channel_id=1, source_target_pairs={{0,240},{16,0},{32,16},{48,32},{64,48},{80,64},{96,80},{112,96},{1... | collective-permute-start | bytes 737288 | tf_op jit(solution)/shard_map/ppermute | solution.py:43
  46.6 0.0 collective-permute-done.1
  46.6 0.0 collective-permute-done.4
  46.6 3.4 %collective-permute-start.5 = (f32[2,8,3840]{2,1,0:T(8,128)S(1)}, f32[2,8,3840]{2,1,0:T(8,128)S(1)}, u32[]{:S(2)}, u32[]{:S(2)}) collective-permute-start(f32[2,8,3840]{2,1,0:T(8,128)S(1)} %collective-permute-done.4), channel_id=1, source_target_pairs={{0,240},{16,0},{32,16},{48,32},{64,48},{80,64},{96,80},{112,96},{1... | collective-permute-start | bytes 737288 | tf_op jit(solution)/shard_map/ppermute | solution.py:43
  50.0 4.4 %collective-permute-start.6 = (f32[2,8,3840]{2,1,0:T(8,128)S(1)}, f32[2,8,3840]{2,1,0:T(8,128)S(1)}, u32[]{:S(2)}, u32[]{:S(2)}) collective-permute-start(f32[2,8,3840]{2,1,0:T(8,128)S(1)} %collective-permute-done.4), channel_id=1, source_target_pairs={{0,224},{16,240},{32,0},{48,16},{64,32},{80,48},{96,64},{112,80},{... | collective-permute-start | bytes 737288 | tf_op jit(solution)/shard_map/ppermute | solution.py:46
  54.4 1.9 %collective-permute-start.10 = (f32[2,8,3840]{2,1,0:T(8,128)S(1)}, f32[2,8,3840]{2,1,0:T(8,128)S(1)}, u32[]{:S(2)}, u32[]{:S(2)}) collective-permute-start(f32[2,8,3840]{2,1,0:T(8,128)S(1)} %collective-permute-done.9), channel_id=1, source_target_pairs={{0,32},{16,48},{32,64},{48,80},{64,96},{80,112},{96,128},{112,144}... | collective-permute-start | bytes 737288 | tf_op jit(solution)/shard_map/ppermute | solution.py:45
  56.4 0.0 collective-permute-done.3
  56.4 3.4 %collective-permute-start.15 = (f32[2,8,3840]{2,1,0:T(8,128)S(1)}, f32[2,8,3840]{2,1,0:T(8,128)S(1)}, u32[]{:S(2)}, u32[]{:S(2)}) collective-permute-start(f32[2,8,3840]{2,1,0:T(8,128)S(1)} %collective-permute-done.8), channel_id=1, source_target_pairs={{0,16},{16,32},{32,48},{48,64},{64,80},{80,96},{96,112},{112,128},... | collective-permute-start | bytes 737288 | tf_op jit(solution)/shard_map/ppermute | solution.py:42
  59.8 3.8 %collective-permute-done.10 = f32[2,8,3840]{2,1,0:T(8,128)S(1)} collective-permute-done((f32[2,8,3840]{2,1,0:T(8,128)S(1)}, f32[2,8,3840]{2,1,0:T(8,128)S(1)}, u32[]{:S(2)}, u32[]{:S(2)}) %collective-permute-start.10) | collective-permute-done | bytes 245792 | tf_op jit(solution)/shard_map/ppermute | solution.py:45
  63.6 7.9 %collective-permute-start.14 = (f32[2,8,3840]{2,1,0:T(8,128)S(1)}, f32[2,8,3840]{2,1,0:T(8,128)S(1)}, u32[]{:S(2)}, u32[]{:S(2)}) collective-permute-start(f32[2,8,3840]{2,1,0:T(8,128)S(1)} %collective-permute-done.9), channel_id=1, source_target_pairs={{0,16},{16,32},{32,48},{48,64},{64,80},{80,96},{96,112},{112,128},... | collective-permute-start | bytes 737288 | tf_op jit(solution)/shard_map/ppermute | solution.py:42
  71.4 0.0 collective-permute-done.6
  71.4 1.9 %collective-permute-start.11 = (f32[2,8,1920]{2,1,0:T(8,128)S(1)}, f32[2,8,1920]{2,1,0:T(8,128)S(1)}, u32[]{:S(2)}, u32[]{:S(2)}) collective-permute-start(f32[2,8,1920]{2,1,0:T(8,128)S(1)} %slice.43), channel_id=1, source_target_pairs={{0,32},{16,48},{32,64},{48,80},{64,96},{80,112},{96,128},{112,144}... | collective-permute-start | bytes 368648 | tf_op jit(solution)/shard_map/ppermute | solution.py:50
  73.4 0.0 collective-permute-done.5
  73.4 5.5 %collective-permute-start.12 = (f32[2,8,1920]{2,1,0:T(8,128)S(1)}, f32[2,8,1920]{2,1,0:T(8,128)S(1)}, u32[]{:S(2)}, u32[]{:S(2)}) collective-permute-start(f32[2,8,1920]{2,1,0:T(8,128)S(1)} %slice.44), channel_id=1, source_target_pairs={{0,224},{16,240},{32,0},{48,16},{64,32},{80,48},{96,64},{112,80},{... | collective-permute-start | bytes 368648 | tf_op jit(solution)/shard_map/ppermute | solution.py:51
  78.9 4.5 %collective-permute-done.11 = f32[2,8,1920]{2,1,0:T(8,128)S(1)} collective-permute-done((f32[2,8,1920]{2,1,0:T(8,128)S(1)}, f32[2,8,1920]{2,1,0:T(8,128)S(1)}, u32[]{:S(2)}, u32[]{:S(2)}) %collective-permute-start.11) | collective-permute-done | bytes 122912 | tf_op jit(solution)/shard_map/ppermute | solution.py:50
  83.5 1.9 %collective-permute-start.7 = (f32[2,8,3840]{2,1,0:T(8,128)S(1)}, f32[2,8,3840]{2,1,0:T(8,128)S(1)}, u32[]{:S(2)}, u32[]{:S(2)}) collective-permute-start(f32[2,8,3840]{2,1,0:T(8,128)S(1)} %collective-permute-done.6), channel_id=1, source_target_pairs={{0,240},{16,0},{32,16},{48,32},{64,48},{80,64},{96,80},{112,96},{1... | collective-permute-start | bytes 737288 | tf_op jit(solution)/shard_map/ppermute | solution.py:43
  85.4 3.4 %collective-permute-start.13 = (f32[2,8,3840]{2,1,0:T(8,128)S(1)}, f32[2,8,3840]{2,1,0:T(8,128)S(1)}, u32[]{:S(2)}, u32[]{:S(2)}) collective-permute-start(f32[2,8,3840]{2,1,0:T(8,128)S(1)} %collective-permute-done.10), channel_id=1, source_target_pairs={{0,16},{16,32},{32,48},{48,64},{64,80},{80,96},{96,112},{112,128},... | collective-permute-start | bytes 737288 | tf_op jit(solution)/shard_map/ppermute | solution.py:42
  88.8 2.0 %collective-permute-done.7 = f32[2,8,3840]{2,1,0:T(8,128)S(1)} collective-permute-done((f32[2,8,3840]{2,1,0:T(8,128)S(1)}, f32[2,8,3840]{2,1,0:T(8,128)S(1)}, u32[]{:S(2)}, u32[]{:S(2)}) %collective-permute-start.7) | collective-permute-done | bytes 245792 | tf_op jit(solution)/shard_map/ppermute | solution.py:43
  90.9 2.7 %collective-permute-done.13 = f32[2,8,3840]{2,1,0:T(8,128)S(1)} collective-permute-done((f32[2,8,3840]{2,1,0:T(8,128)S(1)}, f32[2,8,3840]{2,1,0:T(8,128)S(1)}, u32[]{:S(2)}, u32[]{:S(2)}) %collective-permute-start.13) | collective-permute-done | bytes 245792 | tf_op jit(solution)/shard_map/ppermute | solution.py:42
  93.6 0.0 collective-permute-done.14
  93.7 0.0 collective-permute-done.16
  93.8 3.3 %fusion.3 = f32[2,16,8,5,384]{4,2,3,0,1:T(8,128)S(1)} fusion(f32[16,2,8,5,768]{4,2,3,1,0:T(8,128)S(1)} %constant_dynamic-update-slice_fusion.2, f32[5,768]{1,0:T(8,128)S(1)} %add_convert_fusion, f32[384,768]{1,0:T(8,128)S(1)} %copy-done), kind=kOutput, calls=%fused_computation.8 | convolution fusion | flops 2265907200 | bytes 7093248 | tf_op jit(solution)/shard_map/tlkmj,ij->ltkmi/dot_general | solution.py:120
  97.1 0.1 copy.20
  97.2 2.0 %gather_fusion = f32[32,8,5,384]{3,1,2,0:T(8,128)} fusion(f32[32,8,5,384]{3,1,2,0:T(8,128)S(1)} %bitcast.52, s32[1024]{0:T(1024)S(1)} %get-tuple-element.17), kind=kCustom, calls=%fused_computation | custom fusion | bytes 3932288 | tf_op jit(solution)/shard_map/jit(_take)/gather | solution.py:127
  99.2 1.8 %bitcast_select_fusion = f32[256,5,384]{2,0,1:T(8,128)S(1)} fusion(f32[32,8,5,384]{3,1,2,0:T(8,128)} %gather_fusion, pred[256]{0:T(512)(128)(4,1)S(1)} %broadcast_in_dim.58), kind=kLoop, calls=%fused_computation.6 | loop fusion | flops 491520 | bytes 3932416 | tf_op jit(solution)/shard_map/jit(_take)/select_n | solution.py:127
  101.0 1.3 copy-done.1
  102.3 0.1 slice.45
  102.4 0.6 gather_fusion.2
  103.0 2.0 %fusion.7 = f32[256,2,384]{2,0,1:T(8,128)S(1)} fusion(f32[2,256,256]{2,1,0:T(8,128)} %param.15, f32[256,5,384]{2,0,1:T(8,128)} %copy-done.1, f32[2,256,384]{2,1,0:T(8,128)S(1)} %gather_fusion.2, f32[2,384]{1,0:T(2,128)S(1)} %broadcast_select_fusion, pred[2]{0:T(512)(128)(4,1)S(1)} %compare_and_fusion), kind=kOutput, calls=%fused_computation.11 | convolution fusion | flops 302579712 | bytes 2886658 | tf_op jit(solution)/shard_map/cqk,qci->kci/dot_general | solution.py:132
  105.0 0.1 pad_maximum_fusion
  105.1 0.2 constant_dynamic-slice_fusion.1
  105.3 0.0 copy-start.2
  105.3 1.0 fusion.9
  106.3 8.6 %collective-permute-start.17 = (f32[8,16,5,384]{3,1,2,0:T(8,128)}, f32[8,16,5,384]{3,1,2,0:T(8,128)S(1)}, u32[]{:S(2)}, u32[]{:S(2)}) collective-permute-start(f32[8,16,5,384]{3,1,2,0:T(8,128)} %fusion.9), channel_id=1, source_target_pairs={{0,1},{1,0},{2,3},{3,2},{4,5},{5,4},{6,7},{7,6},{8,9},{9,8},{10,11... | collective-permute-start | bytes 2949128 | tf_op jit(solution)/shard_map/ppermute | solution.py:89
  115.0 2.4 %collective-permute-done.17 = f32[8,16,5,384]{3,1,2,0:T(8,128)S(1)} collective-permute-done((f32[8,16,5,384]{3,1,2,0:T(8,128)}, f32[8,16,5,384]{3,1,2,0:T(8,128)S(1)}, u32[]{:S(2)}, u32[]{:S(2)}) %collective-permute-start.17) | collective-permute-done | bytes 983072 | tf_op jit(solution)/shard_map/ppermute | solution.py:89
  117.4 1.1 fusion.11
  118.4 6.3 %all-to-all-start = ((f32[8,16,5,384]{3,1,2,0:T(8,128)}), f32[8,16,5,384]{3,1,2,0:T(8,128)S(1)}, u32[]{:S(2)}, u32[]{:S(2)}) async-start(f32[8,16,5,384]{3,1,2,0:T(8,128)} %fusion.11), calls=%async_computation | async-start | bytes 1966080 | tf_op jit(solution)/shard_map/all_to_all | solution.py:91
  124.8 0.1 compare_reduce_fusion.3
  124.9 13.7 %all-to-all-done = f32[8,16,5,384]{3,1,2,0:T(8,128)S(1)} async-done(((f32[8,16,5,384]{3,1,2,0:T(8,128)}), f32[8,16,5,384]{3,1,2,0:T(8,128)S(1)}, u32[]{:S(2)}, u32[]{:S(2)}) %all-to-all-start) | async-done | bytes 983072 | tf_op jit(solution)/shard_map/all_to_all | solution.py:91
  138.6 0.1 reduce_sum.9
  138.7 0.6 slice_multiply_fusion
  139.3 0.6 slice_multiply_fusion.1
  (35 shorter events, 0.5 us)
Async XLA Ops:
  0.6 93.1 %copy-start = (f32[384,768]{1,0:T(8,128)S(1)}, f32[384,768]{1,0:T(8,128)}, u32[]{:S(2)}) copy-start(f32[384,768]{1,0:T(8,128)} %param.9) | copy-start | bytes 3538948
  2.4 6.8 %collective-permute-start = (f32[8,3840]{1,0:T(8,128)S(1)}, f32[8,3840]{1,0:T(8,128)S(1)}, u32[]{:S(2)}, u32[]{:S(2)}) collective-permute-start(f32[8,3840]{1,0:T(8,128)S(1)} %bitcast.55), channel_id=1, source_target_pairs={{0,256},{16,272},{32,288},{48,304},{64,320},{80,336},{96,352},{112... | collective-permute-start | bytes 368648 | tf_op jit(solution)/shard_map/ppermute | solution.py:33
  9.3 20.5 %collective-permute-start.2 = (f32[2,8,3840]{2,1,0:T(8,128)S(1)}, f32[2,8,3840]{2,1,0:T(8,128)S(1)}, u32[]{:S(2)}, u32[]{:S(2)}) collective-permute-start(f32[2,8,3840]{2,1,0:T(8,128)S(1)} %pad_maximum_fusion.1), channel_id=1, source_target_pairs={{0,224},{16,240},{32,0},{48,16},{64,32},{80,48},{96,64},{112,80},{... | collective-permute-start | bytes 737288 | tf_op jit(solution)/shard_map/ppermute | solution.py:46
  20.9 15.5 %collective-permute-start.8 = (f32[2,8,3840]{2,1,0:T(8,128)S(1)}, f32[2,8,3840]{2,1,0:T(8,128)S(1)}, u32[]{:S(2)}, u32[]{:S(2)}) collective-permute-start(f32[2,8,3840]{2,1,0:T(8,128)S(1)} %pad_maximum_fusion.1), channel_id=1, source_target_pairs={{0,32},{16,48},{32,64},{48,80},{64,96},{80,112},{96,128},{112,144}... | collective-permute-start | bytes 737288 | tf_op jit(solution)/shard_map/ppermute | solution.py:45
  24.5 22.1 %collective-permute-start.1 = (f32[2,8,3840]{2,1,0:T(8,128)S(1)}, f32[2,8,3840]{2,1,0:T(8,128)S(1)}, u32[]{:S(2)}, u32[]{:S(2)}) collective-permute-start(f32[2,8,3840]{2,1,0:T(8,128)S(1)} %pad_maximum_fusion.1), channel_id=1, source_target_pairs={{0,240},{16,0},{32,16},{48,32},{64,48},{80,64},{96,80},{112,96},{1... | collective-permute-start | bytes 737288 | tf_op jit(solution)/shard_map/ppermute | solution.py:43
  29.7 16.9 %collective-permute-start.4 = (f32[2,8,3840]{2,1,0:T(8,128)S(1)}, f32[2,8,3840]{2,1,0:T(8,128)S(1)}, u32[]{:S(2)}, u32[]{:S(2)}) collective-permute-start(f32[2,8,3840]{2,1,0:T(8,128)S(1)} %collective-permute-done.2), channel_id=1, source_target_pairs={{0,224},{16,240},{32,0},{48,16},{64,32},{80,48},{96,64},{112,80},{... | collective-permute-start | bytes 737288 | tf_op jit(solution)/shard_map/ppermute | solution.py:46
  36.4 18.0 %collective-permute-start.9 = (f32[2,8,3840]{2,1,0:T(8,128)S(1)}, f32[2,8,3840]{2,1,0:T(8,128)S(1)}, u32[]{:S(2)}, u32[]{:S(2)}) collective-permute-start(f32[2,8,3840]{2,1,0:T(8,128)S(1)} %collective-permute-done.8), channel_id=1, source_target_pairs={{0,32},{16,48},{32,64},{48,80},{64,96},{80,112},{96,128},{112,144}... | collective-permute-start | bytes 737288 | tf_op jit(solution)/shard_map/ppermute | solution.py:45
  38.6 55.1 %collective-permute-start.16 = (f32[2,8,3840]{2,1,0:T(8,128)S(1)}, f32[2,8,3840]{2,1,0:T(8,128)S(1)}, u32[]{:S(2)}, u32[]{:S(2)}) collective-permute-start(f32[2,8,3840]{2,1,0:T(8,128)S(1)} %pad_maximum_fusion.1), channel_id=1, source_target_pairs={{0,16},{16,32},{32,48},{48,64},{64,80},{80,96},{96,112},{112,128},... | collective-permute-start | bytes 737288 | tf_op jit(solution)/shard_map/ppermute | solution.py:42
  42.2 14.1 %collective-permute-start.3 = (f32[2,8,3840]{2,1,0:T(8,128)S(1)}, f32[2,8,3840]{2,1,0:T(8,128)S(1)}, u32[]{:S(2)}, u32[]{:S(2)}) collective-permute-start(f32[2,8,3840]{2,1,0:T(8,128)S(1)} %collective-permute-done.2), channel_id=1, source_target_pairs={{0,240},{16,0},{32,16},{48,32},{64,48},{80,64},{96,80},{112,96},{1... | collective-permute-start | bytes 737288 | tf_op jit(solution)/shard_map/ppermute | solution.py:43
  46.6 26.8 %collective-permute-start.5 = (f32[2,8,3840]{2,1,0:T(8,128)S(1)}, f32[2,8,3840]{2,1,0:T(8,128)S(1)}, u32[]{:S(2)}, u32[]{:S(2)}) collective-permute-start(f32[2,8,3840]{2,1,0:T(8,128)S(1)} %collective-permute-done.4), channel_id=1, source_target_pairs={{0,240},{16,0},{32,16},{48,32},{64,48},{80,64},{96,80},{112,96},{1... | collective-permute-start | bytes 737288 | tf_op jit(solution)/shard_map/ppermute | solution.py:43
  50.0 21.5 %collective-permute-start.6 = (f32[2,8,3840]{2,1,0:T(8,128)S(1)}, f32[2,8,3840]{2,1,0:T(8,128)S(1)}, u32[]{:S(2)}, u32[]{:S(2)}) collective-permute-start(f32[2,8,3840]{2,1,0:T(8,128)S(1)} %collective-permute-done.4), channel_id=1, source_target_pairs={{0,224},{16,240},{32,0},{48,16},{64,32},{80,48},{96,64},{112,80},{... | collective-permute-start | bytes 737288 | tf_op jit(solution)/shard_map/ppermute | solution.py:46
  54.4 9.1 %collective-permute-start.10 = (f32[2,8,3840]{2,1,0:T(8,128)S(1)}, f32[2,8,3840]{2,1,0:T(8,128)S(1)}, u32[]{:S(2)}, u32[]{:S(2)}) collective-permute-start(f32[2,8,3840]{2,1,0:T(8,128)S(1)} %collective-permute-done.9), channel_id=1, source_target_pairs={{0,32},{16,48},{32,64},{48,80},{64,96},{80,112},{96,128},{112,144}... | collective-permute-start | bytes 737288 | tf_op jit(solution)/shard_map/ppermute | solution.py:45
  56.4 37.3 %collective-permute-start.15 = (f32[2,8,3840]{2,1,0:T(8,128)S(1)}, f32[2,8,3840]{2,1,0:T(8,128)S(1)}, u32[]{:S(2)}, u32[]{:S(2)}) collective-permute-start(f32[2,8,3840]{2,1,0:T(8,128)S(1)} %collective-permute-done.8), channel_id=1, source_target_pairs={{0,16},{16,32},{32,48},{48,64},{64,80},{80,96},{96,112},{112,128},... | collective-permute-start | bytes 737288 | tf_op jit(solution)/shard_map/ppermute | solution.py:42
  63.6 30.1 %collective-permute-start.14 = (f32[2,8,3840]{2,1,0:T(8,128)S(1)}, f32[2,8,3840]{2,1,0:T(8,128)S(1)}, u32[]{:S(2)}, u32[]{:S(2)}) collective-permute-start(f32[2,8,3840]{2,1,0:T(8,128)S(1)} %collective-permute-done.9), channel_id=1, source_target_pairs={{0,16},{16,32},{32,48},{48,64},{64,80},{80,96},{96,112},{112,128},... | collective-permute-start | bytes 737288 | tf_op jit(solution)/shard_map/ppermute | solution.py:42
  71.4 12.0 %collective-permute-start.11 = (f32[2,8,1920]{2,1,0:T(8,128)S(1)}, f32[2,8,1920]{2,1,0:T(8,128)S(1)}, u32[]{:S(2)}, u32[]{:S(2)}) collective-permute-start(f32[2,8,1920]{2,1,0:T(8,128)S(1)} %slice.43), channel_id=1, source_target_pairs={{0,32},{16,48},{32,64},{48,80},{64,96},{80,112},{96,128},{112,144}... | collective-permute-start | bytes 368648 | tf_op jit(solution)/shard_map/ppermute | solution.py:50
  73.4 12.0 %collective-permute-start.12 = (f32[2,8,1920]{2,1,0:T(8,128)S(1)}, f32[2,8,1920]{2,1,0:T(8,128)S(1)}, u32[]{:S(2)}, u32[]{:S(2)}) collective-permute-start(f32[2,8,1920]{2,1,0:T(8,128)S(1)} %slice.44), channel_id=1, source_target_pairs={{0,224},{16,240},{32,0},{48,16},{64,32},{80,48},{96,64},{112,80},{... | collective-permute-start | bytes 368648 | tf_op jit(solution)/shard_map/ppermute | solution.py:51
  83.5 7.3 %collective-permute-start.7 = (f32[2,8,3840]{2,1,0:T(8,128)S(1)}, f32[2,8,3840]{2,1,0:T(8,128)S(1)}, u32[]{:S(2)}, u32[]{:S(2)}) collective-permute-start(f32[2,8,3840]{2,1,0:T(8,128)S(1)} %collective-permute-done.6), channel_id=1, source_target_pairs={{0,240},{16,0},{32,16},{48,32},{64,48},{80,64},{96,80},{112,96},{1... | collective-permute-start | bytes 737288 | tf_op jit(solution)/shard_map/ppermute | solution.py:43
  85.4 8.2 %collective-permute-start.13 = (f32[2,8,3840]{2,1,0:T(8,128)S(1)}, f32[2,8,3840]{2,1,0:T(8,128)S(1)}, u32[]{:S(2)}, u32[]{:S(2)}) collective-permute-start(f32[2,8,3840]{2,1,0:T(8,128)S(1)} %collective-permute-done.10), channel_id=1, source_target_pairs={{0,16},{16,32},{32,48},{48,64},{64,80},{80,96},{96,112},{112,128},... | collective-permute-start | bytes 737288 | tf_op jit(solution)/shard_map/ppermute | solution.py:42
  101.0 1.3 copy-start.1
  105.3 19.5 %copy-start.2 = (s32[2,36]{1,0:T(2,128)S(1)}, s32[2,36]{1,0:T(2,128)}, u32[]{:S(2)}) copy-start(s32[2,36]{1,0:T(2,128)} %param.13) | copy-start | bytes 868
  106.3 11.0 %collective-permute-start.17 = (f32[8,16,5,384]{3,1,2,0:T(8,128)}, f32[8,16,5,384]{3,1,2,0:T(8,128)S(1)}, u32[]{:S(2)}, u32[]{:S(2)}) collective-permute-start(f32[8,16,5,384]{3,1,2,0:T(8,128)} %fusion.9), channel_id=1, source_target_pairs={{0,1},{1,0},{2,3},{3,2},{4,5},{5,4},{6,7},{7,6},{8,9},{9,8},{10,11... | collective-permute-start | bytes 2949128 | tf_op jit(solution)/shard_map/ppermute | solution.py:89
  118.4 20.2 %all-to-all-start = ((f32[8,16,5,384]{3,1,2,0:T(8,128)}), f32[8,16,5,384]{3,1,2,0:T(8,128)S(1)}, u32[]{:S(2)}, u32[]{:S(2)}) async-start(f32[8,16,5,384]{3,1,2,0:T(8,128)} %fusion.11), calls=%async_computation | async-start | bytes 1966080 | tf_op jit(solution)/shard_map/all_to_all | solution.py:91

commit v16 on v12

--- a/solution.py
+++ b/solution.py
@@ -130,8 +130,9 @@
     combined = jnp.concatenate([first_partial, second_partial], axis=1)
     reduced = reduce_cols_a2a(combined, n_col)
     reduced = jnp.transpose(reduced, (1, 0, 2))
-    first_cols = -out_first[:, None, :] * reduced[:n_first]
-    second_cols = -out_second[:, None, :] * reduced[n_first:]
+    signed = -jnp.concatenate([out_first, out_second], axis=0)[:, None, :] * reduced
+    first_cols = signed[:n_first]
+    second_cols = signed[n_first:]
     return (first_cols, second_cols)
 
 

time: 135 us -> 135 us (level)
  no operation moved by 1% of the time
where the time goes in v16:
time: 135 us; the launch traced here: 134 us
  starting transfers between devices  85.9 us (64%)
  waiting for transfers between devices  28.7 us (21%)
  other arithmetic  6.67 us (5%)
  local copies, waits for them, and re-layouts  6.22 us (5%)
  matrix products  5.33 us (4%)
    ppermute x3, starting transfers between devices, gather_rows(): lane_down = lax.ppermute(lane_down, 'row', shift_pairs(n_row, nz, 1, -2))  23.3 us
    ppermute x4, starting transfers between devices, gather_rows(): lax.ppermute(lane_down, 'row', shift_pairs(n_row, nz, 1, -1))  16.5 us
    ppermute x4, starting transfers between devices, gather_rows(): lax.ppermute(lane_up, 'row', shift_pairs(n_row, nz, 1, 1))  14.3 us
    all_to_all x1, waiting for transfers between devices, reduce_cols_a2a(): lax.all_to_all(summed, 'col', 0, 0, tiled=True, axis_index_groups=groups)  13.7 us
    ppermute x1, starting transfers between devices, reduce_cols_a2a(): lax.ppermute(send, 'col', partner_pairs)  7.45 us
    all_to_all x1, starting transfers between devices, reduce_cols_a2a(): lax.all_to_all(summed, 'col', 0, 0, tiled=True, axis_index_groups=groups)  6.63 us
    ppermute x1, starting transfers between devices, gather_rows(): lax.ppermute(lane_down[..., half:], 'row', shift_pairs(n_row, nz, 1, -2))  6.12 us
    ppermute x3, starting transfers between devices, gather_rows(): lane_up = lax.ppermute(lane_up, 'row', shift_pairs(n_row, nz, 1, 2))  5.76 us
  transfers between devices with their start and end apart: 19, of which 7 were waited for; matrix products, arithmetic and copies ran while one was open for 4% of the time, Pallas kernels for 0%

profile of v16, /device:TPU:1, one launch (start us, length us, event | category | flops | bytes accessed | tf_op | source)
XLA Modules:
  0.0 134.0 jit_solution(3337456026550852371)
XLA Ops:
  0.6 0.0 copy-start
  0.6 1.0 constant_dynamic-update-slice_fusion.1
  1.6 0.8 constant_dynamic-update-slice_fusion
  2.4 3.9 %collective-permute-start = (f32[8,3840]{1,0:T(8,128)S(1)}, f32[8,3840]{1,0:T(8,128)S(1)}, u32[]{:S(2)}, u32[]{:S(2)}) collective-permute-start(f32[8,3840]{1,0:T(8,128)S(1)} %bitcast.53), channel_id=1, source_target_pairs={{0,256},{16,272},{32,288},{48,304},{64,320},{80,336},{96,352},{112... | collective-permute-start | bytes 368648 | tf_op jit(solution)/shard_map/ppermute | solution.py:33
  6.4 0.7 compare_select_fusion
  7.0 0.7 compare_and_fusion
  7.7 0.8 compare_reduce_fusion.2
  8.5 0.6 gather_fusion
  9.1 0.1 broadcast_select_fusion
  9.2 0.0 collective-permute-done
  9.2 11.7 %collective-permute-start.2 = (f32[2,8,3840]{2,1,0:T(8,128)S(1)}, f32[2,8,3840]{2,1,0:T(8,128)S(1)}, u32[]{:S(2)}, u32[]{:S(2)}) collective-permute-start(f32[2,8,3840]{2,1,0:T(8,128)S(1)} %maximum_select_fusion.1), channel_id=1, source_target_pairs={{0,224},{16,240},{32,0},{48,16},{64,32},{80,48},{96,64},{112,80},{... | collective-permute-start | bytes 737288 | tf_op jit(solution)/shard_map/ppermute | solution.py:46
  20.9 1.9 %collective-permute-start.8 = (f32[2,8,3840]{2,1,0:T(8,128)S(1)}, f32[2,8,3840]{2,1,0:T(8,128)S(1)}, u32[]{:S(2)}, u32[]{:S(2)}) collective-permute-start(f32[2,8,3840]{2,1,0:T(8,128)S(1)} %maximum_select_fusion.1), channel_id=1, source_target_pairs={{0,32},{16,48},{32,64},{48,80},{64,96},{80,112},{96,128},{112,144}... | collective-permute-start | bytes 737288 | tf_op jit(solution)/shard_map/ppermute | solution.py:45
  22.9 0.8 compare_reduce_fusion
  23.7 5.0 %collective-permute-start.1 = (f32[2,8,3840]{2,1,0:T(8,128)S(1)}, f32[2,8,3840]{2,1,0:T(8,128)S(1)}, u32[]{:S(2)}, u32[]{:S(2)}) collective-permute-start(f32[2,8,3840]{2,1,0:T(8,128)S(1)} %maximum_select_fusion.1), channel_id=1, source_target_pairs={{0,240},{16,0},{32,16},{48,32},{64,48},{80,64},{96,80},{112,96},{1... | collective-permute-start | bytes 737288 | tf_op jit(solution)/shard_map/ppermute | solution.py:43
  28.7 0.8 compare_reduce_fusion.1
  29.5 0.2 collective-permute-done.2
  29.7 6.7 %collective-permute-start.4 = (f32[2,8,3840]{2,1,0:T(8,128)S(1)}, f32[2,8,3840]{2,1,0:T(8,128)S(1)}, u32[]{:S(2)}, u32[]{:S(2)}) collective-permute-start(f32[2,8,3840]{2,1,0:T(8,128)S(1)} %collective-permute-done.2), channel_id=1, source_target_pairs={{0,224},{16,240},{32,0},{48,16},{64,32},{80,48},{96,64},{112,80},{... | collective-permute-start | bytes 737288 | tf_op jit(solution)/shard_map/ppermute | solution.py:46
  36.4 0.0 collective-permute-done.8
  36.4 1.9 %collective-permute-start.9 = (f32[2,8,3840]{2,1,0:T(8,128)S(1)}, f32[2,8,3840]{2,1,0:T(8,128)S(1)}, u32[]{:S(2)}, u32[]{:S(2)}) collective-permute-start(f32[2,8,3840]{2,1,0:T(8,128)S(1)} %collective-permute-done.8), channel_id=1, source_target_pairs={{0,32},{16,48},{32,64},{48,80},{64,96},{80,112},{96,128},{112,144}... | collective-permute-start | bytes 737288 | tf_op jit(solution)/shard_map/ppermute | solution.py:45
  38.5 3.6 %collective-permute-start.16 = (f32[2,8,3840]{2,1,0:T(8,128)S(1)}, f32[2,8,3840]{2,1,0:T(8,128)S(1)}, u32[]{:S(2)}, u32[]{:S(2)}) collective-permute-start(f32[2,8,3840]{2,1,0:T(8,128)S(1)} %maximum_select_fusion.1), channel_id=1, source_target_pairs={{0,16},{16,32},{32,48},{48,64},{64,80},{80,96},{96,112},{112,128},... | collective-permute-start | bytes 737288 | tf_op jit(solution)/shard_map/ppermute | solution.py:42
  42.1 4.3 %collective-permute-start.3 = (f32[2,8,3840]{2,1,0:T(8,128)S(1)}, f32[2,8,3840]{2,1,0:T(8,128)S(1)}, u32[]{:S(2)}, u32[]{:S(2)}) collective-permute-start(f32[2,8,3840]{2,1,0:T(8,128)S(1)} %collective-permute-done.2), channel_id=1, source_target_pairs={{0,240},{16,0},{32,16},{48,32},{64,48},{80,64},{96,80},{112,96},{1... | collective-permute-start | bytes 737288 | tf_op jit(solution)/shard_map/ppermute | solution.py:43
  46.4 0.0 collective-permute-done.1
  46.5 0.0 collective-permute-done.4
  46.5 3.4 %collective-permute-start.5 = (f32[2,8,3840]{2,1,0:T(8,128)S(1)}, f32[2,8,3840]{2,1,0:T(8,128)S(1)}, u32[]{:S(2)}, u32[]{:S(2)}) collective-permute-start(f32[2,8,3840]{2,1,0:T(8,128)S(1)} %collective-permute-done.4), channel_id=1, source_target_pairs={{0,240},{16,0},{32,16},{48,32},{64,48},{80,64},{96,80},{112,96},{1... | collective-permute-start | bytes 737288 | tf_op jit(solution)/shard_map/ppermute | solution.py:43
  49.8 4.8 %collective-permute-start.6 = (f32[2,8,3840]{2,1,0:T(8,128)S(1)}, f32[2,8,3840]{2,1,0:T(8,128)S(1)}, u32[]{:S(2)}, u32[]{:S(2)}) collective-permute-start(f32[2,8,3840]{2,1,0:T(8,128)S(1)} %collective-permute-done.4), channel_id=1, source_target_pairs={{0,224},{16,240},{32,0},{48,16},{64,32},{80,48},{96,64},{112,80},{... | collective-permute-start | bytes 737288 | tf_op jit(solution)/shard_map/ppermute | solution.py:46
  54.7 0.0 collective-permute-done.9
  54.7 1.9 %collective-permute-start.10 = (f32[2,8,3840]{2,1,0:T(8,128)S(1)}, f32[2,8,3840]{2,1,0:T(8,128)S(1)}, u32[]{:S(2)}, u32[]{:S(2)}) collective-permute-start(f32[2,8,3840]{2,1,0:T(8,128)S(1)} %collective-permute-done.9), channel_id=1, source_target_pairs={{0,32},{16,48},{32,64},{48,80},{64,96},{80,112},{96,128},{112,144}... | collective-permute-start | bytes 737288 | tf_op jit(solution)/shard_map/ppermute | solution.py:45
  56.7 0.0 collective-permute-done.3
  56.7 3.4 %collective-permute-start.15 = (f32[2,8,3840]{2,1,0:T(8,128)S(1)}, f32[2,8,3840]{2,1,0:T(8,128)S(1)}, u32[]{:S(2)}, u32[]{:S(2)}) collective-permute-start(f32[2,8,3840]{2,1,0:T(8,128)S(1)} %collective-permute-done.8), channel_id=1, source_target_pairs={{0,16},{16,32},{32,48},{48,64},{64,80},{80,96},{96,112},{112,128},... | collective-permute-start | bytes 737288 | tf_op jit(solution)/shard_map/ppermute | solution.py:42
  60.1 5.2 %collective-permute-done.6 = f32[2,8,3840]{2,1,0:T(8,128)S(1)} collective-permute-done((f32[2,8,3840]{2,1,0:T(8,128)S(1)}, f32[2,8,3840]{2,1,0:T(8,128)S(1)}, u32[]{:S(2)}, u32[]{:S(2)}) %collective-permute-start.6) | collective-permute-done | bytes 245792 | tf_op jit(solution)/shard_map/ppermute | solution.py:46
  65.3 1.9 %collective-permute-start.14 = (f32[2,8,3840]{2,1,0:T(8,128)S(1)}, f32[2,8,3840]{2,1,0:T(8,128)S(1)}, u32[]{:S(2)}, u32[]{:S(2)}) collective-permute-start(f32[2,8,3840]{2,1,0:T(8,128)S(1)} %collective-permute-done.9), channel_id=1, source_target_pairs={{0,16},{16,32},{32,48},{48,64},{64,80},{80,96},{96,112},{112,128},... | collective-permute-start | bytes 737288 | tf_op jit(solution)/shard_map/ppermute | solution.py:42
  67.2 0.0 collective-permute-done.10
  67.2 6.1 %collective-permute-start.12 = (f32[2,8,1920]{2,1,0:T(8,128)S(1)}, f32[2,8,1920]{2,1,0:T(8,128)S(1)}, u32[]{:S(2)}, u32[]{:S(2)}) collective-permute-start(f32[2,8,1920]{2,1,0:T(8,128)S(1)} %slice.42), channel_id=1, source_target_pairs={{0,224},{16,240},{32,0},{48,16},{64,32},{80,48},{96,64},{112,80},{... | collective-permute-start | bytes 368648 | tf_op jit(solution)/shard_map/ppermute | solution.py:51
  73.4 0.0 collective-permute-done.5
  73.4 1.9 %collective-permute-start.11 = (f32[2,8,1920]{2,1,0:T(8,128)S(1)}, f32[2,8,1920]{2,1,0:T(8,128)S(1)}, u32[]{:S(2)}, u32[]{:S(2)}) collective-permute-start(f32[2,8,1920]{2,1,0:T(8,128)S(1)} %slice.41), channel_id=1, source_target_pairs={{0,32},{16,48},{32,64},{48,80},{64,96},{80,112},{96,128},{112,144}... | collective-permute-start | bytes 368648 | tf_op jit(solution)/shard_map/ppermute | solution.py:50
  75.4 1.2 collective-permute-done.12
  76.6 3.8 %collective-permute-start.7 = (f32[2,8,3840]{2,1,0:T(8,128)S(1)}, f32[2,8,3840]{2,1,0:T(8,128)S(1)}, u32[]{:S(2)}, u32[]{:S(2)}) collective-permute-start(f32[2,8,3840]{2,1,0:T(8,128)S(1)} %collective-permute-done.6), channel_id=1, source_target_pairs={{0,240},{16,0},{32,16},{48,32},{64,48},{80,64},{96,80},{112,96},{1... | collective-permute-start | bytes 737288 | tf_op jit(solution)/shard_map/ppermute | solution.py:43
  80.4 2.5 %collective-permute-done.11 = f32[2,8,1920]{2,1,0:T(8,128)S(1)} collective-permute-done((f32[2,8,1920]{2,1,0:T(8,128)S(1)}, f32[2,8,1920]{2,1,0:T(8,128)S(1)}, u32[]{:S(2)}, u32[]{:S(2)}) %collective-permute-start.11) | collective-permute-done | bytes 122912 | tf_op jit(solution)/shard_map/ppermute | solution.py:50
  82.9 5.4 %collective-permute-start.13 = (f32[2,8,3840]{2,1,0:T(8,128)S(1)}, f32[2,8,3840]{2,1,0:T(8,128)S(1)}, u32[]{:S(2)}, u32[]{:S(2)}) collective-permute-start(f32[2,8,3840]{2,1,0:T(8,128)S(1)} %collective-permute-done.10), channel_id=1, source_target_pairs={{0,16},{16,32},{32,48},{48,64},{64,80},{80,96},{96,112},{112,128},... | collective-permute-start | bytes 737288 | tf_op jit(solution)/shard_map/ppermute | solution.py:42
  88.4 0.0 collective-permute-done.7
  88.4 3.5 %collective-permute-done.13 = f32[2,8,3840]{2,1,0:T(8,128)S(1)} collective-permute-done((f32[2,8,3840]{2,1,0:T(8,128)S(1)}, f32[2,8,3840]{2,1,0:T(8,128)S(1)}, u32[]{:S(2)}, u32[]{:S(2)}) %collective-permute-start.13) | collective-permute-done | bytes 245792 | tf_op jit(solution)/shard_map/ppermute | solution.py:42
  91.9 0.0 collective-permute-done.14
  92.0 0.0 collective-permute-done.15
  92.1 0.0 collective-permute-done.16
  92.1 3.3 %fusion.4 = f32[2,16,8,5,384]{4,2,3,0,1:T(8,128)S(1)} fusion(f32[16,2,8,5,768]{4,2,3,1,0:T(8,128)S(1)} %constant_dynamic-update-slice_fusion.2, f32[5,768]{1,0:T(8,128)S(1)} %add_convert_fusion, f32[384,768]{1,0:T(8,128)S(1)} %copy-done), kind=kOutput, calls=%fused_computation.9 | convolution fusion | flops 2265907200 | bytes 7093248 | tf_op jit(solution)/shard_map/tlkmj,ij->ltkmi/dot_general | solution.py:120
  95.4 0.4 fusion.2
  95.8 0.2 copy.18
  96.0 1.3 copy-done.1
  97.3 0.1 slice.43
  97.4 0.6 gather_fusion.1
  98.0 2.0 %fusion.8 = f32[256,2,384]{2,0,1:T(8,128)S(1)} fusion(f32[2,256,256]{2,1,0:T(8,128)} %param.15, f32[256,5,384]{2,0,1:T(8,128)} %bitcast.50, f32[2,256,384]{2,1,0:T(8,128)S(1)} %gather_fusion.1, f32[2,384]{1,0:T(2,128)S(1)} %broadcast_select_fusion, pred[2]{0:T(512)(128)(4,1)S(1)} %compare_and_fusion), kind=kOutput, calls=%fused_computation.12 | convolution fusion | flops 302579712 | bytes 2886658 | tf_op jit(solution)/shard_map/cqk,qci->kci/dot_general | solution.py:128
  100.0 0.1 pad_maximum_fusion
  100.1 0.2 constant_dynamic-slice_fusion.1
  100.3 0.0 copy-start.2
  100.3 1.0 fusion.10
  101.3 7.4 %collective-permute-start.17 = (f32[8,16,5,384]{3,1,2,0:T(8,128)}, f32[8,16,5,384]{3,1,2,0:T(8,128)S(1)}, u32[]{:S(2)}, u32[]{:S(2)}) collective-permute-start(f32[8,16,5,384]{3,1,2,0:T(8,128)} %fusion.10), channel_id=1, source_target_pairs={{0,1},{1,0},{2,3},{3,2},{4,5},{5,4},{6,7},{7,6},{8,9},{9,8},{10,11... | collective-permute-start | bytes 2949128 | tf_op jit(solution)/shard_map/ppermute | solution.py:89
  108.8 2.4 %collective-permute-done.17 = f32[8,16,5,384]{3,1,2,0:T(8,128)S(1)} collective-permute-done((f32[8,16,5,384]{3,1,2,0:T(8,128)}, f32[8,16,5,384]{3,1,2,0:T(8,128)S(1)}, u32[]{:S(2)}, u32[]{:S(2)}) %collective-permute-start.17) | collective-permute-done | bytes 983072 | tf_op jit(solution)/shard_map/ppermute | solution.py:89
  111.2 1.1 fusion.12
  112.2 6.6 %all-to-all-start = ((f32[8,16,5,384]{3,1,2,0:T(8,128)}), f32[8,16,5,384]{3,1,2,0:T(8,128)S(1)}, u32[]{:S(2)}, u32[]{:S(2)}) async-start(f32[8,16,5,384]{3,1,2,0:T(8,128)} %fusion.12), calls=%async_computation | async-start | bytes 1966080 | tf_op jit(solution)/shard_map/all_to_all | solution.py:91
  118.9 0.1 compare_reduce_fusion.3
  119.0 13.7 %all-to-all-done = f32[8,16,5,384]{3,1,2,0:T(8,128)S(1)} async-done(((f32[8,16,5,384]{3,1,2,0:T(8,128)}), f32[8,16,5,384]{3,1,2,0:T(8,128)S(1)}, u32[]{:S(2)}, u32[]{:S(2)}) %all-to-all-start) | async-done | bytes 983072 | tf_op jit(solution)/shard_map/all_to_all | solution.py:91
  132.7 0.1 reduce_sum.9
  132.8 0.6 slice.45
  133.4 0.6 slice.46
  (31 shorter events, 0.5 us)
Async XLA Ops:
  0.6 91.5 %copy-start = (f32[384,768]{1,0:T(8,128)S(1)}, f32[384,768]{1,0:T(8,128)}, u32[]{:S(2)}) copy-start(f32[384,768]{1,0:T(8,128)} %param.9) | copy-start | bytes 3538948
  2.4 6.8 %collective-permute-start = (f32[8,3840]{1,0:T(8,128)S(1)}, f32[8,3840]{1,0:T(8,128)S(1)}, u32[]{:S(2)}, u32[]{:S(2)}) collective-permute-start(f32[8,3840]{1,0:T(8,128)S(1)} %bitcast.53), channel_id=1, source_target_pairs={{0,256},{16,272},{32,288},{48,304},{64,320},{80,336},{96,352},{112... | collective-permute-start | bytes 368648 | tf_op jit(solution)/shard_map/ppermute | solution.py:33
  9.2 20.5 %collective-permute-start.2 = (f32[2,8,3840]{2,1,0:T(8,128)S(1)}, f32[2,8,3840]{2,1,0:T(8,128)S(1)}, u32[]{:S(2)}, u32[]{:S(2)}) collective-permute-start(f32[2,8,3840]{2,1,0:T(8,128)S(1)} %maximum_select_fusion.1), channel_id=1, source_target_pairs={{0,224},{16,240},{32,0},{48,16},{64,32},{80,48},{96,64},{112,80},{... | collective-permute-start | bytes 737288 | tf_op jit(solution)/shard_map/ppermute | solution.py:46
  20.9 15.5 %collective-permute-start.8 = (f32[2,8,3840]{2,1,0:T(8,128)S(1)}, f32[2,8,3840]{2,1,0:T(8,128)S(1)}, u32[]{:S(2)}, u32[]{:S(2)}) collective-permute-start(f32[2,8,3840]{2,1,0:T(8,128)S(1)} %maximum_select_fusion.1), channel_id=1, source_target_pairs={{0,32},{16,48},{32,64},{48,80},{64,96},{80,112},{96,128},{112,144}... | collective-permute-start | bytes 737288 | tf_op jit(solution)/shard_map/ppermute | solution.py:45
  23.7 22.7 %collective-permute-start.1 = (f32[2,8,3840]{2,1,0:T(8,128)S(1)}, f32[2,8,3840]{2,1,0:T(8,128)S(1)}, u32[]{:S(2)}, u32[]{:S(2)}) collective-permute-start(f32[2,8,3840]{2,1,0:T(8,128)S(1)} %maximum_select_fusion.1), channel_id=1, source_target_pairs={{0,240},{16,0},{32,16},{48,32},{64,48},{80,64},{96,80},{112,96},{1... | collective-permute-start | bytes 737288 | tf_op jit(solution)/shard_map/ppermute | solution.py:43
  29.7 16.7 %collective-permute-start.4 = (f32[2,8,3840]{2,1,0:T(8,128)S(1)}, f32[2,8,3840]{2,1,0:T(8,128)S(1)}, u32[]{:S(2)}, u32[]{:S(2)}) collective-permute-start(f32[2,8,3840]{2,1,0:T(8,128)S(1)} %collective-permute-done.2), channel_id=1, source_target_pairs={{0,224},{16,240},{32,0},{48,16},{64,32},{80,48},{96,64},{112,80},{... | collective-permute-start | bytes 737288 | tf_op jit(solution)/shard_map/ppermute | solution.py:46
  36.4 18.2 %collective-permute-start.9 = (f32[2,8,3840]{2,1,0:T(8,128)S(1)}, f32[2,8,3840]{2,1,0:T(8,128)S(1)}, u32[]{:S(2)}, u32[]{:S(2)}) collective-permute-start(f32[2,8,3840]{2,1,0:T(8,128)S(1)} %collective-permute-done.8), channel_id=1, source_target_pairs={{0,32},{16,48},{32,64},{48,80},{64,96},{80,112},{96,128},{112,144}... | collective-permute-start | bytes 737288 | tf_op jit(solution)/shard_map/ppermute | solution.py:45
  38.5 53.6 %collective-permute-start.16 = (f32[2,8,3840]{2,1,0:T(8,128)S(1)}, f32[2,8,3840]{2,1,0:T(8,128)S(1)}, u32[]{:S(2)}, u32[]{:S(2)}) collective-permute-start(f32[2,8,3840]{2,1,0:T(8,128)S(1)} %maximum_select_fusion.1), channel_id=1, source_target_pairs={{0,16},{16,32},{32,48},{48,64},{64,80},{80,96},{96,112},{112,128},... | collective-permute-start | bytes 737288 | tf_op jit(solution)/shard_map/ppermute | solution.py:42
  42.1 14.6 %collective-permute-start.3 = (f32[2,8,3840]{2,1,0:T(8,128)S(1)}, f32[2,8,3840]{2,1,0:T(8,128)S(1)}, u32[]{:S(2)}, u32[]{:S(2)}) collective-permute-start(f32[2,8,3840]{2,1,0:T(8,128)S(1)} %collective-permute-done.2), channel_id=1, source_target_pairs={{0,240},{16,0},{32,16},{48,32},{64,48},{80,64},{96,80},{112,96},{1... | collective-permute-start | bytes 737288 | tf_op jit(solution)/shard_map/ppermute | solution.py:43
  46.5 26.9 %collective-permute-start.5 = (f32[2,8,3840]{2,1,0:T(8,128)S(1)}, f32[2,8,3840]{2,1,0:T(8,128)S(1)}, u32[]{:S(2)}, u32[]{:S(2)}) collective-permute-start(f32[2,8,3840]{2,1,0:T(8,128)S(1)} %collective-permute-done.4), channel_id=1, source_target_pairs={{0,240},{16,0},{32,16},{48,32},{64,48},{80,64},{96,80},{112,96},{1... | collective-permute-start | bytes 737288 | tf_op jit(solution)/shard_map/ppermute | solution.py:43
  49.8 15.5 %collective-permute-start.6 = (f32[2,8,3840]{2,1,0:T(8,128)S(1)}, f32[2,8,3840]{2,1,0:T(8,128)S(1)}, u32[]{:S(2)}, u32[]{:S(2)}) collective-permute-start(f32[2,8,3840]{2,1,0:T(8,128)S(1)} %collective-permute-done.4), channel_id=1, source_target_pairs={{0,224},{16,240},{32,0},{48,16},{64,32},{80,48},{96,64},{112,80},{... | collective-permute-start | bytes 737288 | tf_op jit(solution)/shard_map/ppermute | solution.py:46
  54.7 12.5 %collective-permute-start.10 = (f32[2,8,3840]{2,1,0:T(8,128)S(1)}, f32[2,8,3840]{2,1,0:T(8,128)S(1)}, u32[]{:S(2)}, u32[]{:S(2)}) collective-permute-start(f32[2,8,3840]{2,1,0:T(8,128)S(1)} %collective-permute-done.9), channel_id=1, source_target_pairs={{0,32},{16,48},{32,64},{48,80},{64,96},{80,112},{96,128},{112,144}... | collective-permute-start | bytes 737288 | tf_op jit(solution)/shard_map/ppermute | solution.py:45
  56.7 35.3 %collective-permute-start.15 = (f32[2,8,3840]{2,1,0:T(8,128)S(1)}, f32[2,8,3840]{2,1,0:T(8,128)S(1)}, u32[]{:S(2)}, u32[]{:S(2)}) collective-permute-start(f32[2,8,3840]{2,1,0:T(8,128)S(1)} %collective-permute-done.8), channel_id=1, source_target_pairs={{0,16},{16,32},{32,48},{48,64},{64,80},{80,96},{96,112},{112,128},... | collective-permute-start | bytes 737288 | tf_op jit(solution)/shard_map/ppermute | solution.py:42
  65.3 26.6 %collective-permute-start.14 = (f32[2,8,3840]{2,1,0:T(8,128)S(1)}, f32[2,8,3840]{2,1,0:T(8,128)S(1)}, u32[]{:S(2)}, u32[]{:S(2)}) collective-permute-start(f32[2,8,3840]{2,1,0:T(8,128)S(1)} %collective-permute-done.9), channel_id=1, source_target_pairs={{0,16},{16,32},{32,48},{48,64},{64,80},{80,96},{96,112},{112,128},... | collective-permute-start | bytes 737288 | tf_op jit(solution)/shard_map/ppermute | solution.py:42
  67.2 9.4 %collective-permute-start.12 = (f32[2,8,1920]{2,1,0:T(8,128)S(1)}, f32[2,8,1920]{2,1,0:T(8,128)S(1)}, u32[]{:S(2)}, u32[]{:S(2)}) collective-permute-start(f32[2,8,1920]{2,1,0:T(8,128)S(1)} %slice.42), channel_id=1, source_target_pairs={{0,224},{16,240},{32,0},{48,16},{64,32},{80,48},{96,64},{112,80},{... | collective-permute-start | bytes 368648 | tf_op jit(solution)/shard_map/ppermute | solution.py:51
  73.4 9.5 %collective-permute-start.11 = (f32[2,8,1920]{2,1,0:T(8,128)S(1)}, f32[2,8,1920]{2,1,0:T(8,128)S(1)}, u32[]{:S(2)}, u32[]{:S(2)}) collective-permute-start(f32[2,8,1920]{2,1,0:T(8,128)S(1)} %slice.41), channel_id=1, source_target_pairs={{0,32},{16,48},{32,64},{48,80},{64,96},{80,112},{96,128},{112,144}... | collective-permute-start | bytes 368648 | tf_op jit(solution)/shard_map/ppermute | solution.py:50
  76.6 11.8 %collective-permute-start.7 = (f32[2,8,3840]{2,1,0:T(8,128)S(1)}, f32[2,8,3840]{2,1,0:T(8,128)S(1)}, u32[]{:S(2)}, u32[]{:S(2)}) collective-permute-start(f32[2,8,3840]{2,1,0:T(8,128)S(1)} %collective-permute-done.6), channel_id=1, source_target_pairs={{0,240},{16,0},{32,16},{48,32},{64,48},{80,64},{96,80},{112,96},{1... | collective-permute-start | bytes 737288 | tf_op jit(solution)/shard_map/ppermute | solution.py:43
  82.9 9.0 %collective-permute-start.13 = (f32[2,8,3840]{2,1,0:T(8,128)S(1)}, f32[2,8,3840]{2,1,0:T(8,128)S(1)}, u32[]{:S(2)}, u32[]{:S(2)}) collective-permute-start(f32[2,8,3840]{2,1,0:T(8,128)S(1)} %collective-permute-done.10), channel_id=1, source_target_pairs={{0,16},{16,32},{32,48},{48,64},{64,80},{80,96},{96,112},{112,128},... | collective-permute-start | bytes 737288 | tf_op jit(solution)/shard_map/ppermute | solution.py:42
  96.0 1.3 copy-start.1
  100.3 18.6 %copy-start.2 = (s32[2,36]{1,0:T(2,128)S(1)}, s32[2,36]{1,0:T(2,128)}, u32[]{:S(2)}) copy-start(s32[2,36]{1,0:T(2,128)} %param.13) | copy-start | bytes 868
  101.3 9.8 %collective-permute-start.17 = (f32[8,16,5,384]{3,1,2,0:T(8,128)}, f32[8,16,5,384]{3,1,2,0:T(8,128)S(1)}, u32[]{:S(2)}, u32[]{:S(2)}) collective-permute-start(f32[8,16,5,384]{3,1,2,0:T(8,128)} %fusion.10), channel_id=1, source_target_pairs={{0,1},{1,0},{2,3},{3,2},{4,5},{5,4},{6,7},{7,6},{8,9},{9,8},{10,11... | collective-permute-start | bytes 2949128 | tf_op jit(solution)/shard_map/ppermute | solution.py:89
  112.2 20.4 %all-to-all-start = ((f32[8,16,5,384]{3,1,2,0:T(8,128)}), f32[8,16,5,384]{3,1,2,0:T(8,128)S(1)}, u32[]{:S(2)}, u32[]{:S(2)}) async-start(f32[8,16,5,384]{3,1,2,0:T(8,128)} %fusion.12), calls=%async_computation | async-start | bytes 1966080 | tf_op jit(solution)/shard_map/all_to_all | solution.py:91

commit v17 on v12

--- a/solution.py
+++ b/solution.py
@@ -85,8 +85,9 @@
     core = lax.axis_index("col") % CORES
     value = value.reshape(chips, CORES, rows, *value.shape[1:])
     partner_pairs = [(p, p ^ 1) for p in range(n_col)]
-    send = jnp.take(value, 1 - core, axis=1)
-    summed = jnp.take(value, core, axis=1) + lax.ppermute(send, "col", partner_pairs)
+    send = lax.dynamic_index_in_dim(value, 1 - core, axis=1, keepdims=False)
+    keep = lax.dynamic_index_in_dim(value, core, axis=1, keepdims=False)
+    summed = keep + lax.ppermute(send, "col", partner_pairs)
     groups = [list(range(e, n_col, CORES)) for e in range(CORES)]
     received = lax.all_to_all(summed, "col", 0, 0, tiled=True, axis_index_groups=groups)
     return jnp.sum(received, axis=0)

time: 135 us -> 134 us (level)
  no operation moved by 1% of the time
where the time goes in v17:
time: 134 us; the launch traced here: 133 us
  starting transfers between devices  85.9 us (64%)
  waiting for transfers between devices  28.5 us (21%)
  other arithmetic  6.91 us (5%)
  matrix products  5.33 us (4%)
  local copies, waits for them, and re-layouts  5.02 us (4%)
    ppermute x3, starting transfers between devices, gather_rows(): lane_down = lax.ppermute(lane_down, 'row', shift_pairs(n_row, nz, 1, -2))  23.3 us
    ppermute x4, starting transfers between devices, gather_rows(): lax.ppermute(lane_down, 'row', shift_pairs(n_row, nz, 1, -1))  16.5 us
    ppermute x4, starting transfers between devices, gather_rows(): lax.ppermute(lane_up, 'row', shift_pairs(n_row, nz, 1, 1))  14.3 us
    all_to_all x1, waiting for transfers between devices, reduce_cols_a2a(): lax.all_to_all(summed, 'col', 0, 0, tiled=True, axis_index_groups=groups)  13.7 us
    ppermute x1, starting transfers between devices, reduce_cols_a2a(): summed = keep + lax.ppermute(send, 'col', partner_pairs)  7.48 us
    all_to_all x1, starting transfers between devices, reduce_cols_a2a(): lax.all_to_all(summed, 'col', 0, 0, tiled=True, axis_index_groups=groups)  6.63 us
    ppermute x1, starting transfers between devices, gather_rows(): lax.ppermute(lane_down[..., half:], 'row', shift_pairs(n_row, nz, 1, -2))  6.13 us
    ppermute x3, starting transfers between devices, gather_rows(): lane_up = lax.ppermute(lane_up, 'row', shift_pairs(n_row, nz, 1, 2))  5.76 us
  transfers between devices with their start and end apart: 19, of which 7 were waited for; matrix products, arithmetic and copies ran while one was open for 4% of the time, Pallas kernels for 0%

profile of v17, /device:TPU:1, one launch (start us, length us, event | category | flops | bytes accessed | tf_op | source)
XLA Modules:
  0.0 132.9 jit_solution(17023027496704109325)
XLA Ops:
  0.6 0.0 copy-start
  0.6 1.0 constant_dynamic-update-slice_fusion.1
  1.6 0.8 constant_dynamic-update-slice_fusion
  2.4 3.9 %collective-permute-start = (f32[8,3840]{1,0:T(8,128)S(1)}, f32[8,3840]{1,0:T(8,128)S(1)}, u32[]{:S(2)}, u32[]{:S(2)}) collective-permute-start(f32[8,3840]{1,0:T(8,128)S(1)} %bitcast.52), channel_id=1, source_target_pairs={{0,256},{16,272},{32,288},{48,304},{64,320},{80,336},{96,352},{112... | collective-permute-start | bytes 368648 | tf_op jit(solution)/shard_map/ppermute | solution.py:33
  6.4 0.7 compare_select_fusion
  7.0 0.7 compare_and_fusion
  7.7 0.8 compare_reduce_fusion.2
  8.5 0.6 gather_fusion
  9.1 0.1 broadcast_select_fusion
  9.2 0.0 collective-permute-done
  9.2 11.7 %collective-permute-start.2 = (f32[2,8,3840]{2,1,0:T(8,128)S(1)}, f32[2,8,3840]{2,1,0:T(8,128)S(1)}, u32[]{:S(2)}, u32[]{:S(2)}) collective-permute-start(f32[2,8,3840]{2,1,0:T(8,128)S(1)} %maximum_select_fusion.1), channel_id=1, source_target_pairs={{0,224},{16,240},{32,0},{48,16},{64,32},{80,48},{96,64},{112,80},{... | collective-permute-start | bytes 737288 | tf_op jit(solution)/shard_map/ppermute | solution.py:46
  20.9 1.9 %collective-permute-start.8 = (f32[2,8,3840]{2,1,0:T(8,128)S(1)}, f32[2,8,3840]{2,1,0:T(8,128)S(1)}, u32[]{:S(2)}, u32[]{:S(2)}) collective-permute-start(f32[2,8,3840]{2,1,0:T(8,128)S(1)} %maximum_select_fusion.1), channel_id=1, source_target_pairs={{0,32},{16,48},{32,64},{48,80},{64,96},{80,112},{96,128},{112,144}... | collective-permute-start | bytes 737288 | tf_op jit(solution)/shard_map/ppermute | solution.py:45
  22.9 0.8 compare_reduce_fusion
  23.7 5.0 %collective-permute-start.1 = (f32[2,8,3840]{2,1,0:T(8,128)S(1)}, f32[2,8,3840]{2,1,0:T(8,128)S(1)}, u32[]{:S(2)}, u32[]{:S(2)}) collective-permute-start(f32[2,8,3840]{2,1,0:T(8,128)S(1)} %maximum_select_fusion.1), channel_id=1, source_target_pairs={{0,240},{16,0},{32,16},{48,32},{64,48},{80,64},{96,80},{112,96},{1... | collective-permute-start | bytes 737288 | tf_op jit(solution)/shard_map/ppermute | solution.py:43
  28.7 0.8 compare_reduce_fusion.1
  29.5 0.2 collective-permute-done.2
  29.7 6.7 %collective-permute-start.4 = (f32[2,8,3840]{2,1,0:T(8,128)S(1)}, f32[2,8,3840]{2,1,0:T(8,128)S(1)}, u32[]{:S(2)}, u32[]{:S(2)}) collective-permute-start(f32[2,8,3840]{2,1,0:T(8,128)S(1)} %collective-permute-done.2), channel_id=1, source_target_pairs={{0,224},{16,240},{32,0},{48,16},{64,32},{80,48},{96,64},{112,80},{... | collective-permute-start | bytes 737288 | tf_op jit(solution)/shard_map/ppermute | solution.py:46
  36.4 0.0 collective-permute-done.8
  36.4 1.9 %collective-permute-start.9 = (f32[2,8,3840]{2,1,0:T(8,128)S(1)}, f32[2,8,3840]{2,1,0:T(8,128)S(1)}, u32[]{:S(2)}, u32[]{:S(2)}) collective-permute-start(f32[2,8,3840]{2,1,0:T(8,128)S(1)} %collective-permute-done.8), channel_id=1, source_target_pairs={{0,32},{16,48},{32,64},{48,80},{64,96},{80,112},{96,128},{112,144}... | collective-permute-start | bytes 737288 | tf_op jit(solution)/shard_map/ppermute | solution.py:45
  38.4 3.6 %collective-permute-start.16 = (f32[2,8,3840]{2,1,0:T(8,128)S(1)}, f32[2,8,3840]{2,1,0:T(8,128)S(1)}, u32[]{:S(2)}, u32[]{:S(2)}) collective-permute-start(f32[2,8,3840]{2,1,0:T(8,128)S(1)} %maximum_select_fusion.1), channel_id=1, source_target_pairs={{0,16},{16,32},{32,48},{48,64},{64,80},{80,96},{96,112},{112,128},... | collective-permute-start | bytes 737288 | tf_op jit(solution)/shard_map/ppermute | solution.py:42
  42.1 4.3 %collective-permute-start.3 = (f32[2,8,3840]{2,1,0:T(8,128)S(1)}, f32[2,8,3840]{2,1,0:T(8,128)S(1)}, u32[]{:S(2)}, u32[]{:S(2)}) collective-permute-start(f32[2,8,3840]{2,1,0:T(8,128)S(1)} %collective-permute-done.2), channel_id=1, source_target_pairs={{0,240},{16,0},{32,16},{48,32},{64,48},{80,64},{96,80},{112,96},{1... | collective-permute-start | bytes 737288 | tf_op jit(solution)/shard_map/ppermute | solution.py:43
  46.4 0.0 collective-permute-done.1
  46.5 0.0 collective-permute-done.4
  46.5 3.4 %collective-permute-start.5 = (f32[2,8,3840]{2,1,0:T(8,128)S(1)}, f32[2,8,3840]{2,1,0:T(8,128)S(1)}, u32[]{:S(2)}, u32[]{:S(2)}) collective-permute-start(f32[2,8,3840]{2,1,0:T(8,128)S(1)} %collective-permute-done.4), channel_id=1, source_target_pairs={{0,240},{16,0},{32,16},{48,32},{64,48},{80,64},{96,80},{112,96},{1... | collective-permute-start | bytes 737288 | tf_op jit(solution)/shard_map/ppermute | solution.py:43
  49.8 4.9 %collective-permute-start.6 = (f32[2,8,3840]{2,1,0:T(8,128)S(1)}, f32[2,8,3840]{2,1,0:T(8,128)S(1)}, u32[]{:S(2)}, u32[]{:S(2)}) collective-permute-start(f32[2,8,3840]{2,1,0:T(8,128)S(1)} %collective-permute-done.4), channel_id=1, source_target_pairs={{0,224},{16,240},{32,0},{48,16},{64,32},{80,48},{96,64},{112,80},{... | collective-permute-start | bytes 737288 | tf_op jit(solution)/shard_map/ppermute | solution.py:46
  54.7 0.0 collective-permute-done.9
  54.7 1.9 %collective-permute-start.10 = (f32[2,8,3840]{2,1,0:T(8,128)S(1)}, f32[2,8,3840]{2,1,0:T(8,128)S(1)}, u32[]{:S(2)}, u32[]{:S(2)}) collective-permute-start(f32[2,8,3840]{2,1,0:T(8,128)S(1)} %collective-permute-done.9), channel_id=1, source_target_pairs={{0,32},{16,48},{32,64},{48,80},{64,96},{80,112},{96,128},{112,144}... | collective-permute-start | bytes 737288 | tf_op jit(solution)/shard_map/ppermute | solution.py:45
  56.7 0.0 collective-permute-done.3
  56.7 3.4 %collective-permute-start.15 = (f32[2,8,3840]{2,1,0:T(8,128)S(1)}, f32[2,8,3840]{2,1,0:T(8,128)S(1)}, u32[]{:S(2)}, u32[]{:S(2)}) collective-permute-start(f32[2,8,3840]{2,1,0:T(8,128)S(1)} %collective-permute-done.8), channel_id=1, source_target_pairs={{0,16},{16,32},{32,48},{48,64},{64,80},{80,96},{96,112},{112,128},... | collective-permute-start | bytes 737288 | tf_op jit(solution)/shard_map/ppermute | solution.py:42
  60.1 5.2 %collective-permute-done.6 = f32[2,8,3840]{2,1,0:T(8,128)S(1)} collective-permute-done((f32[2,8,3840]{2,1,0:T(8,128)S(1)}, f32[2,8,3840]{2,1,0:T(8,128)S(1)}, u32[]{:S(2)}, u32[]{:S(2)}) %collective-permute-start.6) | collective-permute-done | bytes 245792 | tf_op jit(solution)/shard_map/ppermute | solution.py:46
  65.3 1.9 %collective-permute-start.14 = (f32[2,8,3840]{2,1,0:T(8,128)S(1)}, f32[2,8,3840]{2,1,0:T(8,128)S(1)}, u32[]{:S(2)}, u32[]{:S(2)}) collective-permute-start(f32[2,8,3840]{2,1,0:T(8,128)S(1)} %collective-permute-done.9), channel_id=1, source_target_pairs={{0,16},{16,32},{32,48},{48,64},{64,80},{80,96},{96,112},{112,128},... | collective-permute-start | bytes 737288 | tf_op jit(solution)/shard_map/ppermute | solution.py:42
  67.2 0.0 collective-permute-done.10
  67.2 6.1 %collective-permute-start.12 = (f32[2,8,1920]{2,1,0:T(8,128)S(1)}, f32[2,8,1920]{2,1,0:T(8,128)S(1)}, u32[]{:S(2)}, u32[]{:S(2)}) collective-permute-start(f32[2,8,1920]{2,1,0:T(8,128)S(1)} %slice.29), channel_id=1, source_target_pairs={{0,224},{16,240},{32,0},{48,16},{64,32},{80,48},{96,64},{112,80},{... | collective-permute-start | bytes 368648 | tf_op jit(solution)/shard_map/ppermute | solution.py:51
  73.4 0.0 collective-permute-done.5
  73.4 1.9 %collective-permute-start.11 = (f32[2,8,1920]{2,1,0:T(8,128)S(1)}, f32[2,8,1920]{2,1,0:T(8,128)S(1)}, u32[]{:S(2)}, u32[]{:S(2)}) collective-permute-start(f32[2,8,1920]{2,1,0:T(8,128)S(1)} %slice.28), channel_id=1, source_target_pairs={{0,32},{16,48},{32,64},{48,80},{64,96},{80,112},{96,128},{112,144}... | collective-permute-start | bytes 368648 | tf_op jit(solution)/shard_map/ppermute | solution.py:50
  75.4 1.2 collective-permute-done.12
  76.6 3.8 %collective-permute-start.7 = (f32[2,8,3840]{2,1,0:T(8,128)S(1)}, f32[2,8,3840]{2,1,0:T(8,128)S(1)}, u32[]{:S(2)}, u32[]{:S(2)}) collective-permute-start(f32[2,8,3840]{2,1,0:T(8,128)S(1)} %collective-permute-done.6), channel_id=1, source_target_pairs={{0,240},{16,0},{32,16},{48,32},{64,48},{80,64},{96,80},{112,96},{1... | collective-permute-start | bytes 737288 | tf_op jit(solution)/shard_map/ppermute | solution.py:43
  80.4 2.5 %collective-permute-done.11 = f32[2,8,1920]{2,1,0:T(8,128)S(1)} collective-permute-done((f32[2,8,1920]{2,1,0:T(8,128)S(1)}, f32[2,8,1920]{2,1,0:T(8,128)S(1)}, u32[]{:S(2)}, u32[]{:S(2)}) %collective-permute-start.11) | collective-permute-done | bytes 122912 | tf_op jit(solution)/shard_map/ppermute | solution.py:50
  82.9 5.4 %collective-permute-start.13 = (f32[2,8,3840]{2,1,0:T(8,128)S(1)}, f32[2,8,3840]{2,1,0:T(8,128)S(1)}, u32[]{:S(2)}, u32[]{:S(2)}) collective-permute-start(f32[2,8,3840]{2,1,0:T(8,128)S(1)} %collective-permute-done.10), channel_id=1, source_target_pairs={{0,16},{16,32},{32,48},{48,64},{64,80},{80,96},{96,112},{112,128},... | collective-permute-start | bytes 737288 | tf_op jit(solution)/shard_map/ppermute | solution.py:42
  88.4 0.0 collective-permute-done.7
  88.4 3.4 %collective-permute-done.13 = f32[2,8,3840]{2,1,0:T(8,128)S(1)} collective-permute-done((f32[2,8,3840]{2,1,0:T(8,128)S(1)}, f32[2,8,3840]{2,1,0:T(8,128)S(1)}, u32[]{:S(2)}, u32[]{:S(2)}) %collective-permute-start.13) | collective-permute-done | bytes 245792 | tf_op jit(solution)/shard_map/ppermute | solution.py:42
  91.9 0.0 collective-permute-done.14
  92.0 0.0 collective-permute-done.15
  92.1 0.0 collective-permute-done.16
  92.1 3.3 %fusion.4 = f32[2,16,8,5,384]{4,2,3,0,1:T(8,128)S(1)} fusion(f32[16,2,8,5,768]{4,2,3,1,0:T(8,128)S(1)} %constant_dynamic-update-slice_fusion.2, f32[5,768]{1,0:T(8,128)S(1)} %add_convert_fusion, f32[384,768]{1,0:T(8,128)S(1)} %copy-done), kind=kOutput, calls=%fused_computation.9 | convolution fusion | flops 2265907200 | bytes 7093248 | tf_op jit(solution)/shard_map/tlkmj,ij->ltkmi/dot_general | solution.py:121
  95.4 0.4 fusion.2
  95.8 0.2 copy.16
  96.0 1.3 copy-done.1
  97.3 0.1 slice.30
  97.4 0.6 gather_fusion.1
  98.0 2.0 %fusion.8 = f32[256,2,384]{2,0,1:T(8,128)S(1)} fusion(f32[2,256,256]{2,1,0:T(8,128)} %param.13, f32[256,5,384]{2,0,1:T(8,128)} %bitcast.48, f32[2,256,384]{2,1,0:T(8,128)S(1)} %gather_fusion.1, f32[2,384]{1,0:T(2,128)S(1)} %broadcast_select_fusion, pred[2]{0:T(512)(128)(4,1)S(1)} %compare_and_fusion), kind=kOutput, calls=%fused_computation.12 | convolution fusion | flops 302579712 | bytes 2886658 | tf_op jit(solution)/shard_map/cqk,qci->kci/dot_general | solution.py:129
  100.0 0.1 pad_maximum_fusion
  100.1 0.2 constant_dynamic-slice_fusion.1
  100.3 0.0 copy-start.2
  100.3 0.1 copy.24
  100.4 7.5 %collective-permute-start.17 = (f32[8,16,5,384]{3,1,2,0:T(8,128)S(1)}, f32[8,16,5,384]{3,1,2,0:T(8,128)S(1)}, u32[]{:S(2)}, u32[]{:S(2)}) collective-permute-start(f32[8,16,5,384]{3,1,2,0:T(8,128)S(1)} %bitcast.50), channel_id=1, source_target_pairs={{0,1},{1,0},{2,3},{3,2},{4,5},{5,4},{6,7},{7,6},{8,9},{9,8},{10,11... | collective-permute-start | bytes 2949128 | tf_op jit(solution)/shard_map/ppermute | solution.py:90
  107.9 2.2 %collective-permute-done.17 = f32[8,16,5,384]{3,1,2,0:T(8,128)S(1)} collective-permute-done((f32[8,16,5,384]{3,1,2,0:T(8,128)S(1)}, f32[8,16,5,384]{3,1,2,0:T(8,128)S(1)}, u32[]{:S(2)}, u32[]{:S(2)}) %collective-permute-start.17) | collective-permute-done | bytes 983072 | tf_op jit(solution)/shard_map/ppermute | solution.py:90
  110.0 1.1 bitcast_add_fusion
  111.1 6.6 %all-to-all-start = ((f32[8,16,5,384]{3,1,2,0:T(8,128)}), f32[8,16,5,384]{3,1,2,0:T(8,128)S(1)}, u32[]{:S(2)}, u32[]{:S(2)}) async-start(f32[8,16,5,384]{3,1,2,0:T(8,128)} %bitcast_add_fusion), calls=%async_computation | async-start | bytes 1966080 | tf_op jit(solution)/shard_map/all_to_all | solution.py:92
  117.7 0.1 compare_reduce_fusion.3
  117.9 13.7 %all-to-all-done = f32[8,16,5,384]{3,1,2,0:T(8,128)S(1)} async-done(((f32[8,16,5,384]{3,1,2,0:T(8,128)}), f32[8,16,5,384]{3,1,2,0:T(8,128)S(1)}, u32[]{:S(2)}, u32[]{:S(2)}) %all-to-all-start) | async-done | bytes 983072 | tf_op jit(solution)/shard_map/all_to_all | solution.py:92
  131.6 0.1 reduce_sum.9
  131.6 0.6 slice_multiply_fusion
  132.3 0.6 slice_multiply_fusion.1
  (30 shorter events, 0.4 us)
Async XLA Ops:
  0.6 91.5 %copy-start = (f32[384,768]{1,0:T(8,128)S(1)}, f32[384,768]{1,0:T(8,128)}, u32[]{:S(2)}) copy-start(f32[384,768]{1,0:T(8,128)} %param.7) | copy-start | bytes 3538948
  2.4 6.8 %collective-permute-start = (f32[8,3840]{1,0:T(8,128)S(1)}, f32[8,3840]{1,0:T(8,128)S(1)}, u32[]{:S(2)}, u32[]{:S(2)}) collective-permute-start(f32[8,3840]{1,0:T(8,128)S(1)} %bitcast.52), channel_id=1, source_target_pairs={{0,256},{16,272},{32,288},{48,304},{64,320},{80,336},{96,352},{112... | collective-permute-start | bytes 368648 | tf_op jit(solution)/shard_map/ppermute | solution.py:33
  9.2 20.5 %collective-permute-start.2 = (f32[2,8,3840]{2,1,0:T(8,128)S(1)}, f32[2,8,3840]{2,1,0:T(8,128)S(1)}, u32[]{:S(2)}, u32[]{:S(2)}) collective-permute-start(f32[2,8,3840]{2,1,0:T(8,128)S(1)} %maximum_select_fusion.1), channel_id=1, source_target_pairs={{0,224},{16,240},{32,0},{48,16},{64,32},{80,48},{96,64},{112,80},{... | collective-permute-start | bytes 737288 | tf_op jit(solution)/shard_map/ppermute | solution.py:46
  20.9 15.5 %collective-permute-start.8 = (f32[2,8,3840]{2,1,0:T(8,128)S(1)}, f32[2,8,3840]{2,1,0:T(8,128)S(1)}, u32[]{:S(2)}, u32[]{:S(2)}) collective-permute-start(f32[2,8,3840]{2,1,0:T(8,128)S(1)} %maximum_select_fusion.1), channel_id=1, source_target_pairs={{0,32},{16,48},{32,64},{48,80},{64,96},{80,112},{96,128},{112,144}... | collective-permute-start | bytes 737288 | tf_op jit(solution)/shard_map/ppermute | solution.py:45
  23.7 22.7 %collective-permute-start.1 = (f32[2,8,3840]{2,1,0:T(8,128)S(1)}, f32[2,8,3840]{2,1,0:T(8,128)S(1)}, u32[]{:S(2)}, u32[]{:S(2)}) collective-permute-start(f32[2,8,3840]{2,1,0:T(8,128)S(1)} %maximum_select_fusion.1), channel_id=1, source_target_pairs={{0,240},{16,0},{32,16},{48,32},{64,48},{80,64},{96,80},{112,96},{1... | collective-permute-start | bytes 737288 | tf_op jit(solution)/shard_map/ppermute | solution.py:43
  29.7 16.7 %collective-permute-start.4 = (f32[2,8,3840]{2,1,0:T(8,128)S(1)}, f32[2,8,3840]{2,1,0:T(8,128)S(1)}, u32[]{:S(2)}, u32[]{:S(2)}) collective-permute-start(f32[2,8,3840]{2,1,0:T(8,128)S(1)} %collective-permute-done.2), channel_id=1, source_target_pairs={{0,224},{16,240},{32,0},{48,16},{64,32},{80,48},{96,64},{112,80},{... | collective-permute-start | bytes 737288 | tf_op jit(solution)/shard_map/ppermute | solution.py:46
  36.4 18.2 %collective-permute-start.9 = (f32[2,8,3840]{2,1,0:T(8,128)S(1)}, f32[2,8,3840]{2,1,0:T(8,128)S(1)}, u32[]{:S(2)}, u32[]{:S(2)}) collective-permute-start(f32[2,8,3840]{2,1,0:T(8,128)S(1)} %collective-permute-done.8), channel_id=1, source_target_pairs={{0,32},{16,48},{32,64},{48,80},{64,96},{80,112},{96,128},{112,144}... | collective-permute-start | bytes 737288 | tf_op jit(solution)/shard_map/ppermute | solution.py:45
  38.4 53.6 %collective-permute-start.16 = (f32[2,8,3840]{2,1,0:T(8,128)S(1)}, f32[2,8,3840]{2,1,0:T(8,128)S(1)}, u32[]{:S(2)}, u32[]{:S(2)}) collective-permute-start(f32[2,8,3840]{2,1,0:T(8,128)S(1)} %maximum_select_fusion.1), channel_id=1, source_target_pairs={{0,16},{16,32},{32,48},{48,64},{64,80},{80,96},{96,112},{112,128},... | collective-permute-start | bytes 737288 | tf_op jit(solution)/shard_map/ppermute | solution.py:42
  42.1 14.6 %collective-permute-start.3 = (f32[2,8,3840]{2,1,0:T(8,128)S(1)}, f32[2,8,3840]{2,1,0:T(8,128)S(1)}, u32[]{:S(2)}, u32[]{:S(2)}) collective-permute-start(f32[2,8,3840]{2,1,0:T(8,128)S(1)} %collective-permute-done.2), channel_id=1, source_target_pairs={{0,240},{16,0},{32,16},{48,32},{64,48},{80,64},{96,80},{112,96},{1... | collective-permute-start | bytes 737288 | tf_op jit(solution)/shard_map/ppermute | solution.py:43
  46.5 26.9 %collective-permute-start.5 = (f32[2,8,3840]{2,1,0:T(8,128)S(1)}, f32[2,8,3840]{2,1,0:T(8,128)S(1)}, u32[]{:S(2)}, u32[]{:S(2)}) collective-permute-start(f32[2,8,3840]{2,1,0:T(8,128)S(1)} %collective-permute-done.4), channel_id=1, source_target_pairs={{0,240},{16,0},{32,16},{48,32},{64,48},{80,64},{96,80},{112,96},{1... | collective-permute-start | bytes 737288 | tf_op jit(solution)/shard_map/ppermute | solution.py:43
  49.8 15.5 %collective-permute-start.6 = (f32[2,8,3840]{2,1,0:T(8,128)S(1)}, f32[2,8,3840]{2,1,0:T(8,128)S(1)}, u32[]{:S(2)}, u32[]{:S(2)}) collective-permute-start(f32[2,8,3840]{2,1,0:T(8,128)S(1)} %collective-permute-done.4), channel_id=1, source_target_pairs={{0,224},{16,240},{32,0},{48,16},{64,32},{80,48},{96,64},{112,80},{... | collective-permute-start | bytes 737288 | tf_op jit(solution)/shard_map/ppermute | solution.py:46
  54.7 12.5 %collective-permute-start.10 = (f32[2,8,3840]{2,1,0:T(8,128)S(1)}, f32[2,8,3840]{2,1,0:T(8,128)S(1)}, u32[]{:S(2)}, u32[]{:S(2)}) collective-permute-start(f32[2,8,3840]{2,1,0:T(8,128)S(1)} %collective-permute-done.9), channel_id=1, source_target_pairs={{0,32},{16,48},{32,64},{48,80},{64,96},{80,112},{96,128},{112,144}... | collective-permute-start | bytes 737288 | tf_op jit(solution)/shard_map/ppermute | solution.py:45
  56.7 35.3 %collective-permute-start.15 = (f32[2,8,3840]{2,1,0:T(8,128)S(1)}, f32[2,8,3840]{2,1,0:T(8,128)S(1)}, u32[]{:S(2)}, u32[]{:S(2)}) collective-permute-start(f32[2,8,3840]{2,1,0:T(8,128)S(1)} %collective-permute-done.8), channel_id=1, source_target_pairs={{0,16},{16,32},{32,48},{48,64},{64,80},{80,96},{96,112},{112,128},... | collective-permute-start | bytes 737288 | tf_op jit(solution)/shard_map/ppermute | solution.py:42
  65.3 26.6 %collective-permute-start.14 = (f32[2,8,3840]{2,1,0:T(8,128)S(1)}, f32[2,8,3840]{2,1,0:T(8,128)S(1)}, u32[]{:S(2)}, u32[]{:S(2)}) collective-permute-start(f32[2,8,3840]{2,1,0:T(8,128)S(1)} %collective-permute-done.9), channel_id=1, source_target_pairs={{0,16},{16,32},{32,48},{48,64},{64,80},{80,96},{96,112},{112,128},... | collective-permute-start | bytes 737288 | tf_op jit(solution)/shard_map/ppermute | solution.py:42
  67.2 9.4 %collective-permute-start.12 = (f32[2,8,1920]{2,1,0:T(8,128)S(1)}, f32[2,8,1920]{2,1,0:T(8,128)S(1)}, u32[]{:S(2)}, u32[]{:S(2)}) collective-permute-start(f32[2,8,1920]{2,1,0:T(8,128)S(1)} %slice.29), channel_id=1, source_target_pairs={{0,224},{16,240},{32,0},{48,16},{64,32},{80,48},{96,64},{112,80},{... | collective-permute-start | bytes 368648 | tf_op jit(solution)/shard_map/ppermute | solution.py:51
  73.4 9.5 %collective-permute-start.11 = (f32[2,8,1920]{2,1,0:T(8,128)S(1)}, f32[2,8,1920]{2,1,0:T(8,128)S(1)}, u32[]{:S(2)}, u32[]{:S(2)}) collective-permute-start(f32[2,8,1920]{2,1,0:T(8,128)S(1)} %slice.28), channel_id=1, source_target_pairs={{0,32},{16,48},{32,64},{48,80},{64,96},{80,112},{96,128},{112,144}... | collective-permute-start | bytes 368648 | tf_op jit(solution)/shard_map/ppermute | solution.py:50
  76.6 11.7 %collective-permute-start.7 = (f32[2,8,3840]{2,1,0:T(8,128)S(1)}, f32[2,8,3840]{2,1,0:T(8,128)S(1)}, u32[]{:S(2)}, u32[]{:S(2)}) collective-permute-start(f32[2,8,3840]{2,1,0:T(8,128)S(1)} %collective-permute-done.6), channel_id=1, source_target_pairs={{0,240},{16,0},{32,16},{48,32},{64,48},{80,64},{96,80},{112,96},{1... | collective-permute-start | bytes 737288 | tf_op jit(solution)/shard_map/ppermute | solution.py:43
  82.9 9.0 %collective-permute-start.13 = (f32[2,8,3840]{2,1,0:T(8,128)S(1)}, f32[2,8,3840]{2,1,0:T(8,128)S(1)}, u32[]{:S(2)}, u32[]{:S(2)}) collective-permute-start(f32[2,8,3840]{2,1,0:T(8,128)S(1)} %collective-permute-done.10), channel_id=1, source_target_pairs={{0,16},{16,32},{32,48},{48,64},{64,80},{80,96},{96,112},{112,128},... | collective-permute-start | bytes 737288 | tf_op jit(solution)/shard_map/ppermute | solution.py:42
  96.0 1.3 copy-start.1
  100.3 17.4 %copy-start.2 = (s32[2,36]{1,0:T(2,128)S(1)}, s32[2,36]{1,0:T(2,128)}, u32[]{:S(2)}) copy-start(s32[2,36]{1,0:T(2,128)} %param.11) | copy-start | bytes 868
  100.4 9.7 %collective-permute-start.17 = (f32[8,16,5,384]{3,1,2,0:T(8,128)S(1)}, f32[8,16,5,384]{3,1,2,0:T(8,128)S(1)}, u32[]{:S(2)}, u32[]{:S(2)}) collective-permute-start(f32[8,16,5,384]{3,1,2,0:T(8,128)S(1)} %bitcast.50), channel_id=1, source_target_pairs={{0,1},{1,0},{2,3},{3,2},{4,5},{5,4},{6,7},{7,6},{8,9},{9,8},{10,11... | collective-permute-start | bytes 2949128 | tf_op jit(solution)/shard_map/ppermute | solution.py:90
  111.1 20.4 %all-to-all-start = ((f32[8,16,5,384]{3,1,2,0:T(8,128)}), f32[8,16,5,384]{3,1,2,0:T(8,128)S(1)}, u32[]{:S(2)}, u32[]{:S(2)}) async-start(f32[8,16,5,384]{3,1,2,0:T(8,128)} %bitcast_add_fusion), calls=%async_computation | async-start | bytes 1966080 | tf_op jit(solution)/shard_map/all_to_all | solution.py:92

commit v18 on v17

--- a/solution.py
+++ b/solution.py
@@ -124,7 +124,10 @@
     partial_value = jnp.roll(partial_value, z, axis=1)
     partial_value = partial_value.reshape(panel_width, members, local_rows)
     first_partial = partial_value[:, :n_first]
-    chosen = jnp.take(first_partial, parents, axis=1)
+    chosen = jnp.stack(
+        [lax.dynamic_index_in_dim(first_partial, parents[c], axis=1, keepdims=False) for c in range(n_second)],
+        axis=1,
+    )
     chosen_mask = jnp.take(out_first, parents, axis=0)
     coupling = jnp.einsum("cqk,qci->kci", parent_link, chosen, precision=high)
     second_partial = partial_value[:, n_first:] - chosen_mask[None, :, :] * coupling

time: 134 us -> 136 us (1.015)
  starting transfers between devices: 85.9 us -> 81.7 us
  between operations: 1.24 us -> 5.1 us
  waiting for transfers between devices: 28.5 us -> 32.3 us
  matrix products: 5.33 us -> 3.96 us
    ppermute x4, starting transfers between devices: 14.3 us -> 9.8 us  [gather_rows(): lax.ppermute(lane_up, 'row', shift_pairs(n_row, nz, 1, 1))]
    ppermute x3, starting transfers between devices: 23.3 us -> 20.3 us  [gather_rows(): lane_down = lax.ppermute(lane_down, 'row', shift_pairs(n_row, nz, 1, -2))]
    ppermute x3, waiting for transfers between devices: 5.41 us -> 8.08 us  [gather_rows(): lane_down = lax.ppermute(lane_down, 'row', shift_pairs(n_row, nz, 1, -2))]
    ppermute x3, starting transfers between devices: 5.76 us -> 8.1 us  [gather_rows(): lane_up = lax.ppermute(lane_up, 'row', shift_pairs(n_row, nz, 1, 2))]
    ppermute x4, waiting for transfers between devices: 3.45 us -> 5.69 us  [gather_rows(): lax.ppermute(lane_up, 'row', shift_pairs(n_row, nz, 1, 1))]
    dot_general x1, matrix products: 2.01 us -> 0.64 us  [local(): coupling = jnp.einsum('cqk,qci->kci', parent_link, chosen, precision=high)]
  transfers between devices with their start and end apart: 19 -> 19, of which waited for: 7 -> 7; matrix products, arithmetic and copies ran while one was open for 4% -> 5% of each run, Pallas kernels for 0% -> 0%
where the time goes in v18:
time: 136 us; the launch traced here: 135 us
  starting transfers between devices  81.7 us (60%)
  waiting for transfers between devices  32.3 us (24%)
  other arithmetic  6.91 us (5%)
  local copies, waits for them, and re-layouts  5.22 us (4%)
  between operations  5.1 us (4%)
  matrix products  3.96 us (3%)
    ppermute x3, starting transfers between devices, gather_rows(): lane_down = lax.ppermute(lane_down, 'row', shift_pairs(n_row, nz, 1, -2))  20.3 us
    ppermute x4, starting transfers between devices, gather_rows(): lax.ppermute(lane_down, 'row', shift_pairs(n_row, nz, 1, -1))  16.5 us
    all_to_all x1, waiting for transfers between devices, reduce_cols_a2a(): lax.all_to_all(summed, 'col', 0, 0, tiled=True, axis_index_groups=groups)  13.7 us
    ppermute x4, starting transfers between devices, gather_rows(): lax.ppermute(lane_up, 'row', shift_pairs(n_row, nz, 1, 1))  9.8 us
    ppermute x1, starting transfers between devices, reduce_cols_a2a(): summed = keep + lax.ppermute(send, 'col', partner_pairs)  8.57 us
    ppermute x3, starting transfers between devices, gather_rows(): lane_up = lax.ppermute(lane_up, 'row', shift_pairs(n_row, nz, 1, 2))  8.1 us
    ppermute x3, waiting for transfers between devices, gather_rows(): lane_down = lax.ppermute(lane_down, 'row', shift_pairs(n_row, nz, 1, -2))  8.08 us
    all_to_all x1, starting transfers between devices, reduce_cols_a2a(): lax.all_to_all(summed, 'col', 0, 0, tiled=True, axis_index_groups=groups)  6.65 us
  transfers between devices with their start and end apart: 19, of which 7 were waited for; matrix products, arithmetic and copies ran while one was open for 5% of the time, Pallas kernels for 0%

profile of v18, /device:TPU:1, one launch (start us, length us, event | category | flops | bytes accessed | tf_op | source)
XLA Modules:
  0.0 135.2 jit_solution(2011659405953274751)
XLA Ops:
  0.6 0.0 copy-start
  0.6 1.0 constant_dynamic-update-slice_fusion.1
  1.6 0.8 constant_dynamic-update-slice_fusion
  2.4 3.9 %collective-permute-start = (f32[8,3840]{1,0:T(8,128)S(1)}, f32[8,3840]{1,0:T(8,128)S(1)}, u32[]{:S(2)}, u32[]{:S(2)}) collective-permute-start(f32[8,3840]{1,0:T(8,128)S(1)} %bitcast.51), channel_id=1, source_target_pairs={{0,256},{16,272},{32,288},{48,304},{64,320},{80,336},{96,352},{112... | collective-permute-start | bytes 368648 | tf_op jit(solution)/shard_map/ppermute | solution.py:33
  6.4 0.7 compare_select_fusion
  7.0 0.7 compare_and_fusion
  7.7 0.8 compare_reduce_fusion.2
  8.5 0.6 gather_fusion
  9.1 0.1 broadcast_select_fusion
  9.2 0.0 collective-permute-done
  9.2 11.7 %collective-permute-start.2 = (f32[2,8,3840]{2,1,0:T(8,128)S(1)}, f32[2,8,3840]{2,1,0:T(8,128)S(1)}, u32[]{:S(2)}, u32[]{:S(2)}) collective-permute-start(f32[2,8,3840]{2,1,0:T(8,128)S(1)} %maximum_select_fusion.1), channel_id=1, source_target_pairs={{0,224},{16,240},{32,0},{48,16},{64,32},{80,48},{96,64},{112,80},{... | collective-permute-start | bytes 737288 | tf_op jit(solution)/shard_map/ppermute | solution.py:46
  20.9 1.9 %collective-permute-start.8 = (f32[2,8,3840]{2,1,0:T(8,128)S(1)}, f32[2,8,3840]{2,1,0:T(8,128)S(1)}, u32[]{:S(2)}, u32[]{:S(2)}) collective-permute-start(f32[2,8,3840]{2,1,0:T(8,128)S(1)} %maximum_select_fusion.1), channel_id=1, source_target_pairs={{0,32},{16,48},{32,64},{48,80},{64,96},{80,112},{96,128},{112,144}... | collective-permute-start | bytes 737288 | tf_op jit(solution)/shard_map/ppermute | solution.py:45
  22.9 0.8 compare_reduce_fusion.1
  23.7 0.8 compare_reduce_fusion
  24.5 5.0 %collective-permute-start.1 = (f32[2,8,3840]{2,1,0:T(8,128)S(1)}, f32[2,8,3840]{2,1,0:T(8,128)S(1)}, u32[]{:S(2)}, u32[]{:S(2)}) collective-permute-start(f32[2,8,3840]{2,1,0:T(8,128)S(1)} %maximum_select_fusion.1), channel_id=1, source_target_pairs={{0,240},{16,0},{32,16},{48,32},{64,48},{80,64},{96,80},{112,96},{1... | collective-permute-start | bytes 737288 | tf_op jit(solution)/shard_map/ppermute | solution.py:43
  29.5 0.2 collective-permute-done.2
  29.7 6.7 %collective-permute-start.4 = (f32[2,8,3840]{2,1,0:T(8,128)S(1)}, f32[2,8,3840]{2,1,0:T(8,128)S(1)}, u32[]{:S(2)}, u32[]{:S(2)}) collective-permute-start(f32[2,8,3840]{2,1,0:T(8,128)S(1)} %collective-permute-done.2), channel_id=1, source_target_pairs={{0,224},{16,240},{32,0},{48,16},{64,32},{80,48},{96,64},{112,80},{... | collective-permute-start | bytes 737288 | tf_op jit(solution)/shard_map/ppermute | solution.py:46
  36.4 0.0 collective-permute-done.8
  36.4 1.9 %collective-permute-start.9 = (f32[2,8,3840]{2,1,0:T(8,128)S(1)}, f32[2,8,3840]{2,1,0:T(8,128)S(1)}, u32[]{:S(2)}, u32[]{:S(2)}) collective-permute-start(f32[2,8,3840]{2,1,0:T(8,128)S(1)} %collective-permute-done.8), channel_id=1, source_target_pairs={{0,32},{16,48},{32,64},{48,80},{64,96},{80,112},{96,128},{112,144}... | collective-permute-start | bytes 737288 | tf_op jit(solution)/shard_map/ppermute | solution.py:45
  38.4 1.3 fusion.21
  43.6 3.6 %collective-permute-start.16 = (f32[2,8,3840]{2,1,0:T(8,128)S(1)}, f32[2,8,3840]{2,1,0:T(8,128)S(1)}, u32[]{:S(2)}, u32[]{:S(2)}) collective-permute-start(f32[2,8,3840]{2,1,0:T(8,128)S(1)} %maximum_select_fusion.1), channel_id=1, source_target_pairs={{0,16},{16,32},{32,48},{48,64},{64,80},{80,96},{96,112},{112,128},... | collective-permute-start | bytes 737288 | tf_op jit(solution)/shard_map/ppermute | solution.py:42
  47.2 4.3 %collective-permute-start.3 = (f32[2,8,3840]{2,1,0:T(8,128)S(1)}, f32[2,8,3840]{2,1,0:T(8,128)S(1)}, u32[]{:S(2)}, u32[]{:S(2)}) collective-permute-start(f32[2,8,3840]{2,1,0:T(8,128)S(1)} %collective-permute-done.2), channel_id=1, source_target_pairs={{0,240},{16,0},{32,16},{48,32},{64,48},{80,64},{96,80},{112,96},{1... | collective-permute-start | bytes 737288 | tf_op jit(solution)/shard_map/ppermute | solution.py:43
  51.6 0.0 collective-permute-done.1
  51.6 0.0 collective-permute-done.4
  51.6 3.4 %collective-permute-start.5 = (f32[2,8,3840]{2,1,0:T(8,128)S(1)}, f32[2,8,3840]{2,1,0:T(8,128)S(1)}, u32[]{:S(2)}, u32[]{:S(2)}) collective-permute-start(f32[2,8,3840]{2,1,0:T(8,128)S(1)} %collective-permute-done.4), channel_id=1, source_target_pairs={{0,240},{16,0},{32,16},{48,32},{64,48},{80,64},{96,80},{112,96},{1... | collective-permute-start | bytes 737288 | tf_op jit(solution)/shard_map/ppermute | solution.py:43
  55.0 1.9 %collective-permute-start.6 = (f32[2,8,3840]{2,1,0:T(8,128)S(1)}, f32[2,8,3840]{2,1,0:T(8,128)S(1)}, u32[]{:S(2)}, u32[]{:S(2)}) collective-permute-start(f32[2,8,3840]{2,1,0:T(8,128)S(1)} %collective-permute-done.4), channel_id=1, source_target_pairs={{0,224},{16,240},{32,0},{48,16},{64,32},{80,48},{96,64},{112,80},{... | collective-permute-start | bytes 737288 | tf_op jit(solution)/shard_map/ppermute | solution.py:46
  56.9 0.0 collective-permute-done.9
  56.9 4.3 %collective-permute-start.10 = (f32[2,8,3840]{2,1,0:T(8,128)S(1)}, f32[2,8,3840]{2,1,0:T(8,128)S(1)}, u32[]{:S(2)}, u32[]{:S(2)}) collective-permute-start(f32[2,8,3840]{2,1,0:T(8,128)S(1)} %collective-permute-done.9), channel_id=1, source_target_pairs={{0,32},{16,48},{32,64},{48,80},{64,96},{80,112},{96,128},{112,144}... | collective-permute-start | bytes 737288 | tf_op jit(solution)/shard_map/ppermute | solution.py:45
  61.2 0.0 collective-permute-done.3
  61.2 1.9 %collective-permute-start.15 = (f32[2,8,3840]{2,1,0:T(8,128)S(1)}, f32[2,8,3840]{2,1,0:T(8,128)S(1)}, u32[]{:S(2)}, u32[]{:S(2)}) collective-permute-start(f32[2,8,3840]{2,1,0:T(8,128)S(1)} %collective-permute-done.8), channel_id=1, source_target_pairs={{0,16},{16,32},{32,48},{48,64},{64,80},{80,96},{96,112},{112,128},... | collective-permute-start | bytes 737288 | tf_op jit(solution)/shard_map/ppermute | solution.py:42
  63.2 7.9 %collective-permute-done.6 = f32[2,8,3840]{2,1,0:T(8,128)S(1)} collective-permute-done((f32[2,8,3840]{2,1,0:T(8,128)S(1)}, f32[2,8,3840]{2,1,0:T(8,128)S(1)}, u32[]{:S(2)}, u32[]{:S(2)}) %collective-permute-start.6) | collective-permute-done | bytes 245792 | tf_op jit(solution)/shard_map/ppermute | solution.py:46
  71.1 1.9 %collective-permute-start.14 = (f32[2,8,3840]{2,1,0:T(8,128)S(1)}, f32[2,8,3840]{2,1,0:T(8,128)S(1)}, u32[]{:S(2)}, u32[]{:S(2)}) collective-permute-start(f32[2,8,3840]{2,1,0:T(8,128)S(1)} %collective-permute-done.9), channel_id=1, source_target_pairs={{0,16},{16,32},{32,48},{48,64},{64,80},{80,96},{96,112},{112,128},... | collective-permute-start | bytes 737288 | tf_op jit(solution)/shard_map/ppermute | solution.py:42
  73.0 0.0 collective-permute-done.10
  73.0 5.9 %collective-permute-start.12 = (f32[2,8,1920]{2,1,0:T(8,128)S(1)}, f32[2,8,1920]{2,1,0:T(8,128)S(1)}, u32[]{:S(2)}, u32[]{:S(2)}) collective-permute-start(f32[2,8,1920]{2,1,0:T(8,128)S(1)} %slice.35), channel_id=1, source_target_pairs={{0,224},{16,240},{32,0},{48,16},{64,32},{80,48},{96,64},{112,80},{... | collective-permute-start | bytes 368648 | tf_op jit(solution)/shard_map/ppermute | solution.py:51
  79.0 0.0 collective-permute-done.5
  79.0 1.9 %collective-permute-start.11 = (f32[2,8,1920]{2,1,0:T(8,128)S(1)}, f32[2,8,1920]{2,1,0:T(8,128)S(1)}, u32[]{:S(2)}, u32[]{:S(2)}) collective-permute-start(f32[2,8,1920]{2,1,0:T(8,128)S(1)} %slice.34), channel_id=1, source_target_pairs={{0,32},{16,48},{32,64},{48,80},{64,96},{80,112},{96,128},{112,144}... | collective-permute-start | bytes 368648 | tf_op jit(solution)/shard_map/ppermute | solution.py:50
  81.0 0.9 collective-permute-done.12
  81.9 3.8 %collective-permute-start.7 = (f32[2,8,3840]{2,1,0:T(8,128)S(1)}, f32[2,8,3840]{2,1,0:T(8,128)S(1)}, u32[]{:S(2)}, u32[]{:S(2)}) collective-permute-start(f32[2,8,3840]{2,1,0:T(8,128)S(1)} %collective-permute-done.6), channel_id=1, source_target_pairs={{0,240},{16,0},{32,16},{48,32},{64,48},{80,64},{96,80},{112,96},{1... | collective-permute-start | bytes 737288 | tf_op jit(solution)/shard_map/ppermute | solution.py:43
  85.7 1.7 %collective-permute-done.11 = f32[2,8,1920]{2,1,0:T(8,128)S(1)} collective-permute-done((f32[2,8,1920]{2,1,0:T(8,128)S(1)}, f32[2,8,1920]{2,1,0:T(8,128)S(1)}, u32[]{:S(2)}, u32[]{:S(2)}) %collective-permute-start.11) | collective-permute-done | bytes 122912 | tf_op jit(solution)/shard_map/ppermute | solution.py:50
  87.4 2.4 %collective-permute-start.13 = (f32[2,8,3840]{2,1,0:T(8,128)S(1)}, f32[2,8,3840]{2,1,0:T(8,128)S(1)}, u32[]{:S(2)}, u32[]{:S(2)}) collective-permute-start(f32[2,8,3840]{2,1,0:T(8,128)S(1)} %collective-permute-done.10), channel_id=1, source_target_pairs={{0,16},{16,32},{32,48},{48,64},{64,80},{80,96},{96,112},{112,128},... | collective-permute-start | bytes 737288 | tf_op jit(solution)/shard_map/ppermute | solution.py:42
  89.8 0.0 collective-permute-done.7
  89.9 5.7 %collective-permute-done.13 = f32[2,8,3840]{2,1,0:T(8,128)S(1)} collective-permute-done((f32[2,8,3840]{2,1,0:T(8,128)S(1)}, f32[2,8,3840]{2,1,0:T(8,128)S(1)}, u32[]{:S(2)}, u32[]{:S(2)}) %collective-permute-start.13) | collective-permute-done | bytes 245792 | tf_op jit(solution)/shard_map/ppermute | solution.py:42
  95.7 0.0 collective-permute-done.15
  95.8 3.3 %fusion.4 = f32[2,16,8,5,384]{4,2,3,0,1:T(8,128)S(1)} fusion(f32[16,2,8,5,768]{4,2,3,1,0:T(8,128)S(1)} %constant_dynamic-update-slice_fusion.2, f32[5,768]{1,0:T(8,128)S(1)} %add_convert_fusion, f32[384,768]{1,0:T(8,128)S(1)} %copy-done), kind=kOutput, calls=%fused_computation.8 | convolution fusion | flops 2265907200 | bytes 7093248 | tf_op jit(solution)/shard_map/tlkmj,ij->ltkmi/dot_general | solution.py:121
  99.1 0.4 fusion.2
  99.5 0.0 copy-start.1
  99.5 0.2 copy.16
  99.7 0.1 slice.36
  99.7 0.1 constant_dynamic-slice_fusion.3
  99.8 0.7 copy-done.1
  100.5 0.6 fusion.8
  101.2 0.1 pad_maximum_fusion
  101.3 0.2 constant_dynamic-slice_fusion.1
  101.5 0.0 copy-start.2
  101.5 0.1 copy.24
  101.6 8.6 %collective-permute-start.17 = (f32[8,16,5,384]{3,1,2,0:T(8,128)S(1)}, f32[8,16,5,384]{3,1,2,0:T(8,128)S(1)}, u32[]{:S(2)}, u32[]{:S(2)}) collective-permute-start(f32[8,16,5,384]{3,1,2,0:T(8,128)S(1)} %bitcast.49), channel_id=1, source_target_pairs={{0,1},{1,0},{2,3},{3,2},{4,5},{5,4},{6,7},{7,6},{8,9},{9,8},{10,11... | collective-permute-start | bytes 2949128 | tf_op jit(solution)/shard_map/ppermute | solution.py:90
  110.1 2.2 %collective-permute-done.17 = f32[8,16,5,384]{3,1,2,0:T(8,128)S(1)} collective-permute-done((f32[8,16,5,384]{3,1,2,0:T(8,128)S(1)}, f32[8,16,5,384]{3,1,2,0:T(8,128)S(1)}, u32[]{:S(2)}, u32[]{:S(2)}) %collective-permute-start.17) | collective-permute-done | bytes 983072 | tf_op jit(solution)/shard_map/ppermute | solution.py:90
  112.3 1.1 bitcast_add_fusion
  113.4 6.7 %all-to-all-start = ((f32[8,16,5,384]{3,1,2,0:T(8,128)}), f32[8,16,5,384]{3,1,2,0:T(8,128)S(1)}, u32[]{:S(2)}, u32[]{:S(2)}) async-start(f32[8,16,5,384]{3,1,2,0:T(8,128)} %bitcast_add_fusion), calls=%async_computation | async-start | bytes 1966080 | tf_op jit(solution)/shard_map/all_to_all | solution.py:92
  120.0 0.1 compare_reduce_fusion.3
  120.2 13.7 %all-to-all-done = f32[8,16,5,384]{3,1,2,0:T(8,128)S(1)} async-done(((f32[8,16,5,384]{3,1,2,0:T(8,128)}), f32[8,16,5,384]{3,1,2,0:T(8,128)S(1)}, u32[]{:S(2)}, u32[]{:S(2)}) %all-to-all-start) | async-done | bytes 983072 | tf_op jit(solution)/shard_map/all_to_all | solution.py:92
  133.9 0.1 reduce_sum.9
  133.9 0.6 slice_multiply_fusion
  134.6 0.6 slice_multiply_fusion.1
  (31 shorter events, 0.4 us)
Async XLA Ops:
  0.6 95.1 %copy-start = (f32[384,768]{1,0:T(8,128)S(1)}, f32[384,768]{1,0:T(8,128)}, u32[]{:S(2)}) copy-start(f32[384,768]{1,0:T(8,128)} %param.7) | copy-start | bytes 3538948
  2.4 6.7 %collective-permute-start = (f32[8,3840]{1,0:T(8,128)S(1)}, f32[8,3840]{1,0:T(8,128)S(1)}, u32[]{:S(2)}, u32[]{:S(2)}) collective-permute-start(f32[8,3840]{1,0:T(8,128)S(1)} %bitcast.51), channel_id=1, source_target_pairs={{0,256},{16,272},{32,288},{48,304},{64,320},{80,336},{96,352},{112... | collective-permute-start | bytes 368648 | tf_op jit(solution)/shard_map/ppermute | solution.py:33
  9.2 20.5 %collective-permute-start.2 = (f32[2,8,3840]{2,1,0:T(8,128)S(1)}, f32[2,8,3840]{2,1,0:T(8,128)S(1)}, u32[]{:S(2)}, u32[]{:S(2)}) collective-permute-start(f32[2,8,3840]{2,1,0:T(8,128)S(1)} %maximum_select_fusion.1), channel_id=1, source_target_pairs={{0,224},{16,240},{32,0},{48,16},{64,32},{80,48},{96,64},{112,80},{... | collective-permute-start | bytes 737288 | tf_op jit(solution)/shard_map/ppermute | solution.py:46
  20.9 15.5 %collective-permute-start.8 = (f32[2,8,3840]{2,1,0:T(8,128)S(1)}, f32[2,8,3840]{2,1,0:T(8,128)S(1)}, u32[]{:S(2)}, u32[]{:S(2)}) collective-permute-start(f32[2,8,3840]{2,1,0:T(8,128)S(1)} %maximum_select_fusion.1), channel_id=1, source_target_pairs={{0,32},{16,48},{32,64},{48,80},{64,96},{80,112},{96,128},{112,144}... | collective-permute-start | bytes 737288 | tf_op jit(solution)/shard_map/ppermute | solution.py:45
  24.5 27.1 %collective-permute-start.1 = (f32[2,8,3840]{2,1,0:T(8,128)S(1)}, f32[2,8,3840]{2,1,0:T(8,128)S(1)}, u32[]{:S(2)}, u32[]{:S(2)}) collective-permute-start(f32[2,8,3840]{2,1,0:T(8,128)S(1)} %maximum_select_fusion.1), channel_id=1, source_target_pairs={{0,240},{16,0},{32,16},{48,32},{64,48},{80,64},{96,80},{112,96},{1... | collective-permute-start | bytes 737288 | tf_op jit(solution)/shard_map/ppermute | solution.py:43
  29.7 21.9 %collective-permute-start.4 = (f32[2,8,3840]{2,1,0:T(8,128)S(1)}, f32[2,8,3840]{2,1,0:T(8,128)S(1)}, u32[]{:S(2)}, u32[]{:S(2)}) collective-permute-start(f32[2,8,3840]{2,1,0:T(8,128)S(1)} %collective-permute-done.2), channel_id=1, source_target_pairs={{0,224},{16,240},{32,0},{48,16},{64,32},{80,48},{96,64},{112,80},{... | collective-permute-start | bytes 737288 | tf_op jit(solution)/shard_map/ppermute | solution.py:46
  36.4 20.5 %collective-permute-start.9 = (f32[2,8,3840]{2,1,0:T(8,128)S(1)}, f32[2,8,3840]{2,1,0:T(8,128)S(1)}, u32[]{:S(2)}, u32[]{:S(2)}) collective-permute-start(f32[2,8,3840]{2,1,0:T(8,128)S(1)} %collective-permute-done.8), channel_id=1, source_target_pairs={{0,32},{16,48},{32,64},{48,80},{64,96},{80,112},{96,128},{112,144}... | collective-permute-start | bytes 737288 | tf_op jit(solution)/shard_map/ppermute | solution.py:45
  43.6 52.1 %collective-permute-start.16 = (f32[2,8,3840]{2,1,0:T(8,128)S(1)}, f32[2,8,3840]{2,1,0:T(8,128)S(1)}, u32[]{:S(2)}, u32[]{:S(2)}) collective-permute-start(f32[2,8,3840]{2,1,0:T(8,128)S(1)} %maximum_select_fusion.1), channel_id=1, source_target_pairs={{0,16},{16,32},{32,48},{48,64},{64,80},{80,96},{96,112},{112,128},... | collective-permute-start | bytes 737288 | tf_op jit(solution)/shard_map/ppermute | solution.py:42
  47.2 14.0 %collective-permute-start.3 = (f32[2,8,3840]{2,1,0:T(8,128)S(1)}, f32[2,8,3840]{2,1,0:T(8,128)S(1)}, u32[]{:S(2)}, u32[]{:S(2)}) collective-permute-start(f32[2,8,3840]{2,1,0:T(8,128)S(1)} %collective-permute-done.2), channel_id=1, source_target_pairs={{0,240},{16,0},{32,16},{48,32},{64,48},{80,64},{96,80},{112,96},{1... | collective-permute-start | bytes 737288 | tf_op jit(solution)/shard_map/ppermute | solution.py:43
  51.6 27.4 %collective-permute-start.5 = (f32[2,8,3840]{2,1,0:T(8,128)S(1)}, f32[2,8,3840]{2,1,0:T(8,128)S(1)}, u32[]{:S(2)}, u32[]{:S(2)}) collective-permute-start(f32[2,8,3840]{2,1,0:T(8,128)S(1)} %collective-permute-done.4), channel_id=1, source_target_pairs={{0,240},{16,0},{32,16},{48,32},{64,48},{80,64},{96,80},{112,96},{1... | collective-permute-start | bytes 737288 | tf_op jit(solution)/shard_map/ppermute | solution.py:43
  55.0 16.1 %collective-permute-start.6 = (f32[2,8,3840]{2,1,0:T(8,128)S(1)}, f32[2,8,3840]{2,1,0:T(8,128)S(1)}, u32[]{:S(2)}, u32[]{:S(2)}) collective-permute-start(f32[2,8,3840]{2,1,0:T(8,128)S(1)} %collective-permute-done.4), channel_id=1, source_target_pairs={{0,224},{16,240},{32,0},{48,16},{64,32},{80,48},{96,64},{112,80},{... | collective-permute-start | bytes 737288 | tf_op jit(solution)/shard_map/ppermute | solution.py:46
  56.9 16.1 %collective-permute-start.10 = (f32[2,8,3840]{2,1,0:T(8,128)S(1)}, f32[2,8,3840]{2,1,0:T(8,128)S(1)}, u32[]{:S(2)}, u32[]{:S(2)}) collective-permute-start(f32[2,8,3840]{2,1,0:T(8,128)S(1)} %collective-permute-done.9), channel_id=1, source_target_pairs={{0,32},{16,48},{32,64},{48,80},{64,96},{80,112},{96,128},{112,144}... | collective-permute-start | bytes 737288 | tf_op jit(solution)/shard_map/ppermute | solution.py:45
  61.2 34.4 %collective-permute-start.15 = (f32[2,8,3840]{2,1,0:T(8,128)S(1)}, f32[2,8,3840]{2,1,0:T(8,128)S(1)}, u32[]{:S(2)}, u32[]{:S(2)}) collective-permute-start(f32[2,8,3840]{2,1,0:T(8,128)S(1)} %collective-permute-done.8), channel_id=1, source_target_pairs={{0,16},{16,32},{32,48},{48,64},{64,80},{80,96},{96,112},{112,128},... | collective-permute-start | bytes 737288 | tf_op jit(solution)/shard_map/ppermute | solution.py:42
  71.1 24.5 %collective-permute-start.14 = (f32[2,8,3840]{2,1,0:T(8,128)S(1)}, f32[2,8,3840]{2,1,0:T(8,128)S(1)}, u32[]{:S(2)}, u32[]{:S(2)}) collective-permute-start(f32[2,8,3840]{2,1,0:T(8,128)S(1)} %collective-permute-done.9), channel_id=1, source_target_pairs={{0,16},{16,32},{32,48},{48,64},{64,80},{80,96},{96,112},{112,128},... | collective-permute-start | bytes 737288 | tf_op jit(solution)/shard_map/ppermute | solution.py:42
  73.0 8.9 %collective-permute-start.12 = (f32[2,8,1920]{2,1,0:T(8,128)S(1)}, f32[2,8,1920]{2,1,0:T(8,128)S(1)}, u32[]{:S(2)}, u32[]{:S(2)}) collective-permute-start(f32[2,8,1920]{2,1,0:T(8,128)S(1)} %slice.35), channel_id=1, source_target_pairs={{0,224},{16,240},{32,0},{48,16},{64,32},{80,48},{96,64},{112,80},{... | collective-permute-start | bytes 368648 | tf_op jit(solution)/shard_map/ppermute | solution.py:51
  79.0 8.4 %collective-permute-start.11 = (f32[2,8,1920]{2,1,0:T(8,128)S(1)}, f32[2,8,1920]{2,1,0:T(8,128)S(1)}, u32[]{:S(2)}, u32[]{:S(2)}) collective-permute-start(f32[2,8,1920]{2,1,0:T(8,128)S(1)} %slice.34), channel_id=1, source_target_pairs={{0,32},{16,48},{32,64},{48,80},{64,96},{80,112},{96,128},{112,144}... | collective-permute-start | bytes 368648 | tf_op jit(solution)/shard_map/ppermute | solution.py:50
  81.9 7.9 %collective-permute-start.7 = (f32[2,8,3840]{2,1,0:T(8,128)S(1)}, f32[2,8,3840]{2,1,0:T(8,128)S(1)}, u32[]{:S(2)}, u32[]{:S(2)}) collective-permute-start(f32[2,8,3840]{2,1,0:T(8,128)S(1)} %collective-permute-done.6), channel_id=1, source_target_pairs={{0,240},{16,0},{32,16},{48,32},{64,48},{80,64},{96,80},{112,96},{1... | collective-permute-start | bytes 737288 | tf_op jit(solution)/shard_map/ppermute | solution.py:43
  87.4 8.1 %collective-permute-start.13 = (f32[2,8,3840]{2,1,0:T(8,128)S(1)}, f32[2,8,3840]{2,1,0:T(8,128)S(1)}, u32[]{:S(2)}, u32[]{:S(2)}) collective-permute-start(f32[2,8,3840]{2,1,0:T(8,128)S(1)} %collective-permute-done.10), channel_id=1, source_target_pairs={{0,16},{16,32},{32,48},{48,64},{64,80},{80,96},{96,112},{112,128},... | collective-permute-start | bytes 737288 | tf_op jit(solution)/shard_map/ppermute | solution.py:42
  99.5 1.0 copy-start.1
  101.5 18.6 %copy-start.2 = (s32[2,36]{1,0:T(2,128)S(1)}, s32[2,36]{1,0:T(2,128)}, u32[]{:S(2)}) copy-start(s32[2,36]{1,0:T(2,128)} %param.11) | copy-start | bytes 868
  101.6 10.7 %collective-permute-start.17 = (f32[8,16,5,384]{3,1,2,0:T(8,128)S(1)}, f32[8,16,5,384]{3,1,2,0:T(8,128)S(1)}, u32[]{:S(2)}, u32[]{:S(2)}) collective-permute-start(f32[8,16,5,384]{3,1,2,0:T(8,128)S(1)} %bitcast.49), channel_id=1, source_target_pairs={{0,1},{1,0},{2,3},{3,2},{4,5},{5,4},{6,7},{7,6},{8,9},{9,8},{10,11... | collective-permute-start | bytes 2949128 | tf_op jit(solution)/shard_map/ppermute | solution.py:90
  113.4 20.5 %all-to-all-start = ((f32[8,16,5,384]{3,1,2,0:T(8,128)}), f32[8,16,5,384]{3,1,2,0:T(8,128)S(1)}, u32[]{:S(2)}, u32[]{:S(2)}) async-start(f32[8,16,5,384]{3,1,2,0:T(8,128)} %bitcast_add_fusion), calls=%async_computation | async-start | bytes 1966080 | tf_op jit(solution)/shard_map/all_to_all | solution.py:92
